TPU v7x, 32 devices: a whole 2x2x4 slice. The times are simulated.
32 devices in a mesh: ctx: 4 (over y, core), uly: 4 (over z), dp: 2 (over x).
Axes of the slice: x: 2, y: 2, z: 4, core: 2. Of those that a mesh axis runs over, the one named last changes fastest.
Arguments:
- queries: bfloat16 [4096, 4096], P(('dp', 'ctx', 'uly')), parts along dimension 0, may hold values from -110 to 110
- key_vectors: bfloat16 [4096, 512], P(('dp', 'ctx', 'uly')), parts along dimension 0, may hold values from -4 to 4
- value_vectors: bfloat16 [4096, 512], P(('dp', 'ctx', 'uly')), parts along dimension 0, may hold values from -6 to 6
- output_grad: bfloat16 [4096, 4096], P(('dp', 'ctx', 'uly')), parts along dimension 0, may hold values from -2 to 2
- doc_lengths: int32 [32], P('dp'), parts along dimension 0, may hold values from 1 to 256, 2048 in all
Outputs:
- query_grad: bfloat16 [4096, 4096], P(('dp', 'ctx', 'uly')), parts along dimension 0
- key_grad: bfloat16 [4096, 512], P(('dp', 'ctx', 'uly')), parts along dimension 0
There are 2 independent parts, one for each index of `dp`. A program takes and returns all parts, laid end to end along the dimension named above; each array names one. Nothing has to cross between parts.
Inputs may be any that keep to these rules, and one draw needn't show every extreme that they name: `doc_lengths`: the 16 lengths sum to 2048, and the longest is exactly 256.
All inputs are finite; a program needn't handle non-finite values.
Results may differ from a plain program's by a relative error of at most 0.015.
Values may be sent and summed in bfloat16 or wider, within the bound.
No kernel may reach another device: no remote copies, remote signals or barrier semaphores. Data moves between devices by JAX's collectives and lax.ppermute only.
A program may use at most 64 MiB of HBM per device.

v0:
```python
import jax
import jax.numpy as jnp
from jax import lax
from jax.sharding import PartitionSpec as P

QH = 32
KVH = 4
HD = 128
GROUP = 8


def shifted(block, axis, distance):
    devices = range(lax.axis_size(axis))
    route = [(i - distance, i) for i in devices if i - distance in devices]
    return lax.ppermute(block, axis, route)


def doc_index(doc_lengths, positions):
    doc_ends = jnp.cumsum(doc_lengths)
    counted = jnp.sum((positions[:, None] >= doc_ends[None, :]).astype(jnp.int32), axis=1)
    return jnp.where(positions < 0, -1, counted)


def head_grads(query_block, grad_block, key_window, value_window, allowed, score_scale):
    scores = (
        jnp.einsum("tgd,sd->gts", query_block, key_window, preferred_element_type=jnp.float32)
        * score_scale
    )
    scores = jnp.where(allowed[None], scores, -1e30)
    row_max = jnp.max(scores, axis=-1, keepdims=True)
    weights_raw = jnp.exp(scores - row_max)
    prob_full = weights_raw / jnp.sum(weights_raw, axis=-1, keepdims=True)
    grad_p = jnp.einsum("tgd,sd->gts", grad_block, value_window, preferred_element_type=jnp.float32)
    row_delta = jnp.sum(prob_full * grad_p, axis=-1, keepdims=True)
    grad_s = (prob_full * (grad_p - row_delta)).astype(jnp.bfloat16)
    grad_q = (
        jnp.einsum("gts,sd->tgd", grad_s, key_window, preferred_element_type=jnp.float32)
        * score_scale
    )
    grad_k = (
        jnp.einsum("gts,tgd->sd", grad_s, query_block, preferred_element_type=jnp.float32)
        * score_scale
    )
    return (grad_q.astype(jnp.bfloat16), grad_k)


def allowed_pairs(doc_lengths, query_pos, key_pos):
    query_docs = doc_index(doc_lengths, query_pos)
    key_docs = doc_index(doc_lengths, key_pos)
    return (query_docs[:, None] == key_docs[None, :]) & (key_pos[None, :] <= query_pos[:, None])


def fetch_rim(key_value, places):
    return shifted(key_value, ("ctx", "uly"), places)


def send_back(partial_grads, places):
    return shifted(partial_grads, ("ctx", "uly"), places)


def body(queries, key_vectors, value_vectors, output_grad, doc_lengths):
    block_rows = queries.shape[0]
    score_scale = HD ** (-0.5)
    key_value = jnp.stack([key_vectors, value_vectors])
    device_index = lax.axis_index(("ctx", "uly"))
    near_rim = fetch_rim(key_value, 1)
    far_rim = fetch_rim(key_value, 2)
    window = jnp.concatenate([far_rim, near_rim, key_value], axis=1)
    window_heads = jnp.transpose(window.reshape(2, 3 * block_rows, KVH, HD), (0, 2, 1, 3))
    query_heads = jnp.transpose(queries.reshape(block_rows, KVH, GROUP, HD), (1, 0, 2, 3))
    grad_heads = jnp.transpose(output_grad.reshape(block_rows, KVH, GROUP, HD), (1, 0, 2, 3))
    query_pos = device_index * block_rows + jnp.arange(block_rows, dtype=jnp.int32)
    key_pos = (
        device_index * block_rows - 2 * block_rows + jnp.arange(3 * block_rows, dtype=jnp.int32)
    )
    allowed = allowed_pairs(doc_lengths, query_pos, key_pos)

    def per_head(head_item):
        return head_grads(
            head_item[0], head_item[1], head_item[2], head_item[3], allowed, score_scale
        )

    grad_q, grad_k = lax.map(per_head, (query_heads, grad_heads, window_heads[0], window_heads[1]))
    query_grad = jnp.transpose(grad_q, (1, 0, 2, 3)).reshape(block_rows, QH * HD)
    window_grad = jnp.transpose(grad_k, (1, 0, 2)).reshape(3 * block_rows, KVH * HD)
    own_part = (
        window_grad[2 * block_rows :]
        + send_back(window_grad[block_rows : 2 * block_rows], -1)
        + send_back(window_grad[:block_rows], -2)
    )
    key_grad = own_part.astype(jnp.bfloat16)
    return (query_grad, key_grad)


def solution(mesh):
    placed = (
        P(("dp", "ctx", "uly"), None),
        P(("dp", "ctx", "uly"), None),
        P(("dp", "ctx", "uly"), None),
        P(("dp", "ctx", "uly"), None),
        P("dp"),
    )
    return jax.shard_map(
        body,
        mesh=mesh,
        in_specs=placed,
        out_specs=(P(("dp", "ctx", "uly"), None), P(("dp", "ctx", "uly"), None)),
        check_vma=False,
    )
```

profile of v0, /device:TPU:1, one launch (start us, length us, event | category | flops | bytes accessed | tf_op | source)
XLA Modules:
  0.0 67.9 jit_solution(4971085478960169539)
XLA Ops:
  0.6 1.2 %copy.31 = bf16[128,512]{0,1:T(8,128)(2,1)S(1)} copy(bf16[128,512]{1,0:T(8,128)(2,1)} %param.8) | data formatting | bytes 262144 | tf_op args[1]
  1.8 1.0 %copy.32 = bf16[128,512]{0,1:T(8,128)(2,1)S(1)} copy(bf16[128,512]{1,0:T(8,128)(2,1)} %param.9) | data formatting | bytes 262144 | tf_op args[2]
  2.9 5.0 %collective-permute-start = (bf16[2,128,512]{1,2,0:T(8,128)(2,1)S(1)}, bf16[2,128,512]{1,2,0:T(8,128)(2,1)S(1)}, u32[]{:S(2)}, u32[]{:S(2)}) collective-permute-start(bf16[2,128,512]{1,2,0:T(8,128)(2,1)S(1)} %pad_maximum_fusion), channel_id=1, source_target_pairs={{0,4},{2,6},{4,8},{6,10},{8,12},{10,14},{12,16},{14,18},{16,20},{1... | collective-permute-start | bytes 786440 | tf_op jit(solution)/shard_map/ppermute | solution.py:15
  7.9 3.2 %collective-permute-start.1 = (bf16[2,128,512]{1,2,0:T(8,128)(2,1)S(1)}, bf16[2,128,512]{1,2,0:T(8,128)(2,1)S(1)}, u32[]{:S(2)}, u32[]{:S(2)}) collective-permute-start(bf16[2,128,512]{1,2,0:T(8,128)(2,1)S(1)} %pad_maximum_fusion), channel_id=1, source_target_pairs={{0,2},{2,4},{4,6},{6,8},{8,10},{10,12},{12,14},{14,16},{16,18},{18... | collective-permute-start | bytes 786440 | tf_op jit(solution)/shard_map/ppermute | solution.py:15
  12.3 1.3 %copy.34 = bf16[128,4096]{0,1:T(8,128)(2,1)} copy(bf16[128,4096]{1,0:T(8,128)(2,1)S(1)} %copy-done) | data formatting | bytes 2097152 | tf_op args[3]
  14.3 11.7 %collective-permute-done = bf16[2,128,512]{1,2,0:T(8,128)(2,1)S(1)} collective-permute-done((bf16[2,128,512]{1,2,0:T(8,128)(2,1)S(1)}, bf16[2,128,512]{1,2,0:T(8,128)(2,1)S(1)}, u32[]{:S(2)}, u32[]{:S(2)}) %collective-permute-start) | collective-permute-done | bytes 262176 | tf_op jit(solution)/shard_map/ppermute | solution.py:15
  26.1 18.1 %while.13 = (s32[]{:T(128)}, bf16[4,128,8,128]{1,3,2,0:T(8,128)(2,1)}, f32[4,384,128]{2,1,0:T(8,128)}, bf16[4,384,128]{1,2,0:T(8,128)(2,1)S(1)}, bf16[4,128,8,12...) while((s32[]{:T(128)}, ...), condition=%wide.region_7.8_spmd.clone, body=%wide.region_3.7_spmd.clone.sunk | while | flops 407436672 | bytes 11890805 | solution.py:83
  27.0 1.3 %fusion.73 = (f32[8,128]{1,0:T(8,128)S(1)}, f32[384,128,8]{1,0,2:T(8,128)S(1)}) fusion(f32[8,128,384]{1,2,0:T(8,128)S(1)} %get-tuple-element.199, f32[8,128]{1,0:T(8,128)S(1)} %get-tuple-element.200, bf16[4,128,8,128]{1,3,2,0:T(8,128)(2,1)} %get-tuple-element.233, s32[]{:T(128)} %get-tuple-element.215, bf16[4,384,128]{1,2,0:T(8,128)(2,1)S(1)} %get-tuple-element.232), kind=kOutput, calls=%fused_computation.5.clone.1 | convolution fusion | flops 101841920 | bytes 3515392 | tf_op jit(solution)/shard_map/while/body/eval_jaxpr/tgd,sd->gts/dot_general | solution.py:33
  28.6 1.0 %fusion.75 = bf16[4,128,8,128]{1,3,2,0:T(8,128)(2,1)} fusion(bf16[4,128,8,128]{1,3,2,0:T(8,128)(2,1)} %get-tuple-element.216, s32[]{:T(128)} %get-tuple-element.215, bf16[8,128,384]{1,2,0:T(8,128)(2,1)S(1)} %fusion.74, bf16[4,384,128]{1,2,0:T(8,128)(2,1)S(1)} %get-tuple-element.230), kind=kOutput, calls=%fused_computation.13.clone.1 | convolution fusion | flops 100925440 | bytes 1147904 | tf_op jit(solution)/shard_map/while/body/eval_jaxpr/gts,sd->tgd/dot_general | solution.py:37
  29.6 1.1 %fusion.76 = f32[4,384,128]{2,1,0:T(8,128)} fusion(f32[4,384,128]{2,1,0:T(8,128)} %get-tuple-element.217, s32[]{:T(128)} %get-tuple-element.215, bf16[8,128,384]{1,2,0:T(8,128)(2,1)S(1)} %fusion.74, bf16[4,128,8,128]{1,3,2,0:T(8,128)(2,1)S(1)} %get-tuple-element.231), kind=kOutput, calls=%fused_computation.17.clone.1 | convolution fusion | flops 100712448 | bytes 1246208 | tf_op jit(solution)/shard_map/while/body/eval_jaxpr/gts,tgd->sd/dot_general | solution.py:41
  31.5 1.3 %fusion.73 = (f32[8,128]{1,0:T(8,128)S(1)}, f32[384,128,8]{1,0,2:T(8,128)S(1)}) fusion(f32[8,128,384]{1,2,0:T(8,128)S(1)} %get-tuple-element.199, f32[8,128]{1,0:T(8,128)S(1)} %get-tuple-element.200, bf16[4,128,8,128]{1,3,2,0:T(8,128)(2,1)} %get-tuple-element.233, s32[]{:T(128)} %get-tuple-element.215, bf16[4,384,128]{1,2,0:T(8,128)(2,1)S(1)} %get-tuple-element.232), kind=kOutput, calls=%fused_computation.5.clone.1 | convolution fusion | flops 101841920 | bytes 3515392 | tf_op jit(solution)/shard_map/while/body/eval_jaxpr/tgd,sd->gts/dot_general | solution.py:33
  33.1 1.0 %fusion.75 = bf16[4,128,8,128]{1,3,2,0:T(8,128)(2,1)} fusion(bf16[4,128,8,128]{1,3,2,0:T(8,128)(2,1)} %get-tuple-element.216, s32[]{:T(128)} %get-tuple-element.215, bf16[8,128,384]{1,2,0:T(8,128)(2,1)S(1)} %fusion.74, bf16[4,384,128]{1,2,0:T(8,128)(2,1)S(1)} %get-tuple-element.230), kind=kOutput, calls=%fused_computation.13.clone.1 | convolution fusion | flops 100925440 | bytes 1147904 | tf_op jit(solution)/shard_map/while/body/eval_jaxpr/gts,sd->tgd/dot_general | solution.py:37
  34.1 1.0 %fusion.76 = f32[4,384,128]{2,1,0:T(8,128)} fusion(f32[4,384,128]{2,1,0:T(8,128)} %get-tuple-element.217, s32[]{:T(128)} %get-tuple-element.215, bf16[8,128,384]{1,2,0:T(8,128)(2,1)S(1)} %fusion.74, bf16[4,128,8,128]{1,3,2,0:T(8,128)(2,1)S(1)} %get-tuple-element.231), kind=kOutput, calls=%fused_computation.17.clone.1 | convolution fusion | flops 100712448 | bytes 1246208 | tf_op jit(solution)/shard_map/while/body/eval_jaxpr/gts,tgd->sd/dot_general | solution.py:41
  36.0 1.3 %fusion.73 = (f32[8,128]{1,0:T(8,128)S(1)}, f32[384,128,8]{1,0,2:T(8,128)S(1)}) fusion(f32[8,128,384]{1,2,0:T(8,128)S(1)} %get-tuple-element.199, f32[8,128]{1,0:T(8,128)S(1)} %get-tuple-element.200, bf16[4,128,8,128]{1,3,2,0:T(8,128)(2,1)} %get-tuple-element.233, s32[]{:T(128)} %get-tuple-element.215, bf16[4,384,128]{1,2,0:T(8,128)(2,1)S(1)} %get-tuple-element.232), kind=kOutput, calls=%fused_computation.5.clone.1 | convolution fusion | flops 101841920 | bytes 3515392 | tf_op jit(solution)/shard_map/while/body/eval_jaxpr/tgd,sd->gts/dot_general | solution.py:33
  37.6 1.0 %fusion.75 = bf16[4,128,8,128]{1,3,2,0:T(8,128)(2,1)} fusion(bf16[4,128,8,128]{1,3,2,0:T(8,128)(2,1)} %get-tuple-element.216, s32[]{:T(128)} %get-tuple-element.215, bf16[8,128,384]{1,2,0:T(8,128)(2,1)S(1)} %fusion.74, bf16[4,384,128]{1,2,0:T(8,128)(2,1)S(1)} %get-tuple-element.230), kind=kOutput, calls=%fused_computation.13.clone.1 | convolution fusion | flops 100925440 | bytes 1147904 | tf_op jit(solution)/shard_map/while/body/eval_jaxpr/gts,sd->tgd/dot_general | solution.py:37
  38.7 1.1 %fusion.76 = f32[4,384,128]{2,1,0:T(8,128)} fusion(f32[4,384,128]{2,1,0:T(8,128)} %get-tuple-element.217, s32[]{:T(128)} %get-tuple-element.215, bf16[8,128,384]{1,2,0:T(8,128)(2,1)S(1)} %fusion.74, bf16[4,128,8,128]{1,3,2,0:T(8,128)(2,1)S(1)} %get-tuple-element.231), kind=kOutput, calls=%fused_computation.17.clone.1 | convolution fusion | flops 100712448 | bytes 1246208 | tf_op jit(solution)/shard_map/while/body/eval_jaxpr/gts,tgd->sd/dot_general | solution.py:41
  40.6 1.3 %fusion.73 = (f32[8,128]{1,0:T(8,128)S(1)}, f32[384,128,8]{1,0,2:T(8,128)S(1)}) fusion(f32[8,128,384]{1,2,0:T(8,128)S(1)} %get-tuple-element.199, f32[8,128]{1,0:T(8,128)S(1)} %get-tuple-element.200, bf16[4,128,8,128]{1,3,2,0:T(8,128)(2,1)} %get-tuple-element.233, s32[]{:T(128)} %get-tuple-element.215, bf16[4,384,128]{1,2,0:T(8,128)(2,1)S(1)} %get-tuple-element.232), kind=kOutput, calls=%fused_computation.5.clone.1 | convolution fusion | flops 101841920 | bytes 3515392 | tf_op jit(solution)/shard_map/while/body/eval_jaxpr/tgd,sd->gts/dot_general | solution.py:33
  42.2 1.0 %fusion.75 = bf16[4,128,8,128]{1,3,2,0:T(8,128)(2,1)} fusion(bf16[4,128,8,128]{1,3,2,0:T(8,128)(2,1)} %get-tuple-element.216, s32[]{:T(128)} %get-tuple-element.215, bf16[8,128,384]{1,2,0:T(8,128)(2,1)S(1)} %fusion.74, bf16[4,384,128]{1,2,0:T(8,128)(2,1)S(1)} %get-tuple-element.230), kind=kOutput, calls=%fused_computation.13.clone.1 | convolution fusion | flops 100925440 | bytes 1147904 | tf_op jit(solution)/shard_map/while/body/eval_jaxpr/gts,sd->tgd/dot_general | solution.py:37
  43.2 1.0 %fusion.76 = f32[4,384,128]{2,1,0:T(8,128)} fusion(f32[4,384,128]{2,1,0:T(8,128)} %get-tuple-element.217, s32[]{:T(128)} %get-tuple-element.215, bf16[8,128,384]{1,2,0:T(8,128)(2,1)S(1)} %fusion.74, bf16[4,128,8,128]{1,3,2,0:T(8,128)(2,1)S(1)} %get-tuple-element.231), kind=kOutput, calls=%fused_computation.17.clone.1 | convolution fusion | flops 100712448 | bytes 1246208 | tf_op jit(solution)/shard_map/while/body/eval_jaxpr/gts,tgd->sd/dot_general | solution.py:41
  44.3 1.2 %slice_bitcast_fusion.4 = (f32[4,16,8,128]{3,2,1,0:T(8,128)S(1)}, f32[4,16,8,128]{3,2,1,0:T(8,128)S(1)}, f32[4,16,8,128]{3,2,1,0:T(8,128)S(1)}) fusion(f32[384,4,128]{2,0,1:T(8,128)} %bitcast.14), kind=kLoop, calls=%fused_computation.53 | loop fusion | bytes 1572864
  45.4 1.9 %collective-permute-start.2 = (f32[128,512]{1,0:T(8,128)S(1)}, f32[128,512]{1,0:T(8,128)S(1)}, u32[]{:S(2)}, u32[]{:S(2)}) collective-permute-start(f32[128,512]{1,0:T(8,128)S(1)} %bitcast.153), channel_id=1, source_target_pairs={{2,0},{4,2},{6,4},{8,6},{10,8},{12,10},{14,12},{16,14},{18,16},{20... | collective-permute-start | bytes 786440 | tf_op jit(solution)/shard_map/ppermute | solution.py:15
  47.4 4.7 %collective-permute-start.3 = (f32[128,512]{1,0:T(8,128)S(1)}, f32[128,512]{1,0:T(8,128)S(1)}, u32[]{:S(2)}, u32[]{:S(2)}) collective-permute-start(f32[128,512]{1,0:T(8,128)S(1)} %bitcast.154), channel_id=1, source_target_pairs={{4,0},{6,2},{8,4},{10,6},{12,8},{14,10},{16,12},{18,14},{20,16},{2... | collective-permute-start | bytes 786440 | tf_op jit(solution)/shard_map/ppermute | solution.py:15
  52.1 2.3 %copy.46 = bf16[128,4096]{1,0:T(8,128)(2,1)} copy(bf16[128,4096]{0,1:T(8,128)(2,1)} %bitcast.13) | data formatting | bytes 2097152 | tf_op jit(solution)/shard_map/reshape | solution.py:84
  55.1 12.1 %collective-permute-done.3 = f32[128,512]{1,0:T(8,128)S(1)} collective-permute-done((f32[128,512]{1,0:T(8,128)S(1)}, f32[128,512]{1,0:T(8,128)S(1)}, u32[]{:S(2)}, u32[]{:S(2)}) %collective-permute-start.3) | collective-permute-done | bytes 262176 | tf_op jit(solution)/shard_map/ppermute | solution.py:15
  (36 shorter events, 7.8 us)
Async XLA Ops:
  0.6 11.6 %copy-start = (bf16[128,4096]{1,0:T(8,128)(2,1)S(1)}, bf16[128,4096]{1,0:T(8,128)(2,1)}, u32[]{:S(2)}) copy-start(bf16[128,4096]{1,0:T(8,128)(2,1)} %param.10) | copy-start | bytes 3145732
  0.6 13.0 %copy-start.1 = (bf16[128,4096]{1,0:T(8,128)(2,1)S(1)}, bf16[128,4096]{1,0:T(8,128)(2,1)}, u32[]{:S(2)}) copy-start(bf16[128,4096]{1,0:T(8,128)(2,1)} %param.7) | copy-start | bytes 3145732
  2.9 23.0 %collective-permute-start = (bf16[2,128,512]{1,2,0:T(8,128)(2,1)S(1)}, bf16[2,128,512]{1,2,0:T(8,128)(2,1)S(1)}, u32[]{:S(2)}, u32[]{:S(2)}) collective-permute-start(bf16[2,128,512]{1,2,0:T(8,128)(2,1)S(1)} %pad_maximum_fusion), channel_id=1, source_target_pairs={{0,4},{2,6},{4,8},{6,10},{8,12},{10,14},{12,16},{14,18},{16,20},{1... | collective-permute-start | bytes 786440 | tf_op jit(solution)/shard_map/ppermute | solution.py:15
  7.9 18.0 %collective-permute-start.1 = (bf16[2,128,512]{1,2,0:T(8,128)(2,1)S(1)}, bf16[2,128,512]{1,2,0:T(8,128)(2,1)S(1)}, u32[]{:S(2)}, u32[]{:S(2)}) collective-permute-start(bf16[2,128,512]{1,2,0:T(8,128)(2,1)S(1)} %pad_maximum_fusion), channel_id=1, source_target_pairs={{0,2},{2,4},{4,6},{6,8},{8,10},{10,12},{12,14},{14,16},{16,18},{18... | collective-permute-start | bytes 786440 | tf_op jit(solution)/shard_map/ppermute | solution.py:15
  45.4 9.6 %collective-permute-start.2 = (f32[128,512]{1,0:T(8,128)S(1)}, f32[128,512]{1,0:T(8,128)S(1)}, u32[]{:S(2)}, u32[]{:S(2)}) collective-permute-start(f32[128,512]{1,0:T(8,128)S(1)} %bitcast.153), channel_id=1, source_target_pairs={{2,0},{4,2},{6,4},{8,6},{10,8},{12,10},{14,12},{16,14},{18,16},{20... | collective-permute-start | bytes 786440 | tf_op jit(solution)/shard_map/ppermute | solution.py:15
  47.4 19.8 %collective-permute-start.3 = (f32[128,512]{1,0:T(8,128)S(1)}, f32[128,512]{1,0:T(8,128)S(1)}, u32[]{:S(2)}, u32[]{:S(2)}) collective-permute-start(f32[128,512]{1,0:T(8,128)S(1)} %bitcast.154), channel_id=1, source_target_pairs={{4,0},{6,2},{8,4},{10,6},{12,8},{14,10},{16,12},{18,14},{20,16},{2... | collective-permute-start | bytes 786440 | tf_op jit(solution)/shard_map/ppermute | solution.py:15
where the time goes:
time: 69.3 us; the launch traced here: 67.9 us
  waiting for transfers between devices  24.5 us (35%)
  matrix products  16.3 us (24%)
  starting transfers between devices  14.9 us (22%)
  local copies, waits for them, and re-layouts  8.45 us (12%)
  other arithmetic  2.88 us (4%)
  between operations  0.79 us (1%)
    ppermute x4, waiting for transfers between devices, shifted(): return lax.ppermute(block, axis, route)  24.5 us
    ppermute x4, starting transfers between devices, shifted(): return lax.ppermute(block, axis, route)  14.9 us
    dot_general x4, matrix products, head_grads(): jnp.einsum('tgd,sd->gts', grad_block, value_window, preferred_element_typ...  5.39 us
    unnamed x9, local copies, waits for them, and re-layouts  5.32 us
    dot_general x4, matrix products, head_grads(): jnp.einsum('gts,tgd->sd', grad_s, query_block, preferred_element_type=jnp...  4.2 us
    dot_general x4, matrix products, head_grads(): jnp.einsum('gts,sd->tgd', grad_s, key_window, preferred_element_type=jnp....  4.07 us
    sub x4, matrix products, head_grads(): weights_raw = jnp.exp(scores - row_max)  2.69 us
    reshape x1, local copies, waits for them, and re-layouts, body(): jnp.transpose(grad_q, (1, 0, 2, 3)).reshape(block_rows, QH * HD)  2.27 us
  transfers between devices with their start and end apart: 4, of which 3 were waited for; matrix products, arithmetic and copies ran while one was open for 8% of the time, Pallas kernels for 0%

commit v1 on v0

--- a/solution.py
+++ b/solution.py
@@ -64,7 +64,7 @@
     key_value = jnp.stack([key_vectors, value_vectors])
     device_index = lax.axis_index(("ctx", "uly"))
     near_rim = fetch_rim(key_value, 1)
-    far_rim = fetch_rim(key_value, 2)
+    far_rim = fetch_rim(near_rim, 1)
     window = jnp.concatenate([far_rim, near_rim, key_value], axis=1)
     window_heads = jnp.transpose(window.reshape(2, 3 * block_rows, KVH, HD), (0, 2, 1, 3))
     query_heads = jnp.transpose(queries.reshape(block_rows, KVH, GROUP, HD), (1, 0, 2, 3))
@@ -83,11 +83,10 @@
     grad_q, grad_k = lax.map(per_head, (query_heads, grad_heads, window_heads[0], window_heads[1]))
     query_grad = jnp.transpose(grad_q, (1, 0, 2, 3)).reshape(block_rows, QH * HD)
     window_grad = jnp.transpose(grad_k, (1, 0, 2)).reshape(3 * block_rows, KVH * HD)
-    own_part = (
-        window_grad[2 * block_rows :]
-        + send_back(window_grad[block_rows : 2 * block_rows], -1)
-        + send_back(window_grad[:block_rows], -2)
-    )
+    relayed = send_back(window_grad[:block_rows].astype(jnp.bfloat16), -1)
+    near_sum = window_grad[block_rows : 2 * block_rows] + relayed.astype(jnp.float32)
+    arrived = send_back(near_sum.astype(jnp.bfloat16), -1)
+    own_part = window_grad[2 * block_rows :] + arrived.astype(jnp.float32)
     key_grad = own_part.astype(jnp.bfloat16)
     return (query_grad, key_grad)
 

time: 69.3 us -> 62.7 us (0.905)
  the two profiles are of different devices: /device:TPU:1 before, /device:TPU:25 now
where the time goes in v1:
time: 62.7 us; the launch traced here: 62.3 us
  waiting for transfers between devices  18.8 us (30%)
  matrix products  16.3 us (26%)
  starting transfers between devices  14.1 us (22%)
  local copies, waits for them, and re-layouts  9.29 us (15%)
  other arithmetic  2.88 us (5%)
  between operations  0.77 us (1%)
    ppermute x4, waiting for transfers between devices, shifted(): return lax.ppermute(block, axis, route)  18.8 us
    ppermute x4, starting transfers between devices, shifted(): return lax.ppermute(block, axis, route)  14.1 us
    dot_general x4, matrix products, head_grads(): jnp.einsum('tgd,sd->gts', grad_block, value_window, preferred_element_typ...  5.39 us
    unnamed x9, local copies, waits for them, and re-layouts  5.23 us
    dot_general x4, matrix products, head_grads(): jnp.einsum('gts,tgd->sd', grad_s, query_block, preferred_element_type=jnp...  4.2 us
    dot_general x4, matrix products, head_grads(): jnp.einsum('gts,sd->tgd', grad_s, key_window, preferred_element_type=jnp....  4.07 us
    sub x4, matrix products, head_grads(): weights_raw = jnp.exp(scores - row_max)  2.69 us
    reshape x1, local copies, waits for them, and re-layouts, body(): jnp.transpose(grad_q, (1, 0, 2, 3)).reshape(block_rows, QH * HD)  2.27 us
  transfers between devices with their start and end apart: 4, of which 4 were waited for; matrix products, arithmetic and copies ran while one was open for 10% of the time, Pallas kernels for 0%

profile of v1, /device:TPU:25, one launch (start us, length us, event | category | flops | bytes accessed | tf_op | source)
XLA Modules:
  0.0 62.3 jit_solution(9520725073975324126)
XLA Ops:
  0.6 1.2 %copy.31 = bf16[128,512]{0,1:T(8,128)(2,1)S(1)} copy(bf16[128,512]{1,0:T(8,128)(2,1)} %param.8) | data formatting | bytes 262144 | tf_op args[1]
  1.8 1.0 %copy.32 = bf16[128,512]{0,1:T(8,128)(2,1)S(1)} copy(bf16[128,512]{1,0:T(8,128)(2,1)} %param.9) | data formatting | bytes 262144 | tf_op args[2]
  2.9 3.4 %collective-permute-start = (bf16[2,128,512]{1,2,0:T(8,128)(2,1)S(1)}, bf16[2,128,512]{1,2,0:T(8,128)(2,1)S(1)}, u32[]{:S(2)}, u32[]{:S(2)}) collective-permute-start(bf16[2,128,512]{1,2,0:T(8,128)(2,1)S(1)} %pad_maximum_fusion), channel_id=1, source_target_pairs={{0,2},{2,4},{4,6},{6,8},{8,10},{10,12},{12,14},{14,16},{16,18},{18... | collective-permute-start | bytes 786440 | tf_op jit(solution)/shard_map/ppermute | solution.py:15
  7.3 4.7 %collective-permute-done = bf16[2,128,512]{1,2,0:T(8,128)(2,1)S(1)} collective-permute-done((bf16[2,128,512]{1,2,0:T(8,128)(2,1)S(1)}, bf16[2,128,512]{1,2,0:T(8,128)(2,1)S(1)}, u32[]{:S(2)}, u32[]{:S(2)}) %collective-permute-start) | collective-permute-done | bytes 262176 | tf_op jit(solution)/shard_map/ppermute | solution.py:15
  12.0 6.9 %collective-permute-start.1 = (bf16[2,128,512]{1,2,0:T(8,128)(2,1)S(1)}, bf16[2,128,512]{1,2,0:T(8,128)(2,1)S(1)}, u32[]{:S(2)}, u32[]{:S(2)}) collective-permute-start(bf16[2,128,512]{1,2,0:T(8,128)(2,1)S(1)} %collective-permute-done), channel_id=1, source_target_pairs={{0,2},{2,4},{4,6},{6,8},{8,10},{10,12},{12,14},{14,16},{16,18},{18... | collective-permute-start | bytes 786440 | tf_op jit(solution)/shard_map/ppermute | solution.py:15
  19.0 1.3 %copy.34 = bf16[128,4096]{0,1:T(8,128)(2,1)} copy(bf16[128,4096]{1,0:T(8,128)(2,1)S(1)} %copy-done) | data formatting | bytes 2097152 | tf_op args[3]
  21.0 2.6 %collective-permute-done.1 = bf16[2,128,512]{1,2,0:T(8,128)(2,1)S(1)} collective-permute-done((bf16[2,128,512]{1,2,0:T(8,128)(2,1)S(1)}, bf16[2,128,512]{1,2,0:T(8,128)(2,1)S(1)}, u32[]{:S(2)}, u32[]{:S(2)}) %collective-permute-start.1) | collective-permute-done | bytes 262176 | tf_op jit(solution)/shard_map/ppermute | solution.py:15
  23.7 18.1 %while.13 = (s32[]{:T(128)}, bf16[4,128,8,128]{1,3,2,0:T(8,128)(2,1)}, f32[4,384,128]{2,1,0:T(8,128)}, bf16[4,384,128]{1,2,0:T(8,128)(2,1)S(1)}, bf16[4,128,8,12...) while((s32[]{:T(128)}, ...), condition=%wide.region_7.8_spmd.clone, body=%wide.region_3.7_spmd.clone.sunk | while | flops 407436672 | bytes 11890805 | solution.py:83
  24.6 1.3 %fusion.75 = (f32[8,128]{1,0:T(8,128)S(1)}, f32[384,128,8]{1,0,2:T(8,128)S(1)}) fusion(f32[8,128,384]{1,2,0:T(8,128)S(1)} %get-tuple-element.198, f32[8,128]{1,0:T(8,128)S(1)} %get-tuple-element.199, bf16[4,128,8,128]{1,3,2,0:T(8,128)(2,1)} %get-tuple-element.232, s32[]{:T(128)} %get-tuple-element.214, bf16[4,384,128]{1,2,0:T(8,128)(2,1)S(1)} %get-tuple-element.231), kind=kOutput, calls=%fused_computation.5.clone.1 | convolution fusion | flops 101841920 | bytes 3515392 | tf_op jit(solution)/shard_map/while/body/eval_jaxpr/tgd,sd->gts/dot_general | solution.py:33
  27.2 1.1 %fusion.78 = f32[4,384,128]{2,1,0:T(8,128)} fusion(f32[4,384,128]{2,1,0:T(8,128)} %get-tuple-element.216, s32[]{:T(128)} %get-tuple-element.214, bf16[8,128,384]{1,2,0:T(8,128)(2,1)S(1)} %fusion.76, bf16[4,128,8,128]{1,3,2,0:T(8,128)(2,1)S(1)} %get-tuple-element.230), kind=kOutput, calls=%fused_computation.17.clone.1 | convolution fusion | flops 100712448 | bytes 1246208 | tf_op jit(solution)/shard_map/while/body/eval_jaxpr/gts,tgd->sd/dot_general | solution.py:41
  29.1 1.3 %fusion.75 = (f32[8,128]{1,0:T(8,128)S(1)}, f32[384,128,8]{1,0,2:T(8,128)S(1)}) fusion(f32[8,128,384]{1,2,0:T(8,128)S(1)} %get-tuple-element.198, f32[8,128]{1,0:T(8,128)S(1)} %get-tuple-element.199, bf16[4,128,8,128]{1,3,2,0:T(8,128)(2,1)} %get-tuple-element.232, s32[]{:T(128)} %get-tuple-element.214, bf16[4,384,128]{1,2,0:T(8,128)(2,1)S(1)} %get-tuple-element.231), kind=kOutput, calls=%fused_computation.5.clone.1 | convolution fusion | flops 101841920 | bytes 3515392 | tf_op jit(solution)/shard_map/while/body/eval_jaxpr/tgd,sd->gts/dot_general | solution.py:33
  31.7 1.0 %fusion.78 = f32[4,384,128]{2,1,0:T(8,128)} fusion(f32[4,384,128]{2,1,0:T(8,128)} %get-tuple-element.216, s32[]{:T(128)} %get-tuple-element.214, bf16[8,128,384]{1,2,0:T(8,128)(2,1)S(1)} %fusion.76, bf16[4,128,8,128]{1,3,2,0:T(8,128)(2,1)S(1)} %get-tuple-element.230), kind=kOutput, calls=%fused_computation.17.clone.1 | convolution fusion | flops 100712448 | bytes 1246208 | tf_op jit(solution)/shard_map/while/body/eval_jaxpr/gts,tgd->sd/dot_general | solution.py:41
  33.6 1.3 %fusion.75 = (f32[8,128]{1,0:T(8,128)S(1)}, f32[384,128,8]{1,0,2:T(8,128)S(1)}) fusion(f32[8,128,384]{1,2,0:T(8,128)S(1)} %get-tuple-element.198, f32[8,128]{1,0:T(8,128)S(1)} %get-tuple-element.199, bf16[4,128,8,128]{1,3,2,0:T(8,128)(2,1)} %get-tuple-element.232, s32[]{:T(128)} %get-tuple-element.214, bf16[4,384,128]{1,2,0:T(8,128)(2,1)S(1)} %get-tuple-element.231), kind=kOutput, calls=%fused_computation.5.clone.1 | convolution fusion | flops 101841920 | bytes 3515392 | tf_op jit(solution)/shard_map/while/body/eval_jaxpr/tgd,sd->gts/dot_general | solution.py:33
  35.2 1.0 %fusion.77 = bf16[4,128,8,128]{1,3,2,0:T(8,128)(2,1)} fusion(bf16[4,128,8,128]{1,3,2,0:T(8,128)(2,1)} %get-tuple-element.215, s32[]{:T(128)} %get-tuple-element.214, bf16[8,128,384]{1,2,0:T(8,128)(2,1)S(1)} %fusion.76, bf16[4,384,128]{1,2,0:T(8,128)(2,1)S(1)} %get-tuple-element.229), kind=kOutput, calls=%fused_computation.13.clone.1 | convolution fusion | flops 100925440 | bytes 1147904 | tf_op jit(solution)/shard_map/while/body/eval_jaxpr/gts,sd->tgd/dot_general | solution.py:37
  36.3 1.1 %fusion.78 = f32[4,384,128]{2,1,0:T(8,128)} fusion(f32[4,384,128]{2,1,0:T(8,128)} %get-tuple-element.216, s32[]{:T(128)} %get-tuple-element.214, bf16[8,128,384]{1,2,0:T(8,128)(2,1)S(1)} %fusion.76, bf16[4,128,8,128]{1,3,2,0:T(8,128)(2,1)S(1)} %get-tuple-element.230), kind=kOutput, calls=%fused_computation.17.clone.1 | convolution fusion | flops 100712448 | bytes 1246208 | tf_op jit(solution)/shard_map/while/body/eval_jaxpr/gts,tgd->sd/dot_general | solution.py:41
  38.2 1.3 %fusion.75 = (f32[8,128]{1,0:T(8,128)S(1)}, f32[384,128,8]{1,0,2:T(8,128)S(1)}) fusion(f32[8,128,384]{1,2,0:T(8,128)S(1)} %get-tuple-element.198, f32[8,128]{1,0:T(8,128)S(1)} %get-tuple-element.199, bf16[4,128,8,128]{1,3,2,0:T(8,128)(2,1)} %get-tuple-element.232, s32[]{:T(128)} %get-tuple-element.214, bf16[4,384,128]{1,2,0:T(8,128)(2,1)S(1)} %get-tuple-element.231), kind=kOutput, calls=%fused_computation.5.clone.1 | convolution fusion | flops 101841920 | bytes 3515392 | tf_op jit(solution)/shard_map/while/body/eval_jaxpr/tgd,sd->gts/dot_general | solution.py:33
  39.8 1.0 %fusion.77 = bf16[4,128,8,128]{1,3,2,0:T(8,128)(2,1)} fusion(bf16[4,128,8,128]{1,3,2,0:T(8,128)(2,1)} %get-tuple-element.215, s32[]{:T(128)} %get-tuple-element.214, bf16[8,128,384]{1,2,0:T(8,128)(2,1)S(1)} %fusion.76, bf16[4,384,128]{1,2,0:T(8,128)(2,1)S(1)} %get-tuple-element.229), kind=kOutput, calls=%fused_computation.13.clone.1 | convolution fusion | flops 100925440 | bytes 1147904 | tf_op jit(solution)/shard_map/while/body/eval_jaxpr/gts,sd->tgd/dot_general | solution.py:37
  40.8 1.0 %fusion.78 = f32[4,384,128]{2,1,0:T(8,128)} fusion(f32[4,384,128]{2,1,0:T(8,128)} %get-tuple-element.216, s32[]{:T(128)} %get-tuple-element.214, bf16[8,128,384]{1,2,0:T(8,128)(2,1)S(1)} %fusion.76, bf16[4,128,8,128]{1,3,2,0:T(8,128)(2,1)S(1)} %get-tuple-element.230), kind=kOutput, calls=%fused_computation.17.clone.1 | convolution fusion | flops 100712448 | bytes 1246208 | tf_op jit(solution)/shard_map/while/body/eval_jaxpr/gts,tgd->sd/dot_general | solution.py:41
  42.8 1.9 %collective-permute-start.2 = (bf16[128,512]{1,0:T(8,128)(2,1)S(1)}, bf16[128,512]{1,0:T(8,128)(2,1)S(1)}, u32[]{:S(2)}, u32[]{:S(2)}) collective-permute-start(bf16[128,512]{1,0:T(8,128)(2,1)S(1)} %copy_bitcast_fusion), channel_id=1, source_target_pairs={{2,0},{4,2},{6,4},{8,6},{10,8},{12,10},{14,12},{16,14},{18,16},{20... | collective-permute-start | bytes 393224 | tf_op jit(solution)/shard_map/ppermute | solution.py:15
  44.8 1.1 %slice_bitcast_fusion.2 = (f32[4,16,8,128]{3,2,1,0:T(8,128)S(1)}, f32[4,16,8,128]{3,2,1,0:T(8,128)S(1)}) fusion(f32[384,4,128]{2,0,1:T(8,128)} %bitcast.14), kind=kLoop, calls=%fused_computation.51 | loop fusion | bytes 1048576
  45.8 6.7 %collective-permute-done.2 = bf16[128,512]{1,0:T(8,128)(2,1)S(1)} collective-permute-done((bf16[128,512]{1,0:T(8,128)(2,1)S(1)}, bf16[128,512]{1,0:T(8,128)(2,1)S(1)}, u32[]{:S(2)}, u32[]{:S(2)}) %collective-permute-start.2) | collective-permute-done | bytes 131104 | tf_op jit(solution)/shard_map/ppermute | solution.py:15
  52.6 1.9 %collective-permute-start.3 = (bf16[128,512]{1,0:T(8,128)(2,1)S(1)}, bf16[128,512]{1,0:T(8,128)(2,1)S(1)}, u32[]{:S(2)}, u32[]{:S(2)}) collective-permute-start(bf16[128,512]{1,0:T(8,128)(2,1)S(1)} %fusion.46), channel_id=1, source_target_pairs={{2,0},{4,2},{6,4},{8,6},{10,8},{12,10},{14,12},{16,14},{18,16},{20... | collective-permute-start | bytes 393224 | tf_op jit(solution)/shard_map/ppermute | solution.py:15
  54.5 2.3 %copy.46 = bf16[128,4096]{1,0:T(8,128)(2,1)} copy(bf16[128,4096]{0,1:T(8,128)(2,1)} %bitcast.13) | data formatting | bytes 2097152 | tf_op jit(solution)/shard_map/reshape | solution.py:84
  56.8 4.8 %collective-permute-done.3 = bf16[128,512]{1,0:T(8,128)(2,1)S(1)} collective-permute-done((bf16[128,512]{1,0:T(8,128)(2,1)S(1)}, bf16[128,512]{1,0:T(8,128)(2,1)S(1)}, u32[]{:S(2)}, u32[]{:S(2)}) %collective-permute-start.3) | collective-permute-done | bytes 131104 | tf_op jit(solution)/shard_map/ppermute | solution.py:15
  (36 shorter events, 10.0 us)
Async XLA Ops:
  0.6 18.3 %copy-start = (bf16[128,4096]{1,0:T(8,128)(2,1)S(1)}, bf16[128,4096]{1,0:T(8,128)(2,1)}, u32[]{:S(2)}) copy-start(bf16[128,4096]{1,0:T(8,128)(2,1)} %param.10) | copy-start | bytes 3145732
  0.6 19.6 %copy-start.1 = (bf16[128,4096]{1,0:T(8,128)(2,1)S(1)}, bf16[128,4096]{1,0:T(8,128)(2,1)}, u32[]{:S(2)}) copy-start(bf16[128,4096]{1,0:T(8,128)(2,1)} %param.7) | copy-start | bytes 3145732
  2.9 9.1 %collective-permute-start = (bf16[2,128,512]{1,2,0:T(8,128)(2,1)S(1)}, bf16[2,128,512]{1,2,0:T(8,128)(2,1)S(1)}, u32[]{:S(2)}, u32[]{:S(2)}) collective-permute-start(bf16[2,128,512]{1,2,0:T(8,128)(2,1)S(1)} %pad_maximum_fusion), channel_id=1, source_target_pairs={{0,2},{2,4},{4,6},{6,8},{8,10},{10,12},{12,14},{14,16},{16,18},{18... | collective-permute-start | bytes 786440 | tf_op jit(solution)/shard_map/ppermute | solution.py:15
  12.0 11.6 %collective-permute-start.1 = (bf16[2,128,512]{1,2,0:T(8,128)(2,1)S(1)}, bf16[2,128,512]{1,2,0:T(8,128)(2,1)S(1)}, u32[]{:S(2)}, u32[]{:S(2)}) collective-permute-start(bf16[2,128,512]{1,2,0:T(8,128)(2,1)S(1)} %collective-permute-done), channel_id=1, source_target_pairs={{0,2},{2,4},{4,6},{6,8},{8,10},{10,12},{12,14},{14,16},{16,18},{18... | collective-permute-start | bytes 786440 | tf_op jit(solution)/shard_map/ppermute | solution.py:15
  42.8 9.7 %collective-permute-start.2 = (bf16[128,512]{1,0:T(8,128)(2,1)S(1)}, bf16[128,512]{1,0:T(8,128)(2,1)S(1)}, u32[]{:S(2)}, u32[]{:S(2)}) collective-permute-start(bf16[128,512]{1,0:T(8,128)(2,1)S(1)} %copy_bitcast_fusion), channel_id=1, source_target_pairs={{2,0},{4,2},{6,4},{8,6},{10,8},{12,10},{14,12},{16,14},{18,16},{20... | collective-permute-start | bytes 393224 | tf_op jit(solution)/shard_map/ppermute | solution.py:15
  52.6 9.0 %collective-permute-start.3 = (bf16[128,512]{1,0:T(8,128)(2,1)S(1)}, bf16[128,512]{1,0:T(8,128)(2,1)S(1)}, u32[]{:S(2)}, u32[]{:S(2)}) collective-permute-start(bf16[128,512]{1,0:T(8,128)(2,1)S(1)} %fusion.46), channel_id=1, source_target_pairs={{2,0},{4,2},{6,4},{8,6},{10,8},{12,10},{14,12},{16,14},{18,16},{20... | collective-permute-start | bytes 393224 | tf_op jit(solution)/shard_map/ppermute | solution.py:15

commit v2 on v1

v2 whole, which is shorter than its diff:
```python
import jax
import jax.numpy as jnp
from jax import lax
from jax.sharding import PartitionSpec as P

QH = 32
KVH = 4
HD = 128
GROUP = 8
NEG = -1e30


def shifted(block, axis, distance):
    devices = range(lax.axis_size(axis))
    route = [(i - distance, i) for i in devices if i - distance in devices]
    return lax.ppermute(block, axis, route)


def doc_index(doc_lengths, positions):
    doc_ends = jnp.cumsum(doc_lengths)
    counted = jnp.sum((positions[:, None] >= doc_ends[None, :]).astype(jnp.int32), axis=1)
    return jnp.where(positions < 0, -1, counted)


def allowed_pairs(doc_lengths, query_pos, key_pos):
    query_docs = doc_index(doc_lengths, query_pos)
    key_docs = doc_index(doc_lengths, key_pos)
    return (query_docs[:, None] == key_docs[None, :]) & (key_pos[None, :] <= query_pos[:, None])


def scores_of(query_heads, key_heads, allowed, score_scale):
    scores = (
        jnp.einsum("tghd,sgd->ghts", query_heads, key_heads, preferred_element_type=jnp.float32)
        * score_scale
    )
    return jnp.where(allowed[None, None], scores, NEG)


def body(queries, key_vectors, value_vectors, output_grad, doc_lengths):
    rows = queries.shape[0]
    score_scale = HD ** (-0.5)
    axes = ("ctx", "uly")
    key_value = jnp.stack([key_vectors, value_vectors])
    near_rim = shifted(key_value, axes, 1)
    far_rim = shifted(key_value, axes, 2)
    device_index = lax.axis_index(axes)
    query_heads = queries.reshape(rows, KVH, GROUP, HD)
    grad_heads = output_grad.reshape(rows, KVH, GROUP, HD)
    own_keys = key_vectors.reshape(rows, KVH, HD)
    own_values = value_vectors.reshape(rows, KVH, HD)
    query_pos = device_index * rows + jnp.arange(rows, dtype=jnp.int32)
    own_pos = query_pos
    rim_pos = device_index * rows - 2 * rows + jnp.arange(2 * rows, dtype=jnp.int32)
    own_allowed = allowed_pairs(doc_lengths, query_pos, own_pos)
    rim_allowed = allowed_pairs(doc_lengths, query_pos, rim_pos)

    own_scores = scores_of(query_heads, own_keys, own_allowed, score_scale)
    own_max = jnp.max(own_scores, axis=-1, keepdims=True)
    own_exp = jnp.exp(own_scores - own_max)
    own_sum = jnp.sum(own_exp, axis=-1, keepdims=True)
    own_grad_p = jnp.einsum(
        "tghd,sgd->ghts", grad_heads, own_values, preferred_element_type=jnp.float32
    )
    own_dot = jnp.sum(own_exp * own_grad_p, axis=-1, keepdims=True)

    rim = jnp.concatenate([far_rim, near_rim], axis=1).reshape(2, 2 * rows, KVH, HD)
    rim_keys, rim_values = rim[0], rim[1]
    rim_scores = scores_of(query_heads, rim_keys, rim_allowed, score_scale)
    row_max = jnp.maximum(own_max, jnp.max(rim_scores, axis=-1, keepdims=True))
    rim_exp = jnp.exp(rim_scores - row_max)
    own_rescale = jnp.exp(own_max - row_max)
    row_sum = own_sum * own_rescale + jnp.sum(rim_exp, axis=-1, keepdims=True)
    rim_grad_p = jnp.einsum(
        "tghd,sgd->ghts", grad_heads, rim_values, preferred_element_type=jnp.float32
    )
    row_delta = (
        own_dot * own_rescale + jnp.sum(rim_exp * rim_grad_p, axis=-1, keepdims=True)
    ) / row_sum
    rim_grad_s = ((rim_exp / row_sum) * (rim_grad_p - row_delta)).astype(jnp.bfloat16)
    rim_key_grad = (
        jnp.einsum("ghts,tghd->sgd", rim_grad_s, query_heads, preferred_element_type=jnp.float32)
        * score_scale
    ).reshape(2 * rows, KVH * HD)
    far_back = shifted(rim_key_grad[:rows].astype(jnp.bfloat16), axes, -2)
    near_back = shifted(rim_key_grad[rows:].astype(jnp.bfloat16), axes, -1)

    own_prob = own_exp * (own_rescale / row_sum)
    own_grad_s = (own_prob * (own_grad_p - row_delta)).astype(jnp.bfloat16)
    own_key_grad = (
        jnp.einsum("ghts,tghd->sgd", own_grad_s, query_heads, preferred_element_type=jnp.float32)
        * score_scale
    ).reshape(rows, KVH * HD)
    query_grad = (
        jnp.einsum("ghts,sgd->tghd", own_grad_s, own_keys, preferred_element_type=jnp.float32)
        + jnp.einsum("ghts,sgd->tghd", rim_grad_s, rim_keys, preferred_element_type=jnp.float32)
    ) * score_scale
    query_grad = query_grad.astype(jnp.bfloat16).reshape(rows, QH * HD)
    key_grad = (
        own_key_grad + near_back.astype(jnp.float32) + far_back.astype(jnp.float32)
    ).astype(jnp.bfloat16)
    return (query_grad, key_grad)


def solution(mesh):
    placed = (
        P(("dp", "ctx", "uly"), None),
        P(("dp", "ctx", "uly"), None),
        P(("dp", "ctx", "uly"), None),
        P(("dp", "ctx", "uly"), None),
        P("dp"),
    )
    return jax.shard_map(
        body,
        mesh=mesh,
        in_specs=placed,
        out_specs=(P(("dp", "ctx", "uly"), None), P(("dp", "ctx", "uly"), None)),
        check_vma=False,
    )
```

time: 62.7 us -> 50.4 us (0.80)
  the two profiles are of different devices: /device:TPU:25 before, /device:TPU:1 now
where the time goes in v2:
time: 50.4 us; the launch traced here: 49.9 us
  starting transfers between devices  14.2 us (28%)
  waiting for transfers between devices  12.2 us (24%)
  local copies, waits for them, and re-layouts  10.9 us (22%)
  matrix products  6.29 us (12%)
  other arithmetic  5.34 us (11%)
  between operations  0.92 us (2%)
    ppermute x4, starting transfers between devices, shifted(): return lax.ppermute(block, axis, route)  14.2 us
    ppermute x4, waiting for transfers between devices, shifted(): return lax.ppermute(block, axis, route)  12.2 us
    unnamed x9, local copies, waits for them, and re-layouts  4.75 us
    dot_general x1, matrix products, body(): jnp.einsum('tghd,sgd->ghts', grad_heads, rim_values, preferred_element_ty...  1.69 us
    convert_element_type x1, other arithmetic, body(): key_grad = (own_key_grad + near_back.astype(jnp.float32) + far_back.astyp...  1.6 us
    convert_element_type x1, other arithmetic, body(): (rim_exp / row_sum * (rim_grad_p - row_delta)).astype(jnp.bfloat16)  1.57 us
    dot_general x2, matrix products, scores_of(): jnp.einsum('tghd,sgd->ghts', query_heads, key_heads, preferred_element_ty...  1.31 us
    reshape x2, local copies, waits for them, and re-layouts, body(): own_keys = key_vectors.reshape(rows, KVH, HD)  1.08 us
  transfers between devices with their start and end apart: 4, of which 3 were waited for; matrix products, arithmetic and copies ran while one was open for 19% of the time, Pallas kernels for 0%

profile of v2, /device:TPU:1, one launch (start us, length us, event | category | flops | bytes accessed | tf_op | source)
XLA Modules:
  0.0 49.9 jit_solution(9382632657785769729)
XLA Ops:
  0.6 1.2 %copy.52 = bf16[128,512]{0,1:T(8,128)(2,1)S(1)} copy(bf16[128,512]{1,0:T(8,128)(2,1)} %param.7) | data formatting | bytes 262144 | tf_op args[2]
  1.8 1.0 %copy.51 = bf16[128,512]{0,1:T(8,128)(2,1)S(1)} copy(bf16[128,512]{1,0:T(8,128)(2,1)} %param.6) | data formatting | bytes 262144 | tf_op args[1]
  3.6 5.0 %collective-permute-start = (bf16[2,128,512]{1,2,0:T(8,128)(2,1)}, bf16[2,128,512]{1,2,0:T(8,128)(2,1)}, u32[]{:S(2)}, u32[]{:S(2)}) collective-permute-start(bf16[2,128,512]{1,2,0:T(8,128)(2,1)} %pad_maximum_fusion), channel_id=1, source_target_pairs={{0,4},{2,6},{4,8},{6,10},{8,12},{10,14},{12,16},{14,18},{16,20},{1... | collective-permute-start | bytes 786440 | tf_op jit(solution)/shard_map/ppermute | solution.py:16
  8.6 3.2 %collective-permute-start.1 = (bf16[2,128,512]{1,2,0:T(8,128)(2,1)}, bf16[2,128,512]{1,2,0:T(8,128)(2,1)}, u32[]{:S(2)}, u32[]{:S(2)}) collective-permute-start(bf16[2,128,512]{1,2,0:T(8,128)(2,1)} %pad_maximum_fusion), channel_id=1, source_target_pairs={{0,2},{2,4},{4,6},{6,8},{8,10},{10,12},{12,14},{14,16},{16,18},{18... | collective-permute-start | bytes 786440 | tf_op jit(solution)/shard_map/ppermute | solution.py:16
  11.8 0.9 %reshape.253 = bf16[128,4,128]{2,1,0:T(4,128)(2,1)S(1)} reshape(bf16[128,512]{1,0:T(8,128)(2,1)} %param.6) | data formatting | bytes 262144 | tf_op jit(solution)/shard_map/reshape | solution.py:49
  12.8 0.9 %reshape.255 = bf16[128,4,128]{2,1,0:T(4,128)(2,1)S(1)} reshape(bf16[128,512]{1,0:T(8,128)(2,1)} %param.7) | data formatting | bytes 262144 | tf_op jit(solution)/shard_map/reshape | solution.py:50
  13.9 0.7 %copy.48 = s32[16,1]{1,0:T(8,128)S(1)} copy(s32[16,1]{0,1:T(1,128)} %bitcast.126) | data formatting | bytes 128 | tf_op jit(solution)/shard_map/reshape.227
  16.6 1.0 %fusion.7 = (f32[4,8,128]{2,1,0:T(8,128)S(1)}, f32[4,8,128]{2,1,0:T(8,128)S(1)}, f32[4,128,128,8]{2,1,3,0:T(8,128)S(1)}) fusion(f32[4,128,128,8]{2,1,3,0:T(8,128)S(1)} %get-tuple-element.19, f32[4,8,128]{2,1,0:T(8,128)S(1)} %get-tuple-element.18, pred[128,128]{0,1:T(8,128)(4,1)S(1)} %compare_and_fusion.1, bf16[128,4,8,128]{3,2,1,0:T(8,128)(2,1)S(1)} %bitcast.112, ...), kind=kOutput, calls=%fused_computation.14 | convolution fusion | flops 137355264 | bytes 5439488 | tf_op jit(solution)/shard_map/tghd,sgd->ghts/dot_general | solution.py:61
  17.8 9.2 %collective-permute-done = bf16[2,128,512]{1,2,0:T(8,128)(2,1)} collective-permute-done((bf16[2,128,512]{1,2,0:T(8,128)(2,1)}, bf16[2,128,512]{1,2,0:T(8,128)(2,1)}, u32[]{:S(2)}, u32[]{:S(2)}) %collective-permute-start) | collective-permute-done | bytes 262176 | tf_op jit(solution)/shard_map/ppermute | solution.py:16
  26.9 1.0 %constant_dynamic-update-slice_fusion.1 = bf16[2,256,512]{1,2,0:T(8,128)(2,1)S(1)} fusion(bf16[2,128,512]{1,2,0:T(8,128)(2,1)} %collective-permute-done), kind=kLoop, calls=%fused_computation.42 | loop fusion | bytes 524288
  27.9 1.0 %constant_dynamic-update-slice_fusion = bf16[2,256,512]{1,2,0:T(8,128)(2,1)S(1)} fusion(bf16[2,256,512]{1,2,0:T(8,128)(2,1)S(1)} %constant_dynamic-update-slice_fusion.1, bf16[2,128,512]{1,2,0:T(8,128)(2,1)} %collective-permute-done.1), kind=kLoop, calls=%fused_computation.41 | loop fusion | bytes 524288 | tf_op jit(solution)/shard_map/concatenate | solution.py:66
  29.0 0.8 %fusion.3 = (f32[4,8,128]{2,1,0:T(8,128)S(1)}, f32[4,256,128,8]{2,1,3,0:T(8,128)S(1)}) fusion(pred[128,256]{0,1:T(8,128)(4,1)S(1)} %compare_and_fusion, bf16[256,4,128,1]{0,2,3,1:T(8,128)(2,1)S(1)} %bitcast.115, bf16[128,4,8,128]{0,3,2,1:T(8,128)(2,1)S(1)} %bitcast.109), kind=kOutput, calls=%fused_computation.7 | convolution fusion | flops 271577088 | bytes 5554176 | tf_op jit(solution)/shard_map/tghd,sgd->ghts/dot_general | solution.py:33
  29.8 1.7 %fusion = (f32[4,8,128]{2,1,0:T(8,128)S(1)}, f32[4,8,128]{2,1,0:T(8,128)S(1)}, f32[4,256,128,8]{2,1,3,0:T(8,128)S(1)}) fusion(f32[4,256,128,8]{2,1,3,0:T(8,128)S(1)} %get-tuple-element.21, f32[4,8,128]{2,1,0:T(8,128)S(1)} %max.17, pred[128,256]{0,1:T(8,128)(4,1)S(1)} %compare_and_fusion, bf16[256,4,128,1]{0,2,3,1:T(8,128)(2,1)S(1)} %bitcast.119, ...), kind=kOutput, calls=%fused_computation.2 | convolution fusion | flops 274718720 | bytes 9781248 | tf_op jit(solution)/shard_map/tghd,sgd->ghts/dot_general | solution.py:73
  31.6 0.8 %fusion.9 = bf16[4,8,128,128]{2,3,1,0:T(8,128)(2,1)S(1)} fusion(f32[4,128,128,8]{2,1,3,0:T(8,128)S(1)} %get-tuple-element.23, f32[4,128,128,8]{2,1,3,0:T(8,128)S(1)} %get-tuple-element.19, f32[4,8,128]{2,1,0:T(8,128)S(1)} %add_divide_fusion, f32[4,8,128]{2,1,0:T(8,128)S(1)} %get-tuple-element.12, f32[4,8,128]{2,1,0:T(8,128)S(1)} %get-tuple-element.18, ...), kind=kLoop, calls=%fused_computation.16 | loop fusion | flops 3670016 | bytes 5308416 | tf_op jit(solution)/shard_map/convert_element_type | solution.py:88
  32.8 1.6 %fusion.2 = bf16[4,8,128,256]{2,3,1,0:T(8,128)(2,1)S(1)} fusion(f32[4,256,128,8]{2,1,3,0:T(8,128)S(1)} %get-tuple-element.22, f32[4,256,128,8]{2,1,3,0:T(8,128)S(1)} %get-tuple-element.21, f32[4,8,128]{2,1,0:T(8,128)S(1)} %add_divide_fusion, f32[4,8,128]{2,1,0:T(8,128)S(1)} %get-tuple-element.13, f32[4,8,128]{2,1,0:T(8,128)S(1)} %max.17, ...), kind=kLoop, calls=%fused_computation.4 | loop fusion | flops 7340032 | bytes 10567680 | tf_op jit(solution)/shard_map/convert_element_type | solution.py:79
  34.4 0.8 %fusion.13 = bf16[256,4,128]{0,2,1:T(8,128)(2,1)S(1)} fusion(bf16[4,8,128,256]{2,3,1,0:T(8,128)(2,1)S(1)} %fusion.2, bf16[128,4,8,128]{0,3,2,1:T(8,128)(2,1)S(1)} %bitcast.110), kind=kOutput, calls=%fused_computation.23 | convolution fusion | flops 268697600 | bytes 3407872 | tf_op jit(solution)/shard_map/ghts,tghd->sgd/dot_general | solution.py:81
  35.9 0.8 %copy.68 = bf16[128,512]{1,0:T(8,128)(2,1)} copy(bf16[128,512]{0,1:T(8,128)(2,1)S(1)} %bitcast.123) | data formatting | bytes 262144 | tf_op jit(solution)/shard_map/convert_element_type | solution.py:84
  36.6 3.7 %collective-permute-start.3 = (bf16[128,512]{1,0:T(8,128)(2,1)}, bf16[128,512]{1,0:T(8,128)(2,1)S(1)}, u32[]{:S(2)}, u32[]{:S(2)}) collective-permute-start(bf16[128,512]{1,0:T(8,128)(2,1)} %copy.68), channel_id=1, source_target_pairs={{4,0},{6,2},{8,4},{10,6},{12,8},{14,10},{16,12},{18,14},{20,16},{2... | collective-permute-start | bytes 393224 | tf_op jit(solution)/shard_map/ppermute | solution.py:16
  40.3 0.8 %copy.66 = bf16[128,512]{1,0:T(8,128)(2,1)} copy(bf16[128,512]{0,1:T(8,128)(2,1)S(1)} %bitcast.122) | data formatting | bytes 262144 | tf_op jit(solution)/shard_map/convert_element_type | solution.py:85
  41.0 2.3 %collective-permute-start.2 = (bf16[128,512]{1,0:T(8,128)(2,1)}, bf16[128,512]{1,0:T(8,128)(2,1)}, u32[]{:S(2)}, u32[]{:S(2)}) collective-permute-start(bf16[128,512]{1,0:T(8,128)(2,1)} %copy.66), channel_id=1, source_target_pairs={{2,0},{4,2},{6,4},{8,6},{10,8},{12,10},{14,12},{16,14},{18,16},{20... | collective-permute-start | bytes 393224 | tf_op jit(solution)/shard_map/ppermute | solution.py:16
  43.8 1.3 %copy.69 = bf16[128,4096]{1,0:T(8,128)(2,1)} copy(bf16[128,4096]{0,1:T(8,128)(2,1)S(1)} %bitcast.114) | data formatting | bytes 2097152
  45.3 1.8 %collective-permute-done.3 = bf16[128,512]{1,0:T(8,128)(2,1)S(1)} collective-permute-done((bf16[128,512]{1,0:T(8,128)(2,1)}, bf16[128,512]{1,0:T(8,128)(2,1)S(1)}, u32[]{:S(2)}, u32[]{:S(2)}) %collective-permute-start.3) | collective-permute-done | bytes 131104 | tf_op jit(solution)/shard_map/ppermute | solution.py:16
  47.1 1.2 %collective-permute-done.2 = bf16[128,512]{1,0:T(8,128)(2,1)} collective-permute-done((bf16[128,512]{1,0:T(8,128)(2,1)}, bf16[128,512]{1,0:T(8,128)(2,1)}, u32[]{:S(2)}, u32[]{:S(2)}) %collective-permute-start.2) | collective-permute-done | bytes 131104 | tf_op jit(solution)/shard_map/ppermute | solution.py:16
  48.3 1.6 %add_convert_fusion = bf16[128,512]{1,0:T(8,128)(2,1)} fusion(bf16[128,512]{1,0:T(8,128)(2,1)S(1)} %collective-permute-done.3, f32[128,512]{1,0:T(8,128)S(1)} %copy.67, bf16[128,512]{1,0:T(8,128)(2,1)} %collective-permute-done.2), kind=kLoop, calls=%fused_computation.32 | loop fusion | flops 327680 | bytes 655360 | tf_op jit(solution)/shard_map/convert_element_type | solution.py:100
  (29 shorter events, 4.6 us)
Async XLA Ops:
  0.6 14.4 %copy-start = (bf16[128,4096]{1,0:T(8,128)(2,1)S(1)}, bf16[128,4096]{1,0:T(8,128)(2,1)}, u32[]{:S(2)}) copy-start(bf16[128,4096]{1,0:T(8,128)(2,1)} %param.5) | copy-start | bytes 3145732
  0.6 15.0 %copy-start.1 = (bf16[128,4096]{1,0:T(8,128)(2,1)S(1)}, bf16[128,4096]{1,0:T(8,128)(2,1)}, u32[]{:S(2)}) copy-start(bf16[128,4096]{1,0:T(8,128)(2,1)} %param.8) | copy-start | bytes 3145732
  3.6 23.3 %collective-permute-start = (bf16[2,128,512]{1,2,0:T(8,128)(2,1)}, bf16[2,128,512]{1,2,0:T(8,128)(2,1)}, u32[]{:S(2)}, u32[]{:S(2)}) collective-permute-start(bf16[2,128,512]{1,2,0:T(8,128)(2,1)} %pad_maximum_fusion), channel_id=1, source_target_pairs={{0,4},{2,6},{4,8},{6,10},{8,12},{10,14},{12,16},{14,18},{16,20},{1... | collective-permute-start | bytes 786440 | tf_op jit(solution)/shard_map/ppermute | solution.py:16
  8.6 19.3 %collective-permute-start.1 = (bf16[2,128,512]{1,2,0:T(8,128)(2,1)}, bf16[2,128,512]{1,2,0:T(8,128)(2,1)}, u32[]{:S(2)}, u32[]{:S(2)}) collective-permute-start(bf16[2,128,512]{1,2,0:T(8,128)(2,1)} %pad_maximum_fusion), channel_id=1, source_target_pairs={{0,2},{2,4},{4,6},{6,8},{8,10},{10,12},{12,14},{14,16},{16,18},{18... | collective-permute-start | bytes 786440 | tf_op jit(solution)/shard_map/ppermute | solution.py:16
  36.6 10.5 %collective-permute-start.3 = (bf16[128,512]{1,0:T(8,128)(2,1)}, bf16[128,512]{1,0:T(8,128)(2,1)S(1)}, u32[]{:S(2)}, u32[]{:S(2)}) collective-permute-start(bf16[128,512]{1,0:T(8,128)(2,1)} %copy.68), channel_id=1, source_target_pairs={{4,0},{6,2},{8,4},{10,6},{12,8},{14,10},{16,12},{18,14},{20,16},{2... | collective-permute-start | bytes 393224 | tf_op jit(solution)/shard_map/ppermute | solution.py:16
  41.0 7.3 %collective-permute-start.2 = (bf16[128,512]{1,0:T(8,128)(2,1)}, bf16[128,512]{1,0:T(8,128)(2,1)}, u32[]{:S(2)}, u32[]{:S(2)}) collective-permute-start(bf16[128,512]{1,0:T(8,128)(2,1)} %copy.66), channel_id=1, source_target_pairs={{2,0},{4,2},{6,4},{8,6},{10,8},{12,10},{14,12},{16,14},{18,16},{20... | collective-permute-start | bytes 393224 | tf_op jit(solution)/shard_map/ppermute | solution.py:16

commit v3 on v2

v3 whole, which is shorter than its diff:
```python
import functools

import jax
import jax.numpy as jnp
from jax import lax
from jax.experimental import pallas as pl
from jax.experimental.pallas import tpu as pltpu
from jax.sharding import PartitionSpec as P

QH = 32
KVH = 4
HD = 128
GROUP = 8
NEG = -1e30
SCALE = HD ** (-0.5)


def shifted(block, axis, distance):
    devices = range(lax.axis_size(axis))
    route = [(i - distance, i) for i in devices if i - distance in devices]
    return lax.ppermute(block, axis, route)


def doc_index(doc_lengths, positions):
    doc_ends = jnp.cumsum(doc_lengths)
    counted = jnp.sum((positions[:, None] >= doc_ends[None, :]).astype(jnp.int32), axis=1)
    return jnp.where(positions < 0, -1, counted)


def mask_bias(doc_lengths, query_pos, key_pos):
    query_docs = doc_index(doc_lengths, query_pos)
    key_docs = doc_index(doc_lengths, key_pos)
    allowed = (query_docs[:, None] == key_docs[None, :]) & (key_pos[None, :] <= query_pos[:, None])
    return jnp.where(allowed, 0.0, NEG).astype(jnp.float32)


def q_kt(q, k):
    return lax.dot_general(q, k, (((1,), (1,)), ((), ())), preferred_element_type=jnp.float32)


def st_q(s, q):
    return lax.dot_general(s, q, (((0,), (0,)), ((), ())), preferred_element_type=jnp.float32)


def s_k(s, k):
    return jnp.dot(s, k, preferred_element_type=jnp.float32)


def head_cols(h):
    return slice(h * HD, (h + 1) * HD)


def own_stats_kernel(q_ref, do_ref, k_ref, v_ref, bias_ref, m_ref, l_ref, t_ref):
    k = k_ref[...]
    v = v_ref[...]
    bias = bias_ref[...]
    for h in range(GROUP):
        q = q_ref[:, head_cols(h)]
        do = do_ref[:, head_cols(h)]
        s = q_kt(q, k) * SCALE + bias
        m = jnp.max(s, axis=1, keepdims=True)
        e = jnp.exp(s - m)
        dp = q_kt(do, v)
        m_ref[h] = m
        l_ref[h] = jnp.sum(e, axis=1, keepdims=True)
        t_ref[h] = jnp.sum(e * dp, axis=1, keepdims=True)


def rim_kernel(q_ref, do_ref, far_ref, near_ref, bias_far_ref, bias_near_ref,
               m0_ref, l0_ref, t0_ref,
               dk_far_ref, dk_near_ref, dq_ref, m_ref, il_ref, d_ref):
    kf = far_ref[0]
    vf = far_ref[1]
    kn = near_ref[0]
    vn = near_ref[1]
    bias_far = bias_far_ref[...]
    bias_near = bias_near_ref[...]
    acc_far = jnp.zeros((HD, HD), jnp.float32)
    acc_near = jnp.zeros((HD, HD), jnp.float32)
    for h in range(GROUP):
        q = q_ref[:, head_cols(h)]
        do = do_ref[:, head_cols(h)]
        s_f = q_kt(q, kf) * SCALE + bias_far
        s_n = q_kt(q, kn) * SCALE + bias_near
        m0 = m0_ref[h]
        m = jnp.maximum(
            m0,
            jnp.maximum(jnp.max(s_f, axis=1, keepdims=True), jnp.max(s_n, axis=1, keepdims=True)),
        )
        a = jnp.exp(m0 - m)
        e_f = jnp.exp(s_f - m)
        e_n = jnp.exp(s_n - m)
        dp_f = q_kt(do, vf)
        dp_n = q_kt(do, vn)
        row_sum = (
            l0_ref[h] * a
            + jnp.sum(e_f, axis=1, keepdims=True)
            + jnp.sum(e_n, axis=1, keepdims=True)
        )
        row_dot = (
            t0_ref[h] * a
            + jnp.sum(e_f * dp_f, axis=1, keepdims=True)
            + jnp.sum(e_n * dp_n, axis=1, keepdims=True)
        )
        inv_l = 1.0 / row_sum
        delta = row_dot * inv_l
        ds_f = ((e_f * inv_l) * (dp_f - delta)).astype(jnp.bfloat16)
        ds_n = ((e_n * inv_l) * (dp_n - delta)).astype(jnp.bfloat16)
        acc_far = acc_far + st_q(ds_f, q)
        acc_near = acc_near + st_q(ds_n, q)
        dq_ref[:, head_cols(h)] = s_k(ds_f, kf) + s_k(ds_n, kn)
        m_ref[h] = m
        il_ref[h] = inv_l
        d_ref[h] = delta
    dk_far_ref[...] = (acc_far * SCALE).astype(dk_far_ref.dtype)
    dk_near_ref[...] = (acc_near * SCALE).astype(dk_near_ref.dtype)


def own_grads_kernel(q_ref, do_ref, k_ref, v_ref, bias_ref, m_ref, il_ref, d_ref, dq_rim_ref,
                     dq_ref, dk_ref):
    k = k_ref[...]
    v = v_ref[...]
    bias = bias_ref[...]
    acc = jnp.zeros((HD, HD), jnp.float32)
    for h in range(GROUP):
        q = q_ref[:, head_cols(h)]
        do = do_ref[:, head_cols(h)]
        s = q_kt(q, k) * SCALE + bias
        p = jnp.exp(s - m_ref[h]) * il_ref[h]
        dp = q_kt(do, v)
        ds = (p * (dp - d_ref[h])).astype(jnp.bfloat16)
        acc = acc + st_q(ds, q)
        dq = (s_k(ds, k) + dq_rim_ref[:, head_cols(h)]) * SCALE
        dq_ref[:, head_cols(h)] = dq.astype(dq_ref.dtype)
    dk_ref[...] = acc * SCALE


def heads_spec(rows):
    return pl.BlockSpec((rows, GROUP * HD), lambda g: (0, g))


def kv_spec(rows):
    return pl.BlockSpec((rows, HD), lambda g: (0, g))


def stacked_spec(rows):
    return pl.BlockSpec((2, rows, HD), lambda g: (0, 0, g))


def full_spec(shape):
    return pl.BlockSpec(shape, lambda g: (0,) * len(shape))


def stat_spec(rows):
    return pl.BlockSpec((GROUP, rows, 1), lambda g: (g, 0, 0))


def params():
    return pltpu.CompilerParams(dimension_semantics=("arbitrary",))


def cost(rows, matmuls, exps):
    flops = 2 * rows * rows * HD * QH * matmuls
    return pl.CostEstimate(
        flops=flops, transcendentals=rows * rows * QH * exps, bytes_accessed=4 * rows * QH * HD * 2
    )


def own_stats(queries, output_grad, keys, values, bias):
    rows = queries.shape[0]
    stat = jax.ShapeDtypeStruct((QH, rows, 1), jnp.float32)
    return pl.pallas_call(
        own_stats_kernel,
        grid=(KVH,),
        in_specs=[heads_spec(rows), heads_spec(rows), kv_spec(rows), kv_spec(rows),
                  full_spec((rows, rows))],
        out_specs=[stat_spec(rows)] * 3,
        out_shape=[stat] * 3,
        compiler_params=params(),
        cost_estimate=cost(rows, 2, 1),
    )(queries, output_grad, keys, values, bias)


def rim_grads(queries, output_grad, far, near, bias_far, bias_near, m0, l0, t0):
    rows = queries.shape[0]
    stat = jax.ShapeDtypeStruct((QH, rows, 1), jnp.float32)
    part = jax.ShapeDtypeStruct((rows, KVH * HD), jnp.bfloat16)
    return pl.pallas_call(
        rim_kernel,
        grid=(KVH,),
        in_specs=[heads_spec(rows), heads_spec(rows), stacked_spec(rows), stacked_spec(rows),
                  full_spec((rows, rows)), full_spec((rows, rows))]
        + [stat_spec(rows)] * 3,
        out_specs=[kv_spec(rows), kv_spec(rows), heads_spec(rows)] + [stat_spec(rows)] * 3,
        out_shape=[part, part, jax.ShapeDtypeStruct((rows, QH * HD), jnp.float32)] + [stat] * 3,
        compiler_params=params(),
        cost_estimate=cost(rows, 8, 2),
    )(queries, output_grad, far, near, bias_far, bias_near, m0, l0, t0)


def own_grads(queries, output_grad, keys, values, bias, m, il, d, dq_rim):
    rows = queries.shape[0]
    return pl.pallas_call(
        own_grads_kernel,
        grid=(KVH,),
        in_specs=[heads_spec(rows), heads_spec(rows), kv_spec(rows), kv_spec(rows),
                  full_spec((rows, rows))]
        + [stat_spec(rows)] * 3
        + [heads_spec(rows)],
        out_specs=[heads_spec(rows), kv_spec(rows)],
        out_shape=[jax.ShapeDtypeStruct((rows, QH * HD), jnp.bfloat16),
                   jax.ShapeDtypeStruct((rows, KVH * HD), jnp.float32)],
        compiler_params=params(),
        cost_estimate=cost(rows, 4, 1),
    )(queries, output_grad, keys, values, bias, m, il, d, dq_rim)


def body(queries, key_vectors, value_vectors, output_grad, doc_lengths):
    rows = queries.shape[0]
    axes = ("ctx", "uly")
    key_value = jnp.stack([key_vectors, value_vectors])
    near_rim = shifted(key_value, axes, 1)
    far_rim = shifted(key_value, axes, 2)
    device_index = lax.axis_index(axes)
    base = device_index * rows
    query_pos = base + jnp.arange(rows, dtype=jnp.int32)
    bias_own = mask_bias(doc_lengths, query_pos, query_pos)
    bias_near = mask_bias(doc_lengths, query_pos, query_pos - rows)
    bias_far = mask_bias(doc_lengths, query_pos, query_pos - 2 * rows)

    m0, l0, t0 = own_stats(queries, output_grad, key_vectors, value_vectors, bias_own)
    dk_far, dk_near, dq_rim, m, il, d = rim_grads(
        queries, output_grad, far_rim, near_rim, bias_far, bias_near, m0, l0, t0
    )
    far_back = shifted(dk_far, axes, -2)
    near_back = shifted(dk_near, axes, -1)
    query_grad, own_key_grad = own_grads(
        queries, output_grad, key_vectors, value_vectors, bias_own, m, il, d, dq_rim
    )
    key_grad = (
        own_key_grad + near_back.astype(jnp.float32) + far_back.astype(jnp.float32)
    ).astype(jnp.bfloat16)
    return (query_grad, key_grad)


def solution(mesh):
    placed = (
        P(("dp", "ctx", "uly"), None),
        P(("dp", "ctx", "uly"), None),
        P(("dp", "ctx", "uly"), None),
        P(("dp", "ctx", "uly"), None),
        P("dp"),
    )
    return jax.shard_map(
        body,
        mesh=mesh,
        in_specs=placed,
        out_specs=(P(("dp", "ctx", "uly"), None), P(("dp", "ctx", "uly"), None)),
        check_vma=False,
    )
```

time: 50.4 us -> 67 us (1.33)
  Pallas kernels: 0 us -> 39 us
  local copies, waits for them, and re-layouts: 10.9 us -> 1.44 us
  matrix products: 6.29 us -> 0 us
  waiting for transfers between devices: 12.2 us -> 8.59 us
  other arithmetic: 5.34 us -> 3.7 us
  starting transfers between devices: 14.2 us -> 13.2 us
    pallas_call x0 -> x3, Pallas kernels: none -> 39 us  [the longest x1 22.9 us: rim_grads(): pl.pallas_call(rim_kernel, grid=(KVH,), in_specs=[heads_spec(rows), heads...]
    dot_general x8 -> x0, matrix products: 6.29 us -> none  [the longest x1 1.69 us: body(): jnp.einsum('tghd,sgd->ghts', grad_heads, rim_values, preferred_element_ty...]
    unnamed x9 -> x4, local copies, waits for them, and re-layouts: 4.75 us -> 0.7 us
    ppermute x4, waiting for transfers between devices: 12.2 us -> 8.59 us  [shifted(): return lax.ppermute(block, axis, route)]
    reshape x5 -> x0, local copies, waits for them, and re-layouts: 2.81 us -> none  [the longest x2 1.08 us: body(): own_keys = key_vectors.reshape(rows, KVH, HD)]
    convert_element_type x2 -> x0, other arithmetic: 2.37 us -> none  [the longest x1 1.57 us: body(): (rim_exp / row_sum * (rim_grad_p - row_delta)).astype(jnp.bfloat16)]
    convert_element_type x2 -> x0, local copies, waits for them, and re-layouts: 1.52 us -> none  [the longest x1 0.77 us: body(): far_back = shifted(rim_key_grad[:rows].astype(jnp.bfloat16), axes, -2)]
    ppermute x4, starting transfers between devices: 14.2 us -> 13.2 us  [shifted(): return lax.ppermute(block, axis, route)]
  transfers between devices with their start and end apart: 4 -> 4, of which waited for: 3 -> 1; matrix products, arithmetic and copies ran while one was open for 19% -> 3% of each run, Pallas kernels for 0% -> 24%
where the time goes in v3:
time: 67 us; the launch traced here: 66.7 us
  Pallas kernels  39 us (58%)
  starting transfers between devices  13.2 us (20%)
  waiting for transfers between devices  8.59 us (13%)
  other arithmetic  3.7 us (6%)
  local copies, waits for them, and re-layouts  1.44 us (2%)
  between operations  0.73 us (1%)
    pallas_call x1, Pallas kernels, rim_grads(): pl.pallas_call(rim_kernel, grid=(KVH,), in_specs=[heads_spec(rows), heads...  22.9 us
    ppermute x4, starting transfers between devices, shifted(): return lax.ppermute(block, axis, route)  13.2 us
    pallas_call x1, Pallas kernels, own_grads(): pl.pallas_call(own_grads_kernel, grid=(KVH,), in_specs=[heads_spec(rows),...  10.1 us
    ppermute x4, waiting for transfers between devices, shifted(): return lax.ppermute(block, axis, route)  8.59 us
    pallas_call x1, Pallas kernels, own_stats(): pl.pallas_call(own_stats_kernel, grid=(KVH,), in_specs=[heads_spec(rows),...  5.95 us
    convert_element_type x1, other arithmetic, body(): key_grad = (own_key_grad + near_back.astype(jnp.float32) + far_back.astyp...  1.65 us
  transfers between devices with their start and end apart: 4, of which 1 were waited for; matrix products, arithmetic and copies ran while one was open for 3% of the time, Pallas kernels for 24%

profile of v3, /device:TPU:1, one launch (start us, length us, event | category | flops | bytes accessed | tf_op | source)
XLA Modules:
  0.0 66.7 jit_solution(12514037897441894430)
XLA Ops:
  0.6 1.0 %pad_maximum_fusion = bf16[2,128,512]{2,1,0:T(8,128)(2,1)S(1)} fusion(bf16[1,128,512]{2,1,0:T(8,128)(2,1)} %bitcast.4, bf16[1,128,512]{2,1,0:T(8,128)(2,1)} %bitcast.3), kind=kLoop, calls=%fused_computation | loop fusion | flops 131072 | bytes 524288 | tf_op jit(solution)/shard_map/stack | solution.py:221
  1.6 4.0 %collective-permute-start.1 = (bf16[2,128,512]{2,1,0:T(8,128)(2,1)S(1)}, bf16[2,128,512]{2,1,0:T(8,128)(2,1)S(1)}, u32[]{:S(2)}, u32[]{:S(2)}) collective-permute-start(bf16[2,128,512]{2,1,0:T(8,128)(2,1)S(1)} %pad_maximum_fusion), channel_id=1, source_target_pairs={{0,2},{2,4},{4,6},{6,8},{8,10},{10,12},{12,14},{14,16},{16,18},{18... | collective-permute-start | bytes 786440 | tf_op jit(solution)/shard_map/ppermute | solution.py:21
  5.7 4.2 %collective-permute-start = (bf16[2,128,512]{2,1,0:T(8,128)(2,1)S(1)}, bf16[2,128,512]{2,1,0:T(8,128)(2,1)S(1)}, u32[]{:S(2)}, u32[]{:S(2)}) collective-permute-start(bf16[2,128,512]{2,1,0:T(8,128)(2,1)S(1)} %pad_maximum_fusion), channel_id=1, source_target_pairs={{0,4},{2,6},{4,8},{6,10},{8,12},{10,14},{12,16},{14,18},{16,20},{1... | collective-permute-start | bytes 786440 | tf_op jit(solution)/shard_map/ppermute | solution.py:21
  9.9 0.7 %copy.9 = s32[16,1]{1,0:T(8,128)S(1)} copy(s32[16,1]{0,1:T(1,128)} %bitcast.5) | data formatting | bytes 128 | tf_op jit(solution)/shard_map/reshape.62
  10.7 0.1 reduce
  10.8 0.1 convert_reduce_fusion
  10.9 0.8 %and_select_fusion = (f32[128,128]{1,0:T(8,128)}, f32[128,128]{1,0:T(8,128)}, f32[128,128]{1,0:T(8,128)}) fusion(s32[128]{0:T(128)S(1)} %broadcast_add_fusion, s32[128]{0:T(128)S(1)} %get-tuple-element.30, s32[128]{0:T(128)S(1)} %iota_add_fusion, s32[128]{0:T(128)S(1)} %compare_select_fusion.2, s32[128]{0:T(128)S(1)} %broadcast_add_fusion.1, ...), kind=kLoop, calls=%fused_computation.2 | loop fusion | flops 196608 | bytes 199680 | tf_op jit(solution)/shard_map/jit(_where)/select_n | solution.py:34
  11.7 6.0 %shard_map.68 = (f32[32,128,1]{2,1,0:T(8,128)}, f32[32,128,1]{2,1,0:T(8,128)}, f32[32,128,1]{2,1,0:T(8,128)}) custom-call(bf16[128,4096]{1,0:T(8,128)(2,1)} %q_ref.5, bf16[128,4096]{1,0:T(8,128)(2,1)} %do_ref.5, bf16[128,512]{1,0:T(8,128)(2,1)} %k_ref.3, bf16[128,512]{1,0:T(8,128)(2,1)} %v_ref.3, f32[128,128]{1,0:T(8,128)} %get-tuple-element.29.bias_ref), custom_call_target="tpu_custom_call" | custom-call | flops 268435456 | bytes 4194304 | tf_op jit(solution)/shard_map/pallas_call | solution.py:172
  17.7 0.0 collective-permute-done.1.near_ref
  17.7 0.0 copy-start
  17.7 8.6 %collective-permute-done.far_ref = bf16[2,128,512]{2,1,0:T(8,128)(2,1)S(1)} collective-permute-done((bf16[2,128,512]{2,1,0:T(8,128)(2,1)S(1)}, bf16[2,128,512]{2,1,0:T(8,128)(2,1)S(1)}, u32[]{:S(2)}, u32[]{:S(2)}) %collective-permute-start) | collective-permute-done | bytes 262176 | tf_op jit(solution)/shard_map/ppermute | solution.py:21
  26.3 0.0 copy-start.1
  26.3 0.0 copy-done
  26.3 0.7 %copy-done.1 = bf16[2,128,512]{2,1,0:T(8,128)(2,1)} copy-done((bf16[2,128,512]{2,1,0:T(8,128)(2,1)}, bf16[2,128,512]{2,1,0:T(8,128)(2,1)S(1)}, u32[]{:S(2)}) %copy-start.1) | copy-done | bytes 262168
  27.0 22.9 %shard_map.69 = (bf16[128,512]{1,0:T(8,128)(2,1)}, bf16[128,512]{1,0:T(8,128)(2,1)}, f32[128,4096]{1,0:T(8,128)}, f32[32,128,1]{2,1,0:T(8,128)}, f32[32,128,1]{2,1,0:T(8,128)}, /*index=5*/f32[32,128,1]{2,1,0:T(8,128)}) custom-call(bf16[128,4096]{1,0:T(8,128)(2,1)} %q_ref.5, bf16[128,4096]{1,0:T(8,128)(2,1)} %do_ref.5, bf16[2,128,512]{2,1,0:T(8,128)(2,1)} %copy-done.1, ...), custom_call_target="tpu_custom_call" | custom-call | flops 1073741824 | bytes 4194304 | tf_op jit(solution)/shard_map/pallas_call | solution.py:188
  49.9 3.0 %collective-permute-start.2 = (bf16[128,512]{1,0:T(8,128)(2,1)}, bf16[128,512]{1,0:T(8,128)(2,1)S(1)}, u32[]{:S(2)}, u32[]{:S(2)}) collective-permute-start(bf16[128,512]{1,0:T(8,128)(2,1)} %get-tuple-element.22), channel_id=1, source_target_pairs={{2,0},{4,2},{6,4},{8,6},{10,8},{12,10},{14,12},{16,14},{18,16},{20... | collective-permute-start | bytes 393224 | tf_op jit(solution)/shard_map/ppermute | solution.py:21
  52.9 1.9 %collective-permute-start.3 = (bf16[128,512]{1,0:T(8,128)(2,1)}, bf16[128,512]{1,0:T(8,128)(2,1)S(1)}, u32[]{:S(2)}, u32[]{:S(2)}) collective-permute-start(bf16[128,512]{1,0:T(8,128)(2,1)} %get-tuple-element.23), channel_id=1, source_target_pairs={{4,0},{6,2},{8,4},{10,6},{12,8},{14,10},{16,12},{18,14},{20,16},{2... | collective-permute-start | bytes 393224 | tf_op jit(solution)/shard_map/ppermute | solution.py:21
  54.9 10.1 %shard_map.70 = (bf16[128,4096]{1,0:T(8,128)(2,1)}, f32[128,512]{1,0:T(8,128)}) custom-call(bf16[128,4096]{1,0:T(8,128)(2,1)} %q_ref.5, bf16[128,4096]{1,0:T(8,128)(2,1)} %do_ref.5, bf16[128,512]{1,0:T(8,128)(2,1)} %k_ref.3, bf16[128,512]{1,0:T(8,128)(2,1)} %v_ref.3, f32[128,128]{1,0:T(8,128)} %get-tuple-element.29.bias_ref, ...), custom_call_target="tpu_custom_call" | custom-call | flops 536870912 | bytes 4194304 | tf_op jit(solution)/shard_map/pallas_call | solution.py:203
  65.0 0.0 collective-permute-done.2
  65.0 0.0 collective-permute-done.3
  65.0 1.7 %add_convert_fusion = bf16[128,512]{1,0:T(8,128)(2,1)} fusion(bf16[128,512]{1,0:T(8,128)(2,1)S(1)} %collective-permute-done.3, f32[128,512]{1,0:T(8,128)} %get-tuple-element.21, bf16[128,512]{1,0:T(8,128)(2,1)S(1)} %collective-permute-done.2), kind=kLoop, calls=%fused_computation.1 | loop fusion | flops 327680 | bytes 655360 | tf_op jit(solution)/shard_map/convert_element_type | solution.py:242
  (6 shorter events, 0.1 us)
Async XLA Ops:
  1.6 16.0 %collective-permute-start.1 = (bf16[2,128,512]{2,1,0:T(8,128)(2,1)S(1)}, bf16[2,128,512]{2,1,0:T(8,128)(2,1)S(1)}, u32[]{:S(2)}, u32[]{:S(2)}) collective-permute-start(bf16[2,128,512]{2,1,0:T(8,128)(2,1)S(1)} %pad_maximum_fusion), channel_id=1, source_target_pairs={{0,2},{2,4},{4,6},{6,8},{8,10},{10,12},{12,14},{14,16},{16,18},{18... | collective-permute-start | bytes 786440 | tf_op jit(solution)/shard_map/ppermute | solution.py:21
  5.7 20.6 %collective-permute-start = (bf16[2,128,512]{2,1,0:T(8,128)(2,1)S(1)}, bf16[2,128,512]{2,1,0:T(8,128)(2,1)S(1)}, u32[]{:S(2)}, u32[]{:S(2)}) collective-permute-start(bf16[2,128,512]{2,1,0:T(8,128)(2,1)S(1)} %pad_maximum_fusion), channel_id=1, source_target_pairs={{0,4},{2,6},{4,8},{6,10},{8,12},{10,14},{12,16},{14,18},{16,20},{1... | collective-permute-start | bytes 786440 | tf_op jit(solution)/shard_map/ppermute | solution.py:21
  17.7 8.6 %copy-start = (bf16[2,128,512]{2,1,0:T(8,128)(2,1)}, bf16[2,128,512]{2,1,0:T(8,128)(2,1)S(1)}, u32[]{:S(2)}) copy-start(bf16[2,128,512]{2,1,0:T(8,128)(2,1)S(1)} %collective-permute-done.1.near_ref) | copy-start | bytes 786436
  26.3 0.7 %copy-start.1 = (bf16[2,128,512]{2,1,0:T(8,128)(2,1)}, bf16[2,128,512]{2,1,0:T(8,128)(2,1)S(1)}, u32[]{:S(2)}) copy-start(bf16[2,128,512]{2,1,0:T(8,128)(2,1)S(1)} %collective-permute-done.far_ref) | copy-start | bytes 786436
  49.9 15.1 %collective-permute-start.2 = (bf16[128,512]{1,0:T(8,128)(2,1)}, bf16[128,512]{1,0:T(8,128)(2,1)S(1)}, u32[]{:S(2)}, u32[]{:S(2)}) collective-permute-start(bf16[128,512]{1,0:T(8,128)(2,1)} %get-tuple-element.22), channel_id=1, source_target_pairs={{2,0},{4,2},{6,4},{8,6},{10,8},{12,10},{14,12},{16,14},{18,16},{20... | collective-permute-start | bytes 393224 | tf_op jit(solution)/shard_map/ppermute | solution.py:21
  52.9 12.1 %collective-permute-start.3 = (bf16[128,512]{1,0:T(8,128)(2,1)}, bf16[128,512]{1,0:T(8,128)(2,1)S(1)}, u32[]{:S(2)}, u32[]{:S(2)}) collective-permute-start(bf16[128,512]{1,0:T(8,128)(2,1)} %get-tuple-element.23), channel_id=1, source_target_pairs={{4,0},{6,2},{8,4},{10,6},{12,8},{14,10},{16,12},{18,14},{20,16},{2... | collective-permute-start | bytes 393224 | tf_op jit(solution)/shard_map/ppermute | solution.py:21

commit v4 on v2

--- a/solution.py
+++ b/solution.py
@@ -36,13 +36,31 @@
     return jnp.where(allowed[None, None], scores, NEG)
 
 
+def fetch_rims(key_value):
+    width = lax.axis_size("uly")
+    groups = lax.axis_size("ctx")
+    place = lax.axis_index("uly")
+    gathered = lax.all_gather(key_value, "uly")
+    tail = gathered[width - 2 :]
+    route = [
+        ((group - 1) * width + spot, group * width + spot)
+        for group in range(1, groups)
+        for spot in (0, 1)
+    ]
+    wrap = lax.ppermute(tail, ("ctx", "uly"), route)
+    before_one = lax.dynamic_index_in_dim(gathered, jnp.maximum(place - 1, 0), 0, keepdims=False)
+    before_two = lax.dynamic_index_in_dim(gathered, jnp.maximum(place - 2, 0), 0, keepdims=False)
+    near_rim = jnp.where(place >= 1, before_one, wrap[1])
+    far_rim = jnp.where(place >= 2, before_two, jnp.where(place == 1, wrap[1], wrap[0]))
+    return near_rim, far_rim
+
+
 def body(queries, key_vectors, value_vectors, output_grad, doc_lengths):
     rows = queries.shape[0]
     score_scale = HD ** (-0.5)
     axes = ("ctx", "uly")
     key_value = jnp.stack([key_vectors, value_vectors])
-    near_rim = shifted(key_value, axes, 1)
-    far_rim = shifted(key_value, axes, 2)
+    near_rim, far_rim = fetch_rims(key_value)
     device_index = lax.axis_index(axes)
     query_heads = queries.reshape(rows, KVH, GROUP, HD)
     grad_heads = output_grad.reshape(rows, KVH, GROUP, HD)

time: 50.4 us -> 85.7 us (1.70)
  waiting for transfers between devices: 12.2 us -> 26.6 us
  between operations: 0.92 us -> 14.3 us
  local copies, waits for them, and re-layouts: 10.9 us -> 16.4 us
  starting transfers between devices: 14.2 us -> 8.96 us
  other arithmetic: 5.34 us -> 9.09 us
  matrix products: 6.29 us -> 9.89 us
    all_gather x0 -> x1, waiting for transfers between devices: none -> 23.8 us  [fetch_rims(): gathered = lax.all_gather(key_value, 'uly')]
    ppermute x4 -> x2, waiting for transfers between devices: 12.2 us -> 2.31 us  [shifted(): return lax.ppermute(block, axis, route)]
    ppermute x4 -> x2, starting transfers between devices: 14.2 us -> 5.13 us  [shifted(): return lax.ppermute(block, axis, route)]
    slice x1 -> x2, local copies, waits for them, and re-layouts: 0.04 us -> 3.91 us  [fetch_rims(): tail = gathered[width - 2:]]
    ppermute x0 -> x1, starting transfers between devices: none -> 3.79 us  [fetch_rims(): wrap = lax.ppermute(tail, ('ctx', 'uly'), route)]
    dot_general x1, matrix products: 1.03 us -> 3.48 us  [body(): jnp.einsum('tghd,sgd->ghts', grad_heads, own_values, preferred_element_ty...]
    all_gather x0 -> x1, local copies, waits for them, and re-layouts: none -> 2.26 us  [fetch_rims(): gathered = lax.all_gather(key_value, 'uly')]
    convert_element_type x1, other arithmetic: 0.8 us -> 2.5 us  [body(): own_grad_s = (own_prob * (own_grad_p - row_delta)).astype(jnp.bfloat16)]
  transfers between devices with their start and end apart: 4 -> 4, of which waited for: 3 -> 3; matrix products, arithmetic and copies ran while one was open for 19% -> 22% of each run, Pallas kernels for 0% -> 0%
where the time goes in v4:
time: 85.7 us; the launch traced here: 85.2 us
  waiting for transfers between devices  26.6 us (31%)
  local copies, waits for them, and re-layouts  16.4 us (19%)
  between operations  14.3 us (17%)
  matrix products  9.89 us (12%)
  other arithmetic  9.09 us (11%)
  starting transfers between devices  8.96 us (10%)
    all_gather x1, waiting for transfers between devices, fetch_rims(): gathered = lax.all_gather(key_value, 'uly')  23.8 us
    ppermute x2, starting transfers between devices, shifted(): return lax.ppermute(block, axis, route)  5.13 us
    slice x2, local copies, waits for them, and re-layouts, fetch_rims(): tail = gathered[width - 2:]  3.91 us
    ppermute x1, starting transfers between devices, fetch_rims(): wrap = lax.ppermute(tail, ('ctx', 'uly'), route)  3.79 us
    unnamed x14, local copies, waits for them, and re-layouts  3.53 us
    dot_general x1, matrix products, body(): jnp.einsum('tghd,sgd->ghts', grad_heads, own_values, preferred_element_ty...  3.48 us
    reshape x2, local copies, waits for them, and re-layouts, body(): own_keys = key_vectors.reshape(rows, KVH, HD)  2.63 us
    convert_element_type x1, other arithmetic, body(): own_grad_s = (own_prob * (own_grad_p - row_delta)).astype(jnp.bfloat16)  2.5 us
  transfers between devices with their start and end apart: 4, of which 3 were waited for; matrix products, arithmetic and copies ran while one was open for 22% of the time, Pallas kernels for 0%

profile of v4, /device:TPU:1, one launch (start us, length us, event | category | flops | bytes accessed | tf_op | source)
XLA Modules:
  0.0 85.2 jit_solution(6849986986762788022)
XLA Ops:
  7.2 1.8 %pad_maximum_fusion.1 = bf16[2,128,512]{2,1,0:T(8,128)(2,1)} fusion(bf16[1,128,512]{2,1,0:T(8,128)(2,1)} %bitcast.131, bf16[1,128,512]{2,1,0:T(8,128)(2,1)} %bitcast.130), kind=kLoop, calls=%fused_computation.38 | loop fusion | flops 131072 | bytes 524288 | tf_op jit(solution)/shard_map/stack | solution.py:62
  9.1 1.6 %reshape.259 = bf16[128,4,128]{2,1,0:T(4,128)(2,1)} reshape(bf16[128,512]{1,0:T(8,128)(2,1)} %param.6) | data formatting | bytes 262144 | tf_op jit(solution)/shard_map/reshape | solution.py:67
  10.7 0.9 %reshape.261 = bf16[128,4,128]{2,1,0:T(4,128)(2,1)S(1)} reshape(bf16[128,512]{1,0:T(8,128)(2,1)} %param.7) | data formatting | bytes 262144 | tf_op jit(solution)/shard_map/reshape | solution.py:68
  13.2 1.0 %copy.97 = bf16[128,4,128,1]{0,2,3,1:T(8,128)(2,1)S(1)} copy(bf16[128,4,128,1]{2,1,0,3:T(4,128)(2,1)} %bitcast.129) | data formatting | bytes 262144 | tf_op jit(solution)/shard_map/reshape | solution.py:67
  14.3 1.2 %copy.115 = bf16[16,8,32,128]{3,2,1,0:T(8,128)(2,1)} copy(bf16[16,8,32,128]{3,1,2,0:T(8,128)(2,1)S(1)} %bitcast.125) | data formatting | bytes 2097152
  16.3 23.8 %all-gather.3.cloned.1.call-done = bf16[8,128,512]{2,1,0:T(8,128)(2,1)} async-done(((bf16[2,128,512]{2,1,0:T(8,128)(2,1)}), bf16[8,128,512]{2,1,0:T(8,128)(2,1)}) %all-gather.3.cloned.1.call-update) | async-done | bytes 1048592 | tf_op jit(solution)/shard_map/all_gather | solution.py:43
  40.1 1.9 %slice.36 = bf16[4,128,512]{2,1,0:T(8,128)(2,1)} slice(bf16[8,128,512]{2,1,0:T(8,128)(2,1)} %all-gather.3.cloned.1.call-done), slice={[4:8], [0:128], [0:512]} | slice | bytes 1048576 | tf_op jit(solution)/shard_map/slice | solution.py:44
  41.9 2.0 %copy.74 = bf16[4,128,512]{1,2,0:T(8,128)(2,1)} copy(bf16[4,128,512]{2,1,0:T(8,128)(2,1)} %slice.36) | data formatting | bytes 1048576 | tf_op jit(solution)/shard_map/slice | solution.py:44
  44.0 3.8 %collective-permute-start = (bf16[2,2,128,512]{2,3,1,0:T(8,128)(2,1)}, bf16[2,2,128,512]{2,3,1,0:T(8,128)(2,1)}, u32[]{:S(2)}, u32[]{:S(2)}) collective-permute-start(bf16[2,2,128,512]{2,3,1,0:T(8,128)(2,1)} %bitcast.128), channel_id=1, source_target_pairs={{0,8},{2,10},{8,16},{10,18},{16,24},{18,26},{1,9},{3,11},{9,17},{1... | collective-permute-start | bytes 1572872 | tf_op jit(solution)/shard_map/ppermute | solution.py:50
  47.9 3.5 %fusion.7 = (f32[4,8,128]{2,1,0:T(8,128)S(1)}, f32[4,8,128]{2,1,0:T(8,128)S(1)}, f32[4,128,128,8]{2,1,3,0:T(8,128)}) fusion(f32[4,128,128,8]{2,1,3,0:T(8,128)S(1)} %get-tuple-element.23, f32[4,8,128]{2,1,0:T(8,128)S(1)} %get-tuple-element.22, pred[128,128]{0,1:T(8,128)(4,1)S(1)} %compare_and_fusion.1, bf16[128,4,8,128]{3,2,1,0:T(8,128)(2,1)} %bitcast.118, ...), kind=kOutput, calls=%fused_computation.14 | convolution fusion | flops 137355264 | bytes 5439488 | tf_op jit(solution)/shard_map/tghd,sgd->ghts/dot_general | solution.py:79
  51.4 2.3 %copy.73 = bf16[8,128,512]{1,2,0:T(8,128)(2,1)} copy(bf16[8,128,512]{2,1,0:T(8,128)(2,1)} %all-gather.3.cloned.1.call-done) | data formatting | bytes 2097152 | tf_op jit(solution)/shard_map/all_gather | solution.py:43
  54.2 1.3 %select_bitcast_fusion = (bf16[2,128,512]{1,2,0:T(8,128)(2,1)S(1)}, bf16[2,128,512]{1,2,0:T(8,128)(2,1)S(1)}) fusion(bf16[4,2,128,512]{2,3,1,0:T(8,128)(2,1)} %bitcast.121, s32[]{:T(128)S(6)} %max.24, pred[]{:T(512)S(6)} %ge.23, bf16[2,2,128,512]{2,3,1,0:T(8,128)(2,1)} %collective-permute-done, pred[]{:T(512)S(6)} %eq.43, s32[]{:T(128)S(6)} %max.23, pred[]{:T(512)S(6)} %ge.22), kind=kLoop, calls=%fused_computation.40 | loop fusion | flops 393216 | bytes 1572875 | tf_op jit(solution)/shard_map/jit(_where)/select_n | solution.py:53
  55.5 0.8 fusion.3
  56.7 1.6 %fusion = (f32[4,8,128]{2,1,0:T(8,128)S(1)}, f32[4,8,128]{2,1,0:T(8,128)S(1)}, f32[4,256,128,8]{2,1,3,0:T(8,128)S(1)}) fusion(f32[4,256,128,8]{2,1,3,0:T(8,128)S(1)} %get-tuple-element.25, f32[4,8,128]{2,1,0:T(8,128)S(1)} %max.25, pred[128,256]{0,1:T(8,128)(4,1)S(1)} %compare_and_fusion, bf16[256,4,128,1]{0,2,3,1:T(8,128)(2,1)S(1)} %bitcast.126, ...), kind=kOutput, calls=%fused_computation.2 | convolution fusion | flops 274718720 | bytes 9781248 | tf_op jit(solution)/shard_map/tghd,sgd->ghts/dot_general | solution.py:91
  59.6 1.5 %fusion.2 = bf16[4,8,128,256]{2,3,1,0:T(8,128)(2,1)S(1)} fusion(f32[4,256,128,8]{2,1,3,0:T(8,128)S(1)} %get-tuple-element.26, f32[4,256,128,8]{2,1,3,0:T(8,128)S(1)} %get-tuple-element.25, f32[4,8,128]{2,1,0:T(8,128)S(1)} %add_divide_fusion, f32[4,8,128]{2,1,0:T(8,128)S(1)} %get-tuple-element.15, f32[4,8,128]{2,1,0:T(8,128)S(1)} %max.25, ...), kind=kLoop, calls=%fused_computation.4 | loop fusion | flops 7340032 | bytes 10567680 | tf_op jit(solution)/shard_map/convert_element_type | solution.py:97
  61.1 0.8 fusion.13
  62.0 1.8 %fusion.26 = f32[4,128,8,128]{3,1,2,0:T(8,128)} fusion(bf16[256,4,128,1]{0,2,3,1:T(8,128)(2,1)S(1)} %bitcast.123, bf16[4,8,128,256]{2,3,1,0:T(8,128)(2,1)S(1)} %fusion.2), kind=kOutput, calls=%fused_computation.55 | convolution fusion | flops 268435456 | bytes 4456448 | tf_op jit(solution)/shard_map/ghts,sgd->tghd/dot_general | solution.py:113
  63.8 0.8 copy.88
  64.6 1.9 %collective-permute-start.1 = (bf16[128,512]{1,0:T(8,128)(2,1)}, bf16[128,512]{1,0:T(8,128)(2,1)S(1)}, u32[]{:S(2)}, u32[]{:S(2)}) collective-permute-start(bf16[128,512]{1,0:T(8,128)(2,1)} %copy.88), channel_id=1, source_target_pairs={{2,0},{4,2},{6,4},{8,6},{10,8},{12,10},{14,12},{16,14},{18,16},{20... | collective-permute-start | bytes 393224 | tf_op jit(solution)/shard_map/ppermute | solution.py:16
  66.5 0.8 copy.90
  67.2 3.2 %collective-permute-start.2 = (bf16[128,512]{1,0:T(8,128)(2,1)}, bf16[128,512]{1,0:T(8,128)(2,1)S(1)}, u32[]{:S(2)}, u32[]{:S(2)}) collective-permute-start(bf16[128,512]{1,0:T(8,128)(2,1)} %copy.90), channel_id=1, source_target_pairs={{4,0},{6,2},{8,4},{10,6},{12,8},{14,10},{16,12},{18,14},{20,16},{2... | collective-permute-start | bytes 393224 | tf_op jit(solution)/shard_map/ppermute | solution.py:16
  70.5 2.5 %fusion.9 = bf16[4,8,128,128]{2,3,1,0:T(8,128)(2,1)S(1)} fusion(f32[4,128,128,8]{2,1,3,0:T(8,128)} %get-tuple-element.27, f32[4,128,128,8]{2,1,3,0:T(8,128)S(1)} %get-tuple-element.23, f32[4,8,128]{2,1,0:T(8,128)} %copy-done.5, f32[4,8,128]{2,1,0:T(8,128)} %get-tuple-element.14, f32[4,8,128]{2,1,0:T(8,128)S(1)} %get-tuple-element.22, ...), kind=kLoop, calls=%fused_computation.16 | loop fusion | flops 3670016 | bytes 5308416 | tf_op jit(solution)/shard_map/convert_element_type | solution.py:106
  74.0 1.3 %copy.91 = bf16[128,4096]{1,0:T(8,128)(2,1)} copy(bf16[128,4096]{0,1:T(8,128)(2,1)S(1)} %bitcast.120) | data formatting | bytes 2097152
  75.3 2.3 %collective-permute-done.2 = bf16[128,512]{1,0:T(8,128)(2,1)S(1)} collective-permute-done((bf16[128,512]{1,0:T(8,128)(2,1)}, bf16[128,512]{1,0:T(8,128)(2,1)S(1)}, u32[]{:S(2)}, u32[]{:S(2)}) %collective-permute-start.2) | collective-permute-done | bytes 131104 | tf_op jit(solution)/shard_map/ppermute | solution.py:16
  (38 shorter events, 6.5 us)
Async XLA Ops:
  7.2 5.4 %copy-start.2 = (bf16[128,4096]{1,0:T(8,128)(2,1)S(1)}, bf16[128,4096]{1,0:T(8,128)(2,1)}, u32[]{:S(2)}) copy-start(bf16[128,4096]{1,0:T(8,128)(2,1)} %param.5) | copy-start | bytes 3145732
  7.2 7.1 %copy-start.3 = (bf16[128,4096]{1,0:T(8,128)(2,1)S(1)}, bf16[128,4096]{1,0:T(8,128)(2,1)}, u32[]{:S(2)}) copy-start(bf16[128,4096]{1,0:T(8,128)(2,1)} %param.8) | copy-start | bytes 3145732
  7.2 32.9 %all-gather.3.cloned.1.call-start = ((), (), s32[]{:S(2)}) async-start(), calls=%async_computation | async-start | bytes 1310720 | tf_op jit(solution)/shard_map/all_gather | solution.py:43
  15.8 32.1 %copy-start.4 = (pred[128,128]{0,1:T(8,128)(4,1)}, pred[128,128]{0,1:T(8,128)(4,1)S(1)}, u32[]{:S(2)}) copy-start(pred[128,128]{0,1:T(8,128)(4,1)S(1)} %compare_and_fusion.1) | copy-start | bytes 49156
  44.0 10.2 %collective-permute-start = (bf16[2,2,128,512]{2,3,1,0:T(8,128)(2,1)}, bf16[2,2,128,512]{2,3,1,0:T(8,128)(2,1)}, u32[]{:S(2)}, u32[]{:S(2)}) collective-permute-start(bf16[2,2,128,512]{2,3,1,0:T(8,128)(2,1)} %bitcast.128), channel_id=1, source_target_pairs={{0,8},{2,10},{8,16},{10,18},{16,24},{18,26},{1,9},{3,11},{9,17},{1... | collective-permute-start | bytes 1572872 | tf_op jit(solution)/shard_map/ppermute | solution.py:50
  55.5 1.2 %copy-start = (bf16[16,8,32,128]{3,2,1,0:T(8,128)(2,1)S(1)}, bf16[16,8,32,128]{3,2,1,0:T(8,128)(2,1)}, u32[]{:S(2)}) copy-start(bf16[16,8,32,128]{3,2,1,0:T(8,128)(2,1)} %copy.115) | copy-start | bytes 3145732
  59.0 0.6 copy-start.5
  64.6 10.8 %collective-permute-start.1 = (bf16[128,512]{1,0:T(8,128)(2,1)}, bf16[128,512]{1,0:T(8,128)(2,1)S(1)}, u32[]{:S(2)}, u32[]{:S(2)}) collective-permute-start(bf16[128,512]{1,0:T(8,128)(2,1)} %copy.88), channel_id=1, source_target_pairs={{2,0},{4,2},{6,4},{8,6},{10,8},{12,10},{14,12},{16,14},{18,16},{20... | collective-permute-start | bytes 393224 | tf_op jit(solution)/shard_map/ppermute | solution.py:16
  67.2 10.4 %collective-permute-start.2 = (bf16[128,512]{1,0:T(8,128)(2,1)}, bf16[128,512]{1,0:T(8,128)(2,1)S(1)}, u32[]{:S(2)}, u32[]{:S(2)}) collective-permute-start(bf16[128,512]{1,0:T(8,128)(2,1)} %copy.90), channel_id=1, source_target_pairs={{4,0},{6,2},{8,4},{10,6},{12,8},{14,10},{16,12},{18,14},{20,16},{2... | collective-permute-start | bytes 393224 | tf_op jit(solution)/shard_map/ppermute | solution.py:16
  70.5 2.5 %copy-start.1 = (f32[4,128,8,128]{3,1,2,0:T(8,128)S(1)}, f32[4,128,8,128]{3,1,2,0:T(8,128)}, u32[]{:S(2)}) copy-start(f32[4,128,8,128]{3,1,2,0:T(8,128)} %fusion.26) | copy-start | bytes 6291460
Sparse Core Ops, SparseCore 0:
  10.2 29.8 all-gather.2

commit v5 on v2

--- a/solution.py
+++ b/solution.py
@@ -36,6 +36,17 @@
     return jnp.where(allowed[None, None], scores, NEG)
 
 
+def key_grad_of(grad_s, query_heads, score_scale):
+    return (
+        jnp.einsum("ghts,tghd->gsd", grad_s, query_heads, preferred_element_type=jnp.float32)
+        * score_scale
+    )
+
+
+def query_grad_of(grad_s, keys):
+    return jnp.einsum("ghts,sgd->ghtd", grad_s, keys, preferred_element_type=jnp.float32)
+
+
 def body(queries, key_vectors, value_vectors, output_grad, doc_lengths):
     rows = queries.shape[0]
     score_scale = HD ** (-0.5)
@@ -50,9 +61,9 @@
     own_values = value_vectors.reshape(rows, KVH, HD)
     query_pos = device_index * rows + jnp.arange(rows, dtype=jnp.int32)
     own_pos = query_pos
-    rim_pos = device_index * rows - 2 * rows + jnp.arange(2 * rows, dtype=jnp.int32)
     own_allowed = allowed_pairs(doc_lengths, query_pos, own_pos)
-    rim_allowed = allowed_pairs(doc_lengths, query_pos, rim_pos)
+    near_allowed = allowed_pairs(doc_lengths, query_pos, own_pos - rows)
+    far_allowed = allowed_pairs(doc_lengths, query_pos, own_pos - 2 * rows)
 
     own_scores = scores_of(query_heads, own_keys, own_allowed, score_scale)
     own_max = jnp.max(own_scores, axis=-1, keepdims=True)
@@ -63,41 +74,56 @@
     )
     own_dot = jnp.sum(own_exp * own_grad_p, axis=-1, keepdims=True)
 
-    rim = jnp.concatenate([far_rim, near_rim], axis=1).reshape(2, 2 * rows, KVH, HD)
-    rim_keys, rim_values = rim[0], rim[1]
-    rim_scores = scores_of(query_heads, rim_keys, rim_allowed, score_scale)
-    row_max = jnp.maximum(own_max, jnp.max(rim_scores, axis=-1, keepdims=True))
-    rim_exp = jnp.exp(rim_scores - row_max)
+    far_keys = far_rim[0].reshape(rows, KVH, HD)
+    far_values = far_rim[1].reshape(rows, KVH, HD)
+    near_keys = near_rim[0].reshape(rows, KVH, HD)
+    near_values = near_rim[1].reshape(rows, KVH, HD)
+    far_scores = scores_of(query_heads, far_keys, far_allowed, score_scale)
+    near_scores = scores_of(query_heads, near_keys, near_allowed, score_scale)
+    row_max = jnp.maximum(
+        own_max,
+        jnp.maximum(
+            jnp.max(far_scores, axis=-1, keepdims=True),
+            jnp.max(near_scores, axis=-1, keepdims=True),
+        ),
+    )
+    far_exp = jnp.exp(far_scores - row_max)
+    near_exp = jnp.exp(near_scores - row_max)
     own_rescale = jnp.exp(own_max - row_max)
-    row_sum = own_sum * own_rescale + jnp.sum(rim_exp, axis=-1, keepdims=True)
-    rim_grad_p = jnp.einsum(
-        "tghd,sgd->ghts", grad_heads, rim_values, preferred_element_type=jnp.float32
+    row_sum = (
+        own_sum * own_rescale
+        + jnp.sum(far_exp, axis=-1, keepdims=True)
+        + jnp.sum(near_exp, axis=-1, keepdims=True)
+    )
+    far_grad_p = jnp.einsum(
+        "tghd,sgd->ghts", grad_heads, far_values, preferred_element_type=jnp.float32
+    )
+    near_grad_p = jnp.einsum(
+        "tghd,sgd->ghts", grad_heads, near_values, preferred_element_type=jnp.float32
     )
     row_delta = (
-        own_dot * own_rescale + jnp.sum(rim_exp * rim_grad_p, axis=-1, keepdims=True)
+        own_dot * own_rescale
+        + jnp.sum(far_exp * far_grad_p, axis=-1, keepdims=True)
+        + jnp.sum(near_exp * near_grad_p, axis=-1, keepdims=True)
     ) / row_sum
-    rim_grad_s = ((rim_exp / row_sum) * (rim_grad_p - row_delta)).astype(jnp.bfloat16)
-    rim_key_grad = (
-        jnp.einsum("ghts,tghd->sgd", rim_grad_s, query_heads, preferred_element_type=jnp.float32)
-        * score_scale
-    ).reshape(2 * rows, KVH * HD)
-    far_back = shifted(rim_key_grad[:rows].astype(jnp.bfloat16), axes, -2)
-    near_back = shifted(rim_key_grad[rows:].astype(jnp.bfloat16), axes, -1)
+    far_grad_s = ((far_exp / row_sum) * (far_grad_p - row_delta)).astype(jnp.bfloat16)
+    near_grad_s = ((near_exp / row_sum) * (near_grad_p - row_delta)).astype(jnp.bfloat16)
+    far_key_grad = key_grad_of(far_grad_s, query_heads, score_scale)
+    near_key_grad = key_grad_of(near_grad_s, query_heads, score_scale)
+    far_back = shifted(far_key_grad.astype(jnp.bfloat16), axes, -2)
+    near_back = shifted(near_key_grad.astype(jnp.bfloat16), axes, -1)
 
     own_prob = own_exp * (own_rescale / row_sum)
     own_grad_s = (own_prob * (own_grad_p - row_delta)).astype(jnp.bfloat16)
-    own_key_grad = (
-        jnp.einsum("ghts,tghd->sgd", own_grad_s, query_heads, preferred_element_type=jnp.float32)
-        * score_scale
-    ).reshape(rows, KVH * HD)
+    own_key_grad = key_grad_of(own_grad_s, query_heads, score_scale)
     query_grad = (
-        jnp.einsum("ghts,sgd->tghd", own_grad_s, own_keys, preferred_element_type=jnp.float32)
-        + jnp.einsum("ghts,sgd->tghd", rim_grad_s, rim_keys, preferred_element_type=jnp.float32)
+        query_grad_of(own_grad_s, own_keys)
+        + query_grad_of(far_grad_s, far_keys)
+        + query_grad_of(near_grad_s, near_keys)
     ) * score_scale
-    query_grad = query_grad.astype(jnp.bfloat16).reshape(rows, QH * HD)
-    key_grad = (
-        own_key_grad + near_back.astype(jnp.float32) + far_back.astype(jnp.float32)
-    ).astype(jnp.bfloat16)
+    query_grad = jnp.transpose(query_grad.astype(jnp.bfloat16), (2, 0, 1, 3)).reshape(rows, QH * HD)
+    key_grad = own_key_grad + near_back.astype(jnp.float32) + far_back.astype(jnp.float32)
+    key_grad = jnp.transpose(key_grad, (1, 0, 2)).reshape(rows, KVH * HD).astype(jnp.bfloat16)
     return (query_grad, key_grad)
 
 

time: 50.4 us -> 49.8 us (0.988)
  matrix products: 6.29 us -> 9.93 us
  other arithmetic: 5.34 us -> 3.42 us
  local copies, waits for them, and re-layouts: 10.9 us -> 9.5 us
  starting transfers between devices: 14.2 us -> 13.2 us
    dot_general x5 -> x8, matrix products: 3.95 us -> 6.94 us  [the longest x3 3.48 us: key_grad_of(): jnp.einsum('ghts,tghd->gsd', grad_s, query_heads, preferred_element_type=...]
    slice x2, local copies, waits for them, and re-layouts: 0.08 us -> 1.97 us  [the longest x1 0.99 us: body(): near_values = near_rim[1].reshape(rows, KVH, HD)]
    convert_element_type x3 -> x1, other arithmetic: 3.97 us -> 2.2 us  [body(): (near_exp / row_sum * (near_grad_p - row_delta)).astype(jnp.bfloat16)]
    convert_element_type x2 -> x0, local copies, waits for them, and re-layouts: 1.52 us -> none  [the longest x1 0.77 us: body(): far_back = shifted(rim_key_grad[:rows].astype(jnp.bfloat16), axes, -2)]
    ppermute x4, starting transfers between devices: 14.2 us -> 13.2 us  [shifted(): return lax.ppermute(block, axis, route)]
    concatenate x1 -> x0, local copies, waits for them, and re-layouts: 1.01 us -> none  [body(): jnp.concatenate([far_rim, near_rim], axis=1).reshape(2, 2 * rows, KVH, HD)]
    reshape x2 -> x0, local copies, waits for them, and re-layouts: 0.79 us -> none  [the longest x1 0.66 us: body(): query_heads = queries.reshape(rows, KVH, GROUP, HD)]
    dot_general x2 -> x3, matrix products: 1.31 us -> 1.95 us  [scores_of(): jnp.einsum('tghd,sgd->ghts', query_heads, key_heads, preferred_element_ty...]
where the time goes in v5:
time: 49.8 us; the launch traced here: 49.1 us
  starting transfers between devices  13.2 us (27%)
  waiting for transfers between devices  12.2 us (24%)
  matrix products  9.93 us (20%)
  local copies, waits for them, and re-layouts  9.5 us (19%)
  other arithmetic  3.42 us (7%)
  between operations  0.9 us (2%)
    ppermute x4, starting transfers between devices, shifted(): return lax.ppermute(block, axis, route)  13.2 us
    ppermute x4, waiting for transfers between devices, shifted(): return lax.ppermute(block, axis, route)  12.2 us
    unnamed x10, local copies, waits for them, and re-layouts  4.77 us
    dot_general x3, matrix products, key_grad_of(): jnp.einsum('ghts,tghd->gsd', grad_s, query_heads, preferred_element_type=...  3.48 us
    convert_element_type x1, other arithmetic, body(): (near_exp / row_sum * (near_grad_p - row_delta)).astype(jnp.bfloat16)  2.2 us
    dot_general x3, matrix products, scores_of(): jnp.einsum('tghd,sgd->ghts', query_heads, key_heads, preferred_element_ty...  1.95 us
    dot_general x1, matrix products, body(): jnp.einsum('tghd,sgd->ghts', grad_heads, far_values, preferred_element_ty...  1.62 us
    dot_general x3, matrix products, query_grad_of(): jnp.einsum('ghts,sgd->ghtd', grad_s, keys, preferred_element_type=jnp.flo...  1.33 us
  transfers between devices with their start and end apart: 4, of which 3 were waited for; matrix products, arithmetic and copies ran while one was open for 19% of the time, Pallas kernels for 0%

profile of v5, /device:TPU:1, one launch (start us, length us, event | category | flops | bytes accessed | tf_op | source)
XLA Modules:
  0.0 49.1 jit_solution(3503533689713045819)
XLA Ops:
  0.6 1.2 %copy.60 = bf16[128,512]{0,1:T(8,128)(2,1)S(1)} copy(bf16[128,512]{1,0:T(8,128)(2,1)} %param.6) | data formatting | bytes 262144 | tf_op args[1]
  1.8 1.0 %copy.61 = bf16[128,512]{0,1:T(8,128)(2,1)S(1)} copy(bf16[128,512]{1,0:T(8,128)(2,1)} %param.7) | data formatting | bytes 262144 | tf_op args[2]
  2.9 0.7 %pad_maximum_fusion = bf16[2,128,512]{1,2,0:T(8,128)(2,1)} fusion(bf16[1,128,512]{1,2,0:T(8,128)(2,1)S(1)} %bitcast.161, bf16[1,128,512]{1,2,0:T(8,128)(2,1)S(1)} %bitcast.160), kind=kLoop, calls=%fused_computation.51 | loop fusion | flops 131072 | bytes 524288 | tf_op jit(solution)/shard_map/stack | solution.py:54
  3.6 4.0 %collective-permute-start.1 = (bf16[2,128,512]{1,2,0:T(8,128)(2,1)}, bf16[2,128,512]{1,2,0:T(8,128)(2,1)}, u32[]{:S(2)}, u32[]{:S(2)}) collective-permute-start(bf16[2,128,512]{1,2,0:T(8,128)(2,1)} %pad_maximum_fusion), channel_id=1, source_target_pairs={{0,2},{2,4},{4,6},{6,8},{8,10},{10,12},{12,14},{14,16},{16,18},{18... | collective-permute-start | bytes 786440 | tf_op jit(solution)/shard_map/ppermute | solution.py:16
  7.6 4.2 %collective-permute-start = (bf16[2,128,512]{1,2,0:T(8,128)(2,1)}, bf16[2,128,512]{1,2,0:T(8,128)(2,1)}, u32[]{:S(2)}, u32[]{:S(2)}) collective-permute-start(bf16[2,128,512]{1,2,0:T(8,128)(2,1)} %pad_maximum_fusion), channel_id=1, source_target_pairs={{0,4},{2,6},{4,8},{6,10},{8,12},{10,14},{12,16},{14,18},{16,20},{1... | collective-permute-start | bytes 786440 | tf_op jit(solution)/shard_map/ppermute | solution.py:16
  11.9 0.9 %reshape.329 = bf16[128,4,128]{2,1,0:T(4,128)(2,1)S(1)} reshape(bf16[128,512]{1,0:T(8,128)(2,1)} %param.6) | data formatting | bytes 262144 | tf_op jit(solution)/shard_map/reshape | solution.py:60
  12.8 0.9 %reshape.331 = bf16[128,4,128]{2,1,0:T(4,128)(2,1)S(1)} reshape(bf16[128,512]{1,0:T(8,128)(2,1)} %param.7) | data formatting | bytes 262144 | tf_op jit(solution)/shard_map/reshape | solution.py:61
  13.8 0.7 %copy.57 = s32[16,1]{1,0:T(8,128)S(1)} copy(s32[16,1]{0,1:T(1,128)} %bitcast.163) | data formatting | bytes 128 | tf_op jit(solution)/shard_map/reshape.306
  15.6 0.7 %fusion.9 = (f32[4,8,128]{2,1,0:T(8,128)S(1)}, f32[4,128,128,8]{2,1,3,0:T(8,128)S(1)}) fusion(pred[128,128]{0,1:T(8,128)(4,1)S(1)} %get-tuple-element.29, bf16[128,4,128,1]{0,2,3,1:T(8,128)(2,1)S(1)} %copy.91, bf16[128,4,8,128]{3,2,1,0:T(8,128)(2,1)S(1)} %bitcast.140), kind=kOutput, calls=%fused_computation.22 | convolution fusion | flops 135786496 | bytes 3309568 | tf_op jit(solution)/shard_map/tghd,sgd->ghts/dot_general | solution.py:33
  16.3 1.0 %fusion.6 = (f32[4,8,128]{2,1,0:T(8,128)S(1)}, f32[4,8,128]{2,1,0:T(8,128)S(1)}, f32[4,128,128,8]{2,1,3,0:T(8,128)S(1)}) fusion(f32[4,128,128,8]{2,1,3,0:T(8,128)S(1)} %get-tuple-element.32, f32[4,8,128]{2,1,0:T(8,128)S(1)} %get-tuple-element.31, pred[128,128]{0,1:T(8,128)(4,1)S(1)} %get-tuple-element.29, bf16[128,4,8,128]{3,2,1,0:T(8,128)(2,1)S(1)} %bitcast.146, ...), kind=kOutput, calls=%fused_computation.12 | convolution fusion | flops 137355264 | bytes 5439488 | tf_op jit(solution)/shard_map/tghd,sgd->ghts/dot_general | solution.py:72
  17.3 1.0 %fusion.39 = (bf16[1,128,512]{1,2,0:T(8,128)(2,1)S(1)}, bf16[1,128,512]{1,2,0:T(8,128)(2,1)S(1)}) fusion(bf16[2,128,512]{1,2,0:T(8,128)(2,1)} %collective-permute-done.1), kind=kLoop, calls=%fused_computation.71 | loop fusion | bytes 524288 | tf_op jit(solution)/shard_map/slice | solution.py:80
  18.8 9.7 %collective-permute-done = bf16[2,128,512]{1,2,0:T(8,128)(2,1)} collective-permute-done((bf16[2,128,512]{1,2,0:T(8,128)(2,1)}, bf16[2,128,512]{1,2,0:T(8,128)(2,1)}, u32[]{:S(2)}, u32[]{:S(2)}) %collective-permute-start) | collective-permute-done | bytes 262176 | tf_op jit(solution)/shard_map/ppermute | solution.py:16
  28.5 1.0 %fusion.40 = (bf16[1,128,512]{1,2,0:T(8,128)(2,1)S(1)}, bf16[1,128,512]{1,2,0:T(8,128)(2,1)S(1)}) fusion(bf16[2,128,512]{1,2,0:T(8,128)(2,1)} %collective-permute-done), kind=kLoop, calls=%fused_computation.72 | loop fusion | bytes 524288 | tf_op jit(solution)/shard_map/slice | solution.py:78
  30.2 0.7 %fusion.11 = (f32[4,8,128]{2,1,0:T(8,128)S(1)}, f32[4,128,128,8]{2,1,3,0:T(8,128)S(1)}) fusion(pred[128,128]{0,1:T(8,128)(4,1)S(1)} %get-tuple-element.28, bf16[128,4,128,1]{0,2,3,1:T(8,128)(2,1)S(1)} %bitcast.150, bf16[128,4,8,128]{3,2,1,0:T(8,128)(2,1)S(1)} %bitcast.142), kind=kOutput, calls=%fused_computation.24 | convolution fusion | flops 135786496 | bytes 3309568 | tf_op jit(solution)/shard_map/tghd,sgd->ghts/dot_general | solution.py:33
  30.9 1.6 %fusion.3 = (f32[4,8,128]{2,1,0:T(8,128)S(1)}, f32[4,8,128]{2,1,0:T(8,128)S(1)}, f32[4,8,128]{2,1,0:T(8,128)S(1)}, f32[4,8,128]{2,1,0:T(8,128)S(1)}, f32[4,128,128,8]{2,1,3,0:T(8,128)S(1)}) fusion(f32[4,128,128,8]{2,1,3,0:T(8,128)S(1)} %get-tuple-element.34, f32[4,8,128]{2,1,0:T(8,128)S(1)} %maximum_maximum_fusion, ...), kind=kOutput, calls=%fused_computation.7 | convolution fusion | flops 140492800 | bytes 9682944 | tf_op jit(solution)/shard_map/tghd,sgd->ghts/dot_general | solution.py:98
  32.5 2.2 %fusion.2 = (bf16[4,8,128,128]{2,3,1,0:T(8,128)(2,1)S(1)}, bf16[4,8,128,128]{2,3,1,0:T(8,128)(2,1)S(1)}, bf16[4,8,128,128]{2,3,1,0:T(8,128)(2,1)S(1)}) fusion(f32[4,128,128,8]{2,1,3,0:T(8,128)S(1)} %fusion.20, f32[4,128,128,8]{2,1,3,0:T(8,128)S(1)} %get-tuple-element.36, f32[4,8,128]{2,1,0:T(8,128)S(1)} %get-tuple-element.20, ...), kind=kLoop, calls=%fused_computation.4 | loop fusion | flops 11010048 | bytes 15859712 | tf_op jit(solution)/shard_map/convert_element_type | solution.py:110
  35.8 1.3 %fusion.15 = bf16[4,128,128]{1,2,0:T(8,128)(2,1)} fusion(bf16[4,8,128,128]{2,3,1,0:T(8,128)(2,1)S(1)} %get-tuple-element.25, bf16[128,4,8,128]{3,2,1,0:T(8,128)(2,1)S(1)} %bitcast.144), kind=kOutput, calls=%fused_computation.31 | convolution fusion | flops 134348800 | bytes 2228224 | tf_op jit(solution)/shard_map/ghts,tghd->gsd/dot_general | solution.py:41
  37.1 1.9 %collective-permute-start.3 = (bf16[4,128,128]{1,2,0:T(8,128)(2,1)S(1)}, bf16[4,128,128]{1,2,0:T(8,128)(2,1)S(1)}, u32[]{:S(2)}, u32[]{:S(2)}) collective-permute-start(bf16[4,128,128]{1,2,0:T(8,128)(2,1)S(1)} %fusion.16), channel_id=1, source_target_pairs={{4,0},{6,2},{8,4},{10,6},{12,8},{14,10},{16,12},{18,14},{20,16},{2... | collective-permute-start | bytes 393224 | tf_op jit(solution)/shard_map/ppermute | solution.py:16
  39.0 3.0 %collective-permute-start.2 = (bf16[4,128,128]{1,2,0:T(8,128)(2,1)}, bf16[4,128,128]{1,2,0:T(8,128)(2,1)}, u32[]{:S(2)}, u32[]{:S(2)}) collective-permute-start(bf16[4,128,128]{1,2,0:T(8,128)(2,1)} %fusion.15), channel_id=1, source_target_pairs={{2,0},{4,2},{6,4},{8,6},{10,8},{12,10},{14,12},{16,14},{18,16},{20... | collective-permute-start | bytes 393224 | tf_op jit(solution)/shard_map/ppermute | solution.py:16
  43.0 1.3 %copy.82 = bf16[128,4096]{1,0:T(8,128)(2,1)} copy(bf16[128,4096]{0,1:T(8,128)(2,1)S(1)} %bitcast.149) | data formatting | bytes 2097152
  44.3 1.3 %collective-permute-done.3 = bf16[4,128,128]{1,2,0:T(8,128)(2,1)S(1)} collective-permute-done((bf16[4,128,128]{1,2,0:T(8,128)(2,1)S(1)}, bf16[4,128,128]{1,2,0:T(8,128)(2,1)S(1)}, u32[]{:S(2)}, u32[]{:S(2)}) %collective-permute-start.3) | collective-permute-done | bytes 131104 | tf_op jit(solution)/shard_map/ppermute | solution.py:16
  45.6 1.2 %collective-permute-done.2 = bf16[4,128,128]{1,2,0:T(8,128)(2,1)} collective-permute-done((bf16[4,128,128]{1,2,0:T(8,128)(2,1)}, bf16[4,128,128]{1,2,0:T(8,128)(2,1)}, u32[]{:S(2)}, u32[]{:S(2)}) %collective-permute-start.2) | collective-permute-done | bytes 131104 | tf_op jit(solution)/shard_map/ppermute | solution.py:16
  46.8 1.5 %add_convert_fusion = bf16[4,128,128]{1,2,0:T(8,128)(2,1)S(1)} fusion(bf16[4,128,128]{1,2,0:T(8,128)(2,1)S(1)} %collective-permute-done.3, bf16[4,128,128]{1,2,0:T(8,128)(2,1)} %collective-permute-done.2, bf16[4,8,128,128]{2,3,1,0:T(8,128)(2,1)S(1)} %get-tuple-element.27, bf16[128,4,8,128]{3,2,1,0:T(8,128)(2,1)S(1)} %bitcast.145), kind=kOutput, calls=%fused_computation.52 | convolution fusion | flops 134610944 | bytes 2490368 | tf_op jit(solution)/shard_map/ghts,tghd->gsd/dot_general | solution.py:41
  48.3 0.8 %copy.83 = bf16[128,512]{1,0:T(8,128)(2,1)} copy(bf16[128,512]{0,1:T(8,128)(2,1)S(1)} %bitcast.162) | data formatting | bytes 262144
  (26 shorter events, 4.3 us)
Async XLA Ops:
  0.6 14.3 %copy-start = (bf16[128,4096]{1,0:T(8,128)(2,1)S(1)}, bf16[128,4096]{1,0:T(8,128)(2,1)}, u32[]{:S(2)}) copy-start(bf16[128,4096]{1,0:T(8,128)(2,1)} %param.5) | copy-start | bytes 3145732
  0.6 14.5 %copy-start.1 = (bf16[128,4096]{1,0:T(8,128)(2,1)S(1)}, bf16[128,4096]{1,0:T(8,128)(2,1)}, u32[]{:S(2)}) copy-start(bf16[128,4096]{1,0:T(8,128)(2,1)} %param.8) | copy-start | bytes 3145732
  3.6 13.7 %collective-permute-start.1 = (bf16[2,128,512]{1,2,0:T(8,128)(2,1)}, bf16[2,128,512]{1,2,0:T(8,128)(2,1)}, u32[]{:S(2)}, u32[]{:S(2)}) collective-permute-start(bf16[2,128,512]{1,2,0:T(8,128)(2,1)} %pad_maximum_fusion), channel_id=1, source_target_pairs={{0,2},{2,4},{4,6},{6,8},{8,10},{10,12},{12,14},{14,16},{16,18},{18... | collective-permute-start | bytes 786440 | tf_op jit(solution)/shard_map/ppermute | solution.py:16
  7.6 20.9 %collective-permute-start = (bf16[2,128,512]{1,2,0:T(8,128)(2,1)}, bf16[2,128,512]{1,2,0:T(8,128)(2,1)}, u32[]{:S(2)}, u32[]{:S(2)}) collective-permute-start(bf16[2,128,512]{1,2,0:T(8,128)(2,1)} %pad_maximum_fusion), channel_id=1, source_target_pairs={{0,4},{2,6},{4,8},{6,10},{8,12},{10,14},{12,16},{14,18},{16,20},{1... | collective-permute-start | bytes 786440 | tf_op jit(solution)/shard_map/ppermute | solution.py:16
  37.1 8.5 %collective-permute-start.3 = (bf16[4,128,128]{1,2,0:T(8,128)(2,1)S(1)}, bf16[4,128,128]{1,2,0:T(8,128)(2,1)S(1)}, u32[]{:S(2)}, u32[]{:S(2)}) collective-permute-start(bf16[4,128,128]{1,2,0:T(8,128)(2,1)S(1)} %fusion.16), channel_id=1, source_target_pairs={{4,0},{6,2},{8,4},{10,6},{12,8},{14,10},{16,12},{18,14},{20,16},{2... | collective-permute-start | bytes 393224 | tf_op jit(solution)/shard_map/ppermute | solution.py:16
  39.0 7.8 %collective-permute-start.2 = (bf16[4,128,128]{1,2,0:T(8,128)(2,1)}, bf16[4,128,128]{1,2,0:T(8,128)(2,1)}, u32[]{:S(2)}, u32[]{:S(2)}) collective-permute-start(bf16[4,128,128]{1,2,0:T(8,128)(2,1)} %fusion.15), channel_id=1, source_target_pairs={{2,0},{4,2},{6,4},{8,6},{10,8},{12,10},{14,12},{16,14},{18,16},{20... | collective-permute-start | bytes 393224 | tf_op jit(solution)/shard_map/ppermute | solution.py:16

commit v6 on v5

v6 whole, which is shorter than its diff:
```python
import jax
import jax.numpy as jnp
from jax import lax
from jax.sharding import PartitionSpec as P

QH = 32
KVH = 4
HD = 128
GROUP = 8
NEG = -1e30
PARTS = 2


def shifted(block, axis, distance):
    devices = range(lax.axis_size(axis))
    route = [(i - distance, i) for i in devices if i - distance in devices]
    return lax.ppermute(block, axis, route)


def doc_index(doc_lengths, positions):
    doc_ends = jnp.cumsum(doc_lengths)
    counted = jnp.sum((positions[:, None] >= doc_ends[None, :]).astype(jnp.int32), axis=1)
    return jnp.where(positions < 0, -1, counted)


def allowed_pairs(doc_lengths, query_pos, key_pos):
    query_docs = doc_index(doc_lengths, query_pos)
    key_docs = doc_index(doc_lengths, key_pos)
    return (query_docs[:, None] == key_docs[None, :]) & (key_pos[None, :] <= query_pos[:, None])


def scores_of(query_heads, key_heads, allowed, score_scale):
    scores = (
        jnp.einsum("tghd,sgd->ghts", query_heads, key_heads, preferred_element_type=jnp.float32)
        * score_scale
    )
    return jnp.where(allowed[None, None], scores, NEG)


def grad_p_of(grad_heads, values):
    return jnp.einsum("tghd,sgd->ghts", grad_heads, values, preferred_element_type=jnp.float32)


def key_grad_of(grad_s, query_heads, score_scale):
    return (
        jnp.einsum("ghts,tghd->gsd", grad_s, query_heads, preferred_element_type=jnp.float32)
        * score_scale
    )


def query_grad_of(grad_s, keys):
    return jnp.einsum("ghts,sgd->ghtd", grad_s, keys, preferred_element_type=jnp.float32)


def own_stats(query_heads, grad_heads, own_keys, own_values, own_allowed, score_scale):
    own_scores = scores_of(query_heads, own_keys, own_allowed, score_scale)
    own_max = jnp.max(own_scores, axis=-1, keepdims=True)
    own_exp = jnp.exp(own_scores - own_max)
    own_sum = jnp.sum(own_exp, axis=-1, keepdims=True)
    own_grad_p = grad_p_of(grad_heads, own_values)
    own_dot = jnp.sum(own_exp * own_grad_p, axis=-1, keepdims=True)
    return own_max, own_exp, own_sum, own_grad_p, own_dot


def rim_grads(query_heads, grad_heads, far_rim, near_rim, far_allowed, near_allowed, stats,
              score_scale, rows, heads):
    own_max, own_exp, own_sum, own_grad_p, own_dot = stats
    far_keys = far_rim[0].reshape(rows, heads, HD)
    far_values = far_rim[1].reshape(rows, heads, HD)
    near_keys = near_rim[0].reshape(rows, heads, HD)
    near_values = near_rim[1].reshape(rows, heads, HD)
    far_scores = scores_of(query_heads, far_keys, far_allowed, score_scale)
    near_scores = scores_of(query_heads, near_keys, near_allowed, score_scale)
    row_max = jnp.maximum(
        own_max,
        jnp.maximum(
            jnp.max(far_scores, axis=-1, keepdims=True),
            jnp.max(near_scores, axis=-1, keepdims=True),
        ),
    )
    far_exp = jnp.exp(far_scores - row_max)
    near_exp = jnp.exp(near_scores - row_max)
    own_rescale = jnp.exp(own_max - row_max)
    row_sum = (
        own_sum * own_rescale
        + jnp.sum(far_exp, axis=-1, keepdims=True)
        + jnp.sum(near_exp, axis=-1, keepdims=True)
    )
    far_grad_p = grad_p_of(grad_heads, far_values)
    near_grad_p = grad_p_of(grad_heads, near_values)
    row_delta = (
        own_dot * own_rescale
        + jnp.sum(far_exp * far_grad_p, axis=-1, keepdims=True)
        + jnp.sum(near_exp * near_grad_p, axis=-1, keepdims=True)
    ) / row_sum
    far_grad_s = ((far_exp / row_sum) * (far_grad_p - row_delta)).astype(jnp.bfloat16)
    near_grad_s = ((near_exp / row_sum) * (near_grad_p - row_delta)).astype(jnp.bfloat16)
    far_key_grad = key_grad_of(far_grad_s, query_heads, score_scale).astype(jnp.bfloat16)
    near_key_grad = key_grad_of(near_grad_s, query_heads, score_scale).astype(jnp.bfloat16)
    rim_query_grad = query_grad_of(far_grad_s, far_keys) + query_grad_of(near_grad_s, near_keys)
    return far_key_grad, near_key_grad, rim_query_grad, own_rescale / row_sum, row_delta


def own_grads(query_heads, own_keys, stats, scale_row, row_delta, rim_query_grad, score_scale):
    own_max, own_exp, own_sum, own_grad_p, own_dot = stats
    own_prob = own_exp * scale_row
    own_grad_s = (own_prob * (own_grad_p - row_delta)).astype(jnp.bfloat16)
    own_key_grad = key_grad_of(own_grad_s, query_heads, score_scale)
    query_grad = (query_grad_of(own_grad_s, own_keys) + rim_query_grad) * score_scale
    return query_grad.astype(jnp.bfloat16), own_key_grad


def body(queries, key_vectors, value_vectors, output_grad, doc_lengths):
    rows = queries.shape[0]
    score_scale = HD ** (-0.5)
    axes = ("ctx", "uly")
    heads = KVH // PARTS
    width = heads * HD
    key_value = jnp.stack([key_vectors, value_vectors])
    rims = []
    for part in range(PARTS):
        kv_part = key_value[:, :, part * width : (part + 1) * width]
        rims.append((shifted(kv_part, axes, 1), shifted(kv_part, axes, 2)))
    device_index = lax.axis_index(axes)
    query_pos = device_index * rows + jnp.arange(rows, dtype=jnp.int32)
    own_allowed = allowed_pairs(doc_lengths, query_pos, query_pos)
    near_allowed = allowed_pairs(doc_lengths, query_pos, query_pos - rows)
    far_allowed = allowed_pairs(doc_lengths, query_pos, query_pos - 2 * rows)
    query_heads = queries.reshape(rows, KVH, GROUP, HD)
    grad_heads = output_grad.reshape(rows, KVH, GROUP, HD)
    own_keys = key_vectors.reshape(rows, KVH, HD)
    own_values = value_vectors.reshape(rows, KVH, HD)

    query_parts, key_parts = [], []
    for part in range(PARTS):
        pick = slice(part * heads, (part + 1) * heads)
        q_part = query_heads[:, pick]
        g_part = grad_heads[:, pick]
        k_part = own_keys[:, pick]
        stats = own_stats(q_part, g_part, k_part, own_values[:, pick], own_allowed, score_scale)
        near_rim, far_rim = rims[part]
        far_kg, near_kg, rim_qg, scale_row, row_delta = rim_grads(
            q_part, g_part, far_rim, near_rim, far_allowed, near_allowed, stats,
            score_scale, rows, heads,
        )
        far_back = shifted(far_kg, axes, -2)
        near_back = shifted(near_kg, axes, -1)
        query_grad, own_kg = own_grads(
            q_part, k_part, stats, scale_row, row_delta, rim_qg, score_scale
        )
        query_parts.append(query_grad)
        key_parts.append(own_kg + near_back.astype(jnp.float32) + far_back.astype(jnp.float32))
    query_grad = jnp.concatenate(query_parts, axis=0)
    query_grad = jnp.transpose(query_grad, (2, 0, 1, 3)).reshape(rows, QH * HD)
    key_grad = jnp.concatenate(key_parts, axis=0)
    key_grad = jnp.transpose(key_grad, (1, 0, 2)).reshape(rows, KVH * HD).astype(jnp.bfloat16)
    return (query_grad, key_grad)


def solution(mesh):
    placed = (
        P(("dp", "ctx", "uly"), None),
        P(("dp", "ctx", "uly"), None),
        P(("dp", "ctx", "uly"), None),
        P(("dp", "ctx", "uly"), None),
        P("dp"),
    )
    return jax.shard_map(
        body,
        mesh=mesh,
        in_specs=placed,
        out_specs=(P(("dp", "ctx", "uly"), None), P(("dp", "ctx", "uly"), None)),
        check_vma=False,
    )
```

time: 49.8 us -> 58.4 us (1.17)
  starting transfers between devices: 13.2 us -> 27.5 us
  waiting for transfers between devices: 12.2 us -> 0.75 us
  matrix products: 9.93 us -> 13.5 us
  local copies, waits for them, and re-layouts: 9.5 us -> 11.3 us
    ppermute x4 -> x8, starting transfers between devices: 13.2 us -> 27.5 us  [shifted(): return lax.ppermute(block, axis, route)]
    ppermute x4 -> x8, waiting for transfers between devices: 12.2 us -> 0.75 us  [shifted(): return lax.ppermute(block, axis, route)]
    unnamed x10 -> x16, local copies, waits for them, and re-layouts: 4.77 us -> 7.72 us
    reshape x3 -> x0, local copies, waits for them, and re-layouts: 2.02 us -> none  [the longest x2 1.08 us: body(): own_keys = key_vectors.reshape(rows, KVH, HD)]
    slice x2 -> x4, local copies, waits for them, and re-layouts: 1.97 us -> 3.53 us  [the longest x2 1.77 us: rim_grads(): near_values = near_rim[1].reshape(rows, heads, HD)]
    dot_general x3 -> x6, matrix products: 3.48 us -> 4.77 us  [key_grad_of(): jnp.einsum('ghts,tghd->gsd', grad_s, query_heads, preferred_element_type=...]
    dot_general x3 -> x6, matrix products: 1.95 us -> 3.1 us  [scores_of(): jnp.einsum('tghd,sgd->ghts', query_heads, key_heads, preferred_element_ty...]
    dot_general x3 -> x6, matrix products: 3.17 us -> 3.89 us  [grad_p_of(): jnp.einsum('tghd,sgd->ghts', grad_heads, values, preferred_element_type=j...]
  transfers between devices with their start and end apart: 4 -> 8, of which waited for: 3 -> 1; matrix products, arithmetic and copies ran while one was open for 19% -> 32% of each run, Pallas kernels for 0% -> 0%
where the time goes in v6:
time: 58.4 us; the launch traced here: 57.3 us
  starting transfers between devices  27.5 us (47%)
  matrix products  13.5 us (23%)
  local copies, waits for them, and re-layouts  11.3 us (19%)
  other arithmetic  3.13 us (5%)
  between operations  1.1 us (2%)
  waiting for transfers between devices  0.75 us (1%)
    ppermute x8, starting transfers between devices, shifted(): return lax.ppermute(block, axis, route)  27.5 us
    unnamed x16, local copies, waits for them, and re-layouts  7.72 us
    dot_general x6, matrix products, key_grad_of(): jnp.einsum('ghts,tghd->gsd', grad_s, query_heads, preferred_element_type=...  4.77 us
    dot_general x6, matrix products, grad_p_of(): jnp.einsum('tghd,sgd->ghts', grad_heads, values, preferred_element_type=j...  3.89 us
    dot_general x6, matrix products, scores_of(): jnp.einsum('tghd,sgd->ghts', query_heads, key_heads, preferred_element_ty...  3.1 us
    convert_element_type x2, other arithmetic, rim_grads(): (far_exp / row_sum * (far_grad_p - row_delta)).astype(jnp.bfloat16)  1.78 us
    slice x2, local copies, waits for them, and re-layouts, rim_grads(): near_values = near_rim[1].reshape(rows, heads, HD)  1.77 us
    slice x2, local copies, waits for them, and re-layouts, rim_grads(): far_values = far_rim[1].reshape(rows, heads, HD)  1.77 us
  transfers between devices with their start and end apart: 8, of which 1 were waited for; matrix products, arithmetic and copies ran while one was open for 32% of the time, Pallas kernels for 0%

profile of v6, /device:TPU:1, one launch (start us, length us, event | category | flops | bytes accessed | tf_op | source)
XLA Modules:
  0.0 57.3 jit_solution(3008914864172088211)
XLA Ops:
  0.6 1.1 %copy.72 = bf16[128,512]{0,1:T(8,128)(2,1)S(1)} copy(bf16[128,512]{1,0:T(8,128)(2,1)} %param.6) | data formatting | bytes 262144 | tf_op args[1]
  1.8 1.0 %copy.77 = bf16[128,512]{0,1:T(8,128)(2,1)S(1)} copy(bf16[128,512]{1,0:T(8,128)(2,1)} %param.7) | data formatting | bytes 262144 | tf_op args[2]
  3.5 5.0 %collective-permute-start = (bf16[2,128,256]{1,2,0:T(8,128)(2,1)}, bf16[2,128,256]{1,2,0:T(8,128)(2,1)}, u32[]{:S(2)}, u32[]{:S(2)}) collective-permute-start(bf16[2,128,256]{1,2,0:T(8,128)(2,1)} %get-tuple-element.31), channel_id=1, source_target_pairs={{0,4},{2,6},{4,8},{6,10},{8,12},{10,14},{12,16},{14,18},{16,20},{1... | collective-permute-start | bytes 393224 | tf_op jit(solution)/shard_map/ppermute | solution.py:17
  8.5 3.2 %collective-permute-start.1 = (bf16[2,128,256]{1,2,0:T(8,128)(2,1)}, bf16[2,128,256]{1,2,0:T(8,128)(2,1)}, u32[]{:S(2)}, u32[]{:S(2)}) collective-permute-start(bf16[2,128,256]{1,2,0:T(8,128)(2,1)} %get-tuple-element.31), channel_id=1, source_target_pairs={{0,2},{2,4},{4,6},{6,8},{8,10},{10,12},{12,14},{14,16},{16,18},{18... | collective-permute-start | bytes 393224 | tf_op jit(solution)/shard_map/ppermute | solution.py:17
  11.8 2.5 %collective-permute-start.3 = (bf16[2,128,256]{1,2,0:T(8,128)(2,1)}, bf16[2,128,256]{1,2,0:T(8,128)(2,1)}, u32[]{:S(2)}, u32[]{:S(2)}) collective-permute-start(bf16[2,128,256]{1,2,0:T(8,128)(2,1)} %get-tuple-element.32), channel_id=1, source_target_pairs={{0,2},{2,4},{4,6},{6,8},{8,10},{10,12},{12,14},{14,16},{16,18},{18... | collective-permute-start | bytes 393224 | tf_op jit(solution)/shard_map/ppermute | solution.py:17
  14.2 5.4 %collective-permute-start.2 = (bf16[2,128,256]{1,2,0:T(8,128)(2,1)}, bf16[2,128,256]{1,2,0:T(8,128)(2,1)}, u32[]{:S(2)}, u32[]{:S(2)}) collective-permute-start(bf16[2,128,256]{1,2,0:T(8,128)(2,1)} %get-tuple-element.32), channel_id=1, source_target_pairs={{0,4},{2,6},{4,8},{6,10},{8,12},{10,14},{12,16},{14,18},{16,20},{1... | collective-permute-start | bytes 393224 | tf_op jit(solution)/shard_map/ppermute | solution.py:17
  21.6 1.3 %fusion.68 = (f32[2,8,128]{2,1,0:T(8,128)S(1)}, f32[2,8,128,128]{2,3,1,0:T(8,128)}) fusion(bf16[128,4,8,128]{0,3,2,1:T(8,128)(2,1)S(1)} %bitcast.205, bf16[128,4,128]{0,2,1:T(8,128)(2,1)S(1)} %bitcast.225, pred[128,128]{0,1:T(8,128)(4,1)S(1)} %get-tuple-element.48), kind=kOutput, calls=%fused_computation.133 | convolution fusion | flops 67893248 | bytes 1662976 | tf_op jit(solution)/shard_map/tghd,sgd->ghts/dot_general | solution.py:34
  23.2 1.6 %copy.82 = bf16[128,4096]{0,1:T(8,128)(2,1)S(1)} copy(bf16[128,4096]{1,0:T(8,128)(2,1)} %param.8) | data formatting | bytes 2097152 | tf_op args[3]
  24.9 1.6 %multiply_reduce_fusion.5 = (f32[2,8,128]{2,1,0:T(8,128)S(1)}, f32[2,8,128]{2,1,0:T(8,128)S(1)}, f32[2,8,128,128]{2,3,1,0:T(8,128)S(1)}) fusion(f32[2,8,128,128]{2,3,1,0:T(8,128)} %get-tuple-element.59, f32[2,8,128]{2,1,0:T(8,128)S(1)} %get-tuple-element.58, bf16[128,4,8,128]{0,3,2,1:T(8,128)(2,1)S(1)} %bitcast.217, bf16[128,4,128]{0,2,1:T(8,128)(2,1)S(1)} %bitcast.230), kind=kOutput, calls=%fused_computation.63 | convolution fusion | flops 68153344 | bytes 2711552 | tf_op jit(solution)/shard_map/tghd,sgd->ghts/dot_general | solution.py:41
  26.9 0.9 %fusion.61 = (bf16[1,128,256]{1,2,0:T(8,128)(2,1)S(1)}, bf16[1,128,256]{1,2,0:T(8,128)(2,1)S(1)}) fusion(bf16[2,128,256]{1,2,0:T(8,128)(2,1)} %collective-permute-done.1), kind=kLoop, calls=%fused_computation.126 | loop fusion | bytes 262144 | tf_op jit(solution)/shard_map/slice | solution.py:71
  28.1 0.9 %fusion.63 = (bf16[1,128,256]{1,2,0:T(8,128)(2,1)S(1)}, bf16[1,128,256]{1,2,0:T(8,128)(2,1)S(1)}) fusion(bf16[2,128,256]{1,2,0:T(8,128)(2,1)} %collective-permute-done.3), kind=kLoop, calls=%fused_computation.128 | loop fusion | bytes 262144 | tf_op jit(solution)/shard_map/slice | solution.py:71
  29.8 0.9 %fusion.62 = (bf16[1,128,256]{1,2,0:T(8,128)(2,1)S(1)}, bf16[1,128,256]{1,2,0:T(8,128)(2,1)S(1)}) fusion(bf16[2,128,256]{1,2,0:T(8,128)(2,1)} %collective-permute-done), kind=kLoop, calls=%fused_computation.127 | loop fusion | bytes 262144 | tf_op jit(solution)/shard_map/slice | solution.py:69
  32.2 0.9 %multiply_convert_fusion.4 = (bf16[2,8,128,128]{2,3,1,0:T(8,128)(2,1)S(1)}, bf16[2,8,128,128]{2,3,1,0:T(8,128)(2,1)S(1)}, bf16[2,8,128,128]{2,3,1,0:T(8,128)(2,1)S(1)}) fusion(f32[2,8,128,128]{2,3,1,0:T(8,128)S(1)} %get-tuple-element.64, f32[2,8,128,128]{2,3,1,0:T(8,128)S(1)} %get-tuple-element.61, f32[2,8,128]{2,1,0:T(8,128)S(1)} %get-tuple-element.28, ...), kind=kLoop, calls=%fused_computation.59 | loop fusion | flops 3932160 | bytes 7905280 | tf_op jit(solution)/shard_map/convert_element_type | solution.py:96
  33.8 0.9 %fusion.64 = (bf16[1,128,256]{1,2,0:T(8,128)(2,1)S(1)}, bf16[1,128,256]{1,2,0:T(8,128)(2,1)S(1)}) fusion(bf16[2,128,256]{1,2,0:T(8,128)(2,1)} %collective-permute-done.2), kind=kLoop, calls=%fused_computation.129 | loop fusion | bytes 262144 | tf_op jit(solution)/shard_map/slice | solution.py:69
  36.0 0.9 %multiply_convert_fusion.1 = (bf16[2,8,128,128]{2,3,1,0:T(8,128)(2,1)S(1)}, bf16[2,8,128,128]{2,3,1,0:T(8,128)(2,1)S(1)}, bf16[2,8,128,128]{2,3,1,0:T(8,128)(2,1)S(1)}) fusion(f32[2,8,128,128]{2,3,1,0:T(8,128)S(1)} %get-tuple-element.56, f32[2,8,128,128]{2,3,1,0:T(8,128)S(1)} %get-tuple-element.53, f32[2,8,128]{2,1,0:T(8,128)S(1)} %get-tuple-element.30, ...), kind=kLoop, calls=%fused_computation.50 | loop fusion | flops 3932160 | bytes 7905280 | tf_op jit(solution)/shard_map/convert_element_type | solution.py:96
  37.5 2.1 %collective-permute-start.4 = (bf16[2,128,128]{1,2,0:T(8,128)(2,1)S(1)}, bf16[2,128,128]{1,2,0:T(8,128)(2,1)}, u32[]{:S(2)}, u32[]{:S(2)}) collective-permute-start(bf16[2,128,128]{1,2,0:T(8,128)(2,1)S(1)} %fusion.27), channel_id=1, source_target_pairs={{2,0},{4,2},{6,4},{8,6},{10,8},{12,10},{14,12},{16,14},{18,16},{20... | collective-permute-start | bytes 196616 | tf_op jit(solution)/shard_map/ppermute | solution.py:17
  39.6 0.9 %fusion.26 = bf16[2,128,128]{1,2,0:T(8,128)(2,1)} fusion(bf16[2,8,128,128]{2,3,1,0:T(8,128)(2,1)S(1)} %get-tuple-element.41, bf16[128,4,8,128]{0,3,2,1:T(8,128)(2,1)S(1)} %bitcast.213), kind=kOutput, calls=%fused_computation.46 | convolution fusion | flops 67174400 | bytes 1114112 | tf_op jit(solution)/shard_map/ghts,tghd->gsd/dot_general | solution.py:46
  40.5 3.9 %collective-permute-start.5 = (bf16[2,128,128]{1,2,0:T(8,128)(2,1)}, bf16[2,128,128]{1,2,0:T(8,128)(2,1)}, u32[]{:S(2)}, u32[]{:S(2)}) collective-permute-start(bf16[2,128,128]{1,2,0:T(8,128)(2,1)} %fusion.26), channel_id=1, source_target_pairs={{4,0},{6,2},{8,4},{10,6},{12,8},{14,10},{16,12},{18,14},{20,16},{2... | collective-permute-start | bytes 196616 | tf_op jit(solution)/shard_map/ppermute | solution.py:17
  44.4 3.5 %collective-permute-start.6 = (bf16[2,128,128]{1,2,0:T(8,128)(2,1)S(1)}, bf16[2,128,128]{1,2,0:T(8,128)(2,1)S(1)}, u32[]{:S(2)}, u32[]{:S(2)}) collective-permute-start(bf16[2,128,128]{1,2,0:T(8,128)(2,1)S(1)} %fusion.25), channel_id=1, source_target_pairs={{2,0},{4,2},{6,4},{8,6},{10,8},{12,10},{14,12},{16,14},{18,16},{20... | collective-permute-start | bytes 196616 | tf_op jit(solution)/shard_map/ppermute | solution.py:17
  47.9 0.9 %fusion.24 = bf16[2,128,128]{1,2,0:T(8,128)(2,1)} fusion(bf16[2,8,128,128]{2,3,1,0:T(8,128)(2,1)S(1)} %get-tuple-element.43, bf16[128,4,8,128]{0,3,2,1:T(8,128)(2,1)S(1)} %bitcast.214), kind=kOutput, calls=%fused_computation.44 | convolution fusion | flops 67174400 | bytes 1114112 | tf_op jit(solution)/shard_map/ghts,tghd->gsd/dot_general | solution.py:46
  48.9 1.9 %collective-permute-start.7 = (bf16[2,128,128]{1,2,0:T(8,128)(2,1)}, bf16[2,128,128]{1,2,0:T(8,128)(2,1)}, u32[]{:S(2)}, u32[]{:S(2)}) collective-permute-start(bf16[2,128,128]{1,2,0:T(8,128)(2,1)} %fusion.24), channel_id=1, source_target_pairs={{4,0},{6,2},{8,4},{10,6},{12,8},{14,10},{16,12},{18,14},{20,16},{2... | collective-permute-start | bytes 196616 | tf_op jit(solution)/shard_map/ppermute | solution.py:17
  52.1 1.3 %copy.110 = bf16[128,4096]{1,0:T(8,128)(2,1)} copy(bf16[128,4096]{0,1:T(8,128)(2,1)S(1)} %bitcast.223) | data formatting | bytes 2097152
  53.4 1.2 %add_convert_fusion.1 = bf16[2,128,128]{1,2,0:T(8,128)(2,1)S(1)} fusion(bf16[2,128,128]{1,2,0:T(8,128)(2,1)} %collective-permute-done.5, bf16[2,128,128]{1,2,0:T(8,128)(2,1)} %collective-permute-done.4, bf16[2,8,128,128]{2,3,1,0:T(8,128)(2,1)S(1)} %copy-done.2, bf16[128,4,8,128]{0,3,2,1:T(8,128)(2,1)S(1)} %bitcast.215), kind=kOutput, calls=%fused_computation.97 | convolution fusion | flops 67305472 | bytes 1245184 | tf_op jit(solution)/shard_map/ghts,tghd->gsd/dot_general | solution.py:46
  55.3 1.1 %add_convert_fusion = bf16[2,128,128]{1,2,0:T(8,128)(2,1)S(1)} fusion(bf16[2,128,128]{1,2,0:T(8,128)(2,1)} %collective-permute-done.7, bf16[2,128,128]{1,2,0:T(8,128)(2,1)S(1)} %collective-permute-done.6, bf16[2,8,128,128]{2,3,1,0:T(8,128)(2,1)S(1)} %get-tuple-element.46, bf16[128,4,8,128]{0,3,2,1:T(8,128)(2,1)S(1)} %bitcast.216), kind=kOutput, calls=%fused_computation.96 | convolution fusion | flops 67305472 | bytes 1245184 | tf_op jit(solution)/shard_map/ghts,tghd->gsd/dot_general | solution.py:46
  (57 shorter events, 11.2 us)
Async XLA Ops:
  0.6 20.1 %copy-start.3 = (bf16[128,4096]{1,0:T(8,128)(2,1)S(1)}, bf16[128,4096]{1,0:T(8,128)(2,1)}, u32[]{:S(2)}) copy-start(bf16[128,4096]{1,0:T(8,128)(2,1)} %param.5) | copy-start | bytes 3145732
  3.5 26.2 %collective-permute-start = (bf16[2,128,256]{1,2,0:T(8,128)(2,1)}, bf16[2,128,256]{1,2,0:T(8,128)(2,1)}, u32[]{:S(2)}, u32[]{:S(2)}) collective-permute-start(bf16[2,128,256]{1,2,0:T(8,128)(2,1)} %get-tuple-element.31), channel_id=1, source_target_pairs={{0,4},{2,6},{4,8},{6,10},{8,12},{10,14},{12,16},{14,18},{16,20},{1... | collective-permute-start | bytes 393224 | tf_op jit(solution)/shard_map/ppermute | solution.py:17
  8.5 18.3 %collective-permute-start.1 = (bf16[2,128,256]{1,2,0:T(8,128)(2,1)}, bf16[2,128,256]{1,2,0:T(8,128)(2,1)}, u32[]{:S(2)}, u32[]{:S(2)}) collective-permute-start(bf16[2,128,256]{1,2,0:T(8,128)(2,1)} %get-tuple-element.31), channel_id=1, source_target_pairs={{0,2},{2,4},{4,6},{6,8},{8,10},{10,12},{12,14},{14,16},{16,18},{18... | collective-permute-start | bytes 393224 | tf_op jit(solution)/shard_map/ppermute | solution.py:17
  11.8 16.4 %collective-permute-start.3 = (bf16[2,128,256]{1,2,0:T(8,128)(2,1)}, bf16[2,128,256]{1,2,0:T(8,128)(2,1)}, u32[]{:S(2)}, u32[]{:S(2)}) collective-permute-start(bf16[2,128,256]{1,2,0:T(8,128)(2,1)} %get-tuple-element.32), channel_id=1, source_target_pairs={{0,2},{2,4},{4,6},{6,8},{8,10},{10,12},{12,14},{14,16},{16,18},{18... | collective-permute-start | bytes 393224 | tf_op jit(solution)/shard_map/ppermute | solution.py:17
  14.2 19.5 %collective-permute-start.2 = (bf16[2,128,256]{1,2,0:T(8,128)(2,1)}, bf16[2,128,256]{1,2,0:T(8,128)(2,1)}, u32[]{:S(2)}, u32[]{:S(2)}) collective-permute-start(bf16[2,128,256]{1,2,0:T(8,128)(2,1)} %get-tuple-element.32), channel_id=1, source_target_pairs={{0,4},{2,6},{4,8},{6,10},{8,12},{10,14},{12,16},{14,18},{16,20},{1... | collective-permute-start | bytes 393224 | tf_op jit(solution)/shard_map/ppermute | solution.py:17
  19.7 0.7 %copy-start.4 = (s32[16]{0:T(128)S(1)}, s32[16]{0:T(128)}, u32[]{:S(2)}) copy-start(s32[16]{0:T(128)} %param.9) | copy-start | bytes 196
  31.0 1.2 %copy-start = (f32[2,8,128,128]{2,3,1,0:T(8,128)S(1)}, f32[2,8,128,128]{2,3,1,0:T(8,128)}, u32[]{:S(2)}) copy-start(f32[2,8,128,128]{2,3,1,0:T(8,128)} %get-tuple-element.59) | copy-start | bytes 3145732
  33.2 17.6 %copy-start.1 = (bf16[2,8,128,128]{2,3,1,0:T(8,128)(2,1)}, bf16[2,8,128,128]{2,3,1,0:T(8,128)(2,1)S(1)}, u32[]{:S(2)}) copy-start(bf16[2,8,128,128]{2,3,1,0:T(8,128)(2,1)S(1)} %get-tuple-element.45) | copy-start | bytes 1572868
  37.5 15.9 %collective-permute-start.4 = (bf16[2,128,128]{1,2,0:T(8,128)(2,1)S(1)}, bf16[2,128,128]{1,2,0:T(8,128)(2,1)}, u32[]{:S(2)}, u32[]{:S(2)}) collective-permute-start(bf16[2,128,128]{1,2,0:T(8,128)(2,1)S(1)} %fusion.27), channel_id=1, source_target_pairs={{2,0},{4,2},{6,4},{8,6},{10,8},{12,10},{14,12},{16,14},{18,16},{20... | collective-permute-start | bytes 196616 | tf_op jit(solution)/shard_map/ppermute | solution.py:17
  40.5 12.9 %collective-permute-start.5 = (bf16[2,128,128]{1,2,0:T(8,128)(2,1)}, bf16[2,128,128]{1,2,0:T(8,128)(2,1)}, u32[]{:S(2)}, u32[]{:S(2)}) collective-permute-start(bf16[2,128,128]{1,2,0:T(8,128)(2,1)} %fusion.26), channel_id=1, source_target_pairs={{4,0},{6,2},{8,4},{10,6},{12,8},{14,10},{16,12},{18,14},{20,16},{2... | collective-permute-start | bytes 196616 | tf_op jit(solution)/shard_map/ppermute | solution.py:17
  44.4 10.2 %collective-permute-start.6 = (bf16[2,128,128]{1,2,0:T(8,128)(2,1)S(1)}, bf16[2,128,128]{1,2,0:T(8,128)(2,1)S(1)}, u32[]{:S(2)}, u32[]{:S(2)}) collective-permute-start(bf16[2,128,128]{1,2,0:T(8,128)(2,1)S(1)} %fusion.25), channel_id=1, source_target_pairs={{2,0},{4,2},{6,4},{8,6},{10,8},{12,10},{14,12},{16,14},{18,16},{20... | collective-permute-start | bytes 196616 | tf_op jit(solution)/shard_map/ppermute | solution.py:17
  48.9 6.5 %collective-permute-start.7 = (bf16[2,128,128]{1,2,0:T(8,128)(2,1)}, bf16[2,128,128]{1,2,0:T(8,128)(2,1)}, u32[]{:S(2)}, u32[]{:S(2)}) collective-permute-start(bf16[2,128,128]{1,2,0:T(8,128)(2,1)} %fusion.24), channel_id=1, source_target_pairs={{4,0},{6,2},{8,4},{10,6},{12,8},{14,10},{16,12},{18,14},{20,16},{2... | collective-permute-start | bytes 196616 | tf_op jit(solution)/shard_map/ppermute | solution.py:17
  52.1 1.3 %copy-start.2 = (bf16[2,8,128,128]{2,3,1,0:T(8,128)(2,1)S(1)}, bf16[2,8,128,128]{2,3,1,0:T(8,128)(2,1)}, u32[]{:S(2)}) copy-start(bf16[2,8,128,128]{2,3,1,0:T(8,128)(2,1)} %copy-done.1) | copy-start | bytes 1572868

commit v7 on v5

--- a/solution.py
+++ b/solution.py
@@ -47,6 +47,16 @@
     return jnp.einsum("ghts,sgd->ghtd", grad_s, keys, preferred_element_type=jnp.float32)
 
 
+def block_stats(query_heads, grad_heads, keys, values, allowed, score_scale):
+    scores = scores_of(query_heads, keys, allowed, score_scale)
+    block_max = jnp.max(scores, axis=-1, keepdims=True)
+    block_exp = jnp.exp(scores - block_max)
+    block_sum = jnp.sum(block_exp, axis=-1, keepdims=True)
+    grad_p = jnp.einsum("tghd,sgd->ghts", grad_heads, values, preferred_element_type=jnp.float32)
+    block_dot = jnp.sum(block_exp * grad_p, axis=-1, keepdims=True)
+    return block_max, block_exp, block_sum, grad_p, block_dot
+
+
 def body(queries, key_vectors, value_vectors, output_grad, doc_lengths):
     rows = queries.shape[0]
     score_scale = HD ** (-0.5)
@@ -65,47 +75,44 @@
     near_allowed = allowed_pairs(doc_lengths, query_pos, own_pos - rows)
     far_allowed = allowed_pairs(doc_lengths, query_pos, own_pos - 2 * rows)
 
-    own_scores = scores_of(query_heads, own_keys, own_allowed, score_scale)
-    own_max = jnp.max(own_scores, axis=-1, keepdims=True)
-    own_exp = jnp.exp(own_scores - own_max)
-    own_sum = jnp.sum(own_exp, axis=-1, keepdims=True)
-    own_grad_p = jnp.einsum(
-        "tghd,sgd->ghts", grad_heads, own_values, preferred_element_type=jnp.float32
+    own_max, own_exp, own_sum, own_grad_p, own_dot = block_stats(
+        query_heads, grad_heads, own_keys, own_values, own_allowed, score_scale
     )
-    own_dot = jnp.sum(own_exp * own_grad_p, axis=-1, keepdims=True)
+    near_keys = near_rim[0].reshape(rows, KVH, HD)
+    near_values = near_rim[1].reshape(rows, KVH, HD)
+    near_max, near_exp, near_sum, near_grad_p, near_dot = block_stats(
+        query_heads, grad_heads, near_keys, near_values, near_allowed, score_scale
+    )
+    ready, far_rim = lax.optimization_barrier(
+        ((own_max, own_exp, own_sum, own_grad_p, own_dot,
+          near_max, near_exp, near_sum, near_grad_p, near_dot), far_rim)
+    )
+    (own_max, own_exp, own_sum, own_grad_p, own_dot,
+     near_max, near_exp, near_sum, near_grad_p, near_dot) = ready
 
     far_keys = far_rim[0].reshape(rows, KVH, HD)
     far_values = far_rim[1].reshape(rows, KVH, HD)
-    near_keys = near_rim[0].reshape(rows, KVH, HD)
-    near_values = near_rim[1].reshape(rows, KVH, HD)
     far_scores = scores_of(query_heads, far_keys, far_allowed, score_scale)
-    near_scores = scores_of(query_heads, near_keys, near_allowed, score_scale)
     row_max = jnp.maximum(
-        own_max,
-        jnp.maximum(
-            jnp.max(far_scores, axis=-1, keepdims=True),
-            jnp.max(near_scores, axis=-1, keepdims=True),
-        ),
+        jnp.maximum(own_max, near_max), jnp.max(far_scores, axis=-1, keepdims=True)
     )
     far_exp = jnp.exp(far_scores - row_max)
-    near_exp = jnp.exp(near_scores - row_max)
     own_rescale = jnp.exp(own_max - row_max)
+    near_rescale = jnp.exp(near_max - row_max)
     row_sum = (
         own_sum * own_rescale
+        + near_sum * near_rescale
         + jnp.sum(far_exp, axis=-1, keepdims=True)
-        + jnp.sum(near_exp, axis=-1, keepdims=True)
     )
     far_grad_p = jnp.einsum(
         "tghd,sgd->ghts", grad_heads, far_values, preferred_element_type=jnp.float32
     )
-    near_grad_p = jnp.einsum(
-        "tghd,sgd->ghts", grad_heads, near_values, preferred_element_type=jnp.float32
-    )
     row_delta = (
         own_dot * own_rescale
+        + near_dot * near_rescale
         + jnp.sum(far_exp * far_grad_p, axis=-1, keepdims=True)
-        + jnp.sum(near_exp * near_grad_p, axis=-1, keepdims=True)
     ) / row_sum
+    near_exp = near_exp * near_rescale
     far_grad_s = ((far_exp / row_sum) * (far_grad_p - row_delta)).astype(jnp.bfloat16)
     near_grad_s = ((near_exp / row_sum) * (near_grad_p - row_delta)).astype(jnp.bfloat16)
     far_key_grad = key_grad_of(far_grad_s, query_heads, score_scale)

time: 49.8 us -> 51.7 us (1.038)
  starting transfers between devices: 13.2 us -> 17.9 us
  waiting for transfers between devices: 12.2 us -> 10.1 us
    ppermute x4, starting transfers between devices: 13.2 us -> 17.9 us  [shifted(): return lax.ppermute(block, axis, route)]
    ppermute x4, waiting for transfers between devices: 12.2 us -> 10.1 us  [shifted(): return lax.ppermute(block, axis, route)]
    dot_general x1, matrix products: 1.62 us -> 0.96 us  [body(): jnp.einsum('tghd,sgd->ghts', grad_heads, far_values, preferred_element_ty...]
  transfers between devices with their start and end apart: 4 -> 4, of which waited for: 3 -> 4; matrix products, arithmetic and copies ran while one was open for 19% -> 20% of each run, Pallas kernels for 0% -> 0%
where the time goes in v7:
time: 51.7 us; the launch traced here: 51.3 us
  starting transfers between devices  17.9 us (35%)
  waiting for transfers between devices  10.1 us (20%)
  matrix products  9.76 us (19%)
  local copies, waits for them, and re-layouts  9.5 us (18%)
  other arithmetic  3.1 us (6%)
  between operations  0.89 us (2%)
    ppermute x4, starting transfers between devices, shifted(): return lax.ppermute(block, axis, route)  17.9 us
    ppermute x4, waiting for transfers between devices, shifted(): return lax.ppermute(block, axis, route)  10.1 us
    unnamed x10, local copies, waits for them, and re-layouts  4.77 us
    dot_general x3, matrix products, key_grad_of(): jnp.einsum('ghts,tghd->gsd', grad_s, query_heads, preferred_element_type=...  3.52 us
    dot_general x3, matrix products, scores_of(): jnp.einsum('tghd,sgd->ghts', query_heads, key_heads, preferred_element_ty...  2 us
    dot_general x2, matrix products, block_stats(): jnp.einsum('tghd,sgd->ghts', grad_heads, values, preferred_element_type=j...  1.97 us
    convert_element_type x1, other arithmetic, body(): (near_exp / row_sum * (near_grad_p - row_delta)).astype(jnp.bfloat16)  1.87 us
    dot_general x3, matrix products, query_grad_of(): jnp.einsum('ghts,sgd->ghtd', grad_s, keys, preferred_element_type=jnp.flo...  1.3 us
  transfers between devices with their start and end apart: 4, of which 4 were waited for; matrix products, arithmetic and copies ran while one was open for 20% of the time, Pallas kernels for 0%

profile of v7, /device:TPU:1, one launch (start us, length us, event | category | flops | bytes accessed | tf_op | source)
XLA Modules:
  0.0 51.3 jit_solution(7252112608053325609)
XLA Ops:
  0.6 1.2 %copy.62 = bf16[128,512]{0,1:T(8,128)(2,1)S(1)} copy(bf16[128,512]{1,0:T(8,128)(2,1)} %param.6) | data formatting | bytes 262144 | tf_op args[1]
  1.8 1.0 %copy.63 = bf16[128,512]{0,1:T(8,128)(2,1)S(1)} copy(bf16[128,512]{1,0:T(8,128)(2,1)} %param.7) | data formatting | bytes 262144 | tf_op args[2]
  2.9 0.7 %pad_maximum_fusion = bf16[2,128,512]{1,2,0:T(8,128)(2,1)} fusion(bf16[1,128,512]{1,2,0:T(8,128)(2,1)S(1)} %bitcast.178, bf16[1,128,512]{1,2,0:T(8,128)(2,1)S(1)} %bitcast.177), kind=kLoop, calls=%fused_computation.46 | loop fusion | flops 131072 | bytes 524288 | tf_op jit(solution)/shard_map/stack | solution.py:64
  3.6 5.0 %collective-permute-start.1 = (bf16[2,128,512]{1,2,0:T(8,128)(2,1)}, bf16[2,128,512]{1,2,0:T(8,128)(2,1)}, u32[]{:S(2)}, u32[]{:S(2)}) collective-permute-start(bf16[2,128,512]{1,2,0:T(8,128)(2,1)} %pad_maximum_fusion), channel_id=1, source_target_pairs={{0,4},{2,6},{4,8},{6,10},{8,12},{10,14},{12,16},{14,18},{16,20},{1... | collective-permute-start | bytes 786440 | tf_op jit(solution)/shard_map/ppermute | solution.py:16
  8.6 3.2 %collective-permute-start = (bf16[2,128,512]{1,2,0:T(8,128)(2,1)}, bf16[2,128,512]{1,2,0:T(8,128)(2,1)}, u32[]{:S(2)}, u32[]{:S(2)}) collective-permute-start(bf16[2,128,512]{1,2,0:T(8,128)(2,1)} %pad_maximum_fusion), channel_id=1, source_target_pairs={{0,2},{2,4},{4,6},{6,8},{8,10},{10,12},{12,14},{14,16},{16,18},{18... | collective-permute-start | bytes 786440 | tf_op jit(solution)/shard_map/ppermute | solution.py:16
  11.9 0.9 %reshape.258 = bf16[128,4,128]{2,1,0:T(4,128)(2,1)S(1)} reshape(bf16[128,512]{1,0:T(8,128)(2,1)} %param.6) | data formatting | bytes 262144 | tf_op jit(solution)/shard_map/reshape | solution.py:70
  12.8 0.9 %reshape.260 = bf16[128,4,128]{2,1,0:T(4,128)(2,1)S(1)} reshape(bf16[128,512]{1,0:T(8,128)(2,1)} %param.7) | data formatting | bytes 262144 | tf_op jit(solution)/shard_map/reshape | solution.py:71
  13.8 0.7 %copy.57 = s32[16,1]{1,0:T(8,128)S(1)} copy(s32[16,1]{0,1:T(1,128)} %bitcast.191) | data formatting | bytes 128 | tf_op jit(solution)/shard_map/reshape.235
  16.3 1.0 %multiply_reduce_fusion.1 = (f32[4,8,128]{2,1,0:T(8,128)S(1)}, f32[4,8,128]{2,1,0:T(8,128)S(1)}, f32[4,8,128,128]{2,3,1,0:T(8,128)S(1)}, f32[4,8,128,128]{2,3,1,0:T(8,128)S(1)}) fusion(f32[4,8,128]{2,1,0:T(8,128)S(1)} %get-tuple-element.55, f32[4,128,128,8]{2,1,3,0:T(8,128)S(1)} %get-tuple-element.56, pred[128,128]{0,1:T(8,128)(4,1)S(1)} %get-tuple-element.53, ...), kind=kOutput, calls=%fused_computation.14 | convolution fusion | flops 137355264 | bytes 7536640 | tf_op jit(solution)/shard_map/tghd,sgd->ghts/dot_general | solution.py:55
  17.3 5.1 %collective-permute-done = bf16[2,128,512]{1,2,0:T(8,128)(2,1)} collective-permute-done((bf16[2,128,512]{1,2,0:T(8,128)(2,1)}, bf16[2,128,512]{1,2,0:T(8,128)(2,1)}, u32[]{:S(2)}, u32[]{:S(2)}) %collective-permute-start) | collective-permute-done | bytes 262176 | tf_op jit(solution)/shard_map/ppermute | solution.py:16
  22.4 1.0 %fusion.34 = (bf16[1,128,512]{1,2,0:T(8,128)(2,1)S(1)}, bf16[1,128,512]{1,2,0:T(8,128)(2,1)S(1)}) fusion(bf16[2,128,512]{1,2,0:T(8,128)(2,1)} %collective-permute-done), kind=kLoop, calls=%fused_computation.71 | loop fusion | bytes 524288 | tf_op jit(solution)/shard_map/slice | solution.py:82
  24.1 1.0 %multiply_reduce_fusion = (f32[4,8,128]{2,1,0:T(8,128)S(1)}, f32[4,8,128]{2,1,0:T(8,128)S(1)}, f32[4,8,128,128]{2,3,1,0:T(8,128)S(1)}, f32[4,8,128,128]{2,3,1,0:T(8,128)S(1)}) fusion(f32[4,8,128]{2,1,0:T(8,128)S(1)} %get-tuple-element.58, f32[4,128,128,8]{2,1,3,0:T(8,128)S(1)} %get-tuple-element.59, pred[128,128]{0,1:T(8,128)(4,1)S(1)} %get-tuple-element.54, ...), kind=kOutput, calls=%fused_computation.12 | convolution fusion | flops 137355264 | bytes 7536640 | tf_op jit(solution)/shard_map/tghd,sgd->ghts/dot_general | solution.py:55
  25.1 1.8 %collective-permute-done.1 = bf16[2,128,512]{1,2,0:T(8,128)(2,1)} collective-permute-done((bf16[2,128,512]{1,2,0:T(8,128)(2,1)}, bf16[2,128,512]{1,2,0:T(8,128)(2,1)}, u32[]{:S(2)}, u32[]{:S(2)}) %collective-permute-start.1) | collective-permute-done | bytes 262176 | tf_op jit(solution)/shard_map/ppermute | solution.py:16
  26.9 1.0 %fusion.33 = (bf16[1,128,512]{1,2,0:T(8,128)(2,1)S(1)}, bf16[1,128,512]{1,2,0:T(8,128)(2,1)S(1)}) fusion(bf16[2,128,512]{1,2,0:T(8,128)(2,1)} %collective-permute-done.1), kind=kLoop, calls=%fused_computation.70 | loop fusion | bytes 524288 | tf_op jit(solution)/shard_map/slice | solution.py:94
  28.6 1.0 %fusion = (f32[4,8,128]{2,1,0:T(8,128)S(1)}, f32[4,8,128]{2,1,0:T(8,128)S(1)}, f32[4,128,128,8]{2,1,3,0:T(8,128)S(1)}) fusion(f32[4,128,128,8]{2,1,3,0:T(8,128)S(1)} %get-tuple-element.62, f32[4,8,128]{2,1,0:T(8,128)S(1)} %fusion.32, pred[128,128]{0,1:T(8,128)(4,1)S(1)} %get-tuple-element.52, bf16[128,4,128,1]{0,2,3,1:T(8,128)(2,1)S(1)} %bitcast.176, ...), kind=kOutput, calls=%fused_computation.2 | convolution fusion | flops 137355264 | bytes 5439488 | tf_op jit(solution)/shard_map/tghd,sgd->ghts/dot_general | solution.py:107
  29.6 1.9 %multiply_convert_fusion.1 = (bf16[4,8,128,128]{2,3,1,0:T(8,128)(2,1)S(1)}, bf16[4,8,128,128]{2,3,1,0:T(8,128)(2,1)S(1)}, bf16[4,8,128,128]{2,3,1,0:T(8,128)(2,1)S(1)}) fusion(f32[4,8,128,128]{2,3,1,0:T(8,128)S(1)} %get-tuple-element.23, f32[4,8,128,128]{2,3,1,0:T(8,128)S(1)} %get-tuple-element.22, f32[4,8,128]{2,1,0:T(8,128)S(1)} %get-tuple-element.47, ...), kind=kLoop, calls=%fused_computation.9 | loop fusion | flops 8388608 | bytes 15826944 | tf_op jit(solution)/shard_map/convert_element_type | solution.py:117
  32.6 1.3 %fusion.12 = bf16[4,128,128]{1,2,0:T(8,128)(2,1)} fusion(bf16[4,8,128,128]{2,3,1,0:T(8,128)(2,1)S(1)} %get-tuple-element.49, bf16[128,4,8,128]{3,2,1,0:T(8,128)(2,1)S(1)} %bitcast.161), kind=kOutput, calls=%fused_computation.30 | convolution fusion | flops 134348800 | bytes 2228224 | tf_op jit(solution)/shard_map/ghts,tghd->gsd/dot_general | solution.py:41
  33.9 7.3 %collective-permute-start.3 = (bf16[4,128,128]{1,2,0:T(8,128)(2,1)S(1)}, bf16[4,128,128]{1,2,0:T(8,128)(2,1)S(1)}, u32[]{:S(2)}, u32[]{:S(2)}) collective-permute-start(bf16[4,128,128]{1,2,0:T(8,128)(2,1)S(1)} %fusion.13), channel_id=1, source_target_pairs={{4,0},{6,2},{8,4},{10,6},{12,8},{14,10},{16,12},{18,14},{20,16},{2... | collective-permute-start | bytes 393224 | tf_op jit(solution)/shard_map/ppermute | solution.py:16
  41.3 2.4 %collective-permute-start.2 = (bf16[4,128,128]{1,2,0:T(8,128)(2,1)}, bf16[4,128,128]{1,2,0:T(8,128)(2,1)}, u32[]{:S(2)}, u32[]{:S(2)}) collective-permute-start(bf16[4,128,128]{1,2,0:T(8,128)(2,1)} %fusion.12), channel_id=1, source_target_pairs={{2,0},{4,2},{6,4},{8,6},{10,8},{12,10},{14,12},{16,14},{18,16},{20... | collective-permute-start | bytes 393224 | tf_op jit(solution)/shard_map/ppermute | solution.py:16
  44.5 1.3 %copy.82 = bf16[128,4096]{1,0:T(8,128)(2,1)} copy(bf16[128,4096]{0,1:T(8,128)(2,1)S(1)} %bitcast.166) | data formatting | bytes 2097152
  45.9 1.6 %collective-permute-done.3 = bf16[4,128,128]{1,2,0:T(8,128)(2,1)S(1)} collective-permute-done((bf16[4,128,128]{1,2,0:T(8,128)(2,1)S(1)}, bf16[4,128,128]{1,2,0:T(8,128)(2,1)S(1)}, u32[]{:S(2)}, u32[]{:S(2)}) %collective-permute-start.3) | collective-permute-done | bytes 131104 | tf_op jit(solution)/shard_map/ppermute | solution.py:16
  47.5 1.5 %collective-permute-done.2 = bf16[4,128,128]{1,2,0:T(8,128)(2,1)} collective-permute-done((bf16[4,128,128]{1,2,0:T(8,128)(2,1)}, bf16[4,128,128]{1,2,0:T(8,128)(2,1)}, u32[]{:S(2)}, u32[]{:S(2)}) %collective-permute-start.2) | collective-permute-done | bytes 131104 | tf_op jit(solution)/shard_map/ppermute | solution.py:16
  49.0 1.5 %fusion.11 = bf16[4,128,128]{1,2,0:T(8,128)(2,1)S(1)} fusion(bf16[4,8,128,128]{2,3,1,0:T(8,128)(2,1)S(1)} %get-tuple-element.51, bf16[128,4,8,128]{3,2,1,0:T(8,128)(2,1)S(1)} %bitcast.162, bf16[4,128,128]{1,2,0:T(8,128)(2,1)S(1)} %collective-permute-done.3, bf16[4,128,128]{1,2,0:T(8,128)(2,1)} %collective-permute-done.2), kind=kOutput, calls=%fused_computation.29 | convolution fusion | flops 134610944 | bytes 2490368 | tf_op jit(solution)/shard_map/ghts,tghd->gsd/dot_general | solution.py:41
  50.5 0.8 %copy.83 = bf16[128,512]{1,0:T(8,128)(2,1)} copy(bf16[128,512]{0,1:T(8,128)(2,1)S(1)} %bitcast.186) | data formatting | bytes 262144
  (26 shorter events, 5.1 us)
Async XLA Ops:
  0.6 14.3 %copy-start = (bf16[128,4096]{1,0:T(8,128)(2,1)S(1)}, bf16[128,4096]{1,0:T(8,128)(2,1)}, u32[]{:S(2)}) copy-start(bf16[128,4096]{1,0:T(8,128)(2,1)} %param.5) | copy-start | bytes 3145732
  0.6 14.5 %copy-start.1 = (bf16[128,4096]{1,0:T(8,128)(2,1)S(1)}, bf16[128,4096]{1,0:T(8,128)(2,1)}, u32[]{:S(2)}) copy-start(bf16[128,4096]{1,0:T(8,128)(2,1)} %param.8) | copy-start | bytes 3145732
  3.6 23.3 %collective-permute-start.1 = (bf16[2,128,512]{1,2,0:T(8,128)(2,1)}, bf16[2,128,512]{1,2,0:T(8,128)(2,1)}, u32[]{:S(2)}, u32[]{:S(2)}) collective-permute-start(bf16[2,128,512]{1,2,0:T(8,128)(2,1)} %pad_maximum_fusion), channel_id=1, source_target_pairs={{0,4},{2,6},{4,8},{6,10},{8,12},{10,14},{12,16},{14,18},{16,20},{1... | collective-permute-start | bytes 786440 | tf_op jit(solution)/shard_map/ppermute | solution.py:16
  8.6 13.8 %collective-permute-start = (bf16[2,128,512]{1,2,0:T(8,128)(2,1)}, bf16[2,128,512]{1,2,0:T(8,128)(2,1)}, u32[]{:S(2)}, u32[]{:S(2)}) collective-permute-start(bf16[2,128,512]{1,2,0:T(8,128)(2,1)} %pad_maximum_fusion), channel_id=1, source_target_pairs={{0,2},{2,4},{4,6},{6,8},{8,10},{10,12},{12,14},{14,16},{16,18},{18... | collective-permute-start | bytes 786440 | tf_op jit(solution)/shard_map/ppermute | solution.py:16
  33.9 13.6 %collective-permute-start.3 = (bf16[4,128,128]{1,2,0:T(8,128)(2,1)S(1)}, bf16[4,128,128]{1,2,0:T(8,128)(2,1)S(1)}, u32[]{:S(2)}, u32[]{:S(2)}) collective-permute-start(bf16[4,128,128]{1,2,0:T(8,128)(2,1)S(1)} %fusion.13), channel_id=1, source_target_pairs={{4,0},{6,2},{8,4},{10,6},{12,8},{14,10},{16,12},{18,14},{20,16},{2... | collective-permute-start | bytes 393224 | tf_op jit(solution)/shard_map/ppermute | solution.py:16
  41.3 7.7 %collective-permute-start.2 = (bf16[4,128,128]{1,2,0:T(8,128)(2,1)}, bf16[4,128,128]{1,2,0:T(8,128)(2,1)}, u32[]{:S(2)}, u32[]{:S(2)}) collective-permute-start(bf16[4,128,128]{1,2,0:T(8,128)(2,1)} %fusion.12), channel_id=1, source_target_pairs={{2,0},{4,2},{6,4},{8,6},{10,8},{12,10},{14,12},{16,14},{18,16},{20... | collective-permute-start | bytes 393224 | tf_op jit(solution)/shard_map/ppermute | solution.py:16

commit v8 on v5

--- a/solution.py
+++ b/solution.py
@@ -1,6 +1,7 @@
 import jax
 import jax.numpy as jnp
 from jax import lax
+from jax.experimental.layout import Layout, with_layout_constraint
 from jax.sharding import PartitionSpec as P
 
 QH = 32
@@ -51,7 +52,9 @@
     rows = queries.shape[0]
     score_scale = HD ** (-0.5)
     axes = ("ctx", "uly")
-    key_value = jnp.stack([key_vectors, value_vectors])
+    key_value = with_layout_constraint(
+        jnp.stack([key_vectors, value_vectors]), Layout(major_to_minor=(0, 1, 2))
+    )
     near_rim = shifted(key_value, axes, 1)
     far_rim = shifted(key_value, axes, 2)
     device_index = lax.axis_index(axes)

time: 49.8 us -> 57.1 us (1.15)
  matrix products: 9.93 us -> 13.8 us
  local copies, waits for them, and re-layouts: 9.5 us -> 12.7 us
  other arithmetic: 3.42 us -> 5.38 us
  waiting for transfers between devices: 12.2 us -> 10.3 us
    another operation x1 -> x7, local copies, waits for them, and re-layouts: 0.73 us -> 4.89 us  [the longest x2 1.72 us: body(): near_keys = near_rim[0].reshape(rows, KVH, HD)]
    dot_general x1, matrix products: 1.04 us -> 2.92 us  [body(): jnp.einsum('tghd,sgd->ghts', grad_heads, own_values, preferred_element_ty...]
    ppermute x4, waiting for transfers between devices: 12.2 us -> 10.3 us  [shifted(): return lax.ppermute(block, axis, route)]
    unnamed x10 -> x32, local copies, waits for them, and re-layouts: 4.77 us -> 3.16 us
    dot_general x1, matrix products: 0.51 us -> 1.84 us  [body(): jnp.einsum('tghd,sgd->ghts', grad_heads, near_values, preferred_element_t...]
    another operation x3, other arithmetic: 0.89 us -> 2.02 us  [the longest x1 1.87 us: body(): jnp.stack([key_vectors, value_vectors])]
    and x1, other arithmetic: 0.17 us -> 1 us  [allowed_pairs(): (query_docs[:, None] == key_docs[None, :]) & (key_pos[None, :] <= query_p...]
    dot_general x3, matrix products: 3.48 us -> 4.13 us  [key_grad_of(): jnp.einsum('ghts,tghd->gsd', grad_s, query_heads, preferred_element_type=...]
  transfers between devices with their start and end apart: 4 -> 4, of which waited for: 3 -> 3; matrix products, arithmetic and copies ran while one was open for 19% -> 21% of each run, Pallas kernels for 0% -> 0%
where the time goes in v8:
time: 57.1 us; the launch traced here: 56.7 us
  matrix products  13.8 us (24%)
  starting transfers between devices  13.4 us (23%)
  local copies, waits for them, and re-layouts  12.7 us (22%)
  waiting for transfers between devices  10.3 us (18%)
  other arithmetic  5.38 us (9%)
  between operations  1 us (2%)
    ppermute x4, starting transfers between devices, shifted(): return lax.ppermute(block, axis, route)  13.4 us
    ppermute x4, waiting for transfers between devices, shifted(): return lax.ppermute(block, axis, route)  10.3 us
    dot_general x3, matrix products, key_grad_of(): jnp.einsum('ghts,tghd->gsd', grad_s, query_heads, preferred_element_type=...  4.13 us
    unnamed x32, local copies, waits for them, and re-layouts  3.16 us
    dot_general x1, matrix products, body(): jnp.einsum('tghd,sgd->ghts', grad_heads, own_values, preferred_element_ty...  2.92 us
    convert_element_type x1, other arithmetic, body(): (near_exp / row_sum * (near_grad_p - row_delta)).astype(jnp.bfloat16)  2.2 us
    dot_general x3, matrix products, scores_of(): jnp.einsum('tghd,sgd->ghts', query_heads, key_heads, preferred_element_ty...  1.95 us
    another operation x1, other arithmetic, body(): jnp.stack([key_vectors, value_vectors])  1.87 us
  transfers between devices with their start and end apart: 4, of which 3 were waited for; matrix products, arithmetic and copies ran while one was open for 21% of the time, Pallas kernels for 0%

profile of v8, /device:TPU:1, one launch (start us, length us, event | category | flops | bytes accessed | tf_op | source)
XLA Modules:
  0.0 56.7 jit_solution(12884249064539569492)
XLA Ops:
  0.6 1.9 %pad_maximum_fusion = bf16[2,128,512]{2,1,0:T(8,128)(2,1)} fusion(bf16[1,128,512]{2,1,0:T(8,128)(2,1)} %bitcast.137, bf16[1,128,512]{2,1,0:T(8,128)(2,1)} %bitcast.136), kind=kLoop, calls=%fused_computation.51 | loop fusion | flops 131072 | bytes 524288 | tf_op jit(solution)/shard_map/stack | solution.py:56
  2.5 5.0 %collective-permute-start = (bf16[2,128,512]{2,1,0:T(8,128)(2,1)}, bf16[2,128,512]{2,1,0:T(8,128)(2,1)}, u32[]{:S(2)}, u32[]{:S(2)}) collective-permute-start(bf16[2,128,512]{2,1,0:T(8,128)(2,1)} %pad_maximum_fusion), channel_id=1, source_target_pairs={{0,4},{2,6},{4,8},{6,10},{8,12},{10,14},{12,16},{14,18},{16,20},{1... | collective-permute-start | bytes 786440 | tf_op jit(solution)/shard_map/ppermute | solution.py:17
  7.6 3.2 %collective-permute-start.1 = (bf16[2,128,512]{2,1,0:T(8,128)(2,1)}, bf16[2,128,512]{2,1,0:T(8,128)(2,1)}, u32[]{:S(2)}, u32[]{:S(2)}) collective-permute-start(bf16[2,128,512]{2,1,0:T(8,128)(2,1)} %pad_maximum_fusion), channel_id=1, source_target_pairs={{0,2},{2,4},{4,6},{6,8},{8,10},{10,12},{12,14},{14,16},{16,18},{18... | collective-permute-start | bytes 786440 | tf_op jit(solution)/shard_map/ppermute | solution.py:17
  10.8 0.9 %reshape.329 = bf16[128,4,128]{2,1,0:T(4,128)(2,1)S(1)} reshape(bf16[128,512]{1,0:T(8,128)(2,1)} %param.6) | data formatting | bytes 262144 | tf_op jit(solution)/shard_map/reshape | solution.py:63
  11.8 0.9 %reshape.331 = bf16[128,4,128]{2,1,0:T(4,128)(2,1)S(1)} reshape(bf16[128,512]{1,0:T(8,128)(2,1)} %param.7) | data formatting | bytes 262144 | tf_op jit(solution)/shard_map/reshape | solution.py:64
  14.4 1.0 %compare_and_fusion = (pred[128,128]{0,1:T(8,128)(4,1)}, pred[128,128]{0,1:T(8,128)(4,1)S(1)}, pred[128,128]{0,1:T(8,128)(4,1)}) fusion(s32[128]{0:T(128)S(1)} %iota_add_fusion, s32[128]{0:T(128)S(1)} %compare_select_fusion.2, s32[128]{0:T(128)S(1)} %broadcast_add_fusion, s32[128]{0:T(128)S(1)} %get-tuple-element.39, s32[128]{0:T(128)S(1)} %broadcast_add_fusion.1, ...), kind=kLoop, calls=%fused_computation.56 | loop fusion | flops 147456 | bytes 52224 | tf_op jit(solution)/shard_map/and | solution.py:29
  16.0 2.9 %fusion.6 = (f32[4,8,128]{2,1,0:T(8,128)}, f32[4,8,128]{2,1,0:T(8,128)}, f32[4,128,128,8]{2,1,3,0:T(8,128)}) fusion(f32[4,128,128,8]{2,1,3,0:T(8,128)S(1)} %get-tuple-element.32, f32[4,8,128]{2,1,0:T(8,128)S(1)} %get-tuple-element.31, pred[128,128]{0,1:T(8,128)(4,1)S(1)} %get-tuple-element.29, bf16[128,4,8,128]{3,2,1,0:T(8,128)(2,1)S(1)} %bitcast.124, ...), kind=kOutput, calls=%fused_computation.12 | convolution fusion | flops 137355264 | bytes 5439488 | tf_op jit(solution)/shard_map/tghd,sgd->ghts/dot_general | solution.py:75
  19.0 6.9 %collective-permute-done = bf16[2,128,512]{2,1,0:T(8,128)(2,1)} collective-permute-done((bf16[2,128,512]{2,1,0:T(8,128)(2,1)}, bf16[2,128,512]{2,1,0:T(8,128)(2,1)}, u32[]{:S(2)}, u32[]{:S(2)}) %collective-permute-start) | collective-permute-done | bytes 262176 | tf_op jit(solution)/shard_map/ppermute | solution.py:17
  25.9 1.0 %fusion.42 = (bf16[1,128,512]{2,1,0:T(8,128)(2,1)S(1)}, bf16[1,128,512]{2,1,0:T(8,128)(2,1)S(1)}) fusion(bf16[2,128,512]{2,1,0:T(8,128)(2,1)} %collective-permute-done), kind=kLoop, calls=%fused_computation.74 | loop fusion | bytes 524288 | tf_op jit(solution)/shard_map/slice | solution.py:81
  27.7 1.6 %fusion.41 = (bf16[1,128,512]{2,1,0:T(8,128)(2,1)}, bf16[1,128,512]{2,1,0:T(8,128)(2,1)S(1)}) fusion(bf16[2,128,512]{2,1,0:T(8,128)(2,1)} %collective-permute-done.1), kind=kLoop, calls=%fused_computation.73 | loop fusion | bytes 524288 | tf_op jit(solution)/shard_map/slice | solution.py:83
  29.4 1.6 %reshape_squeeze.15 = bf16[128,4,128]{2,1,0:T(4,128)(2,1)} reshape(bf16[1,128,512]{2,1,0:T(8,128)(2,1)} %get-tuple-element.21) | data formatting | bytes 262144 | tf_op jit(solution)/shard_map/reshape;squeeze | solution.py:83
  31.6 1.0 %copy.99 = bf16[128,4,128,1]{0,2,3,1:T(8,128)(2,1)S(1)} copy(bf16[128,4,128,1]{2,1,0,3:T(4,128)(2,1)} %bitcast.135) | data formatting | bytes 262144 | tf_op jit(solution)/shard_map/reshape;squeeze | solution.py:82
  32.7 1.8 %fusion.20 = f32[4,128,128,8]{2,1,3,0:T(8,128)S(1)} fusion(bf16[128,4,8,128]{3,2,1,0:T(8,128)(2,1)} %bitcast.125, bf16[128,4,128,1]{2,1,0,3:T(4,128)(2,1)} %bitcast.132), kind=kOutput, calls=%fused_computation.36 | convolution fusion | flops 134217728 | bytes 3276800 | tf_op jit(solution)/shard_map/tghd,sgd->ghts/dot_general | solution.py:104
  36.5 1.7 %fusion.3 = (f32[4,8,128]{2,1,0:T(8,128)S(1)}, f32[4,8,128]{2,1,0:T(8,128)S(1)}, f32[4,8,128]{2,1,0:T(8,128)S(1)}, f32[4,8,128]{2,1,0:T(8,128)S(1)}, f32[4,128,128,8]{2,1,3,0:T(8,128)S(1)}) fusion(f32[4,128,128,8]{2,1,3,0:T(8,128)S(1)} %get-tuple-element.34, f32[4,8,128]{2,1,0:T(8,128)S(1)} %maximum_maximum_fusion, pred[128,128]{0,1:T(8,128)(4,1)S(1)} %copy-done.11, ...), kind=kOutput, calls=%fused_computation.7 | convolution fusion | flops 140492800 | bytes 9682944 | tf_op jit(solution)/shard_map/tghd,sgd->ghts/dot_general | solution.py:101
  38.2 2.2 %fusion.2 = (bf16[4,8,128,128]{2,3,1,0:T(8,128)(2,1)S(1)}, bf16[4,8,128,128]{2,3,1,0:T(8,128)(2,1)S(1)}, bf16[4,8,128,128]{2,3,1,0:T(8,128)(2,1)S(1)}) fusion(f32[4,128,128,8]{2,1,3,0:T(8,128)S(1)} %fusion.20, f32[4,128,128,8]{2,1,3,0:T(8,128)S(1)} %get-tuple-element.36, f32[4,8,128]{2,1,0:T(8,128)S(1)} %get-tuple-element.20, ...), kind=kLoop, calls=%fused_computation.4 | loop fusion | flops 11010048 | bytes 15859712 | tf_op jit(solution)/shard_map/convert_element_type | solution.py:113
  40.4 1.3 %fusion.16 = bf16[4,128,128]{1,2,0:T(8,128)(2,1)} fusion(bf16[4,8,128,128]{2,3,1,0:T(8,128)(2,1)S(1)} %get-tuple-element.26, bf16[128,4,8,128]{3,2,1,0:T(8,128)(2,1)S(1)} %bitcast.121), kind=kOutput, calls=%fused_computation.32 | convolution fusion | flops 134348800 | bytes 2228224 | tf_op jit(solution)/shard_map/ghts,tghd->gsd/dot_general | solution.py:42
  42.2 1.3 %fusion.15 = bf16[4,128,128]{1,2,0:T(8,128)(2,1)} fusion(bf16[4,8,128,128]{2,3,1,0:T(8,128)(2,1)S(1)} %get-tuple-element.25, bf16[128,4,8,128]{3,2,1,0:T(8,128)(2,1)S(1)} %bitcast.122), kind=kOutput, calls=%fused_computation.31 | convolution fusion | flops 134348800 | bytes 2228224 | tf_op jit(solution)/shard_map/ghts,tghd->gsd/dot_general | solution.py:42
  43.5 2.8 %collective-permute-start.3 = (bf16[4,128,128]{1,2,0:T(8,128)(2,1)}, bf16[4,128,128]{1,2,0:T(8,128)(2,1)S(1)}, u32[]{:S(2)}, u32[]{:S(2)}) collective-permute-start(bf16[4,128,128]{1,2,0:T(8,128)(2,1)} %fusion.16), channel_id=1, source_target_pairs={{4,0},{6,2},{8,4},{10,6},{12,8},{14,10},{16,12},{18,14},{20,16},{2... | collective-permute-start | bytes 393224 | tf_op jit(solution)/shard_map/ppermute | solution.py:17
  46.3 2.4 %collective-permute-start.2 = (bf16[4,128,128]{1,2,0:T(8,128)(2,1)}, bf16[4,128,128]{1,2,0:T(8,128)(2,1)}, u32[]{:S(2)}, u32[]{:S(2)}) collective-permute-start(bf16[4,128,128]{1,2,0:T(8,128)(2,1)} %fusion.15), channel_id=1, source_target_pairs={{2,0},{4,2},{6,4},{8,6},{10,8},{12,10},{14,12},{16,14},{18,16},{20... | collective-permute-start | bytes 393224 | tf_op jit(solution)/shard_map/ppermute | solution.py:17
  49.6 1.3 %copy.86 = bf16[128,4096]{1,0:T(8,128)(2,1)} copy(bf16[128,4096]{0,1:T(8,128)(2,1)S(1)} %bitcast.127) | data formatting | bytes 2097152
  50.9 2.2 %collective-permute-done.3 = bf16[4,128,128]{1,2,0:T(8,128)(2,1)S(1)} collective-permute-done((bf16[4,128,128]{1,2,0:T(8,128)(2,1)}, bf16[4,128,128]{1,2,0:T(8,128)(2,1)S(1)}, u32[]{:S(2)}, u32[]{:S(2)}) %collective-permute-start.3) | collective-permute-done | bytes 131104 | tf_op jit(solution)/shard_map/ppermute | solution.py:17
  53.1 1.3 %collective-permute-done.2 = bf16[4,128,128]{1,2,0:T(8,128)(2,1)} collective-permute-done((bf16[4,128,128]{1,2,0:T(8,128)(2,1)}, bf16[4,128,128]{1,2,0:T(8,128)(2,1)}, u32[]{:S(2)}, u32[]{:S(2)}) %collective-permute-start.2) | collective-permute-done | bytes 131104 | tf_op jit(solution)/shard_map/ppermute | solution.py:17
  54.3 1.5 %add_convert_fusion = bf16[4,128,128]{1,2,0:T(8,128)(2,1)S(1)} fusion(bf16[4,128,128]{1,2,0:T(8,128)(2,1)S(1)} %collective-permute-done.3, bf16[4,128,128]{1,2,0:T(8,128)(2,1)} %collective-permute-done.2, bf16[4,8,128,128]{2,3,1,0:T(8,128)(2,1)S(1)} %copy-done.4, bf16[128,4,8,128]{3,2,1,0:T(8,128)(2,1)S(1)} %bitcast.123), kind=kOutput, calls=%fused_computation.52 | convolution fusion | flops 134610944 | bytes 2490368 | tf_op jit(solution)/shard_map/ghts,tghd->gsd/dot_general | solution.py:42
  55.9 0.8 %copy.87 = bf16[128,512]{1,0:T(8,128)(2,1)} copy(bf16[128,512]{0,1:T(8,128)(2,1)S(1)} %bitcast.138) | data formatting | bytes 262144
  (54 shorter events, 7.1 us)
Async XLA Ops:
  0.6 13.2 %copy-start.5 = (bf16[128,4096]{1,0:T(8,128)(2,1)S(1)}, bf16[128,4096]{1,0:T(8,128)(2,1)}, u32[]{:S(2)}) copy-start(bf16[128,4096]{1,0:T(8,128)(2,1)} %param.5) | copy-start | bytes 3145732
  0.6 13.5 %copy-start.6 = (bf16[128,4096]{1,0:T(8,128)(2,1)S(1)}, bf16[128,4096]{1,0:T(8,128)(2,1)}, u32[]{:S(2)}) copy-start(bf16[128,4096]{1,0:T(8,128)(2,1)} %param.8) | copy-start | bytes 3145732
  2.5 23.3 %collective-permute-start = (bf16[2,128,512]{2,1,0:T(8,128)(2,1)}, bf16[2,128,512]{2,1,0:T(8,128)(2,1)}, u32[]{:S(2)}, u32[]{:S(2)}) collective-permute-start(bf16[2,128,512]{2,1,0:T(8,128)(2,1)} %pad_maximum_fusion), channel_id=1, source_target_pairs={{0,4},{2,6},{4,8},{6,10},{8,12},{10,14},{12,16},{14,18},{16,20},{1... | collective-permute-start | bytes 786440 | tf_op jit(solution)/shard_map/ppermute | solution.py:17
  7.6 20.1 %collective-permute-start.1 = (bf16[2,128,512]{2,1,0:T(8,128)(2,1)}, bf16[2,128,512]{2,1,0:T(8,128)(2,1)}, u32[]{:S(2)}, u32[]{:S(2)}) collective-permute-start(bf16[2,128,512]{2,1,0:T(8,128)(2,1)} %pad_maximum_fusion), channel_id=1, source_target_pairs={{0,2},{2,4},{4,6},{6,8},{8,10},{10,12},{12,14},{14,16},{16,18},{18... | collective-permute-start | bytes 786440 | tf_op jit(solution)/shard_map/ppermute | solution.py:17
  14.4 4.6 %copy-start = (bf16[16,8,32,128]{3,2,1,0:T(8,128)(2,1)}, bf16[16,8,32,128]{3,2,1,0:T(8,128)(2,1)S(1)}, u32[]{:S(2)}) copy-start(bf16[16,8,32,128]{3,2,1,0:T(8,128)(2,1)S(1)} %copy.125) | copy-start | bytes 3145732
  15.4 3.6 %copy-start.9 = (pred[128,128]{0,1:T(8,128)(4,1)}, pred[128,128]{0,1:T(8,128)(4,1)S(1)}, u32[]{:S(2)}) copy-start(pred[128,128]{0,1:T(8,128)(4,1)S(1)} %get-tuple-element.29) | copy-start | bytes 49156
  32.7 1.9 %copy-start.11 = (pred[128,128]{0,1:T(8,128)(4,1)S(1)}, pred[128,128]{0,1:T(8,128)(4,1)}, u32[]{:S(2)}) copy-start(pred[128,128]{0,1:T(8,128)(4,1)} %get-tuple-element.30) | copy-start | bytes 49156
  34.5 0.7 %copy-start.8 = (pred[128,128]{0,1:T(8,128)(4,1)S(1)}, pred[128,128]{0,1:T(8,128)(4,1)}, u32[]{:S(2)}) copy-start(pred[128,128]{0,1:T(8,128)(4,1)} %get-tuple-element.28) | copy-start | bytes 49156
  35.2 1.2 %copy-start.1 = (bf16[16,8,32,128]{3,2,1,0:T(8,128)(2,1)S(1)}, bf16[16,8,32,128]{3,2,1,0:T(8,128)(2,1)}, u32[]{:S(2)}) copy-start(bf16[16,8,32,128]{3,2,1,0:T(8,128)(2,1)} %copy-done) | copy-start | bytes 3145732
  35.2 1.2 %copy-start.7 = (bf16[128,4,128]{2,1,0:T(4,128)(2,1)S(1)}, bf16[128,4,128]{2,1,0:T(4,128)(2,1)}, u32[]{:S(2)}) copy-start(bf16[128,4,128]{2,1,0:T(4,128)(2,1)} %reshape_squeeze.14) | copy-start | bytes 393220
  36.4 1.7 %copy-start.13 = (f32[4,8,128]{2,1,0:T(8,128)S(1)}, f32[4,8,128]{2,1,0:T(8,128)}, u32[]{:S(2)}) copy-start(f32[4,8,128]{2,1,0:T(8,128)} %get-tuple-element.9) | copy-start | bytes 49156
  36.4 1.7 %copy-start.12 = (f32[4,8,128]{2,1,0:T(8,128)S(1)}, f32[4,8,128]{2,1,0:T(8,128)}, u32[]{:S(2)}) copy-start(f32[4,8,128]{2,1,0:T(8,128)} %get-tuple-element.8) | copy-start | bytes 49156
  36.4 1.8 %copy-start.2 = (f32[4,128,128,8]{2,1,3,0:T(8,128)S(1)}, f32[4,128,128,8]{2,1,3,0:T(8,128)}, u32[]{:S(2)}) copy-start(f32[4,128,128,8]{2,1,3,0:T(8,128)} %get-tuple-element.38) | copy-start | bytes 6291460
  36.5 1.8 %copy-start.10 = (pred[128,128]{0,1:T(8,128)(4,1)S(1)}, pred[128,128]{0,1:T(8,128)(4,1)}, u32[]{:S(2)}) copy-start(pred[128,128]{0,1:T(8,128)(4,1)} %copy-done.9) | copy-start | bytes 49156
  40.4 8.2 %copy-start.3 = (bf16[4,8,128,128]{2,3,1,0:T(8,128)(2,1)}, bf16[4,8,128,128]{2,3,1,0:T(8,128)(2,1)S(1)}, u32[]{:S(2)}) copy-start(bf16[4,8,128,128]{2,3,1,0:T(8,128)(2,1)S(1)} %get-tuple-element.27) | copy-start | bytes 3145732
  43.5 9.6 %collective-permute-start.3 = (bf16[4,128,128]{1,2,0:T(8,128)(2,1)}, bf16[4,128,128]{1,2,0:T(8,128)(2,1)S(1)}, u32[]{:S(2)}, u32[]{:S(2)}) collective-permute-start(bf16[4,128,128]{1,2,0:T(8,128)(2,1)} %fusion.16), channel_id=1, source_target_pairs={{4,0},{6,2},{8,4},{10,6},{12,8},{14,10},{16,12},{18,14},{20,16},{2... | collective-permute-start | bytes 393224 | tf_op jit(solution)/shard_map/ppermute | solution.py:17
  46.3 8.1 %collective-permute-start.2 = (bf16[4,128,128]{1,2,0:T(8,128)(2,1)}, bf16[4,128,128]{1,2,0:T(8,128)(2,1)}, u32[]{:S(2)}, u32[]{:S(2)}) collective-permute-start(bf16[4,128,128]{1,2,0:T(8,128)(2,1)} %fusion.15), channel_id=1, source_target_pairs={{2,0},{4,2},{6,4},{8,6},{10,8},{12,10},{14,12},{16,14},{18,16},{20... | collective-permute-start | bytes 393224 | tf_op jit(solution)/shard_map/ppermute | solution.py:17
  49.6 4.8 %copy-start.4 = (bf16[4,8,128,128]{2,3,1,0:T(8,128)(2,1)S(1)}, bf16[4,8,128,128]{2,3,1,0:T(8,128)(2,1)}, u32[]{:S(2)}) copy-start(bf16[4,8,128,128]{2,3,1,0:T(8,128)(2,1)} %copy-done.3) | copy-start | bytes 3145732

commit v9 on v5

--- a/solution.py
+++ b/solution.py
@@ -110,10 +110,15 @@
     near_grad_s = ((near_exp / row_sum) * (near_grad_p - row_delta)).astype(jnp.bfloat16)
     far_key_grad = key_grad_of(far_grad_s, query_heads, score_scale)
     near_key_grad = key_grad_of(near_grad_s, query_heads, score_scale)
-    far_back = shifted(far_key_grad.astype(jnp.bfloat16), axes, -2)
-    near_back = shifted(near_key_grad.astype(jnp.bfloat16), axes, -1)
+    far_key_grad = far_key_grad.astype(jnp.bfloat16)
+    near_key_grad = near_key_grad.astype(jnp.bfloat16)
+    far_back = shifted(far_key_grad, axes, -2)
+    near_back = shifted(near_key_grad, axes, -1)
 
-    own_prob = own_exp * (own_rescale / row_sum)
+    _, own_scale, row_delta, far_grad_s, near_grad_s = lax.optimization_barrier(
+        ((far_key_grad, near_key_grad), own_rescale / row_sum, row_delta, far_grad_s, near_grad_s)
+    )
+    own_prob = own_exp * own_scale
     own_grad_s = (own_prob * (own_grad_p - row_delta)).astype(jnp.bfloat16)
     own_key_grad = key_grad_of(own_grad_s, query_heads, score_scale)
     query_grad = (

time: 49.8 us -> 46.2 us (0.928)
  matrix products: 9.93 us -> 8 us
  waiting for transfers between devices: 12.2 us -> 10.3 us
  local copies, waits for them, and re-layouts: 9.5 us -> 10.1 us
    ppermute x4, waiting for transfers between devices: 12.2 us -> 10.3 us  [shifted(): return lax.ppermute(block, axis, route)]
    dot_general x3, matrix products: 3.48 us -> 1.97 us  [key_grad_of(): jnp.einsum('ghts,tghd->gsd', grad_s, query_heads, preferred_element_type=...]
    convert_element_type x0 -> x1, other arithmetic: none -> 0.82 us  [body(): own_grad_s = (own_prob * (own_grad_p - row_delta)).astype(jnp.bfloat16)]
    convert_element_type x1, other arithmetic: 2.2 us -> 1.46 us  [body(): (near_exp / row_sum * (near_grad_p - row_delta)).astype(jnp.bfloat16)]
    reshape x0 -> x1, local copies, waits for them, and re-layouts: none -> 0.66 us  [body(): query_heads = queries.reshape(rows, KVH, GROUP, HD)]
    unnamed x10 -> x9, local copies, waits for them, and re-layouts: 4.77 us -> 4.53 us
  transfers between devices with their start and end apart: 4 -> 4, of which waited for: 3 -> 3; matrix products, arithmetic and copies ran while one was open for 19% -> 24% of each run, Pallas kernels for 0% -> 0%
where the time goes in v9:
time: 46.2 us; the launch traced here: 45.9 us
  starting transfers between devices  13.2 us (29%)
  waiting for transfers between devices  10.3 us (22%)
  local copies, waits for them, and re-layouts  10.1 us (22%)
  matrix products  8 us (17%)
  other arithmetic  3.5 us (8%)
  between operations  0.91 us (2%)
    ppermute x4, starting transfers between devices, shifted(): return lax.ppermute(block, axis, route)  13.2 us
    ppermute x4, waiting for transfers between devices, shifted(): return lax.ppermute(block, axis, route)  10.3 us
    unnamed x9, local copies, waits for them, and re-layouts  4.53 us
    dot_general x3, matrix products, key_grad_of(): jnp.einsum('ghts,tghd->gsd', grad_s, query_heads, preferred_element_type=...  1.97 us
    dot_general x1, matrix products, body(): jnp.einsum('tghd,sgd->ghts', grad_heads, far_values, preferred_element_ty...  1.66 us
    dot_general x3, matrix products, scores_of(): jnp.einsum('tghd,sgd->ghts', query_heads, key_heads, preferred_element_ty...  1.52 us
    convert_element_type x1, other arithmetic, body(): (near_exp / row_sum * (near_grad_p - row_delta)).astype(jnp.bfloat16)  1.46 us
    dot_general x3, matrix products, query_grad_of(): jnp.einsum('ghts,sgd->ghtd', grad_s, keys, preferred_element_type=jnp.flo...  1.3 us
  transfers between devices with their start and end apart: 4, of which 3 were waited for; matrix products, arithmetic and copies ran while one was open for 24% of the time, Pallas kernels for 0%

profile of v9, /device:TPU:1, one launch (start us, length us, event | category | flops | bytes accessed | tf_op | source)
XLA Modules:
  0.0 45.9 jit_solution(1475345336881721271)
XLA Ops:
  0.6 1.2 %copy.58 = bf16[128,512]{0,1:T(8,128)(2,1)S(1)} copy(bf16[128,512]{1,0:T(8,128)(2,1)} %param.6) | data formatting | bytes 262144 | tf_op args[1]
  1.8 1.0 %copy.59 = bf16[128,512]{0,1:T(8,128)(2,1)S(1)} copy(bf16[128,512]{1,0:T(8,128)(2,1)} %param.7) | data formatting | bytes 262144 | tf_op args[2]
  2.9 0.7 %pad_maximum_fusion = bf16[2,128,512]{1,2,0:T(8,128)(2,1)} fusion(bf16[1,128,512]{1,2,0:T(8,128)(2,1)S(1)} %bitcast.214, bf16[1,128,512]{1,2,0:T(8,128)(2,1)S(1)} %bitcast.213), kind=kLoop, calls=%fused_computation.42 | loop fusion | flops 131072 | bytes 524288 | tf_op jit(solution)/shard_map/stack | solution.py:54
  3.6 4.0 %collective-permute-start.1 = (bf16[2,128,512]{1,2,0:T(8,128)(2,1)}, bf16[2,128,512]{1,2,0:T(8,128)(2,1)}, u32[]{:S(2)}, u32[]{:S(2)}) collective-permute-start(bf16[2,128,512]{1,2,0:T(8,128)(2,1)} %pad_maximum_fusion), channel_id=1, source_target_pairs={{0,2},{2,4},{4,6},{6,8},{8,10},{10,12},{12,14},{14,16},{16,18},{18... | collective-permute-start | bytes 786440 | tf_op jit(solution)/shard_map/ppermute | solution.py:16
  7.6 4.2 %collective-permute-start = (bf16[2,128,512]{1,2,0:T(8,128)(2,1)}, bf16[2,128,512]{1,2,0:T(8,128)(2,1)}, u32[]{:S(2)}, u32[]{:S(2)}) collective-permute-start(bf16[2,128,512]{1,2,0:T(8,128)(2,1)} %pad_maximum_fusion), channel_id=1, source_target_pairs={{0,4},{2,6},{4,8},{6,10},{8,12},{10,14},{12,16},{14,18},{16,20},{1... | collective-permute-start | bytes 786440 | tf_op jit(solution)/shard_map/ppermute | solution.py:16
  11.9 0.9 %reshape.384 = bf16[128,4,128]{2,1,0:T(4,128)(2,1)S(1)} reshape(bf16[128,512]{1,0:T(8,128)(2,1)} %param.6) | data formatting | bytes 262144 | tf_op jit(solution)/shard_map/reshape | solution.py:60
  12.8 0.9 %reshape.387 = bf16[128,4,128]{2,1,0:T(4,128)(2,1)S(1)} reshape(bf16[128,512]{1,0:T(8,128)(2,1)} %param.7) | data formatting | bytes 262144 | tf_op jit(solution)/shard_map/reshape | solution.py:61
  13.8 0.7 %copy.55 = s32[16,1]{1,0:T(8,128)S(1)} copy(s32[16,1]{0,1:T(1,128)} %bitcast.217) | data formatting | bytes 128 | tf_op jit(solution)/shard_map/reshape.360
  14.9 0.7 %copy.113 = bf16[128,4096]{0,1:T(8,128)(2,1)S(1)} copy(bf16[128,4096]{1,0:T(8,128)(2,1)S(1)} %copy-done) | data formatting | bytes 2097152 | tf_op jit(solution)/shard_map/reshape | solution.py:58
  16.0 0.5 %fusion.9 = (f32[4,8,128]{2,1,0:T(8,128)S(1)}, f32[4,128,128,8]{2,1,3,0:T(8,128)S(1)}) fusion(pred[128,128]{0,1:T(8,128)(4,1)S(1)} %get-tuple-element.38, bf16[128,4,128,1]{0,2,3,1:T(8,128)(2,1)S(1)} %copy.91, bf16[128,4,8,128]{0,3,2,1:T(8,128)(2,1)S(1)} %bitcast.193), kind=kOutput, calls=%fused_computation.22 | convolution fusion | flops 135786496 | bytes 3309568 | tf_op jit(solution)/shard_map/tghd,sgd->ghts/dot_general | solution.py:33
  16.6 1.0 %fusion.3 = (f32[4,8,128]{2,1,0:T(8,128)S(1)}, f32[4,8,128]{2,1,0:T(8,128)S(1)}, f32[4,128,128,8]{2,1,3,0:T(8,128)S(1)}) fusion(f32[4,128,128,8]{2,1,3,0:T(8,128)S(1)} %get-tuple-element.41, f32[4,8,128]{2,1,0:T(8,128)S(1)} %get-tuple-element.40, pred[128,128]{0,1:T(8,128)(4,1)S(1)} %get-tuple-element.38, bf16[128,4,8,128]{3,2,1,0:T(8,128)(2,1)S(1)} %bitcast.199, ...), kind=kOutput, calls=%fused_computation.7 | convolution fusion | flops 137355264 | bytes 5439488 | tf_op jit(solution)/shard_map/tghd,sgd->ghts/dot_general | solution.py:72
  17.6 1.0 %fusion.31 = (bf16[1,128,512]{1,2,0:T(8,128)(2,1)S(1)}, bf16[1,128,512]{1,2,0:T(8,128)(2,1)S(1)}) fusion(bf16[2,128,512]{1,2,0:T(8,128)(2,1)} %collective-permute-done.1), kind=kLoop, calls=%fused_computation.72 | loop fusion | bytes 524288 | tf_op jit(solution)/shard_map/slice | solution.py:80
  19.1 0.5 %fusion.20 = f32[4,128,128,8]{2,1,3,0:T(8,128)S(1)} fusion(bf16[128,4,128,1]{0,2,3,1:T(8,128)(2,1)S(1)} %bitcast.211, bf16[128,4,8,128]{3,2,1,0:T(8,128)(2,1)S(1)} %bitcast.200), kind=kOutput, calls=%fused_computation.36 | convolution fusion | flops 134217728 | bytes 3276800 | tf_op jit(solution)/shard_map/tghd,sgd->ghts/dot_general | solution.py:101
  19.6 8.9 %collective-permute-done = bf16[2,128,512]{1,2,0:T(8,128)(2,1)} collective-permute-done((bf16[2,128,512]{1,2,0:T(8,128)(2,1)}, bf16[2,128,512]{1,2,0:T(8,128)(2,1)}, u32[]{:S(2)}, u32[]{:S(2)}) %collective-permute-start) | collective-permute-done | bytes 262176 | tf_op jit(solution)/shard_map/ppermute | solution.py:16
  28.5 1.0 %fusion.32 = (bf16[1,128,512]{1,2,0:T(8,128)(2,1)S(1)}, bf16[1,128,512]{1,2,0:T(8,128)(2,1)S(1)}) fusion(bf16[2,128,512]{1,2,0:T(8,128)(2,1)} %collective-permute-done), kind=kLoop, calls=%fused_computation.73 | loop fusion | bytes 524288 | tf_op jit(solution)/shard_map/slice | solution.py:77
  30.1 1.7 %fusion.6 = (f32[4,8,128]{2,1,0:T(8,128)S(1)}, f32[4,8,128]{2,1,0:T(8,128)S(1)}, f32[4,8,128]{2,1,0:T(8,128)S(1)}, f32[4,8,128]{2,1,0:T(8,128)S(1)}, f32[4,128,128,8]{2,1,3,0:T(8,128)S(1)}) fusion(f32[4,128,128,8]{2,1,3,0:T(8,128)S(1)} %get-tuple-element.43, f32[4,8,128]{2,1,0:T(8,128)S(1)} %maximum_maximum_fusion, ...), kind=kOutput, calls=%fused_computation.12 | convolution fusion | flops 140492800 | bytes 9682944 | tf_op jit(solution)/shard_map/tghd,sgd->ghts/dot_general | solution.py:98
  31.8 1.5 %fusion.2 = (bf16[4,8,128,128]{2,3,1,0:T(8,128)(2,1)S(1)}, bf16[4,8,128,128]{2,3,1,0:T(8,128)(2,1)S(1)}) fusion(f32[4,128,128,8]{2,1,3,0:T(8,128)S(1)} %fusion.20, f32[4,128,128,8]{2,1,3,0:T(8,128)S(1)} %get-tuple-element.45, f32[4,8,128]{2,1,0:T(8,128)S(1)} %get-tuple-element.27, f32[4,8,128]{2,1,0:T(8,128)S(1)} %get-tuple-element.28, ...), kind=kLoop, calls=%fused_computation.4 | loop fusion | flops 7340032 | bytes 10567680 | tf_op jit(solution)/shard_map/convert_element_type | solution.py:110
  33.7 1.1 %fusion.15 = bf16[4,128,128]{2,1,0:T(8,128)(2,1)} fusion(bf16[4,8,128,128]{2,3,1,0:T(8,128)(2,1)S(1)} %get-tuple-element.8, bf16[128,4,8,128]{0,3,2,1:T(8,128)(2,1)S(1)} %bitcast.197), kind=kOutput, calls=%fused_computation.31 | convolution fusion | flops 134348800 | bytes 2228224 | tf_op jit(solution)/shard_map/ghts,tghd->gsd/dot_general | solution.py:41
  34.8 1.9 %collective-permute-start.3 = (bf16[4,128,128]{2,1,0:T(8,128)(2,1)}, bf16[4,128,128]{2,1,0:T(8,128)(2,1)S(1)}, u32[]{:S(2)}, u32[]{:S(2)}) collective-permute-start(bf16[4,128,128]{2,1,0:T(8,128)(2,1)} %fusion.15), channel_id=1, source_target_pairs={{4,0},{6,2},{8,4},{10,6},{12,8},{14,10},{16,12},{18,14},{20,16},{2... | collective-permute-start | bytes 393224 | tf_op jit(solution)/shard_map/ppermute | solution.py:16
  36.7 3.0 %collective-permute-start.2 = (bf16[4,128,128]{2,1,0:T(8,128)(2,1)S(1)}, bf16[4,128,128]{2,1,0:T(8,128)(2,1)S(1)}, u32[]{:S(2)}, u32[]{:S(2)}) collective-permute-start(bf16[4,128,128]{2,1,0:T(8,128)(2,1)S(1)} %fusion.16), channel_id=1, source_target_pairs={{2,0},{4,2},{6,4},{8,6},{10,8},{12,10},{14,12},{16,14},{18,16},{20... | collective-permute-start | bytes 393224 | tf_op jit(solution)/shard_map/ppermute | solution.py:16
  39.7 0.8 %fusion.5 = bf16[4,8,128,128]{2,3,1,0:T(8,128)(2,1)S(1)} fusion(f32[4,128,128,8]{2,1,3,0:T(8,128)S(1)} %get-tuple-element.47, f32[4,128,128,8]{2,1,3,0:T(8,128)S(1)} %get-tuple-element.41, f32[4,8,128]{2,1,0:T(8,128)S(1)} %bitcast.215, f32[4,8,128]{2,1,0:T(8,128)S(1)} %bitcast.216, f32[4,8,128]{2,1,0:T(8,128)S(1)} %get-tuple-element.40, ...), kind=kLoop, calls=%fused_computation.9 | loop fusion | flops 3670016 | bytes 5308416 | tf_op jit(solution)/shard_map/convert_element_type | solution.py:122
  41.9 1.3 %copy.80 = bf16[128,4096]{1,0:T(8,128)(2,1)} copy(bf16[128,4096]{0,1:T(8,128)(2,1)S(1)} %bitcast.202) | data formatting | bytes 2097152
  43.5 1.1 %collective-permute-done.2 = bf16[4,128,128]{2,1,0:T(8,128)(2,1)S(1)} collective-permute-done((bf16[4,128,128]{2,1,0:T(8,128)(2,1)S(1)}, bf16[4,128,128]{2,1,0:T(8,128)(2,1)S(1)}, u32[]{:S(2)}, u32[]{:S(2)}) %collective-permute-start.2) | collective-permute-done | bytes 131104 | tf_op jit(solution)/shard_map/ppermute | solution.py:16
  45.1 0.8 %copy.81 = bf16[128,512]{1,0:T(8,128)(2,1)} copy(bf16[128,512]{0,1:T(8,128)(2,1)S(1)} %bitcast.212) | data formatting | bytes 262144
  (28 shorter events, 4.5 us)
Async XLA Ops:
  0.6 14.3 %copy-start = (bf16[128,4096]{1,0:T(8,128)(2,1)S(1)}, bf16[128,4096]{1,0:T(8,128)(2,1)}, u32[]{:S(2)}) copy-start(bf16[128,4096]{1,0:T(8,128)(2,1)} %param.5) | copy-start | bytes 3145732
  0.6 15.0 %copy-start.1 = (bf16[128,4096]{1,0:T(8,128)(2,1)S(1)}, bf16[128,4096]{1,0:T(8,128)(2,1)}, u32[]{:S(2)}) copy-start(bf16[128,4096]{1,0:T(8,128)(2,1)} %param.8) | copy-start | bytes 3145732
  3.6 14.0 %collective-permute-start.1 = (bf16[2,128,512]{1,2,0:T(8,128)(2,1)}, bf16[2,128,512]{1,2,0:T(8,128)(2,1)}, u32[]{:S(2)}, u32[]{:S(2)}) collective-permute-start(bf16[2,128,512]{1,2,0:T(8,128)(2,1)} %pad_maximum_fusion), channel_id=1, source_target_pairs={{0,2},{2,4},{4,6},{6,8},{8,10},{10,12},{12,14},{14,16},{16,18},{18... | collective-permute-start | bytes 786440 | tf_op jit(solution)/shard_map/ppermute | solution.py:16
  7.6 20.9 %collective-permute-start = (bf16[2,128,512]{1,2,0:T(8,128)(2,1)}, bf16[2,128,512]{1,2,0:T(8,128)(2,1)}, u32[]{:S(2)}, u32[]{:S(2)}) collective-permute-start(bf16[2,128,512]{1,2,0:T(8,128)(2,1)} %pad_maximum_fusion), channel_id=1, source_target_pairs={{0,4},{2,6},{4,8},{6,10},{8,12},{10,14},{12,16},{14,18},{16,20},{1... | collective-permute-start | bytes 786440 | tf_op jit(solution)/shard_map/ppermute | solution.py:16
  34.8 8.7 %collective-permute-start.3 = (bf16[4,128,128]{2,1,0:T(8,128)(2,1)}, bf16[4,128,128]{2,1,0:T(8,128)(2,1)S(1)}, u32[]{:S(2)}, u32[]{:S(2)}) collective-permute-start(bf16[4,128,128]{2,1,0:T(8,128)(2,1)} %fusion.15), channel_id=1, source_target_pairs={{4,0},{6,2},{8,4},{10,6},{12,8},{14,10},{16,12},{18,14},{20,16},{2... | collective-permute-start | bytes 393224 | tf_op jit(solution)/shard_map/ppermute | solution.py:16
  36.7 7.9 %collective-permute-start.2 = (bf16[4,128,128]{2,1,0:T(8,128)(2,1)S(1)}, bf16[4,128,128]{2,1,0:T(8,128)(2,1)S(1)}, u32[]{:S(2)}, u32[]{:S(2)}) collective-permute-start(bf16[4,128,128]{2,1,0:T(8,128)(2,1)S(1)} %fusion.16), channel_id=1, source_target_pairs={{2,0},{4,2},{6,4},{8,6},{10,8},{12,10},{14,12},{16,14},{18,16},{20... | collective-permute-start | bytes 393224 | tf_op jit(solution)/shard_map/ppermute | solution.py:16

commit v10 on v9

--- a/solution.py
+++ b/solution.py
@@ -128,7 +128,7 @@
     ) * score_scale
     query_grad = jnp.transpose(query_grad.astype(jnp.bfloat16), (2, 0, 1, 3)).reshape(rows, QH * HD)
     key_grad = own_key_grad + near_back.astype(jnp.float32) + far_back.astype(jnp.float32)
-    key_grad = jnp.transpose(key_grad, (1, 0, 2)).reshape(rows, KVH * HD).astype(jnp.bfloat16)
+    key_grad = jnp.concatenate([key_grad[g] for g in range(KVH)], axis=1).astype(jnp.bfloat16)
     return (query_grad, key_grad)
 
 

time: 46.2 us -> 46 us (level)
  local copies, waits for them, and re-layouts: 10.1 us -> 9.16 us
  other arithmetic: 3.5 us -> 4.18 us
    unnamed x9 -> x8, local copies, waits for them, and re-layouts: 4.53 us -> 3.76 us
    concatenate x0 -> x1, other arithmetic: none -> 0.67 us  [body(): jnp.concatenate([key_grad[g] for g in range(KVH)], axis=1)]
where the time goes in v10:
time: 46 us; the launch traced here: 45.7 us
  starting transfers between devices  13.2 us (29%)
  waiting for transfers between devices  10.3 us (22%)
  local copies, waits for them, and re-layouts  9.16 us (20%)
  matrix products  8 us (17%)
  other arithmetic  4.18 us (9%)
  between operations  0.91 us (2%)
    ppermute x4, starting transfers between devices, shifted(): return lax.ppermute(block, axis, route)  13.2 us
    ppermute x4, waiting for transfers between devices, shifted(): return lax.ppermute(block, axis, route)  10.3 us
    unnamed x8, local copies, waits for them, and re-layouts  3.76 us
    dot_general x3, matrix products, key_grad_of(): jnp.einsum('ghts,tghd->gsd', grad_s, query_heads, preferred_element_type=...  1.97 us
    dot_general x1, matrix products, body(): jnp.einsum('tghd,sgd->ghts', grad_heads, far_values, preferred_element_ty...  1.66 us
    dot_general x3, matrix products, scores_of(): jnp.einsum('tghd,sgd->ghts', query_heads, key_heads, preferred_element_ty...  1.52 us
    convert_element_type x1, other arithmetic, body(): (near_exp / row_sum * (near_grad_p - row_delta)).astype(jnp.bfloat16)  1.46 us
    dot_general x3, matrix products, query_grad_of(): jnp.einsum('ghts,sgd->ghtd', grad_s, keys, preferred_element_type=jnp.flo...  1.3 us
  transfers between devices with their start and end apart: 4, of which 3 were waited for; matrix products, arithmetic and copies ran while one was open for 24% of the time, Pallas kernels for 0%

profile of v10, /device:TPU:1, one launch (start us, length us, event | category | flops | bytes accessed | tf_op | source)
XLA Modules:
  0.0 45.7 jit_solution(6530421686088489886)
XLA Ops:
  0.6 1.2 %copy.56 = bf16[128,512]{0,1:T(8,128)(2,1)S(1)} copy(bf16[128,512]{1,0:T(8,128)(2,1)} %param.6) | data formatting | bytes 262144 | tf_op args[1]
  1.8 1.0 %copy.57 = bf16[128,512]{0,1:T(8,128)(2,1)S(1)} copy(bf16[128,512]{1,0:T(8,128)(2,1)} %param.7) | data formatting | bytes 262144 | tf_op args[2]
  2.9 0.7 %pad_maximum_fusion = bf16[2,128,512]{1,2,0:T(8,128)(2,1)} fusion(bf16[1,128,512]{1,2,0:T(8,128)(2,1)S(1)} %bitcast.218, bf16[1,128,512]{1,2,0:T(8,128)(2,1)S(1)} %bitcast.217), kind=kLoop, calls=%fused_computation.42 | loop fusion | flops 131072 | bytes 524288 | tf_op jit(solution)/shard_map/stack | solution.py:54
  3.6 4.0 %collective-permute-start.1 = (bf16[2,128,512]{1,2,0:T(8,128)(2,1)}, bf16[2,128,512]{1,2,0:T(8,128)(2,1)}, u32[]{:S(2)}, u32[]{:S(2)}) collective-permute-start(bf16[2,128,512]{1,2,0:T(8,128)(2,1)} %pad_maximum_fusion), channel_id=1, source_target_pairs={{0,2},{2,4},{4,6},{6,8},{8,10},{10,12},{12,14},{14,16},{16,18},{18... | collective-permute-start | bytes 786440 | tf_op jit(solution)/shard_map/ppermute | solution.py:16
  7.6 4.2 %collective-permute-start = (bf16[2,128,512]{1,2,0:T(8,128)(2,1)}, bf16[2,128,512]{1,2,0:T(8,128)(2,1)}, u32[]{:S(2)}, u32[]{:S(2)}) collective-permute-start(bf16[2,128,512]{1,2,0:T(8,128)(2,1)} %pad_maximum_fusion), channel_id=1, source_target_pairs={{0,4},{2,6},{4,8},{6,10},{8,12},{10,14},{12,16},{14,18},{16,20},{1... | collective-permute-start | bytes 786440 | tf_op jit(solution)/shard_map/ppermute | solution.py:16
  11.9 0.9 %reshape.382 = bf16[128,4,128]{2,1,0:T(4,128)(2,1)S(1)} reshape(bf16[128,512]{1,0:T(8,128)(2,1)} %param.6) | data formatting | bytes 262144 | tf_op jit(solution)/shard_map/reshape | solution.py:60
  12.8 0.9 %reshape.385 = bf16[128,4,128]{2,1,0:T(4,128)(2,1)S(1)} reshape(bf16[128,512]{1,0:T(8,128)(2,1)} %param.7) | data formatting | bytes 262144 | tf_op jit(solution)/shard_map/reshape | solution.py:61
  13.8 0.7 %copy.53 = s32[16,1]{1,0:T(8,128)S(1)} copy(s32[16,1]{0,1:T(1,128)} %bitcast.221) | data formatting | bytes 128 | tf_op jit(solution)/shard_map/reshape.359
  14.9 0.7 %copy.109 = bf16[128,4096]{0,1:T(8,128)(2,1)S(1)} copy(bf16[128,4096]{1,0:T(8,128)(2,1)S(1)} %copy-done) | data formatting | bytes 2097152 | tf_op jit(solution)/shard_map/reshape | solution.py:58
  16.0 0.5 %fusion.9 = (f32[4,8,128]{2,1,0:T(8,128)S(1)}, f32[4,128,128,8]{2,1,3,0:T(8,128)S(1)}) fusion(pred[128,128]{0,1:T(8,128)(4,1)S(1)} %get-tuple-element.42, bf16[128,4,128,1]{0,2,3,1:T(8,128)(2,1)S(1)} %copy.87, bf16[128,4,8,128]{0,3,2,1:T(8,128)(2,1)S(1)} %bitcast.198), kind=kOutput, calls=%fused_computation.22 | convolution fusion | flops 135786496 | bytes 3309568 | tf_op jit(solution)/shard_map/tghd,sgd->ghts/dot_general | solution.py:33
  16.6 1.0 %fusion.3 = (f32[4,8,128]{2,1,0:T(8,128)S(1)}, f32[4,8,128]{2,1,0:T(8,128)S(1)}, f32[4,128,128,8]{2,1,3,0:T(8,128)S(1)}) fusion(f32[4,128,128,8]{2,1,3,0:T(8,128)S(1)} %get-tuple-element.45, f32[4,8,128]{2,1,0:T(8,128)S(1)} %get-tuple-element.44, pred[128,128]{0,1:T(8,128)(4,1)S(1)} %get-tuple-element.42, bf16[128,4,8,128]{3,2,1,0:T(8,128)(2,1)S(1)} %bitcast.204, ...), kind=kOutput, calls=%fused_computation.7 | convolution fusion | flops 137355264 | bytes 5439488 | tf_op jit(solution)/shard_map/tghd,sgd->ghts/dot_general | solution.py:72
  17.6 1.0 %fusion.30 = (bf16[1,128,512]{1,2,0:T(8,128)(2,1)S(1)}, bf16[1,128,512]{1,2,0:T(8,128)(2,1)S(1)}) fusion(bf16[2,128,512]{1,2,0:T(8,128)(2,1)} %collective-permute-done.1), kind=kLoop, calls=%fused_computation.76 | loop fusion | bytes 524288 | tf_op jit(solution)/shard_map/slice | solution.py:80
  19.1 0.5 %fusion.20 = f32[4,128,128,8]{2,1,3,0:T(8,128)S(1)} fusion(bf16[128,4,128,1]{0,2,3,1:T(8,128)(2,1)S(1)} %bitcast.216, bf16[128,4,8,128]{3,2,1,0:T(8,128)(2,1)S(1)} %bitcast.205), kind=kOutput, calls=%fused_computation.36 | convolution fusion | flops 134217728 | bytes 3276800 | tf_op jit(solution)/shard_map/tghd,sgd->ghts/dot_general | solution.py:101
  19.6 8.9 %collective-permute-done = bf16[2,128,512]{1,2,0:T(8,128)(2,1)} collective-permute-done((bf16[2,128,512]{1,2,0:T(8,128)(2,1)}, bf16[2,128,512]{1,2,0:T(8,128)(2,1)}, u32[]{:S(2)}, u32[]{:S(2)}) %collective-permute-start) | collective-permute-done | bytes 262176 | tf_op jit(solution)/shard_map/ppermute | solution.py:16
  28.5 1.0 %fusion.31 = (bf16[1,128,512]{1,2,0:T(8,128)(2,1)S(1)}, bf16[1,128,512]{1,2,0:T(8,128)(2,1)S(1)}) fusion(bf16[2,128,512]{1,2,0:T(8,128)(2,1)} %collective-permute-done), kind=kLoop, calls=%fused_computation.77 | loop fusion | bytes 524288 | tf_op jit(solution)/shard_map/slice | solution.py:77
  30.1 1.7 %fusion.6 = (f32[4,8,128]{2,1,0:T(8,128)S(1)}, f32[4,8,128]{2,1,0:T(8,128)S(1)}, f32[4,8,128]{2,1,0:T(8,128)S(1)}, f32[4,8,128]{2,1,0:T(8,128)S(1)}, f32[4,128,128,8]{2,1,3,0:T(8,128)S(1)}) fusion(f32[4,128,128,8]{2,1,3,0:T(8,128)S(1)} %get-tuple-element.47, f32[4,8,128]{2,1,0:T(8,128)S(1)} %maximum_maximum_fusion, ...), kind=kOutput, calls=%fused_computation.12 | convolution fusion | flops 140492800 | bytes 9682944 | tf_op jit(solution)/shard_map/tghd,sgd->ghts/dot_general | solution.py:98
  31.8 1.5 %fusion.2 = (bf16[4,8,128,128]{2,3,1,0:T(8,128)(2,1)S(1)}, bf16[4,8,128,128]{2,3,1,0:T(8,128)(2,1)S(1)}) fusion(f32[4,128,128,8]{2,1,3,0:T(8,128)S(1)} %fusion.20, f32[4,128,128,8]{2,1,3,0:T(8,128)S(1)} %get-tuple-element.49, f32[4,8,128]{2,1,0:T(8,128)S(1)} %get-tuple-element.27, f32[4,8,128]{2,1,0:T(8,128)S(1)} %get-tuple-element.28, ...), kind=kLoop, calls=%fused_computation.4 | loop fusion | flops 7340032 | bytes 10567680 | tf_op jit(solution)/shard_map/convert_element_type | solution.py:110
  33.7 1.1 %fusion.15 = bf16[4,128,128]{2,1,0:T(8,128)(2,1)} fusion(bf16[4,8,128,128]{2,3,1,0:T(8,128)(2,1)S(1)} %get-tuple-element.8, bf16[128,4,8,128]{0,3,2,1:T(8,128)(2,1)S(1)} %bitcast.202), kind=kOutput, calls=%fused_computation.31 | convolution fusion | flops 134348800 | bytes 2228224 | tf_op jit(solution)/shard_map/ghts,tghd->gsd/dot_general | solution.py:41
  34.8 1.9 %collective-permute-start.3 = (bf16[4,128,128]{2,1,0:T(8,128)(2,1)}, bf16[4,128,128]{2,1,0:T(8,128)(2,1)S(1)}, u32[]{:S(2)}, u32[]{:S(2)}) collective-permute-start(bf16[4,128,128]{2,1,0:T(8,128)(2,1)} %fusion.15), channel_id=1, source_target_pairs={{4,0},{6,2},{8,4},{10,6},{12,8},{14,10},{16,12},{18,14},{20,16},{2... | collective-permute-start | bytes 393224 | tf_op jit(solution)/shard_map/ppermute | solution.py:16
  36.7 3.0 %collective-permute-start.2 = (bf16[4,128,128]{2,1,0:T(8,128)(2,1)S(1)}, bf16[4,128,128]{2,1,0:T(8,128)(2,1)S(1)}, u32[]{:S(2)}, u32[]{:S(2)}) collective-permute-start(bf16[4,128,128]{2,1,0:T(8,128)(2,1)S(1)} %fusion.16), channel_id=1, source_target_pairs={{2,0},{4,2},{6,4},{8,6},{10,8},{12,10},{14,12},{16,14},{18,16},{20... | collective-permute-start | bytes 393224 | tf_op jit(solution)/shard_map/ppermute | solution.py:16
  39.7 0.8 %fusion.5 = bf16[4,8,128,128]{2,3,1,0:T(8,128)(2,1)S(1)} fusion(f32[4,128,128,8]{2,1,3,0:T(8,128)S(1)} %get-tuple-element.51, f32[4,128,128,8]{2,1,3,0:T(8,128)S(1)} %get-tuple-element.45, f32[4,8,128]{2,1,0:T(8,128)S(1)} %bitcast.219, f32[4,8,128]{2,1,0:T(8,128)S(1)} %bitcast.220, f32[4,8,128]{2,1,0:T(8,128)S(1)} %get-tuple-element.44, ...), kind=kLoop, calls=%fused_computation.9 | loop fusion | flops 3670016 | bytes 5308416 | tf_op jit(solution)/shard_map/convert_element_type | solution.py:122
  41.9 1.3 %copy.77 = bf16[128,4096]{1,0:T(8,128)(2,1)} copy(bf16[128,4096]{0,1:T(8,128)(2,1)S(1)} %bitcast.207) | data formatting | bytes 2097152
  43.5 1.1 %collective-permute-done.2 = bf16[4,128,128]{2,1,0:T(8,128)(2,1)S(1)} collective-permute-done((bf16[4,128,128]{2,1,0:T(8,128)(2,1)S(1)}, bf16[4,128,128]{2,1,0:T(8,128)(2,1)S(1)}, u32[]{:S(2)}, u32[]{:S(2)}) %collective-permute-start.2) | collective-permute-done | bytes 131104 | tf_op jit(solution)/shard_map/ppermute | solution.py:16
  45.0 0.7 %pad_maximum_fusion.1 = bf16[128,512]{1,0:T(8,128)(2,1)} fusion(bf16[128,128]{1,0:T(8,128)(2,1)S(1)} %get-tuple-element.34, bf16[128,128]{1,0:T(8,128)(2,1)S(1)} %get-tuple-element.35, bf16[128,128]{1,0:T(8,128)(2,1)S(1)} %get-tuple-element.36, bf16[128,128]{1,0:T(8,128)(2,1)S(1)} %get-tuple-element.33), kind=kLoop, calls=%fused_computation.44 | loop fusion | flops 524288 | bytes 262144 | tf_op jit(solution)/shard_map/concatenate | solution.py:131
  (28 shorter events, 4.4 us)
Async XLA Ops:
  0.6 14.3 %copy-start = (bf16[128,4096]{1,0:T(8,128)(2,1)S(1)}, bf16[128,4096]{1,0:T(8,128)(2,1)}, u32[]{:S(2)}) copy-start(bf16[128,4096]{1,0:T(8,128)(2,1)} %param.5) | copy-start | bytes 3145732
  0.6 15.0 %copy-start.1 = (bf16[128,4096]{1,0:T(8,128)(2,1)S(1)}, bf16[128,4096]{1,0:T(8,128)(2,1)}, u32[]{:S(2)}) copy-start(bf16[128,4096]{1,0:T(8,128)(2,1)} %param.8) | copy-start | bytes 3145732
  3.6 14.0 %collective-permute-start.1 = (bf16[2,128,512]{1,2,0:T(8,128)(2,1)}, bf16[2,128,512]{1,2,0:T(8,128)(2,1)}, u32[]{:S(2)}, u32[]{:S(2)}) collective-permute-start(bf16[2,128,512]{1,2,0:T(8,128)(2,1)} %pad_maximum_fusion), channel_id=1, source_target_pairs={{0,2},{2,4},{4,6},{6,8},{8,10},{10,12},{12,14},{14,16},{16,18},{18... | collective-permute-start | bytes 786440 | tf_op jit(solution)/shard_map/ppermute | solution.py:16
  7.6 20.9 %collective-permute-start = (bf16[2,128,512]{1,2,0:T(8,128)(2,1)}, bf16[2,128,512]{1,2,0:T(8,128)(2,1)}, u32[]{:S(2)}, u32[]{:S(2)}) collective-permute-start(bf16[2,128,512]{1,2,0:T(8,128)(2,1)} %pad_maximum_fusion), channel_id=1, source_target_pairs={{0,4},{2,6},{4,8},{6,10},{8,12},{10,14},{12,16},{14,18},{16,20},{1... | collective-permute-start | bytes 786440 | tf_op jit(solution)/shard_map/ppermute | solution.py:16
  34.8 8.7 %collective-permute-start.3 = (bf16[4,128,128]{2,1,0:T(8,128)(2,1)}, bf16[4,128,128]{2,1,0:T(8,128)(2,1)S(1)}, u32[]{:S(2)}, u32[]{:S(2)}) collective-permute-start(bf16[4,128,128]{2,1,0:T(8,128)(2,1)} %fusion.15), channel_id=1, source_target_pairs={{4,0},{6,2},{8,4},{10,6},{12,8},{14,10},{16,12},{18,14},{20,16},{2... | collective-permute-start | bytes 393224 | tf_op jit(solution)/shard_map/ppermute | solution.py:16
  36.7 7.9 %collective-permute-start.2 = (bf16[4,128,128]{2,1,0:T(8,128)(2,1)S(1)}, bf16[4,128,128]{2,1,0:T(8,128)(2,1)S(1)}, u32[]{:S(2)}, u32[]{:S(2)}) collective-permute-start(bf16[4,128,128]{2,1,0:T(8,128)(2,1)S(1)} %fusion.16), channel_id=1, source_target_pairs={{2,0},{4,2},{6,4},{8,6},{10,8},{12,10},{14,12},{16,14},{18,16},{20... | collective-permute-start | bytes 393224 | tf_op jit(solution)/shard_map/ppermute | solution.py:16

commit v11 on v10

--- a/solution.py
+++ b/solution.py
@@ -52,8 +52,8 @@
     score_scale = HD ** (-0.5)
     axes = ("ctx", "uly")
     key_value = jnp.stack([key_vectors, value_vectors])
+    far_rim = shifted(key_value, axes, 2)
     near_rim = shifted(key_value, axes, 1)
-    far_rim = shifted(key_value, axes, 2)
     device_index = lax.axis_index(axes)
     query_heads = queries.reshape(rows, KVH, GROUP, HD)
     grad_heads = output_grad.reshape(rows, KVH, GROUP, HD)
@@ -74,38 +74,44 @@
     )
     own_dot = jnp.sum(own_exp * own_grad_p, axis=-1, keepdims=True)
 
+    near_keys = near_rim[0].reshape(rows, KVH, HD)
+    near_values = near_rim[1].reshape(rows, KVH, HD)
+    near_scores = scores_of(query_heads, near_keys, near_allowed, score_scale)
+    near_max = jnp.max(near_scores, axis=-1, keepdims=True)
+    near_exp = jnp.exp(near_scores - near_max)
+    near_sum = jnp.sum(near_exp, axis=-1, keepdims=True)
+    near_grad_p = jnp.einsum(
+        "tghd,sgd->ghts", grad_heads, near_values, preferred_element_type=jnp.float32
+    )
+    near_dot = jnp.sum(near_exp * near_grad_p, axis=-1, keepdims=True)
+    near_stats, far_rim = lax.optimization_barrier(
+        ((near_max, near_exp, near_sum, near_grad_p, near_dot), far_rim)
+    )
+    near_max, near_exp, near_sum, near_grad_p, near_dot = near_stats
+
     far_keys = far_rim[0].reshape(rows, KVH, HD)
     far_values = far_rim[1].reshape(rows, KVH, HD)
-    near_keys = near_rim[0].reshape(rows, KVH, HD)
-    near_values = near_rim[1].reshape(rows, KVH, HD)
     far_scores = scores_of(query_heads, far_keys, far_allowed, score_scale)
-    near_scores = scores_of(query_heads, near_keys, near_allowed, score_scale)
     row_max = jnp.maximum(
-        own_max,
-        jnp.maximum(
-            jnp.max(far_scores, axis=-1, keepdims=True),
-            jnp.max(near_scores, axis=-1, keepdims=True),
-        ),
+        jnp.maximum(own_max, near_max), jnp.max(far_scores, axis=-1, keepdims=True)
     )
     far_exp = jnp.exp(far_scores - row_max)
-    near_exp = jnp.exp(near_scores - row_max)
     own_rescale = jnp.exp(own_max - row_max)
+    near_rescale = jnp.exp(near_max - row_max)
     row_sum = (
         own_sum * own_rescale
+        + near_sum * near_rescale
         + jnp.sum(far_exp, axis=-1, keepdims=True)
-        + jnp.sum(near_exp, axis=-1, keepdims=True)
     )
     far_grad_p = jnp.einsum(
         "tghd,sgd->ghts", grad_heads, far_values, preferred_element_type=jnp.float32
     )
-    near_grad_p = jnp.einsum(
-        "tghd,sgd->ghts", grad_heads, near_values, preferred_element_type=jnp.float32
-    )
     row_delta = (
         own_dot * own_rescale
+        + near_dot * near_rescale
         + jnp.sum(far_exp * far_grad_p, axis=-1, keepdims=True)
-        + jnp.sum(near_exp * near_grad_p, axis=-1, keepdims=True)
     ) / row_sum
+    near_exp = near_exp * near_rescale
     far_grad_s = ((far_exp / row_sum) * (far_grad_p - row_delta)).astype(jnp.bfloat16)
     near_grad_s = ((near_exp / row_sum) * (near_grad_p - row_delta)).astype(jnp.bfloat16)
     far_key_grad = key_grad_of(far_grad_s, query_heads, score_scale)

time: 46 us -> 48.9 us (1.063)
  starting transfers between devices: 13.2 us -> 17.8 us
  waiting for transfers between devices: 10.3 us -> 8.85 us
    ppermute x4, starting transfers between devices: 13.2 us -> 17.8 us  [shifted(): return lax.ppermute(block, axis, route)]
    ppermute x4, waiting for transfers between devices: 10.3 us -> 8.85 us  [shifted(): return lax.ppermute(block, axis, route)]
    dot_general x1, matrix products: 1.66 us -> 0.96 us  [body(): jnp.einsum('tghd,sgd->ghts', grad_heads, far_values, preferred_element_ty...]
  transfers between devices with their start and end apart: 4 -> 4, of which waited for: 3 -> 4; matrix products, arithmetic and copies ran while one was open for 24% -> 24% of each run, Pallas kernels for 0% -> 0%
where the time goes in v11:
time: 48.9 us; the launch traced here: 48.5 us
  starting transfers between devices  17.8 us (36%)
  local copies, waits for them, and re-layouts  9.16 us (19%)
  waiting for transfers between devices  8.85 us (18%)
  matrix products  7.76 us (16%)
  other arithmetic  4.11 us (8%)
  between operations  0.9 us (2%)
    ppermute x4, starting transfers between devices, shifted(): return lax.ppermute(block, axis, route)  17.8 us
    ppermute x4, waiting for transfers between devices, shifted(): return lax.ppermute(block, axis, route)  8.85 us
    unnamed x8, local copies, waits for them, and re-layouts  3.76 us
    dot_general x3, matrix products, key_grad_of(): jnp.einsum('ghts,tghd->gsd', grad_s, query_heads, preferred_element_type=...  1.97 us
    dot_general x3, matrix products, scores_of(): jnp.einsum('tghd,sgd->ghts', query_heads, key_heads, preferred_element_ty...  1.54 us
    convert_element_type x1, other arithmetic, body(): (near_exp / row_sum * (near_grad_p - row_delta)).astype(jnp.bfloat16)  1.4 us
    dot_general x3, matrix products, query_grad_of(): jnp.einsum('ghts,sgd->ghtd', grad_s, keys, preferred_element_type=jnp.flo...  1.32 us
    reshape x2, local copies, waits for them, and re-layouts, body(): own_keys = key_vectors.reshape(rows, KVH, HD)  1.08 us
  transfers between devices with their start and end apart: 4, of which 4 were waited for; matrix products, arithmetic and copies ran while one was open for 24% of the time, Pallas kernels for 0%

profile of v11, /device:TPU:1, one launch (start us, length us, event | category | flops | bytes accessed | tf_op | source)
XLA Modules:
  0.0 48.5 jit_solution(14294997792199161068)
XLA Ops:
  0.6 1.2 %copy.56 = bf16[128,512]{0,1:T(8,128)(2,1)S(1)} copy(bf16[128,512]{1,0:T(8,128)(2,1)} %param.6) | data formatting | bytes 262144 | tf_op args[1]
  1.8 1.0 %copy.57 = bf16[128,512]{0,1:T(8,128)(2,1)S(1)} copy(bf16[128,512]{1,0:T(8,128)(2,1)} %param.7) | data formatting | bytes 262144 | tf_op args[2]
  2.9 0.7 %pad_maximum_fusion = bf16[2,128,512]{1,2,0:T(8,128)(2,1)} fusion(bf16[1,128,512]{1,2,0:T(8,128)(2,1)S(1)} %bitcast.226, bf16[1,128,512]{1,2,0:T(8,128)(2,1)S(1)} %bitcast.225), kind=kLoop, calls=%fused_computation.38 | loop fusion | flops 131072 | bytes 524288 | tf_op jit(solution)/shard_map/stack | solution.py:54
  3.6 5.0 %collective-permute-start.1 = (bf16[2,128,512]{1,2,0:T(8,128)(2,1)}, bf16[2,128,512]{1,2,0:T(8,128)(2,1)}, u32[]{:S(2)}, u32[]{:S(2)}) collective-permute-start(bf16[2,128,512]{1,2,0:T(8,128)(2,1)} %pad_maximum_fusion), channel_id=1, source_target_pairs={{0,4},{2,6},{4,8},{6,10},{8,12},{10,14},{12,16},{14,18},{16,20},{1... | collective-permute-start | bytes 786440 | tf_op jit(solution)/shard_map/ppermute | solution.py:16
  8.6 3.2 %collective-permute-start = (bf16[2,128,512]{1,2,0:T(8,128)(2,1)}, bf16[2,128,512]{1,2,0:T(8,128)(2,1)}, u32[]{:S(2)}, u32[]{:S(2)}) collective-permute-start(bf16[2,128,512]{1,2,0:T(8,128)(2,1)} %pad_maximum_fusion), channel_id=1, source_target_pairs={{0,2},{2,4},{4,6},{6,8},{8,10},{10,12},{12,14},{14,16},{16,18},{18... | collective-permute-start | bytes 786440 | tf_op jit(solution)/shard_map/ppermute | solution.py:16
  11.9 0.9 %reshape.256 = bf16[128,4,128]{2,1,0:T(4,128)(2,1)S(1)} reshape(bf16[128,512]{1,0:T(8,128)(2,1)} %param.6) | data formatting | bytes 262144 | tf_op jit(solution)/shard_map/reshape | solution.py:60
  12.8 0.9 %reshape.259 = bf16[128,4,128]{2,1,0:T(4,128)(2,1)S(1)} reshape(bf16[128,512]{1,0:T(8,128)(2,1)} %param.7) | data formatting | bytes 262144 | tf_op jit(solution)/shard_map/reshape | solution.py:61
  13.8 0.7 %copy.53 = s32[16,1]{1,0:T(8,128)S(1)} copy(s32[16,1]{0,1:T(1,128)} %bitcast.236) | data formatting | bytes 128 | tf_op jit(solution)/shard_map/reshape.234
  14.9 0.7 %copy.109 = bf16[128,4096]{0,1:T(8,128)(2,1)S(1)} copy(bf16[128,4096]{1,0:T(8,128)(2,1)S(1)} %copy-done) | data formatting | bytes 2097152 | tf_op jit(solution)/shard_map/reshape | solution.py:58
  16.6 1.0 %fusion = (f32[4,8,128]{2,1,0:T(8,128)S(1)}, f32[4,8,128]{2,1,0:T(8,128)S(1)}, f32[4,128,128,8]{2,1,3,0:T(8,128)S(1)}) fusion(f32[4,128,128,8]{2,1,3,0:T(8,128)S(1)} %get-tuple-element.61, f32[4,8,128]{2,1,0:T(8,128)S(1)} %get-tuple-element.60, pred[128,128]{0,1:T(8,128)(4,1)S(1)} %get-tuple-element.53, bf16[128,4,8,128]{3,2,1,0:T(8,128)(2,1)S(1)} %bitcast.212, ...), kind=kOutput, calls=%fused_computation.2 | convolution fusion | flops 137355264 | bytes 5439488 | tf_op jit(solution)/shard_map/tghd,sgd->ghts/dot_general | solution.py:72
  17.6 4.9 %collective-permute-done = bf16[2,128,512]{1,2,0:T(8,128)(2,1)} collective-permute-done((bf16[2,128,512]{1,2,0:T(8,128)(2,1)}, bf16[2,128,512]{1,2,0:T(8,128)(2,1)}, u32[]{:S(2)}, u32[]{:S(2)}) %collective-permute-start) | collective-permute-done | bytes 262176 | tf_op jit(solution)/shard_map/ppermute | solution.py:16
  22.4 1.0 %fusion.30 = (bf16[1,128,512]{1,2,0:T(8,128)(2,1)S(1)}, bf16[1,128,512]{1,2,0:T(8,128)(2,1)S(1)}) fusion(bf16[2,128,512]{1,2,0:T(8,128)(2,1)} %collective-permute-done), kind=kLoop, calls=%fused_computation.74 | loop fusion | bytes 524288 | tf_op jit(solution)/shard_map/slice | solution.py:78
  23.9 1.0 %multiply_reduce_fusion = (f32[4,8,128]{2,1,0:T(8,128)S(1)}, f32[4,8,128]{2,1,0:T(8,128)S(1)}, f32[4,8,128,128]{2,3,1,0:T(8,128)S(1)}, f32[4,8,128,128]{2,3,1,0:T(8,128)S(1)}) fusion(f32[4,8,128]{2,1,0:T(8,128)S(1)} %get-tuple-element.55, f32[4,128,128,8]{2,1,3,0:T(8,128)S(1)} %get-tuple-element.56, pred[128,128]{0,1:T(8,128)(4,1)S(1)} %get-tuple-element.54, ...), kind=kOutput, calls=%fused_computation.16 | convolution fusion | flops 137355264 | bytes 7536640 | tf_op jit(solution)/shard_map/tghd,sgd->ghts/dot_general | solution.py:83
  24.9 2.0 %collective-permute-done.1 = bf16[2,128,512]{1,2,0:T(8,128)(2,1)} collective-permute-done((bf16[2,128,512]{1,2,0:T(8,128)(2,1)}, bf16[2,128,512]{1,2,0:T(8,128)(2,1)}, u32[]{:S(2)}, u32[]{:S(2)}) %collective-permute-start.1) | collective-permute-done | bytes 262176 | tf_op jit(solution)/shard_map/ppermute | solution.py:16
  26.9 1.0 %fusion.29 = (bf16[1,128,512]{1,2,0:T(8,128)(2,1)S(1)}, bf16[1,128,512]{1,2,0:T(8,128)(2,1)S(1)}) fusion(bf16[2,128,512]{1,2,0:T(8,128)(2,1)} %collective-permute-done.1), kind=kLoop, calls=%fused_computation.73 | loop fusion | bytes 524288 | tf_op jit(solution)/shard_map/slice | solution.py:92
  28.5 1.0 %fusion.3 = (f32[4,8,128]{2,1,0:T(8,128)S(1)}, f32[4,8,128]{2,1,0:T(8,128)S(1)}, f32[4,128,128,8]{2,1,3,0:T(8,128)S(1)}) fusion(f32[4,128,128,8]{2,1,3,0:T(8,128)S(1)} %get-tuple-element.59, f32[4,8,128]{2,1,0:T(8,128)S(1)} %fusion.28, pred[128,128]{0,1:T(8,128)(4,1)S(1)} %get-tuple-element.52, bf16[128,4,128,1]{0,2,3,1:T(8,128)(2,1)S(1)} %bitcast.224, ...), kind=kOutput, calls=%fused_computation.7 | convolution fusion | flops 137355264 | bytes 5439488 | tf_op jit(solution)/shard_map/tghd,sgd->ghts/dot_general | solution.py:106
  29.5 1.4 %multiply_convert_fusion.1 = (bf16[4,8,128,128]{2,3,1,0:T(8,128)(2,1)S(1)}, bf16[4,8,128,128]{2,3,1,0:T(8,128)(2,1)S(1)}) fusion(f32[4,8,128,128]{2,3,1,0:T(8,128)S(1)} %get-tuple-element.17, f32[4,8,128,128]{2,3,1,0:T(8,128)S(1)} %get-tuple-element.16, f32[4,8,128]{2,1,0:T(8,128)S(1)} %get-tuple-element.48, f32[4,8,128]{2,1,0:T(8,128)S(1)} %bitcast.231, ...), kind=kLoop, calls=%fused_computation.14 | loop fusion | flops 6291456 | bytes 10567680 | tf_op jit(solution)/shard_map/convert_element_type | solution.py:116
  31.3 1.1 %fusion.12 = bf16[4,128,128]{2,1,0:T(8,128)(2,1)} fusion(bf16[4,8,128,128]{2,3,1,0:T(8,128)(2,1)S(1)} %get-tuple-element.20, bf16[128,4,8,128]{0,3,2,1:T(8,128)(2,1)S(1)} %bitcast.210), kind=kOutput, calls=%fused_computation.29 | convolution fusion | flops 134348800 | bytes 2228224 | tf_op jit(solution)/shard_map/ghts,tghd->gsd/dot_general | solution.py:41
  32.4 7.2 %collective-permute-start.3 = (bf16[4,128,128]{2,1,0:T(8,128)(2,1)}, bf16[4,128,128]{2,1,0:T(8,128)(2,1)S(1)}, u32[]{:S(2)}, u32[]{:S(2)}) collective-permute-start(bf16[4,128,128]{2,1,0:T(8,128)(2,1)} %fusion.12), channel_id=1, source_target_pairs={{4,0},{6,2},{8,4},{10,6},{12,8},{14,10},{16,12},{18,14},{20,16},{2... | collective-permute-start | bytes 393224 | tf_op jit(solution)/shard_map/ppermute | solution.py:16
  39.6 2.4 %collective-permute-start.2 = (bf16[4,128,128]{2,1,0:T(8,128)(2,1)S(1)}, bf16[4,128,128]{2,1,0:T(8,128)(2,1)S(1)}, u32[]{:S(2)}, u32[]{:S(2)}) collective-permute-start(bf16[4,128,128]{2,1,0:T(8,128)(2,1)S(1)} %fusion.13), channel_id=1, source_target_pairs={{2,0},{4,2},{6,4},{8,6},{10,8},{12,10},{14,12},{16,14},{18,16},{20... | collective-permute-start | bytes 393224 | tf_op jit(solution)/shard_map/ppermute | solution.py:16
  42.0 0.8 %fusion.2 = bf16[4,8,128,128]{2,3,1,0:T(8,128)(2,1)S(1)} fusion(f32[4,128,128,8]{2,1,3,0:T(8,128)S(1)} %get-tuple-element.63, f32[4,128,128,8]{2,1,3,0:T(8,128)S(1)} %get-tuple-element.61, f32[4,8,128]{2,1,0:T(8,128)S(1)} %bitcast.232, f32[4,8,128]{2,1,0:T(8,128)S(1)} %bitcast.235, f32[4,8,128]{2,1,0:T(8,128)S(1)} %get-tuple-element.60, ...), kind=kLoop, calls=%fused_computation.4 | loop fusion | flops 3670016 | bytes 5308416 | tf_op jit(solution)/shard_map/convert_element_type | solution.py:128
  44.1 1.3 %copy.77 = bf16[128,4096]{1,0:T(8,128)(2,1)} copy(bf16[128,4096]{0,1:T(8,128)(2,1)S(1)} %bitcast.215) | data formatting | bytes 2097152
  46.1 1.3 %collective-permute-done.2 = bf16[4,128,128]{2,1,0:T(8,128)(2,1)S(1)} collective-permute-done((bf16[4,128,128]{2,1,0:T(8,128)(2,1)S(1)}, bf16[4,128,128]{2,1,0:T(8,128)(2,1)S(1)}, u32[]{:S(2)}, u32[]{:S(2)}) %collective-permute-start.2) | collective-permute-done | bytes 131104 | tf_op jit(solution)/shard_map/ppermute | solution.py:16
  47.9 0.7 %pad_maximum_fusion.1 = bf16[128,512]{1,0:T(8,128)(2,1)} fusion(bf16[128,128]{1,0:T(8,128)(2,1)S(1)} %get-tuple-element.45, bf16[128,128]{1,0:T(8,128)(2,1)S(1)} %get-tuple-element.46, bf16[128,128]{1,0:T(8,128)(2,1)S(1)} %get-tuple-element.47, bf16[128,128]{1,0:T(8,128)(2,1)S(1)} %get-tuple-element.44), kind=kLoop, calls=%fused_computation.40 | loop fusion | flops 524288 | bytes 262144 | tf_op jit(solution)/shard_map/concatenate | solution.py:137
  (28 shorter events, 5.3 us)
Async XLA Ops:
  0.6 14.3 %copy-start = (bf16[128,4096]{1,0:T(8,128)(2,1)S(1)}, bf16[128,4096]{1,0:T(8,128)(2,1)}, u32[]{:S(2)}) copy-start(bf16[128,4096]{1,0:T(8,128)(2,1)} %param.5) | copy-start | bytes 3145732
  0.6 15.0 %copy-start.1 = (bf16[128,4096]{1,0:T(8,128)(2,1)S(1)}, bf16[128,4096]{1,0:T(8,128)(2,1)}, u32[]{:S(2)}) copy-start(bf16[128,4096]{1,0:T(8,128)(2,1)} %param.8) | copy-start | bytes 3145732
  3.6 23.3 %collective-permute-start.1 = (bf16[2,128,512]{1,2,0:T(8,128)(2,1)}, bf16[2,128,512]{1,2,0:T(8,128)(2,1)}, u32[]{:S(2)}, u32[]{:S(2)}) collective-permute-start(bf16[2,128,512]{1,2,0:T(8,128)(2,1)} %pad_maximum_fusion), channel_id=1, source_target_pairs={{0,4},{2,6},{4,8},{6,10},{8,12},{10,14},{12,16},{14,18},{16,20},{1... | collective-permute-start | bytes 786440 | tf_op jit(solution)/shard_map/ppermute | solution.py:16
  8.6 13.8 %collective-permute-start = (bf16[2,128,512]{1,2,0:T(8,128)(2,1)}, bf16[2,128,512]{1,2,0:T(8,128)(2,1)}, u32[]{:S(2)}, u32[]{:S(2)}) collective-permute-start(bf16[2,128,512]{1,2,0:T(8,128)(2,1)} %pad_maximum_fusion), channel_id=1, source_target_pairs={{0,2},{2,4},{4,6},{6,8},{8,10},{10,12},{12,14},{14,16},{16,18},{18... | collective-permute-start | bytes 786440 | tf_op jit(solution)/shard_map/ppermute | solution.py:16
  32.4 13.7 %collective-permute-start.3 = (bf16[4,128,128]{2,1,0:T(8,128)(2,1)}, bf16[4,128,128]{2,1,0:T(8,128)(2,1)S(1)}, u32[]{:S(2)}, u32[]{:S(2)}) collective-permute-start(bf16[4,128,128]{2,1,0:T(8,128)(2,1)} %fusion.12), channel_id=1, source_target_pairs={{4,0},{6,2},{8,4},{10,6},{12,8},{14,10},{16,12},{18,14},{20,16},{2... | collective-permute-start | bytes 393224 | tf_op jit(solution)/shard_map/ppermute | solution.py:16
  39.6 7.8 %collective-permute-start.2 = (bf16[4,128,128]{2,1,0:T(8,128)(2,1)S(1)}, bf16[4,128,128]{2,1,0:T(8,128)(2,1)S(1)}, u32[]{:S(2)}, u32[]{:S(2)}) collective-permute-start(bf16[4,128,128]{2,1,0:T(8,128)(2,1)S(1)} %fusion.13), channel_id=1, source_target_pairs={{2,0},{4,2},{6,4},{8,6},{10,8},{12,10},{14,12},{16,14},{18,16},{20... | collective-permute-start | bytes 393224 | tf_op jit(solution)/shard_map/ppermute | solution.py:16

commit v12 on v10

--- a/solution.py
+++ b/solution.py
@@ -108,11 +108,10 @@
     ) / row_sum
     far_grad_s = ((far_exp / row_sum) * (far_grad_p - row_delta)).astype(jnp.bfloat16)
     near_grad_s = ((near_exp / row_sum) * (near_grad_p - row_delta)).astype(jnp.bfloat16)
-    far_key_grad = key_grad_of(far_grad_s, query_heads, score_scale)
-    near_key_grad = key_grad_of(near_grad_s, query_heads, score_scale)
-    far_key_grad = far_key_grad.astype(jnp.bfloat16)
-    near_key_grad = near_key_grad.astype(jnp.bfloat16)
+    far_key_grad = key_grad_of(far_grad_s, query_heads, score_scale).astype(jnp.bfloat16)
     far_back = shifted(far_key_grad, axes, -2)
+    far_key_grad, near_grad_s = lax.optimization_barrier((far_key_grad, near_grad_s))
+    near_key_grad = key_grad_of(near_grad_s, query_heads, score_scale).astype(jnp.bfloat16)
     near_back = shifted(near_key_grad, axes, -1)
 
     _, own_scale, row_delta, far_grad_s, near_grad_s = lax.optimization_barrier(

time: 46 us -> 45.2 us (0.983); the launches traced: 45.7 us -> 44.4 us
  waiting for transfers between devices: 10.3 us -> 8.98 us
    ppermute x4, waiting for transfers between devices: 10.3 us -> 8.98 us  [shifted(): return lax.ppermute(block, axis, route)]
  transfers between devices with their start and end apart: 4 -> 4, of which waited for: 3 -> 2; matrix products, arithmetic and copies ran while one was open for 24% -> 27% of each run, Pallas kernels for 0% -> 0%
where the time goes in v12:
time: 45.2 us; the launch traced here: 44.4 us
  starting transfers between devices  13.2 us (29%)
  local copies, waits for them, and re-layouts  9.16 us (20%)
  waiting for transfers between devices  8.98 us (20%)
  matrix products  8.01 us (18%)
  other arithmetic  4.18 us (9%)
  between operations  0.91 us (2%)
    ppermute x4, starting transfers between devices, shifted(): return lax.ppermute(block, axis, route)  13.2 us
    ppermute x4, waiting for transfers between devices, shifted(): return lax.ppermute(block, axis, route)  8.98 us
    unnamed x8, local copies, waits for them, and re-layouts  3.76 us
    dot_general x3, matrix products, key_grad_of(): jnp.einsum('ghts,tghd->gsd', grad_s, query_heads, preferred_element_type=...  1.97 us
    dot_general x1, matrix products, body(): jnp.einsum('tghd,sgd->ghts', grad_heads, far_values, preferred_element_ty...  1.66 us
    dot_general x3, matrix products, scores_of(): jnp.einsum('tghd,sgd->ghts', query_heads, key_heads, preferred_element_ty...  1.52 us
    convert_element_type x1, other arithmetic, body(): (near_exp / row_sum * (near_grad_p - row_delta)).astype(jnp.bfloat16)  1.46 us
    dot_general x3, matrix products, query_grad_of(): jnp.einsum('ghts,sgd->ghtd', grad_s, keys, preferred_element_type=jnp.flo...  1.3 us
  transfers between devices with their start and end apart: 4, of which 2 were waited for; matrix products, arithmetic and copies ran while one was open for 27% of the time, Pallas kernels for 0%

profile of v12, /device:TPU:1, one launch (start us, length us, event | category | flops | bytes accessed | tf_op | source)
XLA Modules:
  0.0 44.4 jit_solution(987570589382508981)
XLA Ops:
  0.6 1.2 %copy.56 = bf16[128,512]{0,1:T(8,128)(2,1)S(1)} copy(bf16[128,512]{1,0:T(8,128)(2,1)} %param.6) | data formatting | bytes 262144 | tf_op args[1]
  1.8 1.0 %copy.57 = bf16[128,512]{0,1:T(8,128)(2,1)S(1)} copy(bf16[128,512]{1,0:T(8,128)(2,1)} %param.7) | data formatting | bytes 262144 | tf_op args[2]
  2.9 0.7 %pad_maximum_fusion = bf16[2,128,512]{1,2,0:T(8,128)(2,1)} fusion(bf16[1,128,512]{1,2,0:T(8,128)(2,1)S(1)} %bitcast.218, bf16[1,128,512]{1,2,0:T(8,128)(2,1)S(1)} %bitcast.217), kind=kLoop, calls=%fused_computation.42 | loop fusion | flops 131072 | bytes 524288 | tf_op jit(solution)/shard_map/stack | solution.py:54
  3.6 4.0 %collective-permute-start.1 = (bf16[2,128,512]{1,2,0:T(8,128)(2,1)}, bf16[2,128,512]{1,2,0:T(8,128)(2,1)}, u32[]{:S(2)}, u32[]{:S(2)}) collective-permute-start(bf16[2,128,512]{1,2,0:T(8,128)(2,1)} %pad_maximum_fusion), channel_id=1, source_target_pairs={{0,2},{2,4},{4,6},{6,8},{8,10},{10,12},{12,14},{14,16},{16,18},{18... | collective-permute-start | bytes 786440 | tf_op jit(solution)/shard_map/ppermute | solution.py:16
  7.6 4.2 %collective-permute-start = (bf16[2,128,512]{1,2,0:T(8,128)(2,1)}, bf16[2,128,512]{1,2,0:T(8,128)(2,1)}, u32[]{:S(2)}, u32[]{:S(2)}) collective-permute-start(bf16[2,128,512]{1,2,0:T(8,128)(2,1)} %pad_maximum_fusion), channel_id=1, source_target_pairs={{0,4},{2,6},{4,8},{6,10},{8,12},{10,14},{12,16},{14,18},{16,20},{1... | collective-permute-start | bytes 786440 | tf_op jit(solution)/shard_map/ppermute | solution.py:16
  11.9 0.9 %reshape.382 = bf16[128,4,128]{2,1,0:T(4,128)(2,1)S(1)} reshape(bf16[128,512]{1,0:T(8,128)(2,1)} %param.6) | data formatting | bytes 262144 | tf_op jit(solution)/shard_map/reshape | solution.py:60
  12.8 0.9 %reshape.385 = bf16[128,4,128]{2,1,0:T(4,128)(2,1)S(1)} reshape(bf16[128,512]{1,0:T(8,128)(2,1)} %param.7) | data formatting | bytes 262144 | tf_op jit(solution)/shard_map/reshape | solution.py:61
  13.8 0.7 %copy.53 = s32[16,1]{1,0:T(8,128)S(1)} copy(s32[16,1]{0,1:T(1,128)} %bitcast.221) | data formatting | bytes 128 | tf_op jit(solution)/shard_map/reshape.359
  14.9 0.7 %copy.109 = bf16[128,4096]{0,1:T(8,128)(2,1)S(1)} copy(bf16[128,4096]{1,0:T(8,128)(2,1)S(1)} %copy-done) | data formatting | bytes 2097152 | tf_op jit(solution)/shard_map/reshape | solution.py:58
  16.0 0.5 %fusion.9 = (f32[4,8,128]{2,1,0:T(8,128)S(1)}, f32[4,128,128,8]{2,1,3,0:T(8,128)S(1)}) fusion(pred[128,128]{0,1:T(8,128)(4,1)S(1)} %get-tuple-element.44, bf16[128,4,128,1]{0,2,3,1:T(8,128)(2,1)S(1)} %copy.87, bf16[128,4,8,128]{0,3,2,1:T(8,128)(2,1)S(1)} %bitcast.198), kind=kOutput, calls=%fused_computation.22 | convolution fusion | flops 135786496 | bytes 3309568 | tf_op jit(solution)/shard_map/tghd,sgd->ghts/dot_general | solution.py:33
  16.6 1.0 %fusion.3 = (f32[4,8,128]{2,1,0:T(8,128)S(1)}, f32[4,8,128]{2,1,0:T(8,128)S(1)}, f32[4,128,128,8]{2,1,3,0:T(8,128)S(1)}) fusion(f32[4,128,128,8]{2,1,3,0:T(8,128)S(1)} %get-tuple-element.47, f32[4,8,128]{2,1,0:T(8,128)S(1)} %get-tuple-element.46, pred[128,128]{0,1:T(8,128)(4,1)S(1)} %get-tuple-element.44, bf16[128,4,8,128]{3,2,1,0:T(8,128)(2,1)S(1)} %bitcast.204, ...), kind=kOutput, calls=%fused_computation.7 | convolution fusion | flops 137355264 | bytes 5439488 | tf_op jit(solution)/shard_map/tghd,sgd->ghts/dot_general | solution.py:72
  17.6 1.0 %fusion.30 = (bf16[1,128,512]{1,2,0:T(8,128)(2,1)S(1)}, bf16[1,128,512]{1,2,0:T(8,128)(2,1)S(1)}) fusion(bf16[2,128,512]{1,2,0:T(8,128)(2,1)} %collective-permute-done.1), kind=kLoop, calls=%fused_computation.76 | loop fusion | bytes 524288 | tf_op jit(solution)/shard_map/slice | solution.py:80
  19.1 0.5 %fusion.20 = f32[4,128,128,8]{2,1,3,0:T(8,128)S(1)} fusion(bf16[128,4,128,1]{0,2,3,1:T(8,128)(2,1)S(1)} %bitcast.216, bf16[128,4,8,128]{3,2,1,0:T(8,128)(2,1)S(1)} %bitcast.205), kind=kOutput, calls=%fused_computation.36 | convolution fusion | flops 134217728 | bytes 3276800 | tf_op jit(solution)/shard_map/tghd,sgd->ghts/dot_general | solution.py:101
  19.6 8.9 %collective-permute-done = bf16[2,128,512]{1,2,0:T(8,128)(2,1)} collective-permute-done((bf16[2,128,512]{1,2,0:T(8,128)(2,1)}, bf16[2,128,512]{1,2,0:T(8,128)(2,1)}, u32[]{:S(2)}, u32[]{:S(2)}) %collective-permute-start) | collective-permute-done | bytes 262176 | tf_op jit(solution)/shard_map/ppermute | solution.py:16
  28.5 1.0 %fusion.31 = (bf16[1,128,512]{1,2,0:T(8,128)(2,1)S(1)}, bf16[1,128,512]{1,2,0:T(8,128)(2,1)S(1)}) fusion(bf16[2,128,512]{1,2,0:T(8,128)(2,1)} %collective-permute-done), kind=kLoop, calls=%fused_computation.77 | loop fusion | bytes 524288 | tf_op jit(solution)/shard_map/slice | solution.py:77
  29.5 0.5 %fusion.10 = (f32[4,8,128]{2,1,0:T(8,128)S(1)}, f32[4,128,128,8]{2,1,3,0:T(8,128)S(1)}) fusion(pred[128,128]{0,1:T(8,128)(4,1)S(1)} %get-tuple-element.45, bf16[128,4,128,1]{0,2,3,1:T(8,128)(2,1)S(1)} %bitcast.210, bf16[128,4,8,128]{0,3,2,1:T(8,128)(2,1)S(1)} %bitcast.200), kind=kOutput, calls=%fused_computation.23 | convolution fusion | flops 135786496 | bytes 3309568 | tf_op jit(solution)/shard_map/tghd,sgd->ghts/dot_general | solution.py:33
  30.1 1.7 %fusion.6 = (f32[4,8,128]{2,1,0:T(8,128)S(1)}, f32[4,8,128]{2,1,0:T(8,128)S(1)}, f32[4,8,128]{2,1,0:T(8,128)S(1)}, f32[4,8,128]{2,1,0:T(8,128)S(1)}, f32[4,128,128,8]{2,1,3,0:T(8,128)S(1)}) fusion(f32[4,128,128,8]{2,1,3,0:T(8,128)S(1)} %get-tuple-element.49, f32[4,8,128]{2,1,0:T(8,128)S(1)} %maximum_maximum_fusion, ...), kind=kOutput, calls=%fused_computation.12 | convolution fusion | flops 140492800 | bytes 9682944 | tf_op jit(solution)/shard_map/tghd,sgd->ghts/dot_general | solution.py:98
  31.8 1.5 %fusion.2 = (bf16[4,8,128,128]{2,3,1,0:T(8,128)(2,1)S(1)}, bf16[4,8,128,128]{2,3,1,0:T(8,128)(2,1)S(1)}) fusion(f32[4,128,128,8]{2,1,3,0:T(8,128)S(1)} %fusion.20, f32[4,128,128,8]{2,1,3,0:T(8,128)S(1)} %get-tuple-element.51, f32[4,8,128]{2,1,0:T(8,128)S(1)} %get-tuple-element.29, f32[4,8,128]{2,1,0:T(8,128)S(1)} %get-tuple-element.30, ...), kind=kLoop, calls=%fused_computation.4 | loop fusion | flops 7340032 | bytes 10567680 | tf_op jit(solution)/shard_map/convert_element_type | solution.py:110
  33.7 1.9 %collective-permute-start.3 = (bf16[4,128,128]{2,1,0:T(8,128)(2,1)S(1)}, bf16[4,128,128]{2,1,0:T(8,128)(2,1)S(1)}, u32[]{:S(2)}, u32[]{:S(2)}) collective-permute-start(bf16[4,128,128]{2,1,0:T(8,128)(2,1)S(1)} %fusion.15), channel_id=1, source_target_pairs={{4,0},{6,2},{8,4},{10,6},{12,8},{14,10},{16,12},{18,14},{20,16},{2... | collective-permute-start | bytes 393224 | tf_op jit(solution)/shard_map/ppermute | solution.py:16
  35.6 1.1 %fusion.16 = bf16[4,128,128]{2,1,0:T(8,128)(2,1)} fusion(bf16[4,8,128,128]{2,3,1,0:T(8,128)(2,1)S(1)} %get-tuple-element.11, bf16[128,4,8,128]{0,3,2,1:T(8,128)(2,1)S(1)} %bitcast.202), kind=kOutput, calls=%fused_computation.32 | convolution fusion | flops 134348800 | bytes 2228224 | tf_op jit(solution)/shard_map/ghts,tghd->gsd/dot_general | solution.py:41
  36.7 3.0 %collective-permute-start.2 = (bf16[4,128,128]{2,1,0:T(8,128)(2,1)}, bf16[4,128,128]{2,1,0:T(8,128)(2,1)S(1)}, u32[]{:S(2)}, u32[]{:S(2)}) collective-permute-start(bf16[4,128,128]{2,1,0:T(8,128)(2,1)} %fusion.16), channel_id=1, source_target_pairs={{2,0},{4,2},{6,4},{8,6},{10,8},{12,10},{14,12},{16,14},{18,16},{20... | collective-permute-start | bytes 393224 | tf_op jit(solution)/shard_map/ppermute | solution.py:16
  39.7 0.8 %fusion.5 = bf16[4,8,128,128]{2,3,1,0:T(8,128)(2,1)S(1)} fusion(f32[4,128,128,8]{2,1,3,0:T(8,128)S(1)} %get-tuple-element.53, f32[4,128,128,8]{2,1,3,0:T(8,128)S(1)} %get-tuple-element.47, f32[4,8,128]{2,1,0:T(8,128)S(1)} %bitcast.219, f32[4,8,128]{2,1,0:T(8,128)S(1)} %bitcast.220, f32[4,8,128]{2,1,0:T(8,128)S(1)} %get-tuple-element.46, ...), kind=kLoop, calls=%fused_computation.9 | loop fusion | flops 3670016 | bytes 5308416 | tf_op jit(solution)/shard_map/convert_element_type | solution.py:121
  41.9 1.3 %copy.77 = bf16[128,4096]{1,0:T(8,128)(2,1)} copy(bf16[128,4096]{0,1:T(8,128)(2,1)S(1)} %bitcast.207) | data formatting | bytes 2097152
  43.7 0.7 %pad_maximum_fusion.1 = bf16[128,512]{1,0:T(8,128)(2,1)} fusion(bf16[128,128]{1,0:T(8,128)(2,1)S(1)} %get-tuple-element.36, bf16[128,128]{1,0:T(8,128)(2,1)S(1)} %get-tuple-element.37, bf16[128,128]{1,0:T(8,128)(2,1)S(1)} %get-tuple-element.38, bf16[128,128]{1,0:T(8,128)(2,1)S(1)} %get-tuple-element.35), kind=kLoop, calls=%fused_computation.44 | loop fusion | flops 524288 | bytes 262144 | tf_op jit(solution)/shard_map/concatenate | solution.py:130
  (28 shorter events, 3.6 us)
Async XLA Ops:
  0.6 14.3 %copy-start = (bf16[128,4096]{1,0:T(8,128)(2,1)S(1)}, bf16[128,4096]{1,0:T(8,128)(2,1)}, u32[]{:S(2)}) copy-start(bf16[128,4096]{1,0:T(8,128)(2,1)} %param.5) | copy-start | bytes 3145732
  0.6 15.0 %copy-start.1 = (bf16[128,4096]{1,0:T(8,128)(2,1)S(1)}, bf16[128,4096]{1,0:T(8,128)(2,1)}, u32[]{:S(2)}) copy-start(bf16[128,4096]{1,0:T(8,128)(2,1)} %param.8) | copy-start | bytes 3145732
  3.6 14.0 %collective-permute-start.1 = (bf16[2,128,512]{1,2,0:T(8,128)(2,1)}, bf16[2,128,512]{1,2,0:T(8,128)(2,1)}, u32[]{:S(2)}, u32[]{:S(2)}) collective-permute-start(bf16[2,128,512]{1,2,0:T(8,128)(2,1)} %pad_maximum_fusion), channel_id=1, source_target_pairs={{0,2},{2,4},{4,6},{6,8},{8,10},{10,12},{12,14},{14,16},{16,18},{18... | collective-permute-start | bytes 786440 | tf_op jit(solution)/shard_map/ppermute | solution.py:16
  7.6 20.9 %collective-permute-start = (bf16[2,128,512]{1,2,0:T(8,128)(2,1)}, bf16[2,128,512]{1,2,0:T(8,128)(2,1)}, u32[]{:S(2)}, u32[]{:S(2)}) collective-permute-start(bf16[2,128,512]{1,2,0:T(8,128)(2,1)} %pad_maximum_fusion), channel_id=1, source_target_pairs={{0,4},{2,6},{4,8},{6,10},{8,12},{10,14},{12,16},{14,18},{16,20},{1... | collective-permute-start | bytes 786440 | tf_op jit(solution)/shard_map/ppermute | solution.py:16
  33.7 9.6 %collective-permute-start.3 = (bf16[4,128,128]{2,1,0:T(8,128)(2,1)S(1)}, bf16[4,128,128]{2,1,0:T(8,128)(2,1)S(1)}, u32[]{:S(2)}, u32[]{:S(2)}) collective-permute-start(bf16[4,128,128]{2,1,0:T(8,128)(2,1)S(1)} %fusion.15), channel_id=1, source_target_pairs={{4,0},{6,2},{8,4},{10,6},{12,8},{14,10},{16,12},{18,14},{20,16},{2... | collective-permute-start | bytes 393224 | tf_op jit(solution)/shard_map/ppermute | solution.py:16
  36.7 6.5 %collective-permute-start.2 = (bf16[4,128,128]{2,1,0:T(8,128)(2,1)}, bf16[4,128,128]{2,1,0:T(8,128)(2,1)S(1)}, u32[]{:S(2)}, u32[]{:S(2)}) collective-permute-start(bf16[4,128,128]{2,1,0:T(8,128)(2,1)} %fusion.16), channel_id=1, source_target_pairs={{2,0},{4,2},{6,4},{8,6},{10,8},{12,10},{14,12},{16,14},{18,16},{20... | collective-permute-start | bytes 393224 | tf_op jit(solution)/shard_map/ppermute | solution.py:16

commit v13 on v12

--- a/solution.py
+++ b/solution.py
@@ -107,10 +107,12 @@
         + jnp.sum(near_exp * near_grad_p, axis=-1, keepdims=True)
     ) / row_sum
     far_grad_s = ((far_exp / row_sum) * (far_grad_p - row_delta)).astype(jnp.bfloat16)
-    near_grad_s = ((near_exp / row_sum) * (near_grad_p - row_delta)).astype(jnp.bfloat16)
     far_key_grad = key_grad_of(far_grad_s, query_heads, score_scale).astype(jnp.bfloat16)
     far_back = shifted(far_key_grad, axes, -2)
-    far_key_grad, near_grad_s = lax.optimization_barrier((far_key_grad, near_grad_s))
+    far_key_grad, near_exp, near_grad_p, near_delta, near_sum = lax.optimization_barrier(
+        (far_key_grad, near_exp, near_grad_p, row_delta, row_sum)
+    )
+    near_grad_s = ((near_exp / near_sum) * (near_grad_p - near_delta)).astype(jnp.bfloat16)
     near_key_grad = key_grad_of(near_grad_s, query_heads, score_scale).astype(jnp.bfloat16)
     near_back = shifted(near_key_grad, axes, -1)
 

time: 45.2 us -> 47.9 us (1.060)
  starting transfers between devices: 13.2 us -> 16.8 us
  waiting for transfers between devices: 8.98 us -> 7.47 us
    ppermute x4, starting transfers between devices: 13.2 us -> 16.8 us  [shifted(): return lax.ppermute(block, axis, route)]
    ppermute x4, waiting for transfers between devices: 8.98 us -> 7.47 us  [shifted(): return lax.ppermute(block, axis, route)]
    select_n x2, other arithmetic: 0.01 us -> 0.53 us  [doc_index(): return jnp.where(positions < 0, -1, counted)]
    unnamed x8 -> x14, local copies, waits for them, and re-layouts: 3.76 us -> 4.03 us
    convert_element_type x1 -> x2, other arithmetic: 1.46 us -> 1.38 us  [the longest x1 0.82 us: body(): (far_exp / row_sum * (far_grad_p - row_delta)).astype(jnp.bfloat16)]
  transfers between devices with their start and end apart: 4 -> 4, of which waited for: 2 -> 3; matrix products, arithmetic and copies ran while one was open for 27% -> 27% of each run, Pallas kernels for 0% -> 0%
where the time goes in v13:
time: 47.9 us; the launch traced here: 47.1 us
  starting transfers between devices  16.8 us (35%)
  local copies, waits for them, and re-layouts  9.42 us (20%)
  matrix products  7.93 us (17%)
  waiting for transfers between devices  7.47 us (16%)
  other arithmetic  4.57 us (10%)
  between operations  0.94 us (2%)
    ppermute x4, starting transfers between devices, shifted(): return lax.ppermute(block, axis, route)  16.8 us
    ppermute x4, waiting for transfers between devices, shifted(): return lax.ppermute(block, axis, route)  7.47 us
    unnamed x14, local copies, waits for them, and re-layouts  4.03 us
    dot_general x3, matrix products, key_grad_of(): jnp.einsum('ghts,tghd->gsd', grad_s, query_heads, preferred_element_type=...  1.97 us
    dot_general x1, matrix products, body(): jnp.einsum('tghd,sgd->ghts', grad_heads, far_values, preferred_element_ty...  1.61 us
    dot_general x3, matrix products, scores_of(): jnp.einsum('tghd,sgd->ghts', query_heads, key_heads, preferred_element_ty...  1.54 us
    dot_general x3, matrix products, query_grad_of(): jnp.einsum('ghts,sgd->ghtd', grad_s, keys, preferred_element_type=jnp.flo...  1.3 us
    reshape x2, local copies, waits for them, and re-layouts, body(): own_keys = key_vectors.reshape(rows, KVH, HD)  1.08 us
  transfers between devices with their start and end apart: 4, of which 3 were waited for; matrix products, arithmetic and copies ran while one was open for 27% of the time, Pallas kernels for 0%

profile of v13, /device:TPU:1, one launch (start us, length us, event | category | flops | bytes accessed | tf_op | source)
XLA Modules:
  0.0 47.1 jit_solution(12968720621999944961)
XLA Ops:
  0.6 1.2 %copy.56 = bf16[128,512]{0,1:T(8,128)(2,1)S(1)} copy(bf16[128,512]{1,0:T(8,128)(2,1)} %param.6) | data formatting | bytes 262144 | tf_op args[1]
  1.8 1.0 %copy.57 = bf16[128,512]{0,1:T(8,128)(2,1)S(1)} copy(bf16[128,512]{1,0:T(8,128)(2,1)} %param.7) | data formatting | bytes 262144 | tf_op args[2]
  2.9 0.7 %pad_maximum_fusion = bf16[2,128,512]{1,2,0:T(8,128)(2,1)} fusion(bf16[1,128,512]{1,2,0:T(8,128)(2,1)S(1)} %bitcast.193, bf16[1,128,512]{1,2,0:T(8,128)(2,1)S(1)} %bitcast.192), kind=kLoop, calls=%fused_computation.38 | loop fusion | flops 131072 | bytes 524288 | tf_op jit(solution)/shard_map/stack | solution.py:54
  3.6 5.0 %collective-permute-start = (bf16[2,128,512]{1,2,0:T(8,128)(2,1)}, bf16[2,128,512]{1,2,0:T(8,128)(2,1)}, u32[]{:S(2)}, u32[]{:S(2)}) collective-permute-start(bf16[2,128,512]{1,2,0:T(8,128)(2,1)} %pad_maximum_fusion), channel_id=1, source_target_pairs={{0,4},{2,6},{4,8},{6,10},{8,12},{10,14},{12,16},{14,18},{16,20},{1... | collective-permute-start | bytes 786440 | tf_op jit(solution)/shard_map/ppermute | solution.py:16
  8.6 3.2 %collective-permute-start.1 = (bf16[2,128,512]{1,2,0:T(8,128)(2,1)}, bf16[2,128,512]{1,2,0:T(8,128)(2,1)}, u32[]{:S(2)}, u32[]{:S(2)}) collective-permute-start(bf16[2,128,512]{1,2,0:T(8,128)(2,1)} %pad_maximum_fusion), channel_id=1, source_target_pairs={{0,2},{2,4},{4,6},{6,8},{8,10},{10,12},{12,14},{14,16},{16,18},{18... | collective-permute-start | bytes 786440 | tf_op jit(solution)/shard_map/ppermute | solution.py:16
  11.9 0.9 %reshape.394 = bf16[128,4,128]{2,1,0:T(4,128)(2,1)S(1)} reshape(bf16[128,512]{1,0:T(8,128)(2,1)} %param.6) | data formatting | bytes 262144 | tf_op jit(solution)/shard_map/reshape | solution.py:60
  12.8 0.9 %reshape.397 = bf16[128,4,128]{2,1,0:T(4,128)(2,1)S(1)} reshape(bf16[128,512]{1,0:T(8,128)(2,1)} %param.7) | data formatting | bytes 262144 | tf_op jit(solution)/shard_map/reshape | solution.py:61
  13.8 0.7 %copy.53 = s32[16,1]{1,0:T(8,128)S(1)} copy(s32[16,1]{0,1:T(1,128)} %bitcast.198) | data formatting | bytes 128 | tf_op jit(solution)/shard_map/reshape.371
  14.8 0.5 %compare_select_fusion.2 = s32[128]{0:T(128)} fusion(s32[128]{0:T(128)S(1)} %get-tuple-element.32, s32[]{:T(128)S(6)} %mul.104), kind=kLoop, calls=%fused_computation.67 | loop fusion | flops 384 | bytes 1028 | tf_op jit(solution)/shard_map/jit(_where)/select_n | solution.py:22
  15.3 0.7 %copy.109 = bf16[128,4096]{0,1:T(8,128)(2,1)S(1)} copy(bf16[128,4096]{1,0:T(8,128)(2,1)S(1)} %copy-done) | data formatting | bytes 2097152 | tf_op jit(solution)/shard_map/reshape | solution.py:58
  17.4 1.0 %fusion = (f32[4,8,128]{2,1,0:T(8,128)S(1)}, f32[4,8,128]{2,1,0:T(8,128)S(1)}, f32[4,128,128,8]{2,1,3,0:T(8,128)S(1)}) fusion(f32[4,128,128,8]{2,1,3,0:T(8,128)S(1)} %get-tuple-element.54, f32[4,8,128]{2,1,0:T(8,128)S(1)} %get-tuple-element.53, pred[128,128]{0,1:T(8,128)(4,1)S(1)} %get-tuple-element.51, bf16[128,4,8,128]{3,2,1,0:T(8,128)(2,1)S(1)} %bitcast.179, ...), kind=kOutput, calls=%fused_computation.2 | convolution fusion | flops 137355264 | bytes 5439488 | tf_op jit(solution)/shard_map/tghd,sgd->ghts/dot_general | solution.py:72
  18.4 4.1 %collective-permute-done.1 = bf16[2,128,512]{1,2,0:T(8,128)(2,1)} collective-permute-done((bf16[2,128,512]{1,2,0:T(8,128)(2,1)}, bf16[2,128,512]{1,2,0:T(8,128)(2,1)}, u32[]{:S(2)}, u32[]{:S(2)}) %collective-permute-start.1) | collective-permute-done | bytes 262176 | tf_op jit(solution)/shard_map/ppermute | solution.py:16
  22.4 1.0 %fusion.26 = (bf16[1,128,512]{1,2,0:T(8,128)(2,1)S(1)}, bf16[1,128,512]{1,2,0:T(8,128)(2,1)S(1)}) fusion(bf16[2,128,512]{1,2,0:T(8,128)(2,1)} %collective-permute-done.1), kind=kLoop, calls=%fused_computation.72 | loop fusion | bytes 524288 | tf_op jit(solution)/shard_map/slice | solution.py:79
  23.9 3.0 %collective-permute-done = bf16[2,128,512]{1,2,0:T(8,128)(2,1)} collective-permute-done((bf16[2,128,512]{1,2,0:T(8,128)(2,1)}, bf16[2,128,512]{1,2,0:T(8,128)(2,1)}, u32[]{:S(2)}, u32[]{:S(2)}) %collective-permute-start) | collective-permute-done | bytes 262176 | tf_op jit(solution)/shard_map/ppermute | solution.py:16
  26.9 1.0 %fusion.27 = (bf16[1,128,512]{1,2,0:T(8,128)(2,1)S(1)}, bf16[1,128,512]{1,2,0:T(8,128)(2,1)S(1)}) fusion(bf16[2,128,512]{1,2,0:T(8,128)(2,1)} %collective-permute-done), kind=kLoop, calls=%fused_computation.73 | loop fusion | bytes 524288 | tf_op jit(solution)/shard_map/slice | solution.py:77
  29.0 1.6 %fusion.3 = (f32[4,8,128]{2,1,0:T(8,128)S(1)}, f32[4,8,128]{2,1,0:T(8,128)S(1)}, f32[4,8,128]{2,1,0:T(8,128)S(1)}, f32[4,8,128]{2,1,0:T(8,128)S(1)}, f32[4,8,128...) fusion(f32[4,128,128,8]{2,1,3,0:T(8,128)S(1)} %get-tuple-element.56, f32[4,8,128]{2,1,0:T(8,128)S(1)} %maximum_maximum_fusion, ...), kind=kOutput, calls=%fused_computation.7 | convolution fusion | flops 140492800 | bytes 11780096 | tf_op jit(solution)/shard_map/tghd,sgd->ghts/dot_general | solution.py:98
  30.7 0.8 %fusion.5 = bf16[4,8,128,128]{2,3,1,0:T(8,128)(2,1)S(1)} fusion(f32[4,128,128,8]{2,1,3,0:T(8,128)S(1)} %get-tuple-element.59, f32[4,128,128,8]{2,1,3,0:T(8,128)S(1)} %get-tuple-element.56, f32[4,8,128]{2,1,0:T(8,128)S(1)} %get-tuple-element.36, f32[4,8,128]{2,1,0:T(8,128)S(1)} %get-tuple-element.37, f32[4,8,128]{2,1,0:T(8,128)S(1)} %maximum_maximum_fusion, ...), kind=kLoop, calls=%fused_computation.9 | loop fusion | flops 3670016 | bytes 5308416 | tf_op jit(solution)/shard_map/convert_element_type | solution.py:109
  31.9 6.2 %collective-permute-start.3 = (bf16[4,128,128]{2,1,0:T(8,128)(2,1)S(1)}, bf16[4,128,128]{2,1,0:T(8,128)(2,1)S(1)}, u32[]{:S(2)}, u32[]{:S(2)}) collective-permute-start(bf16[4,128,128]{2,1,0:T(8,128)(2,1)S(1)} %fusion.12), channel_id=1, source_target_pairs={{4,0},{6,2},{8,4},{10,6},{12,8},{14,10},{16,12},{18,14},{20,16},{2... | collective-permute-start | bytes 393224 | tf_op jit(solution)/shard_map/ppermute | solution.py:16
  38.2 0.6 %multiply_convert_fusion.1 = bf16[4,8,128,128]{2,3,1,0:T(8,128)(2,1)S(1)} fusion(f32[4,8,128,128]{2,3,1,0:T(8,128)S(1)} %convolution_bitcast_fusion, f32[4,8,128,128]{2,3,1,0:T(8,128)S(1)} %get-tuple-element.10, f32[4,8,128]{2,1,0:T(8,128)S(1)} %bitcast.195, f32[4,8,128]{2,1,0:T(8,128)S(1)} %bitcast.194), kind=kLoop, calls=%fused_computation.14 | loop fusion | flops 2097152 | bytes 5275648 | tf_op jit(solution)/shard_map/convert_element_type | solution.py:115
  38.7 1.1 %fusion.13 = bf16[4,128,128]{2,1,0:T(8,128)(2,1)} fusion(bf16[4,8,128,128]{2,3,1,0:T(8,128)(2,1)S(1)} %multiply_convert_fusion.1, bf16[128,4,8,128]{0,3,2,1:T(8,128)(2,1)S(1)} %bitcast.177), kind=kOutput, calls=%fused_computation.30 | convolution fusion | flops 134348800 | bytes 2228224 | tf_op jit(solution)/shard_map/ghts,tghd->gsd/dot_general | solution.py:41
  39.8 2.3 %collective-permute-start.2 = (bf16[4,128,128]{2,1,0:T(8,128)(2,1)}, bf16[4,128,128]{2,1,0:T(8,128)(2,1)S(1)}, u32[]{:S(2)}, u32[]{:S(2)}) collective-permute-start(bf16[4,128,128]{2,1,0:T(8,128)(2,1)} %fusion.13), channel_id=1, source_target_pairs={{2,0},{4,2},{6,4},{8,6},{10,8},{12,10},{14,12},{16,14},{18,16},{20... | collective-permute-start | bytes 393224 | tf_op jit(solution)/shard_map/ppermute | solution.py:16
  42.6 0.8 %fusion.2 = bf16[4,8,128,128]{2,3,1,0:T(8,128)(2,1)S(1)} fusion(f32[4,128,128,8]{2,1,3,0:T(8,128)S(1)} %get-tuple-element.60, f32[4,128,128,8]{2,1,3,0:T(8,128)S(1)} %get-tuple-element.54, f32[4,8,128]{2,1,0:T(8,128)S(1)} %bitcast.196, f32[4,8,128]{2,1,0:T(8,128)S(1)} %bitcast.197, f32[4,8,128]{2,1,0:T(8,128)S(1)} %get-tuple-element.53, ...), kind=kLoop, calls=%fused_computation.4 | loop fusion | flops 3670016 | bytes 5308416 | tf_op jit(solution)/shard_map/convert_element_type | solution.py:123
  44.3 1.3 %copy.77 = bf16[128,4096]{1,0:T(8,128)(2,1)} copy(bf16[128,4096]{0,1:T(8,128)(2,1)S(1)} %bitcast.182) | data formatting | bytes 2097152
  46.5 0.7 %pad_maximum_fusion.1 = bf16[128,512]{1,0:T(8,128)(2,1)} fusion(bf16[128,128]{1,0:T(8,128)(2,1)S(1)} %get-tuple-element.44, bf16[128,128]{1,0:T(8,128)(2,1)S(1)} %get-tuple-element.45, bf16[128,128]{1,0:T(8,128)(2,1)S(1)} %get-tuple-element.46, bf16[128,128]{1,0:T(8,128)(2,1)S(1)} %get-tuple-element.43), kind=kLoop, calls=%fused_computation.40 | loop fusion | flops 524288 | bytes 262144 | tf_op jit(solution)/shard_map/concatenate | solution.py:132
  (36 shorter events, 5.8 us)
Async XLA Ops:
  0.6 14.7 %copy-start = (bf16[128,4096]{1,0:T(8,128)(2,1)S(1)}, bf16[128,4096]{1,0:T(8,128)(2,1)}, u32[]{:S(2)}) copy-start(bf16[128,4096]{1,0:T(8,128)(2,1)} %param.5) | copy-start | bytes 3145732
  0.6 15.5 %copy-start.1 = (bf16[128,4096]{1,0:T(8,128)(2,1)S(1)}, bf16[128,4096]{1,0:T(8,128)(2,1)}, u32[]{:S(2)}) copy-start(bf16[128,4096]{1,0:T(8,128)(2,1)} %param.8) | copy-start | bytes 3145732
  3.6 23.3 %collective-permute-start = (bf16[2,128,512]{1,2,0:T(8,128)(2,1)}, bf16[2,128,512]{1,2,0:T(8,128)(2,1)}, u32[]{:S(2)}, u32[]{:S(2)}) collective-permute-start(bf16[2,128,512]{1,2,0:T(8,128)(2,1)} %pad_maximum_fusion), channel_id=1, source_target_pairs={{0,4},{2,6},{4,8},{6,10},{8,12},{10,14},{12,16},{14,18},{16,20},{1... | collective-permute-start | bytes 786440 | tf_op jit(solution)/shard_map/ppermute | solution.py:16
  8.6 13.8 %collective-permute-start.1 = (bf16[2,128,512]{1,2,0:T(8,128)(2,1)}, bf16[2,128,512]{1,2,0:T(8,128)(2,1)}, u32[]{:S(2)}, u32[]{:S(2)}) collective-permute-start(bf16[2,128,512]{1,2,0:T(8,128)(2,1)} %pad_maximum_fusion), channel_id=1, source_target_pairs={{0,2},{2,4},{4,6},{6,8},{8,10},{10,12},{12,14},{14,16},{16,18},{18... | collective-permute-start | bytes 786440 | tf_op jit(solution)/shard_map/ppermute | solution.py:16
  11.9 4.1 %copy-start.2 = (s32[128]{0:T(128)}, s32[128]{0:T(128)S(1)}, u32[]{:S(2)}) copy-start(s32[128]{0:T(128)S(1)} %broadcast_add_fusion.1) | copy-start | bytes 1540
  16.0 0.7 %copy-start.4 = (s32[128]{0:T(128)S(1)}, s32[128]{0:T(128)}, u32[]{:S(2)}) copy-start(s32[128]{0:T(128)} %compare_select_fusion.2) | copy-start | bytes 1540
  16.0 0.7 %copy-start.3 = (s32[128]{0:T(128)S(1)}, s32[128]{0:T(128)}, u32[]{:S(2)}) copy-start(s32[128]{0:T(128)} %copy-done.2) | copy-start | bytes 1540
  31.9 14.1 %collective-permute-start.3 = (bf16[4,128,128]{2,1,0:T(8,128)(2,1)S(1)}, bf16[4,128,128]{2,1,0:T(8,128)(2,1)S(1)}, u32[]{:S(2)}, u32[]{:S(2)}) collective-permute-start(bf16[4,128,128]{2,1,0:T(8,128)(2,1)S(1)} %fusion.12), channel_id=1, source_target_pairs={{4,0},{6,2},{8,4},{10,6},{12,8},{14,10},{16,12},{18,14},{20,16},{2... | collective-permute-start | bytes 393224 | tf_op jit(solution)/shard_map/ppermute | solution.py:16
  39.8 6.2 %collective-permute-start.2 = (bf16[4,128,128]{2,1,0:T(8,128)(2,1)}, bf16[4,128,128]{2,1,0:T(8,128)(2,1)S(1)}, u32[]{:S(2)}, u32[]{:S(2)}) collective-permute-start(bf16[4,128,128]{2,1,0:T(8,128)(2,1)} %fusion.13), channel_id=1, source_target_pairs={{2,0},{4,2},{6,4},{8,6},{10,8},{12,10},{14,12},{16,14},{18,16},{20... | collective-permute-start | bytes 393224 | tf_op jit(solution)/shard_map/ppermute | solution.py:16

commit v14 on v12

--- a/solution.py
+++ b/solution.py
@@ -53,7 +53,7 @@
     axes = ("ctx", "uly")
     key_value = jnp.stack([key_vectors, value_vectors])
     near_rim = shifted(key_value, axes, 1)
-    far_rim = shifted(key_value, axes, 2)
+    far_rim = (shifted(key_vectors, axes, 2), shifted(value_vectors, axes, 2))
     device_index = lax.axis_index(axes)
     query_heads = queries.reshape(rows, KVH, GROUP, HD)
     grad_heads = output_grad.reshape(rows, KVH, GROUP, HD)

time: 45.2 us -> 47.8 us (1.058)
  waiting for transfers between devices: 8.98 us -> 2.97 us
  starting transfers between devices: 13.2 us -> 18.1 us
  matrix products: 8.01 us -> 9.81 us
  other arithmetic: 4.18 us -> 5.73 us
  local copies, waits for them, and re-layouts: 9.16 us -> 9.87 us
    ppermute x4 -> x5, waiting for transfers between devices: 8.98 us -> 2.97 us  [shifted(): return lax.ppermute(block, axis, route)]
    ppermute x4 -> x5, starting transfers between devices: 13.2 us -> 18.1 us  [shifted(): return lax.ppermute(block, axis, route)]
    unnamed x8 -> x14, local copies, waits for them, and re-layouts: 3.76 us -> 5.45 us
    slice x1 -> x0, local copies, waits for them, and re-layouts: 0.99 us -> none  [body(): far_keys = far_rim[0].reshape(rows, KVH, HD)]
    another operation x1, other arithmetic: 0.73 us -> 1.7 us  [body(): key_value = jnp.stack([key_vectors, value_vectors])]
    dot_general x3, matrix products: 1.97 us -> 2.87 us  [key_grad_of(): jnp.einsum('ghts,tghd->gsd', grad_s, query_heads, preferred_element_type=...]
    dot_general x1, matrix products: 1.66 us -> 2.55 us  [body(): jnp.einsum('tghd,sgd->ghts', grad_heads, far_values, preferred_element_ty...]
    select_n x2, other arithmetic: 0.01 us -> 0.61 us  [doc_index(): return jnp.where(positions < 0, -1, counted)]
  transfers between devices with their start and end apart: 4 -> 5, of which waited for: 2 -> 2; matrix products, arithmetic and copies ran while one was open for 27% -> 35% of each run, Pallas kernels for 0% -> 0%
where the time goes in v14:
time: 47.8 us; the launch traced here: 47.4 us
  starting transfers between devices  18.1 us (38%)
  local copies, waits for them, and re-layouts  9.87 us (21%)
  matrix products  9.81 us (21%)
  other arithmetic  5.73 us (12%)
  waiting for transfers between devices  2.97 us (6%)
  between operations  0.94 us (2%)
    ppermute x5, starting transfers between devices, shifted(): return lax.ppermute(block, axis, route)  18.1 us
    unnamed x14, local copies, waits for them, and re-layouts  5.45 us
    ppermute x5, waiting for transfers between devices, shifted(): return lax.ppermute(block, axis, route)  2.97 us
    dot_general x3, matrix products, key_grad_of(): jnp.einsum('ghts,tghd->gsd', grad_s, query_heads, preferred_element_type=...  2.87 us
    dot_general x1, matrix products, body(): jnp.einsum('tghd,sgd->ghts', grad_heads, far_values, preferred_element_ty...  2.55 us
    another operation x1, other arithmetic, body(): key_value = jnp.stack([key_vectors, value_vectors])  1.7 us
    dot_general x3, matrix products, scores_of(): jnp.einsum('tghd,sgd->ghts', query_heads, key_heads, preferred_element_ty...  1.54 us
    convert_element_type x1, other arithmetic, body(): (near_exp / row_sum * (near_grad_p - row_delta)).astype(jnp.bfloat16)  1.46 us
  transfers between devices with their start and end apart: 5, of which 2 were waited for; matrix products, arithmetic and copies ran while one was open for 35% of the time, Pallas kernels for 0%

profile of v14, /device:TPU:1, one launch (start us, length us, event | category | flops | bytes accessed | tf_op | source)
XLA Modules:
  0.0 47.4 jit_solution(4855016703755794411)
XLA Ops:
  0.6 1.8 %copy.62 = bf16[128,512]{0,1:T(8,128)(2,1)} copy(bf16[128,512]{1,0:T(8,128)(2,1)} %param.7) | data formatting | bytes 262144 | tf_op args[2]
  2.5 5.0 %collective-permute-start.2 = (bf16[128,512]{0,1:T(8,128)(2,1)}, bf16[128,512]{0,1:T(8,128)(2,1)}, u32[]{:S(2)}, u32[]{:S(2)}) collective-permute-start(bf16[128,512]{0,1:T(8,128)(2,1)} %copy.62), channel_id=1, source_target_pairs={{0,4},{2,6},{4,8},{6,10},{8,12},{10,14},{12,16},{14,18},{16,20},{1... | collective-permute-start | bytes 393224 | tf_op jit(solution)/shard_map/ppermute | solution.py:16
  7.5 1.7 %copy.58 = bf16[128,512]{0,1:T(8,128)(2,1)} copy(bf16[128,512]{1,0:T(8,128)(2,1)} %param.6) | data formatting | bytes 262144 | tf_op args[1]
  9.2 3.5 %collective-permute-start = (bf16[128,512]{0,1:T(8,128)(2,1)}, bf16[128,512]{0,1:T(8,128)(2,1)S(1)}, u32[]{:S(2)}, u32[]{:S(2)}) collective-permute-start(bf16[128,512]{0,1:T(8,128)(2,1)} %copy.58), channel_id=1, source_target_pairs={{0,4},{2,6},{4,8},{6,10},{8,12},{10,14},{12,16},{14,18},{16,20},{1... | collective-permute-start | bytes 393224 | tf_op jit(solution)/shard_map/ppermute | solution.py:16
  12.7 1.7 %pad_maximum_fusion = bf16[2,128,512]{1,2,0:T(8,128)(2,1)} fusion(bf16[1,128,512]{1,2,0:T(8,128)(2,1)} %bitcast.7, bf16[1,128,512]{1,2,0:T(8,128)(2,1)} %bitcast.6), kind=kLoop, calls=%fused_computation.42 | loop fusion | flops 131072 | bytes 524288 | tf_op jit(solution)/shard_map/stack | solution.py:54
  14.3 3.2 %collective-permute-start.1 = (bf16[2,128,512]{1,2,0:T(8,128)(2,1)}, bf16[2,128,512]{1,2,0:T(8,128)(2,1)}, u32[]{:S(2)}, u32[]{:S(2)}) collective-permute-start(bf16[2,128,512]{1,2,0:T(8,128)(2,1)} %pad_maximum_fusion), channel_id=1, source_target_pairs={{0,2},{2,4},{4,6},{6,8},{8,10},{10,12},{12,14},{14,16},{16,18},{18... | collective-permute-start | bytes 786440 | tf_op jit(solution)/shard_map/ppermute | solution.py:16
  17.6 0.9 %reshape.388 = bf16[128,4,128]{2,1,0:T(4,128)(2,1)S(1)} reshape(bf16[128,512]{1,0:T(8,128)(2,1)} %param.6) | data formatting | bytes 262144 | tf_op jit(solution)/shard_map/reshape | solution.py:60
  18.5 0.9 %reshape.393 = bf16[128,4,128]{2,1,0:T(4,128)(2,1)S(1)} reshape(bf16[128,512]{1,0:T(8,128)(2,1)} %param.7) | data formatting | bytes 262144 | tf_op jit(solution)/shard_map/reshape | solution.py:61
  19.5 0.7 %copy.55 = s32[16,1]{1,0:T(8,128)S(1)} copy(s32[16,1]{0,1:T(1,128)} %bitcast.218) | data formatting | bytes 128 | tf_op jit(solution)/shard_map/reshape.361
  20.5 0.6 %compare_select_fusion.2 = s32[128]{0:T(128)} fusion(s32[128]{0:T(128)S(1)} %get-tuple-element.28, s32[]{:T(128)S(6)} %mul.102), kind=kLoop, calls=%fused_computation.72 | loop fusion | flops 384 | bytes 1028 | tf_op jit(solution)/shard_map/jit(_where)/select_n | solution.py:22
  21.2 0.7 %copy.113 = bf16[128,4096]{0,1:T(8,128)(2,1)S(1)} copy(bf16[128,4096]{1,0:T(8,128)(2,1)S(1)} %copy-done) | data formatting | bytes 2097152 | tf_op jit(solution)/shard_map/reshape | solution.py:58
  23.3 1.0 %fusion.3 = (f32[4,8,128]{2,1,0:T(8,128)S(1)}, f32[4,8,128]{2,1,0:T(8,128)S(1)}, f32[4,128,128,8]{2,1,3,0:T(8,128)S(1)}) fusion(f32[4,128,128,8]{2,1,3,0:T(8,128)S(1)} %get-tuple-element.45, f32[4,8,128]{2,1,0:T(8,128)S(1)} %get-tuple-element.44, pred[128,128]{0,1:T(8,128)(4,1)S(1)} %get-tuple-element.42, bf16[128,4,8,128]{3,2,1,0:T(8,128)(2,1)S(1)} %bitcast.204, ...), kind=kOutput, calls=%fused_computation.7 | convolution fusion | flops 137355264 | bytes 5439488 | tf_op jit(solution)/shard_map/tghd,sgd->ghts/dot_general | solution.py:72
  24.9 1.9 %collective-permute-done.1 = bf16[2,128,512]{1,2,0:T(8,128)(2,1)} collective-permute-done((bf16[2,128,512]{1,2,0:T(8,128)(2,1)}, bf16[2,128,512]{1,2,0:T(8,128)(2,1)}, u32[]{:S(2)}, u32[]{:S(2)}) %collective-permute-start.1) | collective-permute-done | bytes 262176 | tf_op jit(solution)/shard_map/ppermute | solution.py:16
  26.7 1.0 %fusion.30 = (bf16[1,128,512]{1,2,0:T(8,128)(2,1)S(1)}, bf16[1,128,512]{1,2,0:T(8,128)(2,1)S(1)}) fusion(bf16[2,128,512]{1,2,0:T(8,128)(2,1)} %collective-permute-done.1), kind=kLoop, calls=%fused_computation.76 | loop fusion | bytes 524288 | tf_op jit(solution)/shard_map/slice | solution.py:80
  28.8 2.6 %fusion.6 = (f32[4,8,128]{2,1,0:T(8,128)S(1)}, f32[4,8,128]{2,1,0:T(8,128)S(1)}, f32[4,8,128]{2,1,0:T(8,128)S(1)}, f32[4,8,128]{2,1,0:T(8,128)S(1)}, f32[4,128,128,8]{2,1,3,0:T(8,128)S(1)}) fusion(f32[4,128,128,8]{2,1,3,0:T(8,128)S(1)} %get-tuple-element.47, f32[4,8,128]{2,1,0:T(8,128)S(1)} %maximum_maximum_fusion, ...), kind=kOutput, calls=%fused_computation.12 | convolution fusion | flops 140492800 | bytes 9682944 | tf_op jit(solution)/shard_map/tghd,sgd->ghts/dot_general | solution.py:98
  31.4 1.5 %fusion.2 = (bf16[4,8,128,128]{2,3,1,0:T(8,128)(2,1)S(1)}, bf16[4,8,128,128]{2,3,1,0:T(8,128)(2,1)S(1)}) fusion(f32[4,128,128,8]{2,1,3,0:T(8,128)S(1)} %fusion.20, f32[4,128,128,8]{2,1,3,0:T(8,128)S(1)} %get-tuple-element.49, f32[4,8,128]{2,1,0:T(8,128)S(1)} %get-tuple-element.29, f32[4,8,128]{2,1,0:T(8,128)S(1)} %get-tuple-element.30, ...), kind=kLoop, calls=%fused_computation.4 | loop fusion | flops 7340032 | bytes 10567680 | tf_op jit(solution)/shard_map/convert_element_type | solution.py:110
  33.3 3.7 %collective-permute-start.4 = (bf16[4,128,128]{2,1,0:T(8,128)(2,1)S(1)}, bf16[4,128,128]{2,1,0:T(8,128)(2,1)S(1)}, u32[]{:S(2)}, u32[]{:S(2)}) collective-permute-start(bf16[4,128,128]{2,1,0:T(8,128)(2,1)S(1)} %fusion.15), channel_id=1, source_target_pairs={{4,0},{6,2},{8,4},{10,6},{12,8},{14,10},{16,12},{18,14},{20,16},{2... | collective-permute-start | bytes 393224 | tf_op jit(solution)/shard_map/ppermute | solution.py:16
  37.0 1.1 %fusion.16 = bf16[4,128,128]{2,1,0:T(8,128)(2,1)} fusion(bf16[4,8,128,128]{2,3,1,0:T(8,128)(2,1)S(1)} %get-tuple-element.11, bf16[128,4,8,128]{0,3,2,1:T(8,128)(2,1)S(1)} %bitcast.202), kind=kOutput, calls=%fused_computation.32 | convolution fusion | flops 134348800 | bytes 2228224 | tf_op jit(solution)/shard_map/ghts,tghd->gsd/dot_general | solution.py:41
  38.1 2.7 %collective-permute-start.3 = (bf16[4,128,128]{2,1,0:T(8,128)(2,1)}, bf16[4,128,128]{2,1,0:T(8,128)(2,1)}, u32[]{:S(2)}, u32[]{:S(2)}) collective-permute-start(bf16[4,128,128]{2,1,0:T(8,128)(2,1)} %fusion.16), channel_id=1, source_target_pairs={{2,0},{4,2},{6,4},{8,6},{10,8},{12,10},{14,12},{16,14},{18,16},{20... | collective-permute-start | bytes 393224 | tf_op jit(solution)/shard_map/ppermute | solution.py:16
  40.9 0.8 %fusion.5 = bf16[4,8,128,128]{2,3,1,0:T(8,128)(2,1)S(1)} fusion(f32[4,128,128,8]{2,1,3,0:T(8,128)S(1)} %get-tuple-element.51, f32[4,128,128,8]{2,1,3,0:T(8,128)S(1)} %get-tuple-element.45, f32[4,8,128]{2,1,0:T(8,128)S(1)} %bitcast.216, f32[4,8,128]{2,1,0:T(8,128)S(1)} %bitcast.217, f32[4,8,128]{2,1,0:T(8,128)S(1)} %get-tuple-element.44, ...), kind=kLoop, calls=%fused_computation.9 | loop fusion | flops 3670016 | bytes 5308416 | tf_op jit(solution)/shard_map/convert_element_type | solution.py:121
  43.0 1.3 %copy.81 = bf16[128,4096]{1,0:T(8,128)(2,1)} copy(bf16[128,4096]{0,1:T(8,128)(2,1)S(1)} %bitcast.207) | data formatting | bytes 2097152
  44.3 1.1 %collective-permute-done.3 = bf16[4,128,128]{2,1,0:T(8,128)(2,1)} collective-permute-done((bf16[4,128,128]{2,1,0:T(8,128)(2,1)}, bf16[4,128,128]{2,1,0:T(8,128)(2,1)}, u32[]{:S(2)}, u32[]{:S(2)}) %collective-permute-start.3) | collective-permute-done | bytes 131104 | tf_op jit(solution)/shard_map/ppermute | solution.py:16
  45.4 1.3 %add_convert_fusion = bf16[4,128,128]{2,1,0:T(8,128)(2,1)S(1)} fusion(bf16[4,128,128]{2,1,0:T(8,128)(2,1)S(1)} %collective-permute-done.4, bf16[4,128,128]{2,1,0:T(8,128)(2,1)} %collective-permute-done.3, bf16[4,8,128,128]{2,3,1,0:T(8,128)(2,1)S(1)} %fusion.5, bf16[128,4,8,128]{0,3,2,1:T(8,128)(2,1)S(1)} %bitcast.203), kind=kOutput, calls=%fused_computation.43 | convolution fusion | flops 134610944 | bytes 2490368 | tf_op jit(solution)/shard_map/ghts,tghd->gsd/dot_general | solution.py:41
  46.8 0.7 %pad_maximum_fusion.1 = bf16[128,512]{1,0:T(8,128)(2,1)} fusion(bf16[128,128]{1,0:T(8,128)(2,1)S(1)} %get-tuple-element.34, bf16[128,128]{1,0:T(8,128)(2,1)S(1)} %get-tuple-element.35, bf16[128,128]{1,0:T(8,128)(2,1)S(1)} %get-tuple-element.36, bf16[128,128]{1,0:T(8,128)(2,1)S(1)} %get-tuple-element.33), kind=kLoop, calls=%fused_computation.44 | loop fusion | flops 524288 | bytes 262144 | tf_op jit(solution)/shard_map/concatenate | solution.py:130
  (35 shorter events, 5.1 us)
Async XLA Ops:
  0.6 20.6 %copy-start = (bf16[128,4096]{1,0:T(8,128)(2,1)S(1)}, bf16[128,4096]{1,0:T(8,128)(2,1)}, u32[]{:S(2)}) copy-start(bf16[128,4096]{1,0:T(8,128)(2,1)} %param.5) | copy-start | bytes 3145732
  0.6 21.3 %copy-start.1 = (bf16[128,4096]{1,0:T(8,128)(2,1)S(1)}, bf16[128,4096]{1,0:T(8,128)(2,1)}, u32[]{:S(2)}) copy-start(bf16[128,4096]{1,0:T(8,128)(2,1)} %param.8) | copy-start | bytes 3145732
  2.5 26.3 %collective-permute-start.2 = (bf16[128,512]{0,1:T(8,128)(2,1)}, bf16[128,512]{0,1:T(8,128)(2,1)}, u32[]{:S(2)}, u32[]{:S(2)}) collective-permute-start(bf16[128,512]{0,1:T(8,128)(2,1)} %copy.62), channel_id=1, source_target_pairs={{0,4},{2,6},{4,8},{6,10},{8,12},{10,14},{12,16},{14,18},{16,20},{1... | collective-permute-start | bytes 393224 | tf_op jit(solution)/shard_map/ppermute | solution.py:16
  9.2 15.2 %collective-permute-start = (bf16[128,512]{0,1:T(8,128)(2,1)}, bf16[128,512]{0,1:T(8,128)(2,1)S(1)}, u32[]{:S(2)}, u32[]{:S(2)}) collective-permute-start(bf16[128,512]{0,1:T(8,128)(2,1)} %copy.58), channel_id=1, source_target_pairs={{0,4},{2,6},{4,8},{6,10},{8,12},{10,14},{12,16},{14,18},{16,20},{1... | collective-permute-start | bytes 393224 | tf_op jit(solution)/shard_map/ppermute | solution.py:16
  14.3 12.4 %collective-permute-start.1 = (bf16[2,128,512]{1,2,0:T(8,128)(2,1)}, bf16[2,128,512]{1,2,0:T(8,128)(2,1)}, u32[]{:S(2)}, u32[]{:S(2)}) collective-permute-start(bf16[2,128,512]{1,2,0:T(8,128)(2,1)} %pad_maximum_fusion), channel_id=1, source_target_pairs={{0,2},{2,4},{4,6},{6,8},{8,10},{10,12},{12,14},{14,16},{16,18},{18... | collective-permute-start | bytes 786440 | tf_op jit(solution)/shard_map/ppermute | solution.py:16
  17.6 3.5 %copy-start.2 = (s32[128]{0:T(128)}, s32[128]{0:T(128)S(1)}, u32[]{:S(2)}) copy-start(s32[128]{0:T(128)S(1)} %broadcast_add_fusion) | copy-start | bytes 1540
  21.9 0.6 %copy-start.3 = (s32[128]{0:T(128)S(1)}, s32[128]{0:T(128)}, u32[]{:S(2)}) copy-start(s32[128]{0:T(128)} %copy-done.2) | copy-start | bytes 1540
  21.9 0.7 %copy-start.4 = (s32[128]{0:T(128)S(1)}, s32[128]{0:T(128)}, u32[]{:S(2)}) copy-start(s32[128]{0:T(128)} %compare_select_fusion.2) | copy-start | bytes 1540
  33.3 12.1 %collective-permute-start.4 = (bf16[4,128,128]{2,1,0:T(8,128)(2,1)S(1)}, bf16[4,128,128]{2,1,0:T(8,128)(2,1)S(1)}, u32[]{:S(2)}, u32[]{:S(2)}) collective-permute-start(bf16[4,128,128]{2,1,0:T(8,128)(2,1)S(1)} %fusion.15), channel_id=1, source_target_pairs={{4,0},{6,2},{8,4},{10,6},{12,8},{14,10},{16,12},{18,14},{20,16},{2... | collective-permute-start | bytes 393224 | tf_op jit(solution)/shard_map/ppermute | solution.py:16
  38.1 7.3 %collective-permute-start.3 = (bf16[4,128,128]{2,1,0:T(8,128)(2,1)}, bf16[4,128,128]{2,1,0:T(8,128)(2,1)}, u32[]{:S(2)}, u32[]{:S(2)}) collective-permute-start(bf16[4,128,128]{2,1,0:T(8,128)(2,1)} %fusion.16), channel_id=1, source_target_pairs={{2,0},{4,2},{6,4},{8,6},{10,8},{12,10},{14,12},{16,14},{18,16},{20... | collective-permute-start | bytes 393224 | tf_op jit(solution)/shard_map/ppermute | solution.py:16

commit v15 on v12

--- a/solution.py
+++ b/solution.py
@@ -108,11 +108,11 @@
     ) / row_sum
     far_grad_s = ((far_exp / row_sum) * (far_grad_p - row_delta)).astype(jnp.bfloat16)
     near_grad_s = ((near_exp / row_sum) * (near_grad_p - row_delta)).astype(jnp.bfloat16)
+    near_key_grad = key_grad_of(near_grad_s, query_heads, score_scale).astype(jnp.bfloat16)
+    near_back = shifted(near_key_grad, axes, -1)
+    near_key_grad, far_grad_s = lax.optimization_barrier((near_key_grad, far_grad_s))
     far_key_grad = key_grad_of(far_grad_s, query_heads, score_scale).astype(jnp.bfloat16)
     far_back = shifted(far_key_grad, axes, -2)
-    far_key_grad, near_grad_s = lax.optimization_barrier((far_key_grad, near_grad_s))
-    near_key_grad = key_grad_of(near_grad_s, query_heads, score_scale).astype(jnp.bfloat16)
-    near_back = shifted(near_key_grad, axes, -1)
 
     _, own_scale, row_delta, far_grad_s, near_grad_s = lax.optimization_barrier(
         ((far_key_grad, near_key_grad), own_rescale / row_sum, row_delta, far_grad_s, near_grad_s)

time: 45.2 us -> 50.3 us (1.11)
  the two profiles are of different devices: /device:TPU:1 before, /device:TPU:0 now
where the time goes in v15:
time: 50.3 us; the launch traced here: 50 us
  waiting for transfers between devices  14.4 us (29%)
  starting transfers between devices  13.4 us (27%)
  local copies, waits for them, and re-layouts  9.16 us (18%)
  matrix products  8.01 us (16%)
  other arithmetic  4.17 us (8%)
  between operations  0.87 us (2%)
    ppermute x4, waiting for transfers between devices, shifted(): return lax.ppermute(block, axis, route)  14.4 us
    ppermute x4, starting transfers between devices, shifted(): return lax.ppermute(block, axis, route)  13.4 us
    unnamed x8, local copies, waits for them, and re-layouts  3.76 us
    dot_general x3, matrix products, key_grad_of(): jnp.einsum('ghts,tghd->gsd', grad_s, query_heads, preferred_element_type=...  1.97 us
    dot_general x1, matrix products, body(): jnp.einsum('tghd,sgd->ghts', grad_heads, far_values, preferred_element_ty...  1.66 us
    dot_general x3, matrix products, scores_of(): jnp.einsum('tghd,sgd->ghts', query_heads, key_heads, preferred_element_ty...  1.52 us
    convert_element_type x1, other arithmetic, body(): (far_exp / row_sum * (far_grad_p - row_delta)).astype(jnp.bfloat16)  1.46 us
    dot_general x3, matrix products, query_grad_of(): jnp.einsum('ghts,sgd->ghtd', grad_s, keys, preferred_element_type=jnp.flo...  1.29 us
  transfers between devices with their start and end apart: 4, of which 2 were waited for; matrix products, arithmetic and copies ran while one was open for 24% of the time, Pallas kernels for 0%

profile of v15, /device:TPU:0, one launch (start us, length us, event | category | flops | bytes accessed | tf_op | source)
XLA Modules:
  0.0 50.0 jit_solution(6159411096823402836)
XLA Ops:
  0.6 1.2 %copy.56 = bf16[128,512]{0,1:T(8,128)(2,1)S(1)} copy(bf16[128,512]{1,0:T(8,128)(2,1)} %param.6) | data formatting | bytes 262144 | tf_op args[1]
  1.8 1.0 %copy.57 = bf16[128,512]{0,1:T(8,128)(2,1)S(1)} copy(bf16[128,512]{1,0:T(8,128)(2,1)} %param.7) | data formatting | bytes 262144 | tf_op args[2]
  2.9 0.7 %pad_maximum_fusion = bf16[2,128,512]{1,2,0:T(8,128)(2,1)} fusion(bf16[1,128,512]{1,2,0:T(8,128)(2,1)S(1)} %bitcast.218, bf16[1,128,512]{1,2,0:T(8,128)(2,1)S(1)} %bitcast.217), kind=kLoop, calls=%fused_computation.42 | loop fusion | flops 131072 | bytes 524288 | tf_op jit(solution)/shard_map/stack | solution.py:54
  3.6 6.6 %collective-permute-start.1 = (bf16[2,128,512]{1,2,0:T(8,128)(2,1)}, bf16[2,128,512]{1,2,0:T(8,128)(2,1)}, u32[]{:S(2)}, u32[]{:S(2)}) collective-permute-start(bf16[2,128,512]{1,2,0:T(8,128)(2,1)} %pad_maximum_fusion), channel_id=1, source_target_pairs={{0,4},{2,6},{4,8},{6,10},{8,12},{10,14},{12,16},{14,18},{16,20},{1... | collective-permute-start | bytes 786440 | tf_op jit(solution)/shard_map/ppermute | solution.py:16
  10.2 4.2 %collective-permute-start = (bf16[2,128,512]{1,2,0:T(8,128)(2,1)}, bf16[2,128,512]{1,2,0:T(8,128)(2,1)}, u32[]{:S(2)}, u32[]{:S(2)}) collective-permute-start(bf16[2,128,512]{1,2,0:T(8,128)(2,1)} %pad_maximum_fusion), channel_id=1, source_target_pairs={{0,2},{2,4},{4,6},{6,8},{8,10},{10,12},{12,14},{14,16},{16,18},{18... | collective-permute-start | bytes 786440 | tf_op jit(solution)/shard_map/ppermute | solution.py:16
  14.4 0.9 %reshape.382 = bf16[128,4,128]{2,1,0:T(4,128)(2,1)S(1)} reshape(bf16[128,512]{1,0:T(8,128)(2,1)} %param.6) | data formatting | bytes 262144 | tf_op jit(solution)/shard_map/reshape | solution.py:60
  15.4 0.9 %reshape.385 = bf16[128,4,128]{2,1,0:T(4,128)(2,1)S(1)} reshape(bf16[128,512]{1,0:T(8,128)(2,1)} %param.7) | data formatting | bytes 262144 | tf_op jit(solution)/shard_map/reshape | solution.py:61
  16.3 0.7 %copy.53 = s32[16,1]{1,0:T(8,128)S(1)} copy(s32[16,1]{0,1:T(1,128)} %bitcast.221) | data formatting | bytes 128 | tf_op jit(solution)/shard_map/reshape.359
  17.4 0.7 %copy.109 = bf16[128,4096]{0,1:T(8,128)(2,1)S(1)} copy(bf16[128,4096]{1,0:T(8,128)(2,1)S(1)} %copy-done) | data formatting | bytes 2097152 | tf_op jit(solution)/shard_map/reshape | solution.py:58
  18.6 0.5 %fusion.9 = (f32[4,8,128]{2,1,0:T(8,128)S(1)}, f32[4,128,128,8]{2,1,3,0:T(8,128)S(1)}) fusion(pred[128,128]{0,1:T(8,128)(4,1)S(1)} %get-tuple-element.44, bf16[128,4,128,1]{0,2,3,1:T(8,128)(2,1)S(1)} %copy.87, bf16[128,4,8,128]{0,3,2,1:T(8,128)(2,1)S(1)} %bitcast.198), kind=kOutput, calls=%fused_computation.22 | convolution fusion | flops 135786496 | bytes 3309568 | tf_op jit(solution)/shard_map/tghd,sgd->ghts/dot_general | solution.py:33
  19.1 1.0 %fusion.3 = (f32[4,8,128]{2,1,0:T(8,128)S(1)}, f32[4,8,128]{2,1,0:T(8,128)S(1)}, f32[4,128,128,8]{2,1,3,0:T(8,128)S(1)}) fusion(f32[4,128,128,8]{2,1,3,0:T(8,128)S(1)} %get-tuple-element.47, f32[4,8,128]{2,1,0:T(8,128)S(1)} %get-tuple-element.46, pred[128,128]{0,1:T(8,128)(4,1)S(1)} %get-tuple-element.44, bf16[128,4,8,128]{3,2,1,0:T(8,128)(2,1)S(1)} %bitcast.204, ...), kind=kOutput, calls=%fused_computation.7 | convolution fusion | flops 137355264 | bytes 5439488 | tf_op jit(solution)/shard_map/tghd,sgd->ghts/dot_general | solution.py:72
  20.1 0.9 %collective-permute-done = bf16[2,128,512]{1,2,0:T(8,128)(2,1)} collective-permute-done((bf16[2,128,512]{1,2,0:T(8,128)(2,1)}, bf16[2,128,512]{1,2,0:T(8,128)(2,1)}, u32[]{:S(2)}, u32[]{:S(2)}) %collective-permute-start) | collective-permute-done | bytes 262176 | tf_op jit(solution)/shard_map/ppermute | solution.py:16
  21.0 1.0 %fusion.31 = (bf16[1,128,512]{1,2,0:T(8,128)(2,1)S(1)}, bf16[1,128,512]{1,2,0:T(8,128)(2,1)S(1)}) fusion(bf16[2,128,512]{1,2,0:T(8,128)(2,1)} %collective-permute-done), kind=kLoop, calls=%fused_computation.77 | loop fusion | bytes 524288 | tf_op jit(solution)/shard_map/slice | solution.py:79
  22.6 0.5 %fusion.24 = f32[4,128,128,8]{2,1,3,0:T(8,128)S(1)} fusion(bf16[128,4,128,1]{0,2,3,1:T(8,128)(2,1)S(1)} %bitcast.216, bf16[128,4,8,128]{3,2,1,0:T(8,128)(2,1)S(1)} %bitcast.205), kind=kOutput, calls=%fused_computation.40 | convolution fusion | flops 134217728 | bytes 3276800 | tf_op jit(solution)/shard_map/tghd,sgd->ghts/dot_general | solution.py:101
  23.1 1.0 %fusion.30 = (bf16[1,128,512]{1,2,0:T(8,128)(2,1)S(1)}, bf16[1,128,512]{1,2,0:T(8,128)(2,1)S(1)}) fusion(bf16[2,128,512]{1,2,0:T(8,128)(2,1)} %collective-permute-done.1), kind=kLoop, calls=%fused_computation.76 | loop fusion | bytes 524288 | tf_op jit(solution)/shard_map/slice | solution.py:77
  24.6 1.7 %fusion = (f32[4,8,128]{2,1,0:T(8,128)S(1)}, f32[4,8,128]{2,1,0:T(8,128)S(1)}, f32[4,8,128]{2,1,0:T(8,128)S(1)}, f32[4,8,128]{2,1,0:T(8,128)S(1)}, f32[4,128,128,8]{2,1,3,0:T(8,128)S(1)}) fusion(f32[4,128,128,8]{2,1,3,0:T(8,128)S(1)} %get-tuple-element.49, f32[4,8,128]{2,1,0:T(8,128)S(1)} %maximum_maximum_fusion, ...), kind=kOutput, calls=%fused_computation.2 | convolution fusion | flops 140492800 | bytes 9682944 | tf_op jit(solution)/shard_map/tghd,sgd->ghts/dot_general | solution.py:98
  26.3 1.5 %fusion.2 = (bf16[4,8,128,128]{2,3,1,0:T(8,128)(2,1)S(1)}, bf16[4,8,128,128]{2,3,1,0:T(8,128)(2,1)S(1)}) fusion(f32[4,128,128,8]{2,1,3,0:T(8,128)S(1)} %get-tuple-element.52, f32[4,128,128,8]{2,1,3,0:T(8,128)S(1)} %get-tuple-element.49, f32[4,8,128]{2,1,0:T(8,128)S(1)} %get-tuple-element.29, f32[4,8,128]{2,1,0:T(8,128)S(1)} %get-tuple-element.30, ...), kind=kLoop, calls=%fused_computation.4 | loop fusion | flops 7340032 | bytes 10567680 | tf_op jit(solution)/shard_map/convert_element_type | solution.py:109
  28.2 1.3 %collective-permute-start.2 = (bf16[4,128,128]{2,1,0:T(8,128)(2,1)S(1)}, bf16[4,128,128]{2,1,0:T(8,128)(2,1)S(1)}, u32[]{:S(2)}, u32[]{:S(2)}) collective-permute-start(bf16[4,128,128]{2,1,0:T(8,128)(2,1)S(1)} %fusion.15), channel_id=1, source_target_pairs={{2,0},{4,2},{6,4},{8,6},{10,8},{12,10},{14,12},{16,14},{18,16},{20... | collective-permute-start | bytes 393224 | tf_op jit(solution)/shard_map/ppermute | solution.py:16
  29.5 1.1 %fusion.16 = bf16[4,128,128]{2,1,0:T(8,128)(2,1)} fusion(bf16[4,8,128,128]{2,3,1,0:T(8,128)(2,1)S(1)} %get-tuple-element.10, bf16[128,4,8,128]{0,3,2,1:T(8,128)(2,1)S(1)} %bitcast.202), kind=kOutput, calls=%fused_computation.32 | convolution fusion | flops 134348800 | bytes 2228224 | tf_op jit(solution)/shard_map/ghts,tghd->gsd/dot_general | solution.py:41
  30.6 1.3 %collective-permute-start.3 = (bf16[4,128,128]{2,1,0:T(8,128)(2,1)}, bf16[4,128,128]{2,1,0:T(8,128)(2,1)S(1)}, u32[]{:S(2)}, u32[]{:S(2)}) collective-permute-start(bf16[4,128,128]{2,1,0:T(8,128)(2,1)} %fusion.16), channel_id=1, source_target_pairs={{4,0},{6,2},{8,4},{10,6},{12,8},{14,10},{16,12},{18,14},{20,16},{2... | collective-permute-start | bytes 393224 | tf_op jit(solution)/shard_map/ppermute | solution.py:16
  31.9 0.8 %fusion.5 = bf16[4,8,128,128]{2,3,1,0:T(8,128)(2,1)S(1)} fusion(f32[4,128,128,8]{2,1,3,0:T(8,128)S(1)} %get-tuple-element.53, f32[4,128,128,8]{2,1,3,0:T(8,128)S(1)} %get-tuple-element.47, f32[4,8,128]{2,1,0:T(8,128)S(1)} %bitcast.219, f32[4,8,128]{2,1,0:T(8,128)S(1)} %bitcast.220, f32[4,8,128]{2,1,0:T(8,128)S(1)} %get-tuple-element.46, ...), kind=kLoop, calls=%fused_computation.9 | loop fusion | flops 3670016 | bytes 5308416 | tf_op jit(solution)/shard_map/convert_element_type | solution.py:121
  34.1 1.3 %copy.77 = bf16[128,4096]{1,0:T(8,128)(2,1)} copy(bf16[128,4096]{0,1:T(8,128)(2,1)S(1)} %bitcast.207) | data formatting | bytes 2097152
  35.4 13.5 %collective-permute-done.3 = bf16[4,128,128]{2,1,0:T(8,128)(2,1)S(1)} collective-permute-done((bf16[4,128,128]{2,1,0:T(8,128)(2,1)}, bf16[4,128,128]{2,1,0:T(8,128)(2,1)S(1)}, u32[]{:S(2)}, u32[]{:S(2)}) %collective-permute-start.3) | collective-permute-done | bytes 131104 | tf_op jit(solution)/shard_map/ppermute | solution.py:16
  49.3 0.7 %pad_maximum_fusion.1 = bf16[128,512]{1,0:T(8,128)(2,1)} fusion(bf16[128,128]{1,0:T(8,128)(2,1)S(1)} %get-tuple-element.36, bf16[128,128]{1,0:T(8,128)(2,1)S(1)} %get-tuple-element.37, bf16[128,128]{1,0:T(8,128)(2,1)S(1)} %get-tuple-element.38, bf16[128,128]{1,0:T(8,128)(2,1)S(1)} %get-tuple-element.35), kind=kLoop, calls=%fused_computation.44 | loop fusion | flops 524288 | bytes 262144 | tf_op jit(solution)/shard_map/concatenate | solution.py:130
  (28 shorter events, 4.1 us)
Async XLA Ops:
  0.6 16.8 %copy-start = (bf16[128,4096]{1,0:T(8,128)(2,1)S(1)}, bf16[128,4096]{1,0:T(8,128)(2,1)}, u32[]{:S(2)}) copy-start(bf16[128,4096]{1,0:T(8,128)(2,1)} %param.5) | copy-start | bytes 3145732
  0.6 17.5 %copy-start.1 = (bf16[128,4096]{1,0:T(8,128)(2,1)S(1)}, bf16[128,4096]{1,0:T(8,128)(2,1)}, u32[]{:S(2)}) copy-start(bf16[128,4096]{1,0:T(8,128)(2,1)} %param.8) | copy-start | bytes 3145732
  3.6 19.5 %collective-permute-start.1 = (bf16[2,128,512]{1,2,0:T(8,128)(2,1)}, bf16[2,128,512]{1,2,0:T(8,128)(2,1)}, u32[]{:S(2)}, u32[]{:S(2)}) collective-permute-start(bf16[2,128,512]{1,2,0:T(8,128)(2,1)} %pad_maximum_fusion), channel_id=1, source_target_pairs={{0,4},{2,6},{4,8},{6,10},{8,12},{10,14},{12,16},{14,18},{16,20},{1... | collective-permute-start | bytes 786440 | tf_op jit(solution)/shard_map/ppermute | solution.py:16
  10.2 10.8 %collective-permute-start = (bf16[2,128,512]{1,2,0:T(8,128)(2,1)}, bf16[2,128,512]{1,2,0:T(8,128)(2,1)}, u32[]{:S(2)}, u32[]{:S(2)}) collective-permute-start(bf16[2,128,512]{1,2,0:T(8,128)(2,1)} %pad_maximum_fusion), channel_id=1, source_target_pairs={{0,2},{2,4},{4,6},{6,8},{8,10},{10,12},{12,14},{14,16},{16,18},{18... | collective-permute-start | bytes 786440 | tf_op jit(solution)/shard_map/ppermute | solution.py:16
  28.2 20.6 %collective-permute-start.2 = (bf16[4,128,128]{2,1,0:T(8,128)(2,1)S(1)}, bf16[4,128,128]{2,1,0:T(8,128)(2,1)S(1)}, u32[]{:S(2)}, u32[]{:S(2)}) collective-permute-start(bf16[4,128,128]{2,1,0:T(8,128)(2,1)S(1)} %fusion.15), channel_id=1, source_target_pairs={{2,0},{4,2},{6,4},{8,6},{10,8},{12,10},{14,12},{16,14},{18,16},{20... | collective-permute-start | bytes 393224 | tf_op jit(solution)/shard_map/ppermute | solution.py:16
  30.6 18.2 %collective-permute-start.3 = (bf16[4,128,128]{2,1,0:T(8,128)(2,1)}, bf16[4,128,128]{2,1,0:T(8,128)(2,1)S(1)}, u32[]{:S(2)}, u32[]{:S(2)}) collective-permute-start(bf16[4,128,128]{2,1,0:T(8,128)(2,1)} %fusion.16), channel_id=1, source_target_pairs={{4,0},{6,2},{8,4},{10,6},{12,8},{14,10},{16,12},{18,14},{20,16},{2... | collective-permute-start | bytes 393224 | tf_op jit(solution)/shard_map/ppermute | solution.py:16

commit v16 on v11

--- a/solution.py
+++ b/solution.py
@@ -52,8 +52,8 @@
     score_scale = HD ** (-0.5)
     axes = ("ctx", "uly")
     key_value = jnp.stack([key_vectors, value_vectors])
+    near_rim = shifted(key_value, axes, 1)
     far_rim = shifted(key_value, axes, 2)
-    near_rim = shifted(key_value, axes, 1)
     device_index = lax.axis_index(axes)
     query_heads = queries.reshape(rows, KVH, GROUP, HD)
     grad_heads = output_grad.reshape(rows, KVH, GROUP, HD)
@@ -114,11 +114,10 @@
     near_exp = near_exp * near_rescale
     far_grad_s = ((far_exp / row_sum) * (far_grad_p - row_delta)).astype(jnp.bfloat16)
     near_grad_s = ((near_exp / row_sum) * (near_grad_p - row_delta)).astype(jnp.bfloat16)
-    far_key_grad = key_grad_of(far_grad_s, query_heads, score_scale)
-    near_key_grad = key_grad_of(near_grad_s, query_heads, score_scale)
-    far_key_grad = far_key_grad.astype(jnp.bfloat16)
-    near_key_grad = near_key_grad.astype(jnp.bfloat16)
+    far_key_grad = key_grad_of(far_grad_s, query_heads, score_scale).astype(jnp.bfloat16)
     far_back = shifted(far_key_grad, axes, -2)
+    far_key_grad, near_grad_s = lax.optimization_barrier((far_key_grad, near_grad_s))
+    near_key_grad = key_grad_of(near_grad_s, query_heads, score_scale).astype(jnp.bfloat16)
     near_back = shifted(near_key_grad, axes, -1)
 
     _, own_scale, row_delta, far_grad_s, near_grad_s = lax.optimization_barrier(

time: 48.9 us -> 48.1 us (0.984)
  waiting for transfers between devices: 8.85 us -> 7.56 us
    ppermute x4, waiting for transfers between devices: 8.85 us -> 7.56 us  [shifted(): return lax.ppermute(block, axis, route)]
  transfers between devices with their start and end apart: 4 -> 4, of which waited for: 4 -> 3; matrix products, arithmetic and copies ran while one was open for 24% -> 27% of each run, Pallas kernels for 0% -> 0%
where the time goes in v16:
time: 48.1 us; the launch traced here: 47.3 us
  starting transfers between devices  17.8 us (37%)
  local copies, waits for them, and re-layouts  9.16 us (19%)
  matrix products  7.76 us (16%)
  waiting for transfers between devices  7.56 us (16%)
  other arithmetic  4.11 us (9%)
  between operations  0.9 us (2%)
    ppermute x4, starting transfers between devices, shifted(): return lax.ppermute(block, axis, route)  17.8 us
    ppermute x4, waiting for transfers between devices, shifted(): return lax.ppermute(block, axis, route)  7.56 us
    unnamed x8, local copies, waits for them, and re-layouts  3.76 us
    dot_general x3, matrix products, key_grad_of(): jnp.einsum('ghts,tghd->gsd', grad_s, query_heads, preferred_element_type=...  1.97 us
    dot_general x3, matrix products, scores_of(): jnp.einsum('tghd,sgd->ghts', query_heads, key_heads, preferred_element_ty...  1.54 us
    convert_element_type x1, other arithmetic, body(): (near_exp / row_sum * (near_grad_p - row_delta)).astype(jnp.bfloat16)  1.4 us
    dot_general x3, matrix products, query_grad_of(): jnp.einsum('ghts,sgd->ghtd', grad_s, keys, preferred_element_type=jnp.flo...  1.32 us
    reshape x2, local copies, waits for them, and re-layouts, body(): own_keys = key_vectors.reshape(rows, KVH, HD)  1.08 us
  transfers between devices with their start and end apart: 4, of which 3 were waited for; matrix products, arithmetic and copies ran while one was open for 27% of the time, Pallas kernels for 0%

profile of v16, /device:TPU:1, one launch (start us, length us, event | category | flops | bytes accessed | tf_op | source)
XLA Modules:
  0.0 47.3 jit_solution(17783429574528436192)
XLA Ops:
  0.6 1.2 %copy.56 = bf16[128,512]{0,1:T(8,128)(2,1)S(1)} copy(bf16[128,512]{1,0:T(8,128)(2,1)} %param.6) | data formatting | bytes 262144 | tf_op args[1]
  1.8 1.0 %copy.57 = bf16[128,512]{0,1:T(8,128)(2,1)S(1)} copy(bf16[128,512]{1,0:T(8,128)(2,1)} %param.7) | data formatting | bytes 262144 | tf_op args[2]
  2.9 0.7 %pad_maximum_fusion = bf16[2,128,512]{1,2,0:T(8,128)(2,1)} fusion(bf16[1,128,512]{1,2,0:T(8,128)(2,1)S(1)} %bitcast.226, bf16[1,128,512]{1,2,0:T(8,128)(2,1)S(1)} %bitcast.225), kind=kLoop, calls=%fused_computation.38 | loop fusion | flops 131072 | bytes 524288 | tf_op jit(solution)/shard_map/stack | solution.py:54
  3.6 5.0 %collective-permute-start.1 = (bf16[2,128,512]{1,2,0:T(8,128)(2,1)}, bf16[2,128,512]{1,2,0:T(8,128)(2,1)}, u32[]{:S(2)}, u32[]{:S(2)}) collective-permute-start(bf16[2,128,512]{1,2,0:T(8,128)(2,1)} %pad_maximum_fusion), channel_id=1, source_target_pairs={{0,4},{2,6},{4,8},{6,10},{8,12},{10,14},{12,16},{14,18},{16,20},{1... | collective-permute-start | bytes 786440 | tf_op jit(solution)/shard_map/ppermute | solution.py:16
  8.6 3.2 %collective-permute-start = (bf16[2,128,512]{1,2,0:T(8,128)(2,1)}, bf16[2,128,512]{1,2,0:T(8,128)(2,1)}, u32[]{:S(2)}, u32[]{:S(2)}) collective-permute-start(bf16[2,128,512]{1,2,0:T(8,128)(2,1)} %pad_maximum_fusion), channel_id=1, source_target_pairs={{0,2},{2,4},{4,6},{6,8},{8,10},{10,12},{12,14},{14,16},{16,18},{18... | collective-permute-start | bytes 786440 | tf_op jit(solution)/shard_map/ppermute | solution.py:16
  11.9 0.9 %reshape.256 = bf16[128,4,128]{2,1,0:T(4,128)(2,1)S(1)} reshape(bf16[128,512]{1,0:T(8,128)(2,1)} %param.6) | data formatting | bytes 262144 | tf_op jit(solution)/shard_map/reshape | solution.py:60
  12.8 0.9 %reshape.259 = bf16[128,4,128]{2,1,0:T(4,128)(2,1)S(1)} reshape(bf16[128,512]{1,0:T(8,128)(2,1)} %param.7) | data formatting | bytes 262144 | tf_op jit(solution)/shard_map/reshape | solution.py:61
  13.8 0.7 %copy.53 = s32[16,1]{1,0:T(8,128)S(1)} copy(s32[16,1]{0,1:T(1,128)} %bitcast.236) | data formatting | bytes 128 | tf_op jit(solution)/shard_map/reshape.234
  14.9 0.7 %copy.109 = bf16[128,4096]{0,1:T(8,128)(2,1)S(1)} copy(bf16[128,4096]{1,0:T(8,128)(2,1)S(1)} %copy-done) | data formatting | bytes 2097152 | tf_op jit(solution)/shard_map/reshape | solution.py:58
  16.6 1.0 %fusion = (f32[4,8,128]{2,1,0:T(8,128)S(1)}, f32[4,8,128]{2,1,0:T(8,128)S(1)}, f32[4,128,128,8]{2,1,3,0:T(8,128)S(1)}) fusion(f32[4,128,128,8]{2,1,3,0:T(8,128)S(1)} %get-tuple-element.63, f32[4,8,128]{2,1,0:T(8,128)S(1)} %get-tuple-element.62, pred[128,128]{0,1:T(8,128)(4,1)S(1)} %get-tuple-element.55, bf16[128,4,8,128]{3,2,1,0:T(8,128)(2,1)S(1)} %bitcast.212, ...), kind=kOutput, calls=%fused_computation.2 | convolution fusion | flops 137355264 | bytes 5439488 | tf_op jit(solution)/shard_map/tghd,sgd->ghts/dot_general | solution.py:72
  17.6 4.9 %collective-permute-done = bf16[2,128,512]{1,2,0:T(8,128)(2,1)} collective-permute-done((bf16[2,128,512]{1,2,0:T(8,128)(2,1)}, bf16[2,128,512]{1,2,0:T(8,128)(2,1)}, u32[]{:S(2)}, u32[]{:S(2)}) %collective-permute-start) | collective-permute-done | bytes 262176 | tf_op jit(solution)/shard_map/ppermute | solution.py:16
  22.4 1.0 %fusion.30 = (bf16[1,128,512]{1,2,0:T(8,128)(2,1)S(1)}, bf16[1,128,512]{1,2,0:T(8,128)(2,1)S(1)}) fusion(bf16[2,128,512]{1,2,0:T(8,128)(2,1)} %collective-permute-done), kind=kLoop, calls=%fused_computation.74 | loop fusion | bytes 524288 | tf_op jit(solution)/shard_map/slice | solution.py:78
  23.9 1.0 %multiply_reduce_fusion = (f32[4,8,128]{2,1,0:T(8,128)S(1)}, f32[4,8,128]{2,1,0:T(8,128)S(1)}, f32[4,8,128,128]{2,3,1,0:T(8,128)S(1)}, f32[4,8,128,128]{2,3,1,0:T(8,128)S(1)}) fusion(f32[4,8,128]{2,1,0:T(8,128)S(1)} %get-tuple-element.57, f32[4,128,128,8]{2,1,3,0:T(8,128)S(1)} %get-tuple-element.58, pred[128,128]{0,1:T(8,128)(4,1)S(1)} %get-tuple-element.56, ...), kind=kOutput, calls=%fused_computation.16 | convolution fusion | flops 137355264 | bytes 7536640 | tf_op jit(solution)/shard_map/tghd,sgd->ghts/dot_general | solution.py:83
  24.9 2.0 %collective-permute-done.1 = bf16[2,128,512]{1,2,0:T(8,128)(2,1)} collective-permute-done((bf16[2,128,512]{1,2,0:T(8,128)(2,1)}, bf16[2,128,512]{1,2,0:T(8,128)(2,1)}, u32[]{:S(2)}, u32[]{:S(2)}) %collective-permute-start.1) | collective-permute-done | bytes 262176 | tf_op jit(solution)/shard_map/ppermute | solution.py:16
  26.9 1.0 %fusion.29 = (bf16[1,128,512]{1,2,0:T(8,128)(2,1)S(1)}, bf16[1,128,512]{1,2,0:T(8,128)(2,1)S(1)}) fusion(bf16[2,128,512]{1,2,0:T(8,128)(2,1)} %collective-permute-done.1), kind=kLoop, calls=%fused_computation.73 | loop fusion | bytes 524288 | tf_op jit(solution)/shard_map/slice | solution.py:92
  28.5 1.0 %fusion.3 = (f32[4,8,128]{2,1,0:T(8,128)S(1)}, f32[4,8,128]{2,1,0:T(8,128)S(1)}, f32[4,128,128,8]{2,1,3,0:T(8,128)S(1)}) fusion(f32[4,128,128,8]{2,1,3,0:T(8,128)S(1)} %get-tuple-element.61, f32[4,8,128]{2,1,0:T(8,128)S(1)} %fusion.28, pred[128,128]{0,1:T(8,128)(4,1)S(1)} %get-tuple-element.54, bf16[128,4,128,1]{0,2,3,1:T(8,128)(2,1)S(1)} %bitcast.224, ...), kind=kOutput, calls=%fused_computation.7 | convolution fusion | flops 137355264 | bytes 5439488 | tf_op jit(solution)/shard_map/tghd,sgd->ghts/dot_general | solution.py:106
  29.5 1.4 %multiply_convert_fusion.1 = (bf16[4,8,128,128]{2,3,1,0:T(8,128)(2,1)S(1)}, bf16[4,8,128,128]{2,3,1,0:T(8,128)(2,1)S(1)}) fusion(f32[4,8,128,128]{2,3,1,0:T(8,128)S(1)} %get-tuple-element.18, f32[4,8,128,128]{2,3,1,0:T(8,128)S(1)} %get-tuple-element.17, f32[4,8,128]{2,1,0:T(8,128)S(1)} %get-tuple-element.50, f32[4,8,128]{2,1,0:T(8,128)S(1)} %bitcast.231, ...), kind=kLoop, calls=%fused_computation.14 | loop fusion | flops 6291456 | bytes 10567680 | tf_op jit(solution)/shard_map/convert_element_type | solution.py:116
  31.3 7.2 %collective-permute-start.3 = (bf16[4,128,128]{2,1,0:T(8,128)(2,1)S(1)}, bf16[4,128,128]{2,1,0:T(8,128)(2,1)S(1)}, u32[]{:S(2)}, u32[]{:S(2)}) collective-permute-start(bf16[4,128,128]{2,1,0:T(8,128)(2,1)S(1)} %fusion.12), channel_id=1, source_target_pairs={{4,0},{6,2},{8,4},{10,6},{12,8},{14,10},{16,12},{18,14},{20,16},{2... | collective-permute-start | bytes 393224 | tf_op jit(solution)/shard_map/ppermute | solution.py:16
  38.5 1.1 %fusion.13 = bf16[4,128,128]{2,1,0:T(8,128)(2,1)} fusion(bf16[4,8,128,128]{2,3,1,0:T(8,128)(2,1)S(1)} %get-tuple-element.23, bf16[128,4,8,128]{0,3,2,1:T(8,128)(2,1)S(1)} %bitcast.210), kind=kOutput, calls=%fused_computation.30 | convolution fusion | flops 134348800 | bytes 2228224 | tf_op jit(solution)/shard_map/ghts,tghd->gsd/dot_general | solution.py:41
  39.6 2.3 %collective-permute-start.2 = (bf16[4,128,128]{2,1,0:T(8,128)(2,1)}, bf16[4,128,128]{2,1,0:T(8,128)(2,1)S(1)}, u32[]{:S(2)}, u32[]{:S(2)}) collective-permute-start(bf16[4,128,128]{2,1,0:T(8,128)(2,1)} %fusion.13), channel_id=1, source_target_pairs={{2,0},{4,2},{6,4},{8,6},{10,8},{12,10},{14,12},{16,14},{18,16},{20... | collective-permute-start | bytes 393224 | tf_op jit(solution)/shard_map/ppermute | solution.py:16
  42.0 0.8 %fusion.2 = bf16[4,8,128,128]{2,3,1,0:T(8,128)(2,1)S(1)} fusion(f32[4,128,128,8]{2,1,3,0:T(8,128)S(1)} %get-tuple-element.65, f32[4,128,128,8]{2,1,3,0:T(8,128)S(1)} %get-tuple-element.63, f32[4,8,128]{2,1,0:T(8,128)S(1)} %bitcast.232, f32[4,8,128]{2,1,0:T(8,128)S(1)} %bitcast.235, f32[4,8,128]{2,1,0:T(8,128)S(1)} %get-tuple-element.62, ...), kind=kLoop, calls=%fused_computation.4 | loop fusion | flops 3670016 | bytes 5308416 | tf_op jit(solution)/shard_map/convert_element_type | solution.py:127
  44.1 1.3 %copy.77 = bf16[128,4096]{1,0:T(8,128)(2,1)} copy(bf16[128,4096]{0,1:T(8,128)(2,1)S(1)} %bitcast.215) | data formatting | bytes 2097152
  45.4 0.7 %collective-permute-done.2 = bf16[4,128,128]{2,1,0:T(8,128)(2,1)S(1)} collective-permute-done((bf16[4,128,128]{2,1,0:T(8,128)(2,1)}, bf16[4,128,128]{2,1,0:T(8,128)(2,1)S(1)}, u32[]{:S(2)}, u32[]{:S(2)}) %collective-permute-start.2) | collective-permute-done | bytes 131104 | tf_op jit(solution)/shard_map/ppermute | solution.py:16
  46.6 0.7 %pad_maximum_fusion.1 = bf16[128,512]{1,0:T(8,128)(2,1)} fusion(bf16[128,128]{1,0:T(8,128)(2,1)S(1)} %get-tuple-element.47, bf16[128,128]{1,0:T(8,128)(2,1)S(1)} %get-tuple-element.48, bf16[128,128]{1,0:T(8,128)(2,1)S(1)} %get-tuple-element.49, bf16[128,128]{1,0:T(8,128)(2,1)S(1)} %get-tuple-element.46), kind=kLoop, calls=%fused_computation.40 | loop fusion | flops 524288 | bytes 262144 | tf_op jit(solution)/shard_map/concatenate | solution.py:136
  (28 shorter events, 4.6 us)
Async XLA Ops:
  0.6 14.3 %copy-start = (bf16[128,4096]{1,0:T(8,128)(2,1)S(1)}, bf16[128,4096]{1,0:T(8,128)(2,1)}, u32[]{:S(2)}) copy-start(bf16[128,4096]{1,0:T(8,128)(2,1)} %param.5) | copy-start | bytes 3145732
  0.6 15.0 %copy-start.1 = (bf16[128,4096]{1,0:T(8,128)(2,1)S(1)}, bf16[128,4096]{1,0:T(8,128)(2,1)}, u32[]{:S(2)}) copy-start(bf16[128,4096]{1,0:T(8,128)(2,1)} %param.8) | copy-start | bytes 3145732
  3.6 23.3 %collective-permute-start.1 = (bf16[2,128,512]{1,2,0:T(8,128)(2,1)}, bf16[2,128,512]{1,2,0:T(8,128)(2,1)}, u32[]{:S(2)}, u32[]{:S(2)}) collective-permute-start(bf16[2,128,512]{1,2,0:T(8,128)(2,1)} %pad_maximum_fusion), channel_id=1, source_target_pairs={{0,4},{2,6},{4,8},{6,10},{8,12},{10,14},{12,16},{14,18},{16,20},{1... | collective-permute-start | bytes 786440 | tf_op jit(solution)/shard_map/ppermute | solution.py:16
  8.6 13.8 %collective-permute-start = (bf16[2,128,512]{1,2,0:T(8,128)(2,1)}, bf16[2,128,512]{1,2,0:T(8,128)(2,1)}, u32[]{:S(2)}, u32[]{:S(2)}) collective-permute-start(bf16[2,128,512]{1,2,0:T(8,128)(2,1)} %pad_maximum_fusion), channel_id=1, source_target_pairs={{0,2},{2,4},{4,6},{6,8},{8,10},{10,12},{12,14},{14,16},{16,18},{18... | collective-permute-start | bytes 786440 | tf_op jit(solution)/shard_map/ppermute | solution.py:16
  31.3 14.8 %collective-permute-start.3 = (bf16[4,128,128]{2,1,0:T(8,128)(2,1)S(1)}, bf16[4,128,128]{2,1,0:T(8,128)(2,1)S(1)}, u32[]{:S(2)}, u32[]{:S(2)}) collective-permute-start(bf16[4,128,128]{2,1,0:T(8,128)(2,1)S(1)} %fusion.12), channel_id=1, source_target_pairs={{4,0},{6,2},{8,4},{10,6},{12,8},{14,10},{16,12},{18,14},{20,16},{2... | collective-permute-start | bytes 393224 | tf_op jit(solution)/shard_map/ppermute | solution.py:16
  39.6 6.5 %collective-permute-start.2 = (bf16[4,128,128]{2,1,0:T(8,128)(2,1)}, bf16[4,128,128]{2,1,0:T(8,128)(2,1)S(1)}, u32[]{:S(2)}, u32[]{:S(2)}) collective-permute-start(bf16[4,128,128]{2,1,0:T(8,128)(2,1)} %fusion.13), channel_id=1, source_target_pairs={{2,0},{4,2},{6,4},{8,6},{10,8},{12,10},{14,12},{16,14},{18,16},{20... | collective-permute-start | bytes 393224 | tf_op jit(solution)/shard_map/ppermute | solution.py:16

commit v17 on v16

--- a/solution.py
+++ b/solution.py
@@ -53,7 +53,7 @@
     axes = ("ctx", "uly")
     key_value = jnp.stack([key_vectors, value_vectors])
     near_rim = shifted(key_value, axes, 1)
-    far_rim = shifted(key_value, axes, 2)
+    far_rim = shifted(lax.optimization_barrier(key_value), axes, 2)
     device_index = lax.axis_index(axes)
     query_heads = queries.reshape(rows, KVH, GROUP, HD)
     grad_heads = output_grad.reshape(rows, KVH, GROUP, HD)

time: 48.1 us -> 44.4 us (0.923)
  starting transfers between devices: 17.8 us -> 13.2 us
  waiting for transfers between devices: 7.56 us -> 8.55 us
    ppermute x4, starting transfers between devices: 17.8 us -> 13.2 us  [shifted(): return lax.ppermute(block, axis, route)]
    ppermute x4, waiting for transfers between devices: 7.56 us -> 8.55 us  [shifted(): return lax.ppermute(block, axis, route)]
  transfers between devices with their start and end apart: 4 -> 4, of which waited for: 3 -> 2; matrix products, arithmetic and copies ran while one was open for 27% -> 29% of each run, Pallas kernels for 0% -> 0%
where the time goes in v17:
time: 44.4 us; the launch traced here: 43.7 us
  starting transfers between devices  13.2 us (30%)
  local copies, waits for them, and re-layouts  9.16 us (21%)
  waiting for transfers between devices  8.55 us (19%)
  matrix products  7.75 us (17%)
  other arithmetic  4.11 us (9%)
  between operations  0.91 us (2%)
    ppermute x4, starting transfers between devices, shifted(): return lax.ppermute(block, axis, route)  13.2 us
    ppermute x4, waiting for transfers between devices, shifted(): return lax.ppermute(block, axis, route)  8.55 us
    unnamed x8, local copies, waits for them, and re-layouts  3.76 us
    dot_general x3, matrix products, key_grad_of(): jnp.einsum('ghts,tghd->gsd', grad_s, query_heads, preferred_element_type=...  1.97 us
    dot_general x3, matrix products, scores_of(): jnp.einsum('tghd,sgd->ghts', query_heads, key_heads, preferred_element_ty...  1.52 us
    convert_element_type x1, other arithmetic, body(): (near_exp / row_sum * (near_grad_p - row_delta)).astype(jnp.bfloat16)  1.4 us
    dot_general x3, matrix products, query_grad_of(): jnp.einsum('ghts,sgd->ghtd', grad_s, keys, preferred_element_type=jnp.flo...  1.32 us
    reshape x2, local copies, waits for them, and re-layouts, body(): own_keys = key_vectors.reshape(rows, KVH, HD)  1.08 us
  transfers between devices with their start and end apart: 4, of which 2 were waited for; matrix products, arithmetic and copies ran while one was open for 29% of the time, Pallas kernels for 0%

profile of v17, /device:TPU:1, one launch (start us, length us, event | category | flops | bytes accessed | tf_op | source)
XLA Modules:
  0.0 43.7 jit_solution(12766845559883033193)
XLA Ops:
  0.6 1.2 %copy.56 = bf16[128,512]{0,1:T(8,128)(2,1)S(1)} copy(bf16[128,512]{1,0:T(8,128)(2,1)} %param.6) | data formatting | bytes 262144 | tf_op args[1]
  1.8 1.0 %copy.57 = bf16[128,512]{0,1:T(8,128)(2,1)S(1)} copy(bf16[128,512]{1,0:T(8,128)(2,1)} %param.7) | data formatting | bytes 262144 | tf_op args[2]
  2.9 0.7 %pad_maximum_fusion = bf16[2,128,512]{1,2,0:T(8,128)(2,1)} fusion(bf16[1,128,512]{1,2,0:T(8,128)(2,1)S(1)} %bitcast.226, bf16[1,128,512]{1,2,0:T(8,128)(2,1)S(1)} %bitcast.225), kind=kLoop, calls=%fused_computation.38 | loop fusion | flops 131072 | bytes 524288 | tf_op jit(solution)/shard_map/stack | solution.py:54
  3.6 4.0 %collective-permute-start = (bf16[2,128,512]{1,2,0:T(8,128)(2,1)}, bf16[2,128,512]{1,2,0:T(8,128)(2,1)}, u32[]{:S(2)}, u32[]{:S(2)}) collective-permute-start(bf16[2,128,512]{1,2,0:T(8,128)(2,1)} %pad_maximum_fusion), channel_id=1, source_target_pairs={{0,2},{2,4},{4,6},{6,8},{8,10},{10,12},{12,14},{14,16},{16,18},{18... | collective-permute-start | bytes 786440 | tf_op jit(solution)/shard_map/ppermute | solution.py:16
  7.6 4.2 %collective-permute-start.1 = (bf16[2,128,512]{1,2,0:T(8,128)(2,1)}, bf16[2,128,512]{1,2,0:T(8,128)(2,1)}, u32[]{:S(2)}, u32[]{:S(2)}) collective-permute-start(bf16[2,128,512]{1,2,0:T(8,128)(2,1)} %pad_maximum_fusion), channel_id=1, source_target_pairs={{0,4},{2,6},{4,8},{6,10},{8,12},{10,14},{12,16},{14,18},{16,20},{1... | collective-permute-start | bytes 786440 | tf_op jit(solution)/shard_map/ppermute | solution.py:16
  11.9 0.9 %reshape.256 = bf16[128,4,128]{2,1,0:T(4,128)(2,1)S(1)} reshape(bf16[128,512]{1,0:T(8,128)(2,1)} %param.6) | data formatting | bytes 262144 | tf_op jit(solution)/shard_map/reshape | solution.py:60
  12.8 0.9 %reshape.259 = bf16[128,4,128]{2,1,0:T(4,128)(2,1)S(1)} reshape(bf16[128,512]{1,0:T(8,128)(2,1)} %param.7) | data formatting | bytes 262144 | tf_op jit(solution)/shard_map/reshape | solution.py:61
  13.8 0.7 %copy.53 = s32[16,1]{1,0:T(8,128)S(1)} copy(s32[16,1]{0,1:T(1,128)} %bitcast.236) | data formatting | bytes 128 | tf_op jit(solution)/shard_map/reshape.234
  14.9 0.7 %copy.109 = bf16[128,4096]{0,1:T(8,128)(2,1)S(1)} copy(bf16[128,4096]{1,0:T(8,128)(2,1)S(1)} %copy-done) | data formatting | bytes 2097152 | tf_op jit(solution)/shard_map/reshape | solution.py:58
  16.0 0.5 %fusion.6 = (f32[4,8,128]{2,1,0:T(8,128)S(1)}, f32[4,128,128,8]{2,1,3,0:T(8,128)S(1)}) fusion(pred[128,128]{0,1:T(8,128)(4,1)S(1)} %get-tuple-element.55, bf16[128,4,128,1]{0,2,3,1:T(8,128)(2,1)S(1)} %copy.87, bf16[128,4,8,128]{0,3,2,1:T(8,128)(2,1)S(1)} %bitcast.206), kind=kOutput, calls=%fused_computation.19 | convolution fusion | flops 135786496 | bytes 3309568 | tf_op jit(solution)/shard_map/tghd,sgd->ghts/dot_general | solution.py:33
  16.6 1.0 %fusion = (f32[4,8,128]{2,1,0:T(8,128)S(1)}, f32[4,8,128]{2,1,0:T(8,128)S(1)}, f32[4,128,128,8]{2,1,3,0:T(8,128)S(1)}) fusion(f32[4,128,128,8]{2,1,3,0:T(8,128)S(1)} %get-tuple-element.63, f32[4,8,128]{2,1,0:T(8,128)S(1)} %get-tuple-element.62, pred[128,128]{0,1:T(8,128)(4,1)S(1)} %get-tuple-element.55, bf16[128,4,8,128]{3,2,1,0:T(8,128)(2,1)S(1)} %bitcast.212, ...), kind=kOutput, calls=%fused_computation.2 | convolution fusion | flops 137355264 | bytes 5439488 | tf_op jit(solution)/shard_map/tghd,sgd->ghts/dot_general | solution.py:72
  17.6 1.0 %fusion.30 = (bf16[1,128,512]{1,2,0:T(8,128)(2,1)S(1)}, bf16[1,128,512]{1,2,0:T(8,128)(2,1)S(1)}) fusion(bf16[2,128,512]{1,2,0:T(8,128)(2,1)} %collective-permute-done), kind=kLoop, calls=%fused_computation.74 | loop fusion | bytes 524288 | tf_op jit(solution)/shard_map/slice | solution.py:78
  19.1 1.0 %multiply_reduce_fusion = (f32[4,8,128]{2,1,0:T(8,128)S(1)}, f32[4,8,128]{2,1,0:T(8,128)S(1)}, f32[4,8,128,128]{2,3,1,0:T(8,128)S(1)}, f32[4,8,128,128]{2,3,1,0:T(8,128)S(1)}) fusion(f32[4,8,128]{2,1,0:T(8,128)S(1)} %get-tuple-element.57, f32[4,128,128,8]{2,1,3,0:T(8,128)S(1)} %get-tuple-element.58, pred[128,128]{0,1:T(8,128)(4,1)S(1)} %get-tuple-element.56, ...), kind=kOutput, calls=%fused_computation.16 | convolution fusion | flops 137355264 | bytes 7536640 | tf_op jit(solution)/shard_map/tghd,sgd->ghts/dot_general | solution.py:83
  20.1 8.5 %collective-permute-done.1 = bf16[2,128,512]{1,2,0:T(8,128)(2,1)} collective-permute-done((bf16[2,128,512]{1,2,0:T(8,128)(2,1)}, bf16[2,128,512]{1,2,0:T(8,128)(2,1)}, u32[]{:S(2)}, u32[]{:S(2)}) %collective-permute-start.1) | collective-permute-done | bytes 262176 | tf_op jit(solution)/shard_map/ppermute | solution.py:16
  28.5 1.0 %fusion.29 = (bf16[1,128,512]{1,2,0:T(8,128)(2,1)S(1)}, bf16[1,128,512]{1,2,0:T(8,128)(2,1)S(1)}) fusion(bf16[2,128,512]{1,2,0:T(8,128)(2,1)} %collective-permute-done.1), kind=kLoop, calls=%fused_computation.73 | loop fusion | bytes 524288 | tf_op jit(solution)/shard_map/slice | solution.py:92
  29.5 0.5 %fusion.8 = (f32[4,8,128]{2,1,0:T(8,128)S(1)}, f32[4,128,128,8]{2,1,3,0:T(8,128)S(1)}) fusion(pred[128,128]{0,1:T(8,128)(4,1)S(1)} %get-tuple-element.54, bf16[128,4,128,1]{0,2,3,1:T(8,128)(2,1)S(1)} %bitcast.218, bf16[128,4,8,128]{0,3,2,1:T(8,128)(2,1)S(1)} %bitcast.208), kind=kOutput, calls=%fused_computation.21 | convolution fusion | flops 135786496 | bytes 3309568 | tf_op jit(solution)/shard_map/tghd,sgd->ghts/dot_general | solution.py:33
  30.1 1.0 %fusion.3 = (f32[4,8,128]{2,1,0:T(8,128)S(1)}, f32[4,8,128]{2,1,0:T(8,128)S(1)}, f32[4,128,128,8]{2,1,3,0:T(8,128)S(1)}) fusion(f32[4,128,128,8]{2,1,3,0:T(8,128)S(1)} %get-tuple-element.61, f32[4,8,128]{2,1,0:T(8,128)S(1)} %fusion.28, pred[128,128]{0,1:T(8,128)(4,1)S(1)} %get-tuple-element.54, bf16[128,4,128,1]{0,2,3,1:T(8,128)(2,1)S(1)} %bitcast.224, ...), kind=kOutput, calls=%fused_computation.7 | convolution fusion | flops 137355264 | bytes 5439488 | tf_op jit(solution)/shard_map/tghd,sgd->ghts/dot_general | solution.py:106
  31.1 1.4 %multiply_convert_fusion.1 = (bf16[4,8,128,128]{2,3,1,0:T(8,128)(2,1)S(1)}, bf16[4,8,128,128]{2,3,1,0:T(8,128)(2,1)S(1)}) fusion(f32[4,8,128,128]{2,3,1,0:T(8,128)S(1)} %get-tuple-element.18, f32[4,8,128,128]{2,3,1,0:T(8,128)S(1)} %get-tuple-element.17, f32[4,8,128]{2,1,0:T(8,128)S(1)} %get-tuple-element.50, f32[4,8,128]{2,1,0:T(8,128)S(1)} %bitcast.231, ...), kind=kLoop, calls=%fused_computation.14 | loop fusion | flops 6291456 | bytes 10567680 | tf_op jit(solution)/shard_map/convert_element_type | solution.py:116
  32.9 1.9 %collective-permute-start.3 = (bf16[4,128,128]{2,1,0:T(8,128)(2,1)S(1)}, bf16[4,128,128]{2,1,0:T(8,128)(2,1)S(1)}, u32[]{:S(2)}, u32[]{:S(2)}) collective-permute-start(bf16[4,128,128]{2,1,0:T(8,128)(2,1)S(1)} %fusion.12), channel_id=1, source_target_pairs={{4,0},{6,2},{8,4},{10,6},{12,8},{14,10},{16,12},{18,14},{20,16},{2... | collective-permute-start | bytes 393224 | tf_op jit(solution)/shard_map/ppermute | solution.py:16
  34.9 1.1 %fusion.13 = bf16[4,128,128]{2,1,0:T(8,128)(2,1)} fusion(bf16[4,8,128,128]{2,3,1,0:T(8,128)(2,1)S(1)} %get-tuple-element.23, bf16[128,4,8,128]{0,3,2,1:T(8,128)(2,1)S(1)} %bitcast.210), kind=kOutput, calls=%fused_computation.30 | convolution fusion | flops 134348800 | bytes 2228224 | tf_op jit(solution)/shard_map/ghts,tghd->gsd/dot_general | solution.py:41
  36.0 3.0 %collective-permute-start.2 = (bf16[4,128,128]{2,1,0:T(8,128)(2,1)}, bf16[4,128,128]{2,1,0:T(8,128)(2,1)S(1)}, u32[]{:S(2)}, u32[]{:S(2)}) collective-permute-start(bf16[4,128,128]{2,1,0:T(8,128)(2,1)} %fusion.13), channel_id=1, source_target_pairs={{2,0},{4,2},{6,4},{8,6},{10,8},{12,10},{14,12},{16,14},{18,16},{20... | collective-permute-start | bytes 393224 | tf_op jit(solution)/shard_map/ppermute | solution.py:16
  39.0 0.8 %fusion.2 = bf16[4,8,128,128]{2,3,1,0:T(8,128)(2,1)S(1)} fusion(f32[4,128,128,8]{2,1,3,0:T(8,128)S(1)} %get-tuple-element.65, f32[4,128,128,8]{2,1,3,0:T(8,128)S(1)} %get-tuple-element.63, f32[4,8,128]{2,1,0:T(8,128)S(1)} %bitcast.232, f32[4,8,128]{2,1,0:T(8,128)S(1)} %bitcast.235, f32[4,8,128]{2,1,0:T(8,128)S(1)} %get-tuple-element.62, ...), kind=kLoop, calls=%fused_computation.4 | loop fusion | flops 3670016 | bytes 5308416 | tf_op jit(solution)/shard_map/convert_element_type | solution.py:127
  41.1 1.3 %copy.77 = bf16[128,4096]{1,0:T(8,128)(2,1)} copy(bf16[128,4096]{0,1:T(8,128)(2,1)S(1)} %bitcast.215) | data formatting | bytes 2097152
  43.0 0.7 %pad_maximum_fusion.1 = bf16[128,512]{1,0:T(8,128)(2,1)} fusion(bf16[128,128]{1,0:T(8,128)(2,1)S(1)} %get-tuple-element.47, bf16[128,128]{1,0:T(8,128)(2,1)S(1)} %get-tuple-element.48, bf16[128,128]{1,0:T(8,128)(2,1)S(1)} %get-tuple-element.49, bf16[128,128]{1,0:T(8,128)(2,1)S(1)} %get-tuple-element.46), kind=kLoop, calls=%fused_computation.40 | loop fusion | flops 524288 | bytes 262144 | tf_op jit(solution)/shard_map/concatenate | solution.py:136
  (28 shorter events, 3.7 us)
Async XLA Ops:
  0.6 14.3 %copy-start = (bf16[128,4096]{1,0:T(8,128)(2,1)S(1)}, bf16[128,4096]{1,0:T(8,128)(2,1)}, u32[]{:S(2)}) copy-start(bf16[128,4096]{1,0:T(8,128)(2,1)} %param.5) | copy-start | bytes 3145732
  0.6 15.0 %copy-start.1 = (bf16[128,4096]{1,0:T(8,128)(2,1)S(1)}, bf16[128,4096]{1,0:T(8,128)(2,1)}, u32[]{:S(2)}) copy-start(bf16[128,4096]{1,0:T(8,128)(2,1)} %param.8) | copy-start | bytes 3145732
  3.6 14.0 %collective-permute-start = (bf16[2,128,512]{1,2,0:T(8,128)(2,1)}, bf16[2,128,512]{1,2,0:T(8,128)(2,1)}, u32[]{:S(2)}, u32[]{:S(2)}) collective-permute-start(bf16[2,128,512]{1,2,0:T(8,128)(2,1)} %pad_maximum_fusion), channel_id=1, source_target_pairs={{0,2},{2,4},{4,6},{6,8},{8,10},{10,12},{12,14},{14,16},{16,18},{18... | collective-permute-start | bytes 786440 | tf_op jit(solution)/shard_map/ppermute | solution.py:16
  7.6 20.9 %collective-permute-start.1 = (bf16[2,128,512]{1,2,0:T(8,128)(2,1)}, bf16[2,128,512]{1,2,0:T(8,128)(2,1)}, u32[]{:S(2)}, u32[]{:S(2)}) collective-permute-start(bf16[2,128,512]{1,2,0:T(8,128)(2,1)} %pad_maximum_fusion), channel_id=1, source_target_pairs={{0,4},{2,6},{4,8},{6,10},{8,12},{10,14},{12,16},{14,18},{16,20},{1... | collective-permute-start | bytes 786440 | tf_op jit(solution)/shard_map/ppermute | solution.py:16
  32.9 9.6 %collective-permute-start.3 = (bf16[4,128,128]{2,1,0:T(8,128)(2,1)S(1)}, bf16[4,128,128]{2,1,0:T(8,128)(2,1)S(1)}, u32[]{:S(2)}, u32[]{:S(2)}) collective-permute-start(bf16[4,128,128]{2,1,0:T(8,128)(2,1)S(1)} %fusion.12), channel_id=1, source_target_pairs={{4,0},{6,2},{8,4},{10,6},{12,8},{14,10},{16,12},{18,14},{20,16},{2... | collective-permute-start | bytes 393224 | tf_op jit(solution)/shard_map/ppermute | solution.py:16
  36.0 6.5 %collective-permute-start.2 = (bf16[4,128,128]{2,1,0:T(8,128)(2,1)}, bf16[4,128,128]{2,1,0:T(8,128)(2,1)S(1)}, u32[]{:S(2)}, u32[]{:S(2)}) collective-permute-start(bf16[4,128,128]{2,1,0:T(8,128)(2,1)} %fusion.13), channel_id=1, source_target_pairs={{2,0},{4,2},{6,4},{8,6},{10,8},{12,10},{14,12},{16,14},{18,16},{20... | collective-permute-start | bytes 393224 | tf_op jit(solution)/shard_map/ppermute | solution.py:16

commit v18 on v17

--- a/solution.py
+++ b/solution.py
@@ -53,7 +53,8 @@
     axes = ("ctx", "uly")
     key_value = jnp.stack([key_vectors, value_vectors])
     near_rim = shifted(key_value, axes, 1)
-    far_rim = shifted(lax.optimization_barrier(key_value), axes, 2)
+    far_sources = lax.optimization_barrier((key_vectors, value_vectors, key_value))[:2]
+    far_rim = tuple(shifted(source, axes, 2) for source in far_sources)
     device_index = lax.axis_index(axes)
     query_heads = queries.reshape(rows, KVH, GROUP, HD)
     grad_heads = output_grad.reshape(rows, KVH, GROUP, HD)

time: 44.4 us -> 54.2 us (1.22)
  waiting for transfers between devices: 8.55 us -> 0.73 us
  matrix products: 7.75 us -> 14.7 us
  starting transfers between devices: 13.2 us -> 18.8 us
  local copies, waits for them, and re-layouts: 9.16 us -> 13.1 us
  other arithmetic: 4.11 us -> 5.13 us
    ppermute x4 -> x5, waiting for transfers between devices: 8.55 us -> 0.73 us  [shifted(): return lax.ppermute(block, axis, route)]
    ppermute x4 -> x5, starting transfers between devices: 13.2 us -> 18.8 us  [shifted(): return lax.ppermute(block, axis, route)]
    reshape x0 -> x3, local copies, waits for them, and re-layouts: none -> 3.32 us  [the longest x2 1.72 us: body(): far_keys = far_rim[0].reshape(rows, KVH, HD)]
    dot_general x1, matrix products: 0.98 us -> 3.52 us  [body(): jnp.einsum('tghd,sgd->ghts', grad_heads, near_values, preferred_element_t...]
    dot_general x1, matrix products: 0.99 us -> 2.85 us  [body(): jnp.einsum('tghd,sgd->ghts', grad_heads, own_values, preferred_element_ty...]
    dot_general x3, matrix products: 1.97 us -> 3.59 us  [key_grad_of(): jnp.einsum('ghts,tghd->gsd', grad_s, query_heads, preferred_element_type=...]
    unnamed x8 -> x56, local copies, waits for them, and re-layouts: 3.76 us -> 5.35 us
    slice x1 -> x0, local copies, waits for them, and re-layouts: 0.99 us -> none  [body(): far_keys = far_rim[0].reshape(rows, KVH, HD)]
  transfers between devices with their start and end apart: 4 -> 5, of which waited for: 2 -> 1; matrix products, arithmetic and copies ran while one was open for 29% -> 34% of each run, Pallas kernels for 0% -> 0%
where the time goes in v18:
time: 54.2 us; the launch traced here: 53.6 us
  starting transfers between devices  18.8 us (35%)
  matrix products  14.7 us (27%)
  local copies, waits for them, and re-layouts  13.1 us (24%)
  other arithmetic  5.13 us (9%)
  between operations  1.15 us (2%)
  waiting for transfers between devices  0.73 us (1%)
    ppermute x5, starting transfers between devices, shifted(): return lax.ppermute(block, axis, route)  18.8 us
    unnamed x56, local copies, waits for them, and re-layouts  5.35 us
    dot_general x3, matrix products, key_grad_of(): jnp.einsum('ghts,tghd->gsd', grad_s, query_heads, preferred_element_type=...  3.59 us
    dot_general x1, matrix products, body(): jnp.einsum('tghd,sgd->ghts', grad_heads, near_values, preferred_element_t...  3.52 us
    dot_general x1, matrix products, body(): jnp.einsum('tghd,sgd->ghts', grad_heads, own_values, preferred_element_ty...  2.85 us
    dot_general x3, matrix products, scores_of(): jnp.einsum('tghd,sgd->ghts', query_heads, key_heads, preferred_element_ty...  2.35 us
    reshape x2, local copies, waits for them, and re-layouts, body(): far_keys = far_rim[0].reshape(rows, KVH, HD)  1.72 us
    reshape x1, local copies, waits for them, and re-layouts, body(): far_values = far_rim[1].reshape(rows, KVH, HD)  1.6 us
  transfers between devices with their start and end apart: 5, of which 1 were waited for; matrix products, arithmetic and copies ran while one was open for 34% of the time, Pallas kernels for 0%

profile of v18, /device:TPU:1, one launch (start us, length us, event | category | flops | bytes accessed | tf_op | source)
XLA Modules:
  0.0 53.6 jit_solution(14155944760755731378)
XLA Ops:
  0.6 1.2 %copy.59 = bf16[128,512]{0,1:T(8,128)(2,1)S(1)} copy(bf16[128,512]{1,0:T(8,128)(2,1)} %param.6) | data formatting | bytes 262144 | tf_op args[1]
  1.8 1.0 %copy.60 = bf16[128,512]{0,1:T(8,128)(2,1)S(1)} copy(bf16[128,512]{1,0:T(8,128)(2,1)} %param.7) | data formatting | bytes 262144 | tf_op args[2]
  2.9 0.7 %pad_maximum_fusion = bf16[2,128,512]{1,2,0:T(8,128)(2,1)} fusion(bf16[1,128,512]{1,2,0:T(8,128)(2,1)S(1)} %bitcast.214, bf16[1,128,512]{1,2,0:T(8,128)(2,1)S(1)} %bitcast.213), kind=kLoop, calls=%fused_computation.38 | loop fusion | flops 131072 | bytes 524288 | tf_op jit(solution)/shard_map/stack | solution.py:54
  3.6 4.0 %collective-permute-start = (bf16[2,128,512]{1,2,0:T(8,128)(2,1)}, bf16[2,128,512]{1,2,0:T(8,128)(2,1)}, u32[]{:S(2)}, u32[]{:S(2)}) collective-permute-start(bf16[2,128,512]{1,2,0:T(8,128)(2,1)} %pad_maximum_fusion), channel_id=1, source_target_pairs={{0,2},{2,4},{4,6},{6,8},{8,10},{10,12},{12,14},{14,16},{16,18},{18... | collective-permute-start | bytes 786440 | tf_op jit(solution)/shard_map/ppermute | solution.py:16
  7.6 4.2 %collective-permute-start.1 = (bf16[128,512]{1,0:T(8,128)(2,1)}, bf16[128,512]{1,0:T(8,128)(2,1)S(1)}, u32[]{:S(2)}, u32[]{:S(2)}) collective-permute-start(bf16[128,512]{1,0:T(8,128)(2,1)} %param.6), channel_id=1, source_target_pairs={{0,4},{2,6},{4,8},{6,10},{8,12},{10,14},{12,16},{14,18},{16,20},{1... | collective-permute-start | bytes 393224 | tf_op jit(solution)/shard_map/ppermute | solution.py:16
  11.9 3.8 %collective-permute-start.2 = (bf16[128,512]{1,0:T(8,128)(2,1)}, bf16[128,512]{1,0:T(8,128)(2,1)}, u32[]{:S(2)}, u32[]{:S(2)}) collective-permute-start(bf16[128,512]{1,0:T(8,128)(2,1)} %param.7), channel_id=1, source_target_pairs={{0,4},{2,6},{4,8},{6,10},{8,12},{10,14},{12,16},{14,18},{16,20},{1... | collective-permute-start | bytes 393224 | tf_op jit(solution)/shard_map/ppermute | solution.py:16
  15.7 0.9 %reshape.262 = bf16[128,4,128]{2,1,0:T(4,128)(2,1)S(1)} reshape(bf16[128,512]{1,0:T(8,128)(2,1)} %param.6) | data formatting | bytes 262144 | tf_op jit(solution)/shard_map/reshape | solution.py:61
  16.7 0.9 %reshape.267 = bf16[128,4,128]{2,1,0:T(4,128)(2,1)S(1)} reshape(bf16[128,512]{1,0:T(8,128)(2,1)} %param.7) | data formatting | bytes 262144 | tf_op jit(solution)/shard_map/reshape | solution.py:62
  20.6 0.8 %compare_and_fusion.1 = (pred[128,128]{0,1:T(8,128)(4,1)}, pred[128,128]{0,1:T(8,128)(4,1)S(1)}, pred[128,128]{0,1:T(8,128)(4,1)S(1)}) fusion(s32[128]{0:T(128)S(1)} %copy-done.20, s32[128]{0:T(128)S(1)} %copy-done.25, s32[128]{0:T(128)S(1)} %copy-done.22, s32[128]{0:T(128)S(1)} %get-tuple-element.71, s32[128]{0:T(128)S(1)} %copy-done.24, ...), kind=kLoop, calls=%fused_computation.44 | loop fusion | flops 147456 | bytes 52224 | tf_op jit(solution)/shard_map/and | solution.py:28
  21.9 2.9 %fusion = (f32[4,8,128]{2,1,0:T(8,128)}, f32[4,8,128]{2,1,0:T(8,128)}, f32[4,128,128,8]{2,1,3,0:T(8,128)}) fusion(f32[4,128,128,8]{2,1,3,0:T(8,128)S(1)} %get-tuple-element.67, f32[4,8,128]{2,1,0:T(8,128)S(1)} %get-tuple-element.66, pred[128,128]{0,1:T(8,128)(4,1)S(1)} %get-tuple-element.59, bf16[128,4,8,128]{3,2,1,0:T(8,128)(2,1)S(1)} %bitcast.201, ...), kind=kOutput, calls=%fused_computation.2 | convolution fusion | flops 137355264 | bytes 5439488 | tf_op jit(solution)/shard_map/tghd,sgd->ghts/dot_general | solution.py:73
  24.8 1.0 %fusion.30 = (bf16[1,128,512]{1,2,0:T(8,128)(2,1)S(1)}, bf16[1,128,512]{1,2,0:T(8,128)(2,1)S(1)}) fusion(bf16[2,128,512]{1,2,0:T(8,128)(2,1)} %collective-permute-done), kind=kLoop, calls=%fused_computation.74 | loop fusion | bytes 524288 | tf_op jit(solution)/shard_map/slice | solution.py:79
  26.3 3.5 %multiply_reduce_fusion = (f32[4,8,128]{2,1,0:T(8,128)}, f32[4,8,128]{2,1,0:T(8,128)}, f32[4,8,128,128]{2,3,1,0:T(8,128)}, f32[4,8,128,128]{2,3,1,0:T(8,128)}) fusion(f32[4,8,128]{2,1,0:T(8,128)S(1)} %get-tuple-element.61, f32[4,128,128,8]{2,1,3,0:T(8,128)S(1)} %get-tuple-element.62, pred[128,128]{0,1:T(8,128)(4,1)S(1)} %get-tuple-element.60, ...), kind=kOutput, calls=%fused_computation.16 | convolution fusion | flops 137355264 | bytes 7536640 | tf_op jit(solution)/shard_map/tghd,sgd->ghts/dot_general | solution.py:84
  30.5 1.0 %copy.93 = bf16[128,4,128,1]{0,2,3,1:T(8,128)(2,1)S(1)} copy(bf16[128,4,128,1]{2,1,0,3:T(4,128)(2,1)} %bitcast.212) | data formatting | bytes 262144 | tf_op jit(solution)/shard_map/reshape | solution.py:93
  31.5 1.6 %reshape.266 = bf16[128,4,128]{2,1,0:T(4,128)(2,1)} reshape(bf16[128,512]{1,0:T(8,128)(2,1)} %collective-permute-done.2) | data formatting | bytes 262144 | tf_op jit(solution)/shard_map/reshape | solution.py:94
  33.2 1.3 %fusion.8 = (f32[4,8,128]{2,1,0:T(8,128)S(1)}, f32[4,128,128,8]{2,1,3,0:T(8,128)S(1)}) fusion(pred[128,128]{0,1:T(8,128)(4,1)} %get-tuple-element.58, bf16[128,4,128,1]{0,2,3,1:T(8,128)(2,1)S(1)} %copy.93, bf16[128,4,8,128]{0,3,2,1:T(8,128)(2,1)S(1)} %bitcast.197), kind=kOutput, calls=%fused_computation.21 | convolution fusion | flops 135786496 | bytes 3309568 | tf_op jit(solution)/shard_map/tghd,sgd->ghts/dot_general | solution.py:33
  34.6 1.0 %fusion.3 = (f32[4,8,128]{2,1,0:T(8,128)S(1)}, f32[4,8,128]{2,1,0:T(8,128)S(1)}, f32[4,128,128,8]{2,1,3,0:T(8,128)S(1)}) fusion(f32[4,128,128,8]{2,1,3,0:T(8,128)S(1)} %get-tuple-element.65, f32[4,8,128]{2,1,0:T(8,128)S(1)} %fusion.29, pred[128,128]{0,1:T(8,128)(4,1)S(1)} %copy-done.12, bf16[128,4,8,128]{3,2,1,0:T(8,128)(2,1)S(1)} %bitcast.203, ...), kind=kOutput, calls=%fused_computation.7 | convolution fusion | flops 137355264 | bytes 5439488 | tf_op jit(solution)/shard_map/tghd,sgd->ghts/dot_general | solution.py:107
  36.8 1.3 %multiply_convert_fusion.1 = (bf16[4,8,128,128]{2,3,1,0:T(8,128)(2,1)S(1)}, bf16[4,8,128,128]{2,3,1,0:T(8,128)(2,1)S(1)}) fusion(f32[4,8,128,128]{2,3,1,0:T(8,128)S(1)} %copy-done.5, f32[4,8,128,128]{2,3,1,0:T(8,128)S(1)} %copy-done.4, f32[4,8,128]{2,1,0:T(8,128)S(1)} %get-tuple-element.54, f32[4,8,128]{2,1,0:T(8,128)S(1)} %bitcast.219, ...), kind=kLoop, calls=%fused_computation.14 | loop fusion | flops 6291456 | bytes 10567680 | tf_op jit(solution)/shard_map/convert_element_type | solution.py:117
  38.1 1.1 %fusion.12 = bf16[4,128,128]{2,1,0:T(8,128)(2,1)} fusion(bf16[4,8,128,128]{2,3,1,0:T(8,128)(2,1)S(1)} %get-tuple-element.28, bf16[128,4,8,128]{0,3,2,1:T(8,128)(2,1)S(1)} %bitcast.198), kind=kOutput, calls=%fused_computation.29 | convolution fusion | flops 134348800 | bytes 2228224 | tf_op jit(solution)/shard_map/ghts,tghd->gsd/dot_general | solution.py:41
  39.2 2.7 %collective-permute-start.4 = (bf16[4,128,128]{2,1,0:T(8,128)(2,1)}, bf16[4,128,128]{2,1,0:T(8,128)(2,1)}, u32[]{:S(2)}, u32[]{:S(2)}) collective-permute-start(bf16[4,128,128]{2,1,0:T(8,128)(2,1)} %fusion.12), channel_id=1, source_target_pairs={{4,0},{6,2},{8,4},{10,6},{12,8},{14,10},{16,12},{18,14},{20,16},{2... | collective-permute-start | bytes 393224 | tf_op jit(solution)/shard_map/ppermute | solution.py:16
  41.9 1.1 %fusion.13 = bf16[4,128,128]{2,1,0:T(8,128)(2,1)} fusion(bf16[4,8,128,128]{2,3,1,0:T(8,128)(2,1)S(1)} %get-tuple-element.29, bf16[128,4,8,128]{0,3,2,1:T(8,128)(2,1)S(1)} %bitcast.199), kind=kOutput, calls=%fused_computation.30 | convolution fusion | flops 134348800 | bytes 2228224 | tf_op jit(solution)/shard_map/ghts,tghd->gsd/dot_general | solution.py:41
  43.0 4.1 %collective-permute-start.3 = (bf16[4,128,128]{2,1,0:T(8,128)(2,1)}, bf16[4,128,128]{2,1,0:T(8,128)(2,1)}, u32[]{:S(2)}, u32[]{:S(2)}) collective-permute-start(bf16[4,128,128]{2,1,0:T(8,128)(2,1)} %fusion.13), channel_id=1, source_target_pairs={{2,0},{4,2},{6,4},{8,6},{10,8},{12,10},{14,12},{16,14},{18,16},{20... | collective-permute-start | bytes 393224 | tf_op jit(solution)/shard_map/ppermute | solution.py:16
  47.2 0.8 %fusion.2 = bf16[4,8,128,128]{2,3,1,0:T(8,128)(2,1)S(1)} fusion(f32[4,128,128,8]{2,1,3,0:T(8,128)S(1)} %copy-done.6, f32[4,128,128,8]{2,1,3,0:T(8,128)S(1)} %get-tuple-element.67, f32[4,8,128]{2,1,0:T(8,128)S(1)} %bitcast.220, f32[4,8,128]{2,1,0:T(8,128)S(1)} %bitcast.223, f32[4,8,128]{2,1,0:T(8,128)S(1)} %get-tuple-element.66, pred[128,128]{0,1:T(8,128)(4,1)S(1)} %copy-done.14), kind=kLoop, calls=%fused_computation.4 | loop fusion | flops 3670016 | bytes 5308416 | tf_op jit(solution)/shard_map/convert_element_type | solution.py:128
  49.5 1.3 %copy.81 = bf16[128,4096]{1,0:T(8,128)(2,1)} copy(bf16[128,4096]{0,1:T(8,128)(2,1)S(1)} %bitcast.204) | data formatting | bytes 2097152
  51.5 1.4 %add_convert_fusion = bf16[4,128,128]{2,1,0:T(8,128)(2,1)S(1)} fusion(bf16[4,128,128]{2,1,0:T(8,128)(2,1)} %collective-permute-done.4, bf16[4,128,128]{2,1,0:T(8,128)(2,1)} %collective-permute-done.3, bf16[4,8,128,128]{2,3,1,0:T(8,128)(2,1)S(1)} %copy-done.3, bf16[128,4,8,128]{0,3,2,1:T(8,128)(2,1)S(1)} %bitcast.200), kind=kOutput, calls=%fused_computation.39 | convolution fusion | flops 134610944 | bytes 2490368 | tf_op jit(solution)/shard_map/ghts,tghd->gsd/dot_general | solution.py:41
  (80 shorter events, 8.7 us)
Async XLA Ops:
  0.6 18.7 %copy-start.7 = (bf16[128,4096]{1,0:T(8,128)(2,1)S(1)}, bf16[128,4096]{1,0:T(8,128)(2,1)}, u32[]{:S(2)}) copy-start(bf16[128,4096]{1,0:T(8,128)(2,1)} %param.5) | copy-start | bytes 3145732
  0.6 19.4 %copy-start.8 = (bf16[128,4096]{1,0:T(8,128)(2,1)S(1)}, bf16[128,4096]{1,0:T(8,128)(2,1)}, u32[]{:S(2)}) copy-start(bf16[128,4096]{1,0:T(8,128)(2,1)} %param.8) | copy-start | bytes 3145732
  3.6 21.2 %collective-permute-start = (bf16[2,128,512]{1,2,0:T(8,128)(2,1)}, bf16[2,128,512]{1,2,0:T(8,128)(2,1)}, u32[]{:S(2)}, u32[]{:S(2)}) collective-permute-start(bf16[2,128,512]{1,2,0:T(8,128)(2,1)} %pad_maximum_fusion), channel_id=1, source_target_pairs={{0,2},{2,4},{4,6},{6,8},{8,10},{10,12},{12,14},{14,16},{16,18},{18... | collective-permute-start | bytes 786440 | tf_op jit(solution)/shard_map/ppermute | solution.py:16
  7.6 22.2 %collective-permute-start.1 = (bf16[128,512]{1,0:T(8,128)(2,1)}, bf16[128,512]{1,0:T(8,128)(2,1)S(1)}, u32[]{:S(2)}, u32[]{:S(2)}) collective-permute-start(bf16[128,512]{1,0:T(8,128)(2,1)} %param.6), channel_id=1, source_target_pairs={{0,4},{2,6},{4,8},{6,10},{8,12},{10,14},{12,16},{14,18},{16,20},{1... | collective-permute-start | bytes 393224 | tf_op jit(solution)/shard_map/ppermute | solution.py:16
  11.9 18.0 %collective-permute-start.2 = (bf16[128,512]{1,0:T(8,128)(2,1)}, bf16[128,512]{1,0:T(8,128)(2,1)}, u32[]{:S(2)}, u32[]{:S(2)}) collective-permute-start(bf16[128,512]{1,0:T(8,128)(2,1)} %param.7), channel_id=1, source_target_pairs={{0,4},{2,6},{4,8},{6,10},{8,12},{10,14},{12,16},{14,18},{16,20},{1... | collective-permute-start | bytes 393224 | tf_op jit(solution)/shard_map/ppermute | solution.py:16
  15.7 3.5 %copy-start.21 = (s32[128]{0:T(128)}, s32[128]{0:T(128)S(1)}, u32[]{:S(2)}) copy-start(s32[128]{0:T(128)S(1)} %broadcast_add_fusion.1) | copy-start | bytes 1540
  15.7 3.5 %copy-start.23 = (s32[128]{0:T(128)}, s32[128]{0:T(128)S(1)}, u32[]{:S(2)}) copy-start(s32[128]{0:T(128)S(1)} %broadcast_add_fusion) | copy-start | bytes 1540
  15.7 3.4 %copy-start.19 = (s32[128]{0:T(128)}, s32[128]{0:T(128)S(1)}, u32[]{:S(2)}) copy-start(s32[128]{0:T(128)S(1)} %iota_add_fusion) | copy-start | bytes 1540
  20.3 6.0 %copy-start = (bf16[16,8,32,128]{3,2,1,0:T(8,128)(2,1)}, bf16[16,8,32,128]{3,2,1,0:T(8,128)(2,1)S(1)}, u32[]{:S(2)}) copy-start(bf16[16,8,32,128]{3,2,1,0:T(8,128)(2,1)S(1)} %copy.116) | copy-start | bytes 3145732
  21.4 3.4 %copy-start.13 = (pred[128,128]{0,1:T(8,128)(4,1)}, pred[128,128]{0,1:T(8,128)(4,1)S(1)}, u32[]{:S(2)}) copy-start(pred[128,128]{0,1:T(8,128)(4,1)S(1)} %get-tuple-element.59) | copy-start | bytes 49156
  26.3 3.5 %copy-start.10 = (f32[4,8,128]{2,1,0:T(8,128)}, f32[4,8,128]{2,1,0:T(8,128)S(1)}, u32[]{:S(2)}) copy-start(f32[4,8,128]{2,1,0:T(8,128)S(1)} %get-tuple-element.61) | copy-start | bytes 49156
  33.1 1.3 %copy-start.11 = (f32[4,8,128]{2,1,0:T(8,128)S(1)}, f32[4,8,128]{2,1,0:T(8,128)}, u32[]{:S(2)}) copy-start(f32[4,8,128]{2,1,0:T(8,128)} %copy-done.10) | copy-start | bytes 49156
  33.1 1.4 %copy-start.1 = (bf16[16,8,32,128]{3,2,1,0:T(8,128)(2,1)S(1)}, bf16[16,8,32,128]{3,2,1,0:T(8,128)(2,1)}, u32[]{:S(2)}) copy-start(bf16[16,8,32,128]{3,2,1,0:T(8,128)(2,1)} %copy-done) | copy-start | bytes 3145732
  33.1 1.4 %copy-start.9 = (bf16[128,4,128]{2,1,0:T(4,128)(2,1)S(1)}, bf16[128,4,128]{2,1,0:T(4,128)(2,1)}, u32[]{:S(2)}) copy-start(bf16[128,4,128]{2,1,0:T(4,128)(2,1)} %reshape.266) | copy-start | bytes 393220
  33.2 1.4 %copy-start.12 = (pred[128,128]{0,1:T(8,128)(4,1)S(1)}, pred[128,128]{0,1:T(8,128)(4,1)}, u32[]{:S(2)}) copy-start(pred[128,128]{0,1:T(8,128)(4,1)} %get-tuple-element.58) | copy-start | bytes 49156
  34.6 1.1 %copy-start.15 = (f32[4,8,128]{2,1,0:T(8,128)S(1)}, f32[4,8,128]{2,1,0:T(8,128)}, u32[]{:S(2)}) copy-start(f32[4,8,128]{2,1,0:T(8,128)} %get-tuple-element.36) | copy-start | bytes 49156
  34.6 1.1 %copy-start.16 = (f32[4,8,128]{2,1,0:T(8,128)S(1)}, f32[4,8,128]{2,1,0:T(8,128)}, u32[]{:S(2)}) copy-start(f32[4,8,128]{2,1,0:T(8,128)} %get-tuple-element.40) | copy-start | bytes 49156
  34.6 1.6 %copy-start.4 = (f32[4,8,128,128]{2,3,1,0:T(8,128)S(1)}, f32[4,8,128,128]{2,3,1,0:T(8,128)}, u32[]{:S(2)}) copy-start(f32[4,8,128,128]{2,3,1,0:T(8,128)} %get-tuple-element.23) | copy-start | bytes 6291460
  34.6 2.2 %copy-start.5 = (f32[4,8,128,128]{2,3,1,0:T(8,128)S(1)}, f32[4,8,128,128]{2,3,1,0:T(8,128)}, u32[]{:S(2)}) copy-start(f32[4,8,128,128]{2,3,1,0:T(8,128)} %get-tuple-element.24) | copy-start | bytes 6291460
  38.1 9.1 %copy-start.6 = (f32[4,128,128,8]{2,1,3,0:T(8,128)S(1)}, f32[4,128,128,8]{2,1,3,0:T(8,128)}, u32[]{:S(2)}) copy-start(f32[4,128,128,8]{2,1,3,0:T(8,128)} %get-tuple-element.69) | copy-start | bytes 6291460
  38.1 9.1 %copy-start.14 = (pred[128,128]{0,1:T(8,128)(4,1)S(1)}, pred[128,128]{0,1:T(8,128)(4,1)}, u32[]{:S(2)}) copy-start(pred[128,128]{0,1:T(8,128)(4,1)} %copy-done.13) | copy-start | bytes 49156
  39.2 12.2 %collective-permute-start.4 = (bf16[4,128,128]{2,1,0:T(8,128)(2,1)}, bf16[4,128,128]{2,1,0:T(8,128)(2,1)}, u32[]{:S(2)}, u32[]{:S(2)}) collective-permute-start(bf16[4,128,128]{2,1,0:T(8,128)(2,1)} %fusion.12), channel_id=1, source_target_pairs={{4,0},{6,2},{8,4},{10,6},{12,8},{14,10},{16,12},{18,14},{20,16},{2... | collective-permute-start | bytes 393224 | tf_op jit(solution)/shard_map/ppermute | solution.py:16
  43.0 8.5 %collective-permute-start.3 = (bf16[4,128,128]{2,1,0:T(8,128)(2,1)}, bf16[4,128,128]{2,1,0:T(8,128)(2,1)}, u32[]{:S(2)}, u32[]{:S(2)}) collective-permute-start(bf16[4,128,128]{2,1,0:T(8,128)(2,1)} %fusion.13), channel_id=1, source_target_pairs={{2,0},{4,2},{6,4},{8,6},{10,8},{12,10},{14,12},{16,14},{18,16},{20... | collective-permute-start | bytes 393224 | tf_op jit(solution)/shard_map/ppermute | solution.py:16
  49.4 2.0 %copy-start.3 = (bf16[4,8,128,128]{2,3,1,0:T(8,128)(2,1)S(1)}, bf16[4,8,128,128]{2,3,1,0:T(8,128)(2,1)}, u32[]{:S(2)}) copy-start(bf16[4,8,128,128]{2,3,1,0:T(8,128)(2,1)} %copy-done.2) | copy-start | bytes 3145732
  (7 other events, 6.4 us)

commit v19 on v17

--- a/solution.py
+++ b/solution.py
@@ -113,10 +113,12 @@
     ) / row_sum
     near_exp = near_exp * near_rescale
     far_grad_s = ((far_exp / row_sum) * (far_grad_p - row_delta)).astype(jnp.bfloat16)
-    near_grad_s = ((near_exp / row_sum) * (near_grad_p - row_delta)).astype(jnp.bfloat16)
     far_key_grad = key_grad_of(far_grad_s, query_heads, score_scale).astype(jnp.bfloat16)
     far_back = shifted(far_key_grad, axes, -2)
-    far_key_grad, near_grad_s = lax.optimization_barrier((far_key_grad, near_grad_s))
+    far_key_grad, near_exp, near_grad_p, near_delta, near_sum = lax.optimization_barrier(
+        (far_key_grad, near_exp, near_grad_p, row_delta, row_sum)
+    )
+    near_grad_s = ((near_exp / near_sum) * (near_grad_p - near_delta)).astype(jnp.bfloat16)
     near_key_grad = key_grad_of(near_grad_s, query_heads, score_scale).astype(jnp.bfloat16)
     near_back = shifted(near_key_grad, axes, -1)
 

time: 44.4 us -> 44.3 us (level)
    convert_element_type x1 -> x2, other arithmetic: 1.4 us -> 1.35 us  [the longest x1 0.79 us: body(): (far_exp / row_sum * (far_grad_p - row_delta)).astype(jnp.bfloat16)]
  transfers between devices with their start and end apart: 4 -> 4, of which waited for: 2 -> 1; matrix products, arithmetic and copies ran while one was open for 29% -> 31% of each run, Pallas kernels for 0% -> 0%
where the time goes in v19:
time: 44.3 us; the launch traced here: 43.9 us
  starting transfers between devices  13.2 us (30%)
  local copies, waits for them, and re-layouts  9.16 us (21%)
  waiting for transfers between devices  8.38 us (19%)
  matrix products  7.91 us (18%)
  other arithmetic  4.33 us (10%)
  between operations  0.92 us (2%)
    ppermute x4, starting transfers between devices, shifted(): return lax.ppermute(block, axis, route)  13.2 us
    ppermute x4, waiting for transfers between devices, shifted(): return lax.ppermute(block, axis, route)  8.38 us
    unnamed x8, local copies, waits for them, and re-layouts  3.76 us
    dot_general x3, matrix products, key_grad_of(): jnp.einsum('ghts,tghd->gsd', grad_s, query_heads, preferred_element_type=...  1.97 us
    dot_general x3, matrix products, scores_of(): jnp.einsum('tghd,sgd->ghts', query_heads, key_heads, preferred_element_ty...  1.54 us
    dot_general x3, matrix products, query_grad_of(): jnp.einsum('ghts,sgd->ghtd', grad_s, keys, preferred_element_type=jnp.flo...  1.34 us
    reshape x2, local copies, waits for them, and re-layouts, body(): own_keys = key_vectors.reshape(rows, KVH, HD)  1.08 us
    dot_general x1, matrix products, body(): jnp.einsum('tghd,sgd->ghts', grad_heads, own_values, preferred_element_ty...  1.04 us
  transfers between devices with their start and end apart: 4, of which 1 were waited for; matrix products, arithmetic and copies ran while one was open for 31% of the time, Pallas kernels for 0%

profile of v19, /device:TPU:1, one launch (start us, length us, event | category | flops | bytes accessed | tf_op | source)
XLA Modules:
  0.0 43.9 jit_solution(902642560231248264)
XLA Ops:
  0.6 1.2 %copy.57 = bf16[128,512]{0,1:T(8,128)(2,1)S(1)} copy(bf16[128,512]{1,0:T(8,128)(2,1)} %param.7) | data formatting | bytes 262144 | tf_op args[2]
  1.8 1.0 %copy.56 = bf16[128,512]{0,1:T(8,128)(2,1)S(1)} copy(bf16[128,512]{1,0:T(8,128)(2,1)} %param.6) | data formatting | bytes 262144 | tf_op args[1]
  2.9 0.7 %pad_maximum_fusion = bf16[2,128,512]{1,2,0:T(8,128)(2,1)} fusion(bf16[1,128,512]{1,2,0:T(8,128)(2,1)S(1)} %bitcast.227, bf16[1,128,512]{1,2,0:T(8,128)(2,1)S(1)} %bitcast.228), kind=kLoop, calls=%fused_computation.39 | loop fusion | flops 131072 | bytes 524288 | tf_op jit(solution)/shard_map/stack | solution.py:54
  3.6 4.0 %collective-permute-start = (bf16[2,128,512]{1,2,0:T(8,128)(2,1)}, bf16[2,128,512]{1,2,0:T(8,128)(2,1)}, u32[]{:S(2)}, u32[]{:S(2)}) collective-permute-start(bf16[2,128,512]{1,2,0:T(8,128)(2,1)} %pad_maximum_fusion), channel_id=1, source_target_pairs={{0,2},{2,4},{4,6},{6,8},{8,10},{10,12},{12,14},{14,16},{16,18},{18... | collective-permute-start | bytes 786440 | tf_op jit(solution)/shard_map/ppermute | solution.py:16
  7.6 4.2 %collective-permute-start.1 = (bf16[2,128,512]{1,2,0:T(8,128)(2,1)}, bf16[2,128,512]{1,2,0:T(8,128)(2,1)}, u32[]{:S(2)}, u32[]{:S(2)}) collective-permute-start(bf16[2,128,512]{1,2,0:T(8,128)(2,1)} %pad_maximum_fusion), channel_id=1, source_target_pairs={{0,4},{2,6},{4,8},{6,10},{8,12},{10,14},{12,16},{14,18},{16,20},{1... | collective-permute-start | bytes 786440 | tf_op jit(solution)/shard_map/ppermute | solution.py:16
  11.8 0.9 %reshape.256 = bf16[128,4,128]{2,1,0:T(4,128)(2,1)S(1)} reshape(bf16[128,512]{1,0:T(8,128)(2,1)} %param.6) | data formatting | bytes 262144 | tf_op jit(solution)/shard_map/reshape | solution.py:60
  12.8 0.9 %reshape.259 = bf16[128,4,128]{2,1,0:T(4,128)(2,1)S(1)} reshape(bf16[128,512]{1,0:T(8,128)(2,1)} %param.7) | data formatting | bytes 262144 | tf_op jit(solution)/shard_map/reshape | solution.py:61
  13.9 0.7 %copy.53 = s32[16,1]{1,0:T(8,128)S(1)} copy(s32[16,1]{0,1:T(1,128)} %bitcast.240) | data formatting | bytes 128 | tf_op jit(solution)/shard_map/reshape.234
  14.9 0.7 %copy.109 = bf16[128,4096]{0,1:T(8,128)(2,1)S(1)} copy(bf16[128,4096]{1,0:T(8,128)(2,1)S(1)} %copy-done) | data formatting | bytes 2097152 | tf_op jit(solution)/shard_map/reshape | solution.py:58
  16.6 1.0 %fusion = (f32[4,8,128]{2,1,0:T(8,128)S(1)}, f32[4,8,128]{2,1,0:T(8,128)S(1)}, f32[4,128,128,8]{2,1,3,0:T(8,128)S(1)}) fusion(f32[4,128,128,8]{2,1,3,0:T(8,128)S(1)} %get-tuple-element.67, f32[4,8,128]{2,1,0:T(8,128)S(1)} %get-tuple-element.66, pred[128,128]{0,1:T(8,128)(4,1)S(1)} %get-tuple-element.59, bf16[128,4,8,128]{3,2,1,0:T(8,128)(2,1)S(1)} %bitcast.214, ...), kind=kOutput, calls=%fused_computation.2 | convolution fusion | flops 137355264 | bytes 5439488 | tf_op jit(solution)/shard_map/tghd,sgd->ghts/dot_general | solution.py:72
  17.6 1.0 %fusion.30 = (bf16[1,128,512]{1,2,0:T(8,128)(2,1)S(1)}, bf16[1,128,512]{1,2,0:T(8,128)(2,1)S(1)}) fusion(bf16[2,128,512]{1,2,0:T(8,128)(2,1)} %collective-permute-done), kind=kLoop, calls=%fused_computation.75 | loop fusion | bytes 524288 | tf_op jit(solution)/shard_map/slice | solution.py:78
  18.6 0.5 %fusion.7 = (f32[4,8,128]{2,1,0:T(8,128)S(1)}, f32[4,128,128,8]{2,1,3,0:T(8,128)S(1)}) fusion(pred[128,128]{0,1:T(8,128)(4,1)S(1)} %get-tuple-element.60, bf16[128,4,128,1]{0,2,3,1:T(8,128)(2,1)S(1)} %bitcast.218, bf16[128,4,8,128]{0,3,2,1:T(8,128)(2,1)S(1)} %bitcast.209), kind=kOutput, calls=%fused_computation.20 | convolution fusion | flops 135786496 | bytes 3309568 | tf_op jit(solution)/shard_map/tghd,sgd->ghts/dot_general | solution.py:33
  19.1 1.0 %multiply_reduce_fusion = (f32[4,8,128]{2,1,0:T(8,128)S(1)}, f32[4,8,128]{2,1,0:T(8,128)S(1)}, f32[4,8,128,128]{2,3,1,0:T(8,128)S(1)}, f32[4,8,128,128]{2,3,1,0:T(8,128)S(1)}) fusion(f32[4,8,128]{2,1,0:T(8,128)S(1)} %get-tuple-element.61, f32[4,128,128,8]{2,1,3,0:T(8,128)S(1)} %get-tuple-element.62, pred[128,128]{0,1:T(8,128)(4,1)S(1)} %get-tuple-element.60, ...), kind=kOutput, calls=%fused_computation.16 | convolution fusion | flops 137355264 | bytes 7536640 | tf_op jit(solution)/shard_map/tghd,sgd->ghts/dot_general | solution.py:83
  20.2 8.4 %collective-permute-done.1 = bf16[2,128,512]{1,2,0:T(8,128)(2,1)} collective-permute-done((bf16[2,128,512]{1,2,0:T(8,128)(2,1)}, bf16[2,128,512]{1,2,0:T(8,128)(2,1)}, u32[]{:S(2)}, u32[]{:S(2)}) %collective-permute-start.1) | collective-permute-done | bytes 262176 | tf_op jit(solution)/shard_map/ppermute | solution.py:16
  28.5 1.0 %fusion.29 = (bf16[1,128,512]{1,2,0:T(8,128)(2,1)S(1)}, bf16[1,128,512]{1,2,0:T(8,128)(2,1)S(1)}) fusion(bf16[2,128,512]{1,2,0:T(8,128)(2,1)} %collective-permute-done.1), kind=kLoop, calls=%fused_computation.74 | loop fusion | bytes 524288 | tf_op jit(solution)/shard_map/slice | solution.py:92
  30.1 1.0 %fusion.3 = (f32[4,8,128]{2,1,0:T(8,128)S(1)}, f32[4,8,128]{2,1,0:T(8,128)S(1)}, f32[4,128,128,8]{2,1,3,0:T(8,128)S(1)}) fusion(f32[4,128,128,8]{2,1,3,0:T(8,128)S(1)} %get-tuple-element.65, f32[4,8,128]{2,1,0:T(8,128)S(1)} %fusion.28, pred[128,128]{0,1:T(8,128)(4,1)S(1)} %get-tuple-element.58, bf16[128,4,128,1]{0,2,3,1:T(8,128)(2,1)S(1)} %bitcast.226, ...), kind=kOutput, calls=%fused_computation.7 | convolution fusion | flops 137355264 | bytes 5439488 | tf_op jit(solution)/shard_map/tghd,sgd->ghts/dot_general | solution.py:106
  31.1 0.8 %fusion.5 = bf16[4,8,128,128]{2,3,1,0:T(8,128)(2,1)S(1)} fusion(f32[4,128,128,8]{2,1,3,0:T(8,128)S(1)} %get-tuple-element.68, f32[4,128,128,8]{2,1,3,0:T(8,128)S(1)} %get-tuple-element.65, f32[4,8,128]{2,1,0:T(8,128)S(1)} %bitcast.234, f32[4,8,128]{2,1,0:T(8,128)S(1)} %bitcast.232, f32[4,8,128]{2,1,0:T(8,128)S(1)} %fusion.28, ...), kind=kLoop, calls=%fused_computation.9 | loop fusion | flops 3670016 | bytes 5308416 | tf_op jit(solution)/shard_map/convert_element_type | solution.py:115
  32.4 1.9 %collective-permute-start.3 = (bf16[4,128,128]{2,1,0:T(8,128)(2,1)S(1)}, bf16[4,128,128]{2,1,0:T(8,128)(2,1)S(1)}, u32[]{:S(2)}, u32[]{:S(2)}) collective-permute-start(bf16[4,128,128]{2,1,0:T(8,128)(2,1)S(1)} %fusion.12), channel_id=1, source_target_pairs={{4,0},{6,2},{8,4},{10,6},{12,8},{14,10},{16,12},{18,14},{20,16},{2... | collective-permute-start | bytes 393224 | tf_op jit(solution)/shard_map/ppermute | solution.py:16
  34.6 0.6 %multiply_convert_fusion.1 = bf16[4,8,128,128]{2,3,1,0:T(8,128)(2,1)S(1)} fusion(f32[4,8,128,128]{2,3,1,0:T(8,128)S(1)} %get-tuple-element.24, f32[4,8,128,128]{2,3,1,0:T(8,128)S(1)} %broadcast_multiply_fusion, f32[4,8,128]{2,1,0:T(8,128)S(1)} %bitcast.235, f32[4,8,128]{2,1,0:T(8,128)S(1)} %bitcast.233), kind=kLoop, calls=%fused_computation.14 | loop fusion | flops 2097152 | bytes 5275648 | tf_op jit(solution)/shard_map/convert_element_type | solution.py:121
  35.1 1.1 %fusion.13 = bf16[4,128,128]{2,1,0:T(8,128)(2,1)} fusion(bf16[4,8,128,128]{2,3,1,0:T(8,128)(2,1)S(1)} %multiply_convert_fusion.1, bf16[128,4,8,128]{0,3,2,1:T(8,128)(2,1)S(1)} %bitcast.212), kind=kOutput, calls=%fused_computation.30 | convolution fusion | flops 134348800 | bytes 2228224 | tf_op jit(solution)/shard_map/ghts,tghd->gsd/dot_general | solution.py:41
  36.2 3.0 %collective-permute-start.2 = (bf16[4,128,128]{2,1,0:T(8,128)(2,1)}, bf16[4,128,128]{2,1,0:T(8,128)(2,1)S(1)}, u32[]{:S(2)}, u32[]{:S(2)}) collective-permute-start(bf16[4,128,128]{2,1,0:T(8,128)(2,1)} %fusion.13), channel_id=1, source_target_pairs={{2,0},{4,2},{6,4},{8,6},{10,8},{12,10},{14,12},{16,14},{18,16},{20... | collective-permute-start | bytes 393224 | tf_op jit(solution)/shard_map/ppermute | solution.py:16
  39.3 0.8 %fusion.2 = bf16[4,8,128,128]{2,3,1,0:T(8,128)(2,1)S(1)} fusion(f32[4,128,128,8]{2,1,3,0:T(8,128)S(1)} %get-tuple-element.69, f32[4,128,128,8]{2,1,3,0:T(8,128)S(1)} %get-tuple-element.67, f32[4,8,128]{2,1,0:T(8,128)S(1)} %bitcast.236, f32[4,8,128]{2,1,0:T(8,128)S(1)} %bitcast.239, f32[4,8,128]{2,1,0:T(8,128)S(1)} %get-tuple-element.66, ...), kind=kLoop, calls=%fused_computation.4 | loop fusion | flops 3670016 | bytes 5308416 | tf_op jit(solution)/shard_map/convert_element_type | solution.py:129
  41.4 1.3 %copy.77 = bf16[128,4096]{1,0:T(8,128)(2,1)} copy(bf16[128,4096]{0,1:T(8,128)(2,1)S(1)} %bitcast.217) | data formatting | bytes 2097152
  43.2 0.7 %pad_maximum_fusion.1 = bf16[128,512]{1,0:T(8,128)(2,1)} fusion(bf16[128,128]{1,0:T(8,128)(2,1)S(1)} %get-tuple-element.53, bf16[128,128]{1,0:T(8,128)(2,1)S(1)} %get-tuple-element.54, bf16[128,128]{1,0:T(8,128)(2,1)S(1)} %get-tuple-element.55, bf16[128,128]{1,0:T(8,128)(2,1)S(1)} %get-tuple-element.52), kind=kLoop, calls=%fused_computation.41 | loop fusion | flops 524288 | bytes 262144 | tf_op jit(solution)/shard_map/concatenate | solution.py:138
  (30 shorter events, 4.4 us)
Async XLA Ops:
  0.6 14.3 %copy-start = (bf16[128,4096]{1,0:T(8,128)(2,1)S(1)}, bf16[128,4096]{1,0:T(8,128)(2,1)}, u32[]{:S(2)}) copy-start(bf16[128,4096]{1,0:T(8,128)(2,1)} %param.5) | copy-start | bytes 3145732
  0.6 15.0 %copy-start.1 = (bf16[128,4096]{1,0:T(8,128)(2,1)S(1)}, bf16[128,4096]{1,0:T(8,128)(2,1)}, u32[]{:S(2)}) copy-start(bf16[128,4096]{1,0:T(8,128)(2,1)} %param.8) | copy-start | bytes 3145732
  3.6 14.0 %collective-permute-start = (bf16[2,128,512]{1,2,0:T(8,128)(2,1)}, bf16[2,128,512]{1,2,0:T(8,128)(2,1)}, u32[]{:S(2)}, u32[]{:S(2)}) collective-permute-start(bf16[2,128,512]{1,2,0:T(8,128)(2,1)} %pad_maximum_fusion), channel_id=1, source_target_pairs={{0,2},{2,4},{4,6},{6,8},{8,10},{10,12},{12,14},{14,16},{16,18},{18... | collective-permute-start | bytes 786440 | tf_op jit(solution)/shard_map/ppermute | solution.py:16
  7.6 20.9 %collective-permute-start.1 = (bf16[2,128,512]{1,2,0:T(8,128)(2,1)}, bf16[2,128,512]{1,2,0:T(8,128)(2,1)}, u32[]{:S(2)}, u32[]{:S(2)}) collective-permute-start(bf16[2,128,512]{1,2,0:T(8,128)(2,1)} %pad_maximum_fusion), channel_id=1, source_target_pairs={{0,4},{2,6},{4,8},{6,10},{8,12},{10,14},{12,16},{14,18},{16,20},{1... | collective-permute-start | bytes 786440 | tf_op jit(solution)/shard_map/ppermute | solution.py:16
  32.4 10.4 %collective-permute-start.3 = (bf16[4,128,128]{2,1,0:T(8,128)(2,1)S(1)}, bf16[4,128,128]{2,1,0:T(8,128)(2,1)S(1)}, u32[]{:S(2)}, u32[]{:S(2)}) collective-permute-start(bf16[4,128,128]{2,1,0:T(8,128)(2,1)S(1)} %fusion.12), channel_id=1, source_target_pairs={{4,0},{6,2},{8,4},{10,6},{12,8},{14,10},{16,12},{18,14},{20,16},{2... | collective-permute-start | bytes 393224 | tf_op jit(solution)/shard_map/ppermute | solution.py:16
  36.2 6.5 %collective-permute-start.2 = (bf16[4,128,128]{2,1,0:T(8,128)(2,1)}, bf16[4,128,128]{2,1,0:T(8,128)(2,1)S(1)}, u32[]{:S(2)}, u32[]{:S(2)}) collective-permute-start(bf16[4,128,128]{2,1,0:T(8,128)(2,1)} %fusion.13), channel_id=1, source_target_pairs={{2,0},{4,2},{6,4},{8,6},{10,8},{12,10},{14,12},{16,14},{18,16},{20... | collective-permute-start | bytes 393224 | tf_op jit(solution)/shard_map/ppermute | solution.py:16

commit v20 on v17

--- a/solution.py
+++ b/solution.py
@@ -114,11 +114,11 @@
     near_exp = near_exp * near_rescale
     far_grad_s = ((far_exp / row_sum) * (far_grad_p - row_delta)).astype(jnp.bfloat16)
     near_grad_s = ((near_exp / row_sum) * (near_grad_p - row_delta)).astype(jnp.bfloat16)
+    near_key_grad = key_grad_of(near_grad_s, query_heads, score_scale).astype(jnp.bfloat16)
+    near_back = shifted(near_key_grad, axes, -1)
+    near_key_grad, far_grad_s = lax.optimization_barrier((near_key_grad, far_grad_s))
     far_key_grad = key_grad_of(far_grad_s, query_heads, score_scale).astype(jnp.bfloat16)
     far_back = shifted(far_key_grad, axes, -2)
-    far_key_grad, near_grad_s = lax.optimization_barrier((far_key_grad, near_grad_s))
-    near_key_grad = key_grad_of(near_grad_s, query_heads, score_scale).astype(jnp.bfloat16)
-    near_back = shifted(near_key_grad, axes, -1)
 
     _, own_scale, row_delta, far_grad_s, near_grad_s = lax.optimization_barrier(
         ((far_key_grad, near_key_grad), own_rescale / row_sum, row_delta, far_grad_s, near_grad_s)

time: 44.4 us -> 47.6 us (1.072)
  the two profiles are of different devices: /device:TPU:1 before, /device:TPU:7 now
where the time goes in v20:
time: 47.6 us; the launch traced here: 47.3 us
  starting transfers between devices  20.4 us (43%)
  local copies, waits for them, and re-layouts  9.16 us (19%)
  matrix products  7.72 us (16%)
  waiting for transfers between devices  4.94 us (10%)
  other arithmetic  4.1 us (9%)
  between operations  0.91 us (2%)
    ppermute x4, starting transfers between devices, shifted(): return lax.ppermute(block, axis, route)  20.4 us
    ppermute x4, waiting for transfers between devices, shifted(): return lax.ppermute(block, axis, route)  4.94 us
    unnamed x8, local copies, waits for them, and re-layouts  3.76 us
    dot_general x3, matrix products, key_grad_of(): jnp.einsum('ghts,tghd->gsd', grad_s, query_heads, preferred_element_type=...  1.97 us
    dot_general x3, matrix products, scores_of(): jnp.einsum('tghd,sgd->ghts', query_heads, key_heads, preferred_element_ty...  1.52 us
    convert_element_type x1, other arithmetic, body(): (far_exp / row_sum * (far_grad_p - row_delta)).astype(jnp.bfloat16)  1.38 us
    dot_general x3, matrix products, query_grad_of(): jnp.einsum('ghts,sgd->ghtd', grad_s, keys, preferred_element_type=jnp.flo...  1.32 us
    reshape x2, local copies, waits for them, and re-layouts, body(): own_keys = key_vectors.reshape(rows, KVH, HD)  1.08 us
  transfers between devices with their start and end apart: 4, of which 2 were waited for; matrix products, arithmetic and copies ran while one was open for 27% of the time, Pallas kernels for 0%

profile of v20, /device:TPU:7, one launch (start us, length us, event | category | flops | bytes accessed | tf_op | source)
XLA Modules:
  0.0 47.3 jit_solution(7896940862254558766)
XLA Ops:
  0.6 1.2 %copy.56 = bf16[128,512]{0,1:T(8,128)(2,1)S(1)} copy(bf16[128,512]{1,0:T(8,128)(2,1)} %param.6) | data formatting | bytes 262144 | tf_op args[1]
  1.8 1.0 %copy.57 = bf16[128,512]{0,1:T(8,128)(2,1)S(1)} copy(bf16[128,512]{1,0:T(8,128)(2,1)} %param.7) | data formatting | bytes 262144 | tf_op args[2]
  2.9 0.7 %pad_maximum_fusion = bf16[2,128,512]{1,2,0:T(8,128)(2,1)} fusion(bf16[1,128,512]{1,2,0:T(8,128)(2,1)S(1)} %bitcast.226, bf16[1,128,512]{1,2,0:T(8,128)(2,1)S(1)} %bitcast.225), kind=kLoop, calls=%fused_computation.38 | loop fusion | flops 131072 | bytes 524288 | tf_op jit(solution)/shard_map/stack | solution.py:54
  3.6 3.2 %collective-permute-start = (bf16[2,128,512]{1,2,0:T(8,128)(2,1)}, bf16[2,128,512]{1,2,0:T(8,128)(2,1)}, u32[]{:S(2)}, u32[]{:S(2)}) collective-permute-start(bf16[2,128,512]{1,2,0:T(8,128)(2,1)} %pad_maximum_fusion), channel_id=1, source_target_pairs={{0,2},{2,4},{4,6},{6,8},{8,10},{10,12},{12,14},{14,16},{16,18},{18... | collective-permute-start | bytes 786440 | tf_op jit(solution)/shard_map/ppermute | solution.py:16
  6.8 4.2 %collective-permute-start.1 = (bf16[2,128,512]{1,2,0:T(8,128)(2,1)}, bf16[2,128,512]{1,2,0:T(8,128)(2,1)}, u32[]{:S(2)}, u32[]{:S(2)}) collective-permute-start(bf16[2,128,512]{1,2,0:T(8,128)(2,1)} %pad_maximum_fusion), channel_id=1, source_target_pairs={{0,4},{2,6},{4,8},{6,10},{8,12},{10,14},{12,16},{14,18},{16,20},{1... | collective-permute-start | bytes 786440 | tf_op jit(solution)/shard_map/ppermute | solution.py:16
  11.1 0.9 %reshape.256 = bf16[128,4,128]{2,1,0:T(4,128)(2,1)S(1)} reshape(bf16[128,512]{1,0:T(8,128)(2,1)} %param.6) | data formatting | bytes 262144 | tf_op jit(solution)/shard_map/reshape | solution.py:60
  12.0 0.9 %reshape.259 = bf16[128,4,128]{2,1,0:T(4,128)(2,1)S(1)} reshape(bf16[128,512]{1,0:T(8,128)(2,1)} %param.7) | data formatting | bytes 262144 | tf_op jit(solution)/shard_map/reshape | solution.py:61
  12.9 0.7 %copy.53 = s32[16,1]{1,0:T(8,128)S(1)} copy(s32[16,1]{0,1:T(1,128)} %bitcast.236) | data formatting | bytes 128 | tf_op jit(solution)/shard_map/reshape.234
  14.1 0.7 %copy.109 = bf16[128,4096]{0,1:T(8,128)(2,1)S(1)} copy(bf16[128,4096]{1,0:T(8,128)(2,1)S(1)} %copy-done) | data formatting | bytes 2097152 | tf_op jit(solution)/shard_map/reshape | solution.py:58
  15.2 0.5 %fusion.6 = (f32[4,8,128]{2,1,0:T(8,128)S(1)}, f32[4,128,128,8]{2,1,3,0:T(8,128)S(1)}) fusion(pred[128,128]{0,1:T(8,128)(4,1)S(1)} %get-tuple-element.55, bf16[128,4,128,1]{0,2,3,1:T(8,128)(2,1)S(1)} %copy.87, bf16[128,4,8,128]{0,3,2,1:T(8,128)(2,1)S(1)} %bitcast.206), kind=kOutput, calls=%fused_computation.19 | convolution fusion | flops 135786496 | bytes 3309568 | tf_op jit(solution)/shard_map/tghd,sgd->ghts/dot_general | solution.py:33
  15.7 1.0 %fusion.3 = (f32[4,8,128]{2,1,0:T(8,128)S(1)}, f32[4,8,128]{2,1,0:T(8,128)S(1)}, f32[4,128,128,8]{2,1,3,0:T(8,128)S(1)}) fusion(f32[4,128,128,8]{2,1,3,0:T(8,128)S(1)} %get-tuple-element.61, f32[4,8,128]{2,1,0:T(8,128)S(1)} %get-tuple-element.60, pred[128,128]{0,1:T(8,128)(4,1)S(1)} %get-tuple-element.55, bf16[128,4,8,128]{3,2,1,0:T(8,128)(2,1)S(1)} %bitcast.212, ...), kind=kOutput, calls=%fused_computation.7 | convolution fusion | flops 137355264 | bytes 5439488 | tf_op jit(solution)/shard_map/tghd,sgd->ghts/dot_general | solution.py:72
  16.7 1.0 %fusion.30 = (bf16[1,128,512]{1,2,0:T(8,128)(2,1)S(1)}, bf16[1,128,512]{1,2,0:T(8,128)(2,1)S(1)}) fusion(bf16[2,128,512]{1,2,0:T(8,128)(2,1)} %collective-permute-done), kind=kLoop, calls=%fused_computation.74 | loop fusion | bytes 524288 | tf_op jit(solution)/shard_map/slice | solution.py:78
  17.7 0.5 %fusion.7 = (f32[4,8,128]{2,1,0:T(8,128)S(1)}, f32[4,128,128,8]{2,1,3,0:T(8,128)S(1)}) fusion(pred[128,128]{0,1:T(8,128)(4,1)S(1)} %get-tuple-element.56, bf16[128,4,128,1]{0,2,3,1:T(8,128)(2,1)S(1)} %bitcast.216, bf16[128,4,8,128]{0,3,2,1:T(8,128)(2,1)S(1)} %bitcast.207), kind=kOutput, calls=%fused_computation.20 | convolution fusion | flops 135786496 | bytes 3309568 | tf_op jit(solution)/shard_map/tghd,sgd->ghts/dot_general | solution.py:33
  18.2 1.0 %multiply_reduce_fusion = (f32[4,8,128]{2,1,0:T(8,128)S(1)}, f32[4,8,128]{2,1,0:T(8,128)S(1)}, f32[4,8,128,128]{2,3,1,0:T(8,128)S(1)}, f32[4,8,128,128]{2,3,1,0:T(8,128)S(1)}) fusion(f32[4,8,128]{2,1,0:T(8,128)S(1)} %get-tuple-element.57, f32[4,128,128,8]{2,1,3,0:T(8,128)S(1)} %get-tuple-element.58, pred[128,128]{0,1:T(8,128)(4,1)S(1)} %get-tuple-element.56, ...), kind=kOutput, calls=%fused_computation.16 | convolution fusion | flops 137355264 | bytes 7536640 | tf_op jit(solution)/shard_map/tghd,sgd->ghts/dot_general | solution.py:83
  19.6 1.0 %fusion.29 = (bf16[1,128,512]{1,2,0:T(8,128)(2,1)S(1)}, bf16[1,128,512]{1,2,0:T(8,128)(2,1)S(1)}) fusion(bf16[2,128,512]{1,2,0:T(8,128)(2,1)} %collective-permute-done.1), kind=kLoop, calls=%fused_computation.73 | loop fusion | bytes 524288 | tf_op jit(solution)/shard_map/slice | solution.py:93
  21.2 1.0 %fusion = (f32[4,8,128]{2,1,0:T(8,128)S(1)}, f32[4,8,128]{2,1,0:T(8,128)S(1)}, f32[4,128,128,8]{2,1,3,0:T(8,128)S(1)}) fusion(f32[4,128,128,8]{2,1,3,0:T(8,128)S(1)} %get-tuple-element.63, f32[4,8,128]{2,1,0:T(8,128)S(1)} %get-tuple-element.51, pred[128,128]{0,1:T(8,128)(4,1)S(1)} %get-tuple-element.54, bf16[128,4,128,1]{0,2,3,1:T(8,128)(2,1)S(1)} %bitcast.223, ...), kind=kOutput, calls=%fused_computation.2 | convolution fusion | flops 137355264 | bytes 5439488 | tf_op jit(solution)/shard_map/tghd,sgd->ghts/dot_general | solution.py:106
  22.2 1.4 %fusion.2 = (bf16[4,8,128,128]{2,3,1,0:T(8,128)(2,1)S(1)}, bf16[4,8,128,128]{2,3,1,0:T(8,128)(2,1)S(1)}) fusion(f32[4,128,128,8]{2,1,3,0:T(8,128)S(1)} %get-tuple-element.64, f32[4,128,128,8]{2,1,3,0:T(8,128)S(1)} %get-tuple-element.63, f32[4,8,128]{2,1,0:T(8,128)S(1)} %bitcast.231, f32[4,8,128]{2,1,0:T(8,128)S(1)} %bitcast.230, ...), kind=kLoop, calls=%fused_computation.4 | loop fusion | flops 6291456 | bytes 10567680 | tf_op jit(solution)/shard_map/convert_element_type | solution.py:115
  24.0 11.1 %collective-permute-start.2 = (bf16[4,128,128]{2,1,0:T(8,128)(2,1)S(1)}, bf16[4,128,128]{2,1,0:T(8,128)(2,1)S(1)}, u32[]{:S(2)}, u32[]{:S(2)}) collective-permute-start(bf16[4,128,128]{2,1,0:T(8,128)(2,1)S(1)} %fusion.12), channel_id=1, source_target_pairs={{2,0},{4,2},{6,4},{8,6},{10,8},{12,10},{14,12},{16,14},{18,16},{20... | collective-permute-start | bytes 393224 | tf_op jit(solution)/shard_map/ppermute | solution.py:16
  35.2 1.1 %fusion.13 = bf16[4,128,128]{2,1,0:T(8,128)(2,1)} fusion(bf16[4,8,128,128]{2,3,1,0:T(8,128)(2,1)S(1)} %get-tuple-element.22, bf16[128,4,8,128]{0,3,2,1:T(8,128)(2,1)S(1)} %bitcast.210), kind=kOutput, calls=%fused_computation.30 | convolution fusion | flops 134348800 | bytes 2228224 | tf_op jit(solution)/shard_map/ghts,tghd->gsd/dot_general | solution.py:41
  36.3 1.9 %collective-permute-start.3 = (bf16[4,128,128]{2,1,0:T(8,128)(2,1)}, bf16[4,128,128]{2,1,0:T(8,128)(2,1)S(1)}, u32[]{:S(2)}, u32[]{:S(2)}) collective-permute-start(bf16[4,128,128]{2,1,0:T(8,128)(2,1)} %fusion.13), channel_id=1, source_target_pairs={{4,0},{6,2},{8,4},{10,6},{12,8},{14,10},{16,12},{18,14},{20,16},{2... | collective-permute-start | bytes 393224 | tf_op jit(solution)/shard_map/ppermute | solution.py:16
  38.2 0.8 %fusion.5 = bf16[4,8,128,128]{2,3,1,0:T(8,128)(2,1)S(1)} fusion(f32[4,128,128,8]{2,1,3,0:T(8,128)S(1)} %get-tuple-element.65, f32[4,128,128,8]{2,1,3,0:T(8,128)S(1)} %get-tuple-element.61, f32[4,8,128]{2,1,0:T(8,128)S(1)} %bitcast.232, f32[4,8,128]{2,1,0:T(8,128)S(1)} %bitcast.235, f32[4,8,128]{2,1,0:T(8,128)S(1)} %get-tuple-element.60, ...), kind=kLoop, calls=%fused_computation.9 | loop fusion | flops 3670016 | bytes 5308416 | tf_op jit(solution)/shard_map/convert_element_type | solution.py:127
  40.3 1.3 %copy.77 = bf16[128,4096]{1,0:T(8,128)(2,1)} copy(bf16[128,4096]{0,1:T(8,128)(2,1)S(1)} %bitcast.215) | data formatting | bytes 2097152
  41.6 4.5 %collective-permute-done.3 = bf16[4,128,128]{2,1,0:T(8,128)(2,1)S(1)} collective-permute-done((bf16[4,128,128]{2,1,0:T(8,128)(2,1)}, bf16[4,128,128]{2,1,0:T(8,128)(2,1)S(1)}, u32[]{:S(2)}, u32[]{:S(2)}) %collective-permute-start.3) | collective-permute-done | bytes 131104 | tf_op jit(solution)/shard_map/ppermute | solution.py:16
  46.6 0.7 %pad_maximum_fusion.1 = bf16[128,512]{1,0:T(8,128)(2,1)} fusion(bf16[128,128]{1,0:T(8,128)(2,1)S(1)} %get-tuple-element.47, bf16[128,128]{1,0:T(8,128)(2,1)S(1)} %get-tuple-element.48, bf16[128,128]{1,0:T(8,128)(2,1)S(1)} %get-tuple-element.49, bf16[128,128]{1,0:T(8,128)(2,1)S(1)} %get-tuple-element.46), kind=kLoop, calls=%fused_computation.40 | loop fusion | flops 524288 | bytes 262144 | tf_op jit(solution)/shard_map/concatenate | solution.py:136
  (28 shorter events, 4.0 us)
Async XLA Ops:
  0.6 13.5 %copy-start = (bf16[128,4096]{1,0:T(8,128)(2,1)S(1)}, bf16[128,4096]{1,0:T(8,128)(2,1)}, u32[]{:S(2)}) copy-start(bf16[128,4096]{1,0:T(8,128)(2,1)} %param.5) | copy-start | bytes 3145732
  0.6 14.1 %copy-start.1 = (bf16[128,4096]{1,0:T(8,128)(2,1)S(1)}, bf16[128,4096]{1,0:T(8,128)(2,1)}, u32[]{:S(2)}) copy-start(bf16[128,4096]{1,0:T(8,128)(2,1)} %param.8) | copy-start | bytes 3145732
  3.6 13.1 %collective-permute-start = (bf16[2,128,512]{1,2,0:T(8,128)(2,1)}, bf16[2,128,512]{1,2,0:T(8,128)(2,1)}, u32[]{:S(2)}, u32[]{:S(2)}) collective-permute-start(bf16[2,128,512]{1,2,0:T(8,128)(2,1)} %pad_maximum_fusion), channel_id=1, source_target_pairs={{0,2},{2,4},{4,6},{6,8},{8,10},{10,12},{12,14},{14,16},{16,18},{18... | collective-permute-start | bytes 786440 | tf_op jit(solution)/shard_map/ppermute | solution.py:16
  6.8 12.9 %collective-permute-start.1 = (bf16[2,128,512]{1,2,0:T(8,128)(2,1)}, bf16[2,128,512]{1,2,0:T(8,128)(2,1)}, u32[]{:S(2)}, u32[]{:S(2)}) collective-permute-start(bf16[2,128,512]{1,2,0:T(8,128)(2,1)} %pad_maximum_fusion), channel_id=1, source_target_pairs={{0,4},{2,6},{4,8},{6,10},{8,12},{10,14},{12,16},{14,18},{16,20},{1... | collective-permute-start | bytes 786440 | tf_op jit(solution)/shard_map/ppermute | solution.py:16
  24.0 22.1 %collective-permute-start.2 = (bf16[4,128,128]{2,1,0:T(8,128)(2,1)S(1)}, bf16[4,128,128]{2,1,0:T(8,128)(2,1)S(1)}, u32[]{:S(2)}, u32[]{:S(2)}) collective-permute-start(bf16[4,128,128]{2,1,0:T(8,128)(2,1)S(1)} %fusion.12), channel_id=1, source_target_pairs={{2,0},{4,2},{6,4},{8,6},{10,8},{12,10},{14,12},{16,14},{18,16},{20... | collective-permute-start | bytes 393224 | tf_op jit(solution)/shard_map/ppermute | solution.py:16
  36.3 9.9 %collective-permute-start.3 = (bf16[4,128,128]{2,1,0:T(8,128)(2,1)}, bf16[4,128,128]{2,1,0:T(8,128)(2,1)S(1)}, u32[]{:S(2)}, u32[]{:S(2)}) collective-permute-start(bf16[4,128,128]{2,1,0:T(8,128)(2,1)} %fusion.13), channel_id=1, source_target_pairs={{4,0},{6,2},{8,4},{10,6},{12,8},{14,10},{16,12},{18,14},{20,16},{2... | collective-permute-start | bytes 393224 | tf_op jit(solution)/shard_map/ppermute | solution.py:16

commit v21 on v17

--- a/solution.py
+++ b/solution.py
@@ -44,7 +44,7 @@
 
 
 def query_grad_of(grad_s, keys):
-    return jnp.einsum("ghts,sgd->ghtd", grad_s, keys, preferred_element_type=jnp.float32)
+    return jnp.einsum("ghts,sgd->tghd", grad_s, keys, preferred_element_type=jnp.float32)
 
 
 def body(queries, key_vectors, value_vectors, output_grad, doc_lengths):
@@ -131,7 +131,7 @@
         + query_grad_of(far_grad_s, far_keys)
         + query_grad_of(near_grad_s, near_keys)
     ) * score_scale
-    query_grad = jnp.transpose(query_grad.astype(jnp.bfloat16), (2, 0, 1, 3)).reshape(rows, QH * HD)
+    query_grad = query_grad.astype(jnp.bfloat16).reshape(rows, QH * HD)
     key_grad = own_key_grad + near_back.astype(jnp.float32) + far_back.astype(jnp.float32)
     key_grad = jnp.concatenate([key_grad[g] for g in range(KVH)], axis=1).astype(jnp.bfloat16)
     return (query_grad, key_grad)

time: 44.4 us -> 44.4 us (level)
  no operation moved by 1% of the time
where the time goes in v21:
time: 44.4 us; the launch traced here: 43.7 us
  starting transfers between devices  13.2 us (30%)
  local copies, waits for them, and re-layouts  9.16 us (21%)
  waiting for transfers between devices  8.55 us (19%)
  matrix products  7.75 us (17%)
  other arithmetic  4.11 us (9%)
  between operations  0.91 us (2%)
    ppermute x4, starting transfers between devices, shifted(): return lax.ppermute(block, axis, route)  13.2 us
    ppermute x4, waiting for transfers between devices, shifted(): return lax.ppermute(block, axis, route)  8.55 us
    unnamed x8, local copies, waits for them, and re-layouts  3.76 us
    dot_general x3, matrix products, key_grad_of(): jnp.einsum('ghts,tghd->gsd', grad_s, query_heads, preferred_element_type=...  1.97 us
    dot_general x3, matrix products, scores_of(): jnp.einsum('tghd,sgd->ghts', query_heads, key_heads, preferred_element_ty...  1.52 us
    convert_element_type x1, other arithmetic, body(): (near_exp / row_sum * (near_grad_p - row_delta)).astype(jnp.bfloat16)  1.4 us
    dot_general x3, matrix products, query_grad_of(): jnp.einsum('ghts,sgd->tghd', grad_s, keys, preferred_element_type=jnp.flo...  1.32 us
    reshape x2, local copies, waits for them, and re-layouts, body(): own_keys = key_vectors.reshape(rows, KVH, HD)  1.08 us
  transfers between devices with their start and end apart: 4, of which 2 were waited for; matrix products, arithmetic and copies ran while one was open for 29% of the time, Pallas kernels for 0%

profile of v21, /device:TPU:1, one launch (start us, length us, event | category | flops | bytes accessed | tf_op | source)
XLA Modules:
  0.0 43.7 jit_solution(5351152754099366004)
XLA Ops:
  0.6 1.2 %copy.56 = bf16[128,512]{0,1:T(8,128)(2,1)S(1)} copy(bf16[128,512]{1,0:T(8,128)(2,1)} %param.6) | data formatting | bytes 262144 | tf_op args[1]
  1.8 1.0 %copy.57 = bf16[128,512]{0,1:T(8,128)(2,1)S(1)} copy(bf16[128,512]{1,0:T(8,128)(2,1)} %param.7) | data formatting | bytes 262144 | tf_op args[2]
  2.9 0.7 %pad_maximum_fusion = bf16[2,128,512]{1,2,0:T(8,128)(2,1)} fusion(bf16[1,128,512]{1,2,0:T(8,128)(2,1)S(1)} %bitcast.236, bf16[1,128,512]{1,2,0:T(8,128)(2,1)S(1)} %bitcast.235), kind=kLoop, calls=%fused_computation.41 | loop fusion | flops 131072 | bytes 524288 | tf_op jit(solution)/shard_map/stack | solution.py:54
  3.6 4.0 %collective-permute-start = (bf16[2,128,512]{1,2,0:T(8,128)(2,1)}, bf16[2,128,512]{1,2,0:T(8,128)(2,1)}, u32[]{:S(2)}, u32[]{:S(2)}) collective-permute-start(bf16[2,128,512]{1,2,0:T(8,128)(2,1)} %pad_maximum_fusion), channel_id=1, source_target_pairs={{0,2},{2,4},{4,6},{6,8},{8,10},{10,12},{12,14},{14,16},{16,18},{18... | collective-permute-start | bytes 786440 | tf_op jit(solution)/shard_map/ppermute | solution.py:16
  7.6 4.2 %collective-permute-start.1 = (bf16[2,128,512]{1,2,0:T(8,128)(2,1)}, bf16[2,128,512]{1,2,0:T(8,128)(2,1)}, u32[]{:S(2)}, u32[]{:S(2)}) collective-permute-start(bf16[2,128,512]{1,2,0:T(8,128)(2,1)} %pad_maximum_fusion), channel_id=1, source_target_pairs={{0,4},{2,6},{4,8},{6,10},{8,12},{10,14},{12,16},{14,18},{16,20},{1... | collective-permute-start | bytes 786440 | tf_op jit(solution)/shard_map/ppermute | solution.py:16
  11.9 0.9 %reshape.256 = bf16[128,4,128]{2,1,0:T(4,128)(2,1)S(1)} reshape(bf16[128,512]{1,0:T(8,128)(2,1)} %param.6) | data formatting | bytes 262144 | tf_op jit(solution)/shard_map/reshape | solution.py:60
  12.8 0.9 %reshape.259 = bf16[128,4,128]{2,1,0:T(4,128)(2,1)S(1)} reshape(bf16[128,512]{1,0:T(8,128)(2,1)} %param.7) | data formatting | bytes 262144 | tf_op jit(solution)/shard_map/reshape | solution.py:61
  13.8 0.7 %copy.53 = s32[16,1]{1,0:T(8,128)S(1)} copy(s32[16,1]{0,1:T(1,128)} %bitcast.246) | data formatting | bytes 128 | tf_op jit(solution)/shard_map/reshape.234
  14.9 0.7 %copy.109 = bf16[128,4096]{0,1:T(8,128)(2,1)S(1)} copy(bf16[128,4096]{1,0:T(8,128)(2,1)S(1)} %copy-done) | data formatting | bytes 2097152 | tf_op jit(solution)/shard_map/reshape | solution.py:58
  16.0 0.5 %fusion.8 = (f32[4,8,128]{2,1,0:T(8,128)S(1)}, f32[4,128,128,8]{2,1,3,0:T(8,128)S(1)}) fusion(pred[128,128]{0,1:T(8,128)(4,1)S(1)} %get-tuple-element.55, bf16[128,4,128,1]{0,2,3,1:T(8,128)(2,1)S(1)} %copy.87, bf16[128,4,8,128]{0,3,2,1:T(8,128)(2,1)S(1)} %bitcast.216), kind=kOutput, calls=%fused_computation.22 | convolution fusion | flops 135786496 | bytes 3309568 | tf_op jit(solution)/shard_map/tghd,sgd->ghts/dot_general | solution.py:33
  16.6 1.0 %fusion.2 = (f32[4,8,128]{2,1,0:T(8,128)S(1)}, f32[4,8,128]{2,1,0:T(8,128)S(1)}, f32[4,128,128,8]{2,1,3,0:T(8,128)S(1)}) fusion(f32[4,128,128,8]{2,1,3,0:T(8,128)S(1)} %get-tuple-element.63, f32[4,8,128]{2,1,0:T(8,128)S(1)} %get-tuple-element.62, pred[128,128]{0,1:T(8,128)(4,1)S(1)} %get-tuple-element.55, bf16[128,4,8,128]{3,2,1,0:T(8,128)(2,1)S(1)} %bitcast.222, ...), kind=kOutput, calls=%fused_computation.6 | convolution fusion | flops 137355264 | bytes 5439488 | tf_op jit(solution)/shard_map/tghd,sgd->ghts/dot_general | solution.py:72
  17.6 1.0 %fusion.32 = (bf16[1,128,512]{1,2,0:T(8,128)(2,1)S(1)}, bf16[1,128,512]{1,2,0:T(8,128)(2,1)S(1)}) fusion(bf16[2,128,512]{1,2,0:T(8,128)(2,1)} %collective-permute-done), kind=kLoop, calls=%fused_computation.77 | loop fusion | bytes 524288 | tf_op jit(solution)/shard_map/slice | solution.py:78
  19.1 1.0 %multiply_reduce_fusion = (f32[4,8,128]{2,1,0:T(8,128)S(1)}, f32[4,8,128]{2,1,0:T(8,128)S(1)}, f32[4,8,128,128]{2,3,1,0:T(8,128)S(1)}, f32[4,8,128,128]{2,3,1,0:T(8,128)S(1)}) fusion(f32[4,8,128]{2,1,0:T(8,128)S(1)} %get-tuple-element.57, f32[4,128,128,8]{2,1,3,0:T(8,128)S(1)} %get-tuple-element.58, pred[128,128]{0,1:T(8,128)(4,1)S(1)} %get-tuple-element.56, ...), kind=kOutput, calls=%fused_computation.19 | convolution fusion | flops 137355264 | bytes 7536640 | tf_op jit(solution)/shard_map/tghd,sgd->ghts/dot_general | solution.py:83
  20.1 8.5 %collective-permute-done.1 = bf16[2,128,512]{1,2,0:T(8,128)(2,1)} collective-permute-done((bf16[2,128,512]{1,2,0:T(8,128)(2,1)}, bf16[2,128,512]{1,2,0:T(8,128)(2,1)}, u32[]{:S(2)}, u32[]{:S(2)}) %collective-permute-start.1) | collective-permute-done | bytes 262176 | tf_op jit(solution)/shard_map/ppermute | solution.py:16
  28.5 1.0 %fusion.31 = (bf16[1,128,512]{1,2,0:T(8,128)(2,1)S(1)}, bf16[1,128,512]{1,2,0:T(8,128)(2,1)S(1)}) fusion(bf16[2,128,512]{1,2,0:T(8,128)(2,1)} %collective-permute-done.1), kind=kLoop, calls=%fused_computation.76 | loop fusion | bytes 524288 | tf_op jit(solution)/shard_map/slice | solution.py:93
  29.5 0.5 %fusion.10 = (f32[4,8,128]{2,1,0:T(8,128)S(1)}, f32[4,128,128,8]{2,1,3,0:T(8,128)S(1)}) fusion(pred[128,128]{0,1:T(8,128)(4,1)S(1)} %get-tuple-element.54, bf16[128,4,128,1]{0,2,3,1:T(8,128)(2,1)S(1)} %bitcast.228, bf16[128,4,8,128]{0,3,2,1:T(8,128)(2,1)S(1)} %bitcast.218), kind=kOutput, calls=%fused_computation.24 | convolution fusion | flops 135786496 | bytes 3309568 | tf_op jit(solution)/shard_map/tghd,sgd->ghts/dot_general | solution.py:33
  30.1 1.0 %fusion.5 = (f32[4,8,128]{2,1,0:T(8,128)S(1)}, f32[4,8,128]{2,1,0:T(8,128)S(1)}, f32[4,128,128,8]{2,1,3,0:T(8,128)S(1)}) fusion(f32[4,128,128,8]{2,1,3,0:T(8,128)S(1)} %get-tuple-element.61, f32[4,8,128]{2,1,0:T(8,128)S(1)} %fusion.30, pred[128,128]{0,1:T(8,128)(4,1)S(1)} %get-tuple-element.54, bf16[128,4,128,1]{0,2,3,1:T(8,128)(2,1)S(1)} %bitcast.234, ...), kind=kOutput, calls=%fused_computation.11 | convolution fusion | flops 137355264 | bytes 5439488 | tf_op jit(solution)/shard_map/tghd,sgd->ghts/dot_general | solution.py:106
  31.1 1.4 %multiply_convert_fusion = (bf16[4,8,128,128]{2,3,1,0:T(8,128)(2,1)S(1)}, bf16[4,8,128,128]{2,3,1,0:T(8,128)(2,1)S(1)}) fusion(f32[4,8,128,128]{2,3,1,0:T(8,128)S(1)} %get-tuple-element.18, f32[4,8,128,128]{2,3,1,0:T(8,128)S(1)} %get-tuple-element.17, f32[4,8,128]{2,1,0:T(8,128)S(1)} %get-tuple-element.50, f32[4,8,128]{2,1,0:T(8,128)S(1)} %bitcast.241, ...), kind=kLoop, calls=%fused_computation.17 | loop fusion | flops 6291456 | bytes 10567680 | tf_op jit(solution)/shard_map/convert_element_type | solution.py:116
  32.9 1.9 %collective-permute-start.3 = (bf16[4,128,128]{2,1,0:T(8,128)(2,1)S(1)}, bf16[4,128,128]{2,1,0:T(8,128)(2,1)S(1)}, u32[]{:S(2)}, u32[]{:S(2)}) collective-permute-start(bf16[4,128,128]{2,1,0:T(8,128)(2,1)S(1)} %fusion.14), channel_id=1, source_target_pairs={{4,0},{6,2},{8,4},{10,6},{12,8},{14,10},{16,12},{18,14},{20,16},{2... | collective-permute-start | bytes 393224 | tf_op jit(solution)/shard_map/ppermute | solution.py:16
  34.9 1.1 %fusion.15 = bf16[4,128,128]{2,1,0:T(8,128)(2,1)} fusion(bf16[4,8,128,128]{2,3,1,0:T(8,128)(2,1)S(1)} %get-tuple-element.23, bf16[128,4,8,128]{0,3,2,1:T(8,128)(2,1)S(1)} %bitcast.220), kind=kOutput, calls=%fused_computation.33 | convolution fusion | flops 134348800 | bytes 2228224 | tf_op jit(solution)/shard_map/ghts,tghd->gsd/dot_general | solution.py:41
  36.0 3.0 %collective-permute-start.2 = (bf16[4,128,128]{2,1,0:T(8,128)(2,1)}, bf16[4,128,128]{2,1,0:T(8,128)(2,1)S(1)}, u32[]{:S(2)}, u32[]{:S(2)}) collective-permute-start(bf16[4,128,128]{2,1,0:T(8,128)(2,1)} %fusion.15), channel_id=1, source_target_pairs={{2,0},{4,2},{6,4},{8,6},{10,8},{12,10},{14,12},{16,14},{18,16},{20... | collective-permute-start | bytes 393224 | tf_op jit(solution)/shard_map/ppermute | solution.py:16
  39.0 0.8 %fusion.4 = bf16[4,8,128,128]{2,3,1,0:T(8,128)(2,1)S(1)} fusion(f32[4,128,128,8]{2,1,3,0:T(8,128)S(1)} %get-tuple-element.65, f32[4,128,128,8]{2,1,3,0:T(8,128)S(1)} %get-tuple-element.63, f32[4,8,128]{2,1,0:T(8,128)S(1)} %bitcast.242, f32[4,8,128]{2,1,0:T(8,128)S(1)} %bitcast.245, f32[4,8,128]{2,1,0:T(8,128)S(1)} %get-tuple-element.62, ...), kind=kLoop, calls=%fused_computation.8 | loop fusion | flops 3670016 | bytes 5308416 | tf_op jit(solution)/shard_map/convert_element_type | solution.py:127
  41.1 1.3 %copy.77 = bf16[128,4096]{1,0:T(8,128)(2,1)} copy(bf16[128,4096]{0,1:T(8,128)(2,1)S(1)} %bitcast.225) | data formatting | bytes 2097152
  43.0 0.7 %pad_maximum_fusion.1 = bf16[128,512]{1,0:T(8,128)(2,1)} fusion(bf16[128,128]{1,0:T(8,128)(2,1)S(1)} %get-tuple-element.47, bf16[128,128]{1,0:T(8,128)(2,1)S(1)} %get-tuple-element.48, bf16[128,128]{1,0:T(8,128)(2,1)S(1)} %get-tuple-element.49, bf16[128,128]{1,0:T(8,128)(2,1)S(1)} %get-tuple-element.46), kind=kLoop, calls=%fused_computation.43 | loop fusion | flops 524288 | bytes 262144 | tf_op jit(solution)/shard_map/concatenate | solution.py:136
  (28 shorter events, 3.7 us)
Async XLA Ops:
  0.6 14.3 %copy-start = (bf16[128,4096]{1,0:T(8,128)(2,1)S(1)}, bf16[128,4096]{1,0:T(8,128)(2,1)}, u32[]{:S(2)}) copy-start(bf16[128,4096]{1,0:T(8,128)(2,1)} %param.5) | copy-start | bytes 3145732
  0.6 15.0 %copy-start.1 = (bf16[128,4096]{1,0:T(8,128)(2,1)S(1)}, bf16[128,4096]{1,0:T(8,128)(2,1)}, u32[]{:S(2)}) copy-start(bf16[128,4096]{1,0:T(8,128)(2,1)} %param.8) | copy-start | bytes 3145732
  3.6 14.0 %collective-permute-start = (bf16[2,128,512]{1,2,0:T(8,128)(2,1)}, bf16[2,128,512]{1,2,0:T(8,128)(2,1)}, u32[]{:S(2)}, u32[]{:S(2)}) collective-permute-start(bf16[2,128,512]{1,2,0:T(8,128)(2,1)} %pad_maximum_fusion), channel_id=1, source_target_pairs={{0,2},{2,4},{4,6},{6,8},{8,10},{10,12},{12,14},{14,16},{16,18},{18... | collective-permute-start | bytes 786440 | tf_op jit(solution)/shard_map/ppermute | solution.py:16
  7.6 20.9 %collective-permute-start.1 = (bf16[2,128,512]{1,2,0:T(8,128)(2,1)}, bf16[2,128,512]{1,2,0:T(8,128)(2,1)}, u32[]{:S(2)}, u32[]{:S(2)}) collective-permute-start(bf16[2,128,512]{1,2,0:T(8,128)(2,1)} %pad_maximum_fusion), channel_id=1, source_target_pairs={{0,4},{2,6},{4,8},{6,10},{8,12},{10,14},{12,16},{14,18},{16,20},{1... | collective-permute-start | bytes 786440 | tf_op jit(solution)/shard_map/ppermute | solution.py:16
  32.9 9.6 %collective-permute-start.3 = (bf16[4,128,128]{2,1,0:T(8,128)(2,1)S(1)}, bf16[4,128,128]{2,1,0:T(8,128)(2,1)S(1)}, u32[]{:S(2)}, u32[]{:S(2)}) collective-permute-start(bf16[4,128,128]{2,1,0:T(8,128)(2,1)S(1)} %fusion.14), channel_id=1, source_target_pairs={{4,0},{6,2},{8,4},{10,6},{12,8},{14,10},{16,12},{18,14},{20,16},{2... | collective-permute-start | bytes 393224 | tf_op jit(solution)/shard_map/ppermute | solution.py:16
  36.0 6.5 %collective-permute-start.2 = (bf16[4,128,128]{2,1,0:T(8,128)(2,1)}, bf16[4,128,128]{2,1,0:T(8,128)(2,1)S(1)}, u32[]{:S(2)}, u32[]{:S(2)}) collective-permute-start(bf16[4,128,128]{2,1,0:T(8,128)(2,1)} %fusion.15), channel_id=1, source_target_pairs={{2,0},{4,2},{6,4},{8,6},{10,8},{12,10},{14,12},{16,14},{18,16},{20... | collective-permute-start | bytes 393224 | tf_op jit(solution)/shard_map/ppermute | solution.py:16

commit v22 on v21

--- a/solution.py
+++ b/solution.py
@@ -111,9 +111,10 @@
         + near_dot * near_rescale
         + jnp.sum(far_exp * far_grad_p, axis=-1, keepdims=True)
     ) / row_sum
-    near_exp = near_exp * near_rescale
     far_grad_s = ((far_exp / row_sum) * (far_grad_p - row_delta)).astype(jnp.bfloat16)
-    near_grad_s = ((near_exp / row_sum) * (near_grad_p - row_delta)).astype(jnp.bfloat16)
+    near_grad_s = ((near_exp * (near_rescale / row_sum)) * (near_grad_p - row_delta)).astype(
+        jnp.bfloat16
+    )
     far_key_grad = key_grad_of(far_grad_s, query_heads, score_scale).astype(jnp.bfloat16)
     far_back = shifted(far_key_grad, axes, -2)
     far_key_grad, near_grad_s = lax.optimization_barrier((far_key_grad, near_grad_s))

time: 44.4 us -> 44.4 us (level)
  no operation moved by 1% of the time
where the time goes in v22:
time: 44.4 us; the launch traced here: 43.6 us
  starting transfers between devices  13.2 us (30%)
  local copies, waits for them, and re-layouts  9.16 us (21%)
  waiting for transfers between devices  8.55 us (19%)
  matrix products  7.75 us (17%)
  other arithmetic  4.09 us (9%)
  between operations  0.91 us (2%)
    ppermute x4, starting transfers between devices, shifted(): return lax.ppermute(block, axis, route)  13.2 us
    ppermute x4, waiting for transfers between devices, shifted(): return lax.ppermute(block, axis, route)  8.55 us
    unnamed x8, local copies, waits for them, and re-layouts  3.76 us
    dot_general x3, matrix products, key_grad_of(): jnp.einsum('ghts,tghd->gsd', grad_s, query_heads, preferred_element_type=...  1.97 us
    dot_general x3, matrix products, scores_of(): jnp.einsum('tghd,sgd->ghts', query_heads, key_heads, preferred_element_ty...  1.52 us
    convert_element_type x1, other arithmetic, body(): (near_exp * (near_rescale / row_sum) * (near_grad_p - row_delta)).astype(...  1.39 us
    dot_general x3, matrix products, query_grad_of(): jnp.einsum('ghts,sgd->tghd', grad_s, keys, preferred_element_type=jnp.flo...  1.32 us
    reshape x2, local copies, waits for them, and re-layouts, body(): own_keys = key_vectors.reshape(rows, KVH, HD)  1.08 us
  transfers between devices with their start and end apart: 4, of which 2 were waited for; matrix products, arithmetic and copies ran while one was open for 29% of the time, Pallas kernels for 0%

profile of v22, /device:TPU:1, one launch (start us, length us, event | category | flops | bytes accessed | tf_op | source)
XLA Modules:
  0.0 43.6 jit_solution(13016071403575935593)
XLA Ops:
  0.6 1.2 %copy.56 = bf16[128,512]{0,1:T(8,128)(2,1)S(1)} copy(bf16[128,512]{1,0:T(8,128)(2,1)} %param.6) | data formatting | bytes 262144 | tf_op args[1]
  1.8 1.0 %copy.57 = bf16[128,512]{0,1:T(8,128)(2,1)S(1)} copy(bf16[128,512]{1,0:T(8,128)(2,1)} %param.7) | data formatting | bytes 262144 | tf_op args[2]
  2.9 0.7 %pad_maximum_fusion = bf16[2,128,512]{1,2,0:T(8,128)(2,1)} fusion(bf16[1,128,512]{1,2,0:T(8,128)(2,1)S(1)} %bitcast.236, bf16[1,128,512]{1,2,0:T(8,128)(2,1)S(1)} %bitcast.235), kind=kLoop, calls=%fused_computation.41 | loop fusion | flops 131072 | bytes 524288 | tf_op jit(solution)/shard_map/stack | solution.py:54
  3.6 4.0 %collective-permute-start = (bf16[2,128,512]{1,2,0:T(8,128)(2,1)}, bf16[2,128,512]{1,2,0:T(8,128)(2,1)}, u32[]{:S(2)}, u32[]{:S(2)}) collective-permute-start(bf16[2,128,512]{1,2,0:T(8,128)(2,1)} %pad_maximum_fusion), channel_id=1, source_target_pairs={{0,2},{2,4},{4,6},{6,8},{8,10},{10,12},{12,14},{14,16},{16,18},{18... | collective-permute-start | bytes 786440 | tf_op jit(solution)/shard_map/ppermute | solution.py:16
  7.6 4.2 %collective-permute-start.1 = (bf16[2,128,512]{1,2,0:T(8,128)(2,1)}, bf16[2,128,512]{1,2,0:T(8,128)(2,1)}, u32[]{:S(2)}, u32[]{:S(2)}) collective-permute-start(bf16[2,128,512]{1,2,0:T(8,128)(2,1)} %pad_maximum_fusion), channel_id=1, source_target_pairs={{0,4},{2,6},{4,8},{6,10},{8,12},{10,14},{12,16},{14,18},{16,20},{1... | collective-permute-start | bytes 786440 | tf_op jit(solution)/shard_map/ppermute | solution.py:16
  11.9 0.9 %reshape.256 = bf16[128,4,128]{2,1,0:T(4,128)(2,1)S(1)} reshape(bf16[128,512]{1,0:T(8,128)(2,1)} %param.6) | data formatting | bytes 262144 | tf_op jit(solution)/shard_map/reshape | solution.py:60
  12.8 0.9 %reshape.259 = bf16[128,4,128]{2,1,0:T(4,128)(2,1)S(1)} reshape(bf16[128,512]{1,0:T(8,128)(2,1)} %param.7) | data formatting | bytes 262144 | tf_op jit(solution)/shard_map/reshape | solution.py:61
  13.8 0.7 %copy.53 = s32[16,1]{1,0:T(8,128)S(1)} copy(s32[16,1]{0,1:T(1,128)} %bitcast.246) | data formatting | bytes 128 | tf_op jit(solution)/shard_map/reshape.234
  14.9 0.7 %copy.109 = bf16[128,4096]{0,1:T(8,128)(2,1)S(1)} copy(bf16[128,4096]{1,0:T(8,128)(2,1)S(1)} %copy-done) | data formatting | bytes 2097152 | tf_op jit(solution)/shard_map/reshape | solution.py:58
  16.0 0.5 %fusion.8 = (f32[4,8,128]{2,1,0:T(8,128)S(1)}, f32[4,128,128,8]{2,1,3,0:T(8,128)S(1)}) fusion(pred[128,128]{0,1:T(8,128)(4,1)S(1)} %get-tuple-element.55, bf16[128,4,128,1]{0,2,3,1:T(8,128)(2,1)S(1)} %copy.87, bf16[128,4,8,128]{0,3,2,1:T(8,128)(2,1)S(1)} %bitcast.216), kind=kOutput, calls=%fused_computation.22 | convolution fusion | flops 135786496 | bytes 3309568 | tf_op jit(solution)/shard_map/tghd,sgd->ghts/dot_general | solution.py:33
  16.6 1.0 %fusion.2 = (f32[4,8,128]{2,1,0:T(8,128)S(1)}, f32[4,8,128]{2,1,0:T(8,128)S(1)}, f32[4,128,128,8]{2,1,3,0:T(8,128)S(1)}) fusion(f32[4,128,128,8]{2,1,3,0:T(8,128)S(1)} %get-tuple-element.61, f32[4,8,128]{2,1,0:T(8,128)S(1)} %get-tuple-element.60, pred[128,128]{0,1:T(8,128)(4,1)S(1)} %get-tuple-element.55, bf16[128,4,8,128]{3,2,1,0:T(8,128)(2,1)S(1)} %bitcast.222, ...), kind=kOutput, calls=%fused_computation.6 | convolution fusion | flops 137355264 | bytes 5439488 | tf_op jit(solution)/shard_map/tghd,sgd->ghts/dot_general | solution.py:72
  17.6 1.0 %fusion.31 = (bf16[1,128,512]{1,2,0:T(8,128)(2,1)S(1)}, bf16[1,128,512]{1,2,0:T(8,128)(2,1)S(1)}) fusion(bf16[2,128,512]{1,2,0:T(8,128)(2,1)} %collective-permute-done), kind=kLoop, calls=%fused_computation.77 | loop fusion | bytes 524288 | tf_op jit(solution)/shard_map/slice | solution.py:78
  19.1 1.0 %multiply_reduce_fusion = (f32[4,8,128]{2,1,0:T(8,128)S(1)}, f32[4,8,128]{2,1,0:T(8,128)S(1)}, f32[4,8,128,128]{2,3,1,0:T(8,128)S(1)}, f32[4,8,128,128]{2,3,1,0:T(8,128)S(1)}) fusion(f32[4,8,128]{2,1,0:T(8,128)S(1)} %get-tuple-element.57, f32[4,128,128,8]{2,1,3,0:T(8,128)S(1)} %get-tuple-element.58, pred[128,128]{0,1:T(8,128)(4,1)S(1)} %get-tuple-element.56, ...), kind=kOutput, calls=%fused_computation.19 | convolution fusion | flops 137355264 | bytes 7536640 | tf_op jit(solution)/shard_map/tghd,sgd->ghts/dot_general | solution.py:83
  20.1 8.5 %collective-permute-done.1 = bf16[2,128,512]{1,2,0:T(8,128)(2,1)} collective-permute-done((bf16[2,128,512]{1,2,0:T(8,128)(2,1)}, bf16[2,128,512]{1,2,0:T(8,128)(2,1)}, u32[]{:S(2)}, u32[]{:S(2)}) %collective-permute-start.1) | collective-permute-done | bytes 262176 | tf_op jit(solution)/shard_map/ppermute | solution.py:16
  28.5 1.0 %fusion.30 = (bf16[1,128,512]{1,2,0:T(8,128)(2,1)S(1)}, bf16[1,128,512]{1,2,0:T(8,128)(2,1)S(1)}) fusion(bf16[2,128,512]{1,2,0:T(8,128)(2,1)} %collective-permute-done.1), kind=kLoop, calls=%fused_computation.76 | loop fusion | bytes 524288 | tf_op jit(solution)/shard_map/slice | solution.py:93
  29.5 0.5 %fusion.10 = (f32[4,8,128]{2,1,0:T(8,128)S(1)}, f32[4,128,128,8]{2,1,3,0:T(8,128)S(1)}) fusion(pred[128,128]{0,1:T(8,128)(4,1)S(1)} %get-tuple-element.54, bf16[128,4,128,1]{0,2,3,1:T(8,128)(2,1)S(1)} %bitcast.228, bf16[128,4,8,128]{0,3,2,1:T(8,128)(2,1)S(1)} %bitcast.218), kind=kOutput, calls=%fused_computation.24 | convolution fusion | flops 135786496 | bytes 3309568 | tf_op jit(solution)/shard_map/tghd,sgd->ghts/dot_general | solution.py:33
  30.1 1.0 %fusion.5 = (f32[4,8,128]{2,1,0:T(8,128)S(1)}, f32[4,8,128]{2,1,0:T(8,128)S(1)}, f32[4,128,128,8]{2,1,3,0:T(8,128)S(1)}) fusion(f32[4,128,128,8]{2,1,3,0:T(8,128)S(1)} %get-tuple-element.63, f32[4,8,128]{2,1,0:T(8,128)S(1)} %fusion.29, pred[128,128]{0,1:T(8,128)(4,1)S(1)} %get-tuple-element.54, bf16[128,4,128,1]{0,2,3,1:T(8,128)(2,1)S(1)} %bitcast.234, ...), kind=kOutput, calls=%fused_computation.11 | convolution fusion | flops 137355264 | bytes 5439488 | tf_op jit(solution)/shard_map/tghd,sgd->ghts/dot_general | solution.py:106
  31.1 1.4 %multiply_convert_fusion = (bf16[4,8,128,128]{2,3,1,0:T(8,128)(2,1)S(1)}, bf16[4,8,128,128]{2,3,1,0:T(8,128)(2,1)S(1)}) fusion(f32[4,8,128,128]{2,3,1,0:T(8,128)S(1)} %get-tuple-element.18, f32[4,8,128,128]{2,3,1,0:T(8,128)S(1)} %get-tuple-element.17, f32[4,8,128]{2,1,0:T(8,128)S(1)} %get-tuple-element.50, f32[4,8,128]{2,1,0:T(8,128)S(1)} %bitcast.241, ...), kind=kLoop, calls=%fused_computation.17 | loop fusion | flops 5767168 | bytes 10567680 | tf_op jit(solution)/shard_map/convert_element_type | solution.py:115
  32.9 1.9 %collective-permute-start.3 = (bf16[4,128,128]{2,1,0:T(8,128)(2,1)S(1)}, bf16[4,128,128]{2,1,0:T(8,128)(2,1)S(1)}, u32[]{:S(2)}, u32[]{:S(2)}) collective-permute-start(bf16[4,128,128]{2,1,0:T(8,128)(2,1)S(1)} %fusion.14), channel_id=1, source_target_pairs={{4,0},{6,2},{8,4},{10,6},{12,8},{14,10},{16,12},{18,14},{20,16},{2... | collective-permute-start | bytes 393224 | tf_op jit(solution)/shard_map/ppermute | solution.py:16
  34.9 1.1 %fusion.15 = bf16[4,128,128]{2,1,0:T(8,128)(2,1)} fusion(bf16[4,8,128,128]{2,3,1,0:T(8,128)(2,1)S(1)} %get-tuple-element.23, bf16[128,4,8,128]{0,3,2,1:T(8,128)(2,1)S(1)} %bitcast.220), kind=kOutput, calls=%fused_computation.33 | convolution fusion | flops 134348800 | bytes 2228224 | tf_op jit(solution)/shard_map/ghts,tghd->gsd/dot_general | solution.py:41
  36.0 3.0 %collective-permute-start.2 = (bf16[4,128,128]{2,1,0:T(8,128)(2,1)}, bf16[4,128,128]{2,1,0:T(8,128)(2,1)S(1)}, u32[]{:S(2)}, u32[]{:S(2)}) collective-permute-start(bf16[4,128,128]{2,1,0:T(8,128)(2,1)} %fusion.15), channel_id=1, source_target_pairs={{2,0},{4,2},{6,4},{8,6},{10,8},{12,10},{14,12},{16,14},{18,16},{20... | collective-permute-start | bytes 393224 | tf_op jit(solution)/shard_map/ppermute | solution.py:16
  39.0 0.8 %fusion.4 = bf16[4,8,128,128]{2,3,1,0:T(8,128)(2,1)S(1)} fusion(f32[4,128,128,8]{2,1,3,0:T(8,128)S(1)} %get-tuple-element.65, f32[4,128,128,8]{2,1,3,0:T(8,128)S(1)} %get-tuple-element.61, f32[4,8,128]{2,1,0:T(8,128)S(1)} %bitcast.242, f32[4,8,128]{2,1,0:T(8,128)S(1)} %bitcast.245, f32[4,8,128]{2,1,0:T(8,128)S(1)} %get-tuple-element.60, ...), kind=kLoop, calls=%fused_computation.8 | loop fusion | flops 3670016 | bytes 5308416 | tf_op jit(solution)/shard_map/convert_element_type | solution.py:128
  41.1 1.3 %copy.77 = bf16[128,4096]{1,0:T(8,128)(2,1)} copy(bf16[128,4096]{0,1:T(8,128)(2,1)S(1)} %bitcast.225) | data formatting | bytes 2097152
  43.0 0.7 %pad_maximum_fusion.1 = bf16[128,512]{1,0:T(8,128)(2,1)} fusion(bf16[128,128]{1,0:T(8,128)(2,1)S(1)} %get-tuple-element.47, bf16[128,128]{1,0:T(8,128)(2,1)S(1)} %get-tuple-element.48, bf16[128,128]{1,0:T(8,128)(2,1)S(1)} %get-tuple-element.49, bf16[128,128]{1,0:T(8,128)(2,1)S(1)} %get-tuple-element.46), kind=kLoop, calls=%fused_computation.43 | loop fusion | flops 524288 | bytes 262144 | tf_op jit(solution)/shard_map/concatenate | solution.py:137
  (28 shorter events, 3.7 us)
Async XLA Ops:
  0.6 14.3 %copy-start = (bf16[128,4096]{1,0:T(8,128)(2,1)S(1)}, bf16[128,4096]{1,0:T(8,128)(2,1)}, u32[]{:S(2)}) copy-start(bf16[128,4096]{1,0:T(8,128)(2,1)} %param.5) | copy-start | bytes 3145732
  0.6 15.0 %copy-start.1 = (bf16[128,4096]{1,0:T(8,128)(2,1)S(1)}, bf16[128,4096]{1,0:T(8,128)(2,1)}, u32[]{:S(2)}) copy-start(bf16[128,4096]{1,0:T(8,128)(2,1)} %param.8) | copy-start | bytes 3145732
  3.6 14.0 %collective-permute-start = (bf16[2,128,512]{1,2,0:T(8,128)(2,1)}, bf16[2,128,512]{1,2,0:T(8,128)(2,1)}, u32[]{:S(2)}, u32[]{:S(2)}) collective-permute-start(bf16[2,128,512]{1,2,0:T(8,128)(2,1)} %pad_maximum_fusion), channel_id=1, source_target_pairs={{0,2},{2,4},{4,6},{6,8},{8,10},{10,12},{12,14},{14,16},{16,18},{18... | collective-permute-start | bytes 786440 | tf_op jit(solution)/shard_map/ppermute | solution.py:16
  7.6 20.9 %collective-permute-start.1 = (bf16[2,128,512]{1,2,0:T(8,128)(2,1)}, bf16[2,128,512]{1,2,0:T(8,128)(2,1)}, u32[]{:S(2)}, u32[]{:S(2)}) collective-permute-start(bf16[2,128,512]{1,2,0:T(8,128)(2,1)} %pad_maximum_fusion), channel_id=1, source_target_pairs={{0,4},{2,6},{4,8},{6,10},{8,12},{10,14},{12,16},{14,18},{16,20},{1... | collective-permute-start | bytes 786440 | tf_op jit(solution)/shard_map/ppermute | solution.py:16
  32.9 9.6 %collective-permute-start.3 = (bf16[4,128,128]{2,1,0:T(8,128)(2,1)S(1)}, bf16[4,128,128]{2,1,0:T(8,128)(2,1)S(1)}, u32[]{:S(2)}, u32[]{:S(2)}) collective-permute-start(bf16[4,128,128]{2,1,0:T(8,128)(2,1)S(1)} %fusion.14), channel_id=1, source_target_pairs={{4,0},{6,2},{8,4},{10,6},{12,8},{14,10},{16,12},{18,14},{20,16},{2... | collective-permute-start | bytes 393224 | tf_op jit(solution)/shard_map/ppermute | solution.py:16
  36.0 6.5 %collective-permute-start.2 = (bf16[4,128,128]{2,1,0:T(8,128)(2,1)}, bf16[4,128,128]{2,1,0:T(8,128)(2,1)S(1)}, u32[]{:S(2)}, u32[]{:S(2)}) collective-permute-start(bf16[4,128,128]{2,1,0:T(8,128)(2,1)} %fusion.15), channel_id=1, source_target_pairs={{2,0},{4,2},{6,4},{8,6},{10,8},{12,10},{14,12},{16,14},{18,16},{20... | collective-permute-start | bytes 393224 | tf_op jit(solution)/shard_map/ppermute | solution.py:16
